TPU v7x, 256 devices: a whole 4x4x8 slice. The times are simulated.
256 devices in a mesh: dp: 64 (over x, y_hi, z), tensor: 4 (over y_lo, core).
Axes of the slice: x: 4, y: 4 (y_hi: 2, y_lo: 2; y = y_hi * 2 + y_lo), z: 8, core: 2. Of those that a mesh axis runs over, the one named last changes fastest.
Arguments:
- residual: bfloat16 [512, 64, 4096], P('dp', None, 'tensor'), may hold values from -128 to 128
- queries: bfloat16 [512, 64, 4096], P('dp', None, 'tensor'), may hold values from -30 to 30
- attn_keys: bfloat16 [512, 64, 512], P('dp', None, 'tensor'), may hold values from -6 to 6
- values: bfloat16 [512, 64, 512], P('dp', None, 'tensor'), may hold values from -6 to 6
- out_weight: bfloat16 [4096, 4096], P('tensor'), may hold values from -0.09375 to 0.09375
- norm_gain: float32 [4096], P('tensor'), may hold values from 0.1 to 1.9
- probe_weight: float32 [4096, 64], P('tensor'), may hold values from -0.09375 to 0.09375
- partner_slot: int32 [512], P('dp'), may hold values from 0 to 7, as said below
- patch_list: int32 [512, 64, 2], P('dp', 'tensor'), may hold values from 0 to 63, as said below
- concept_labels: int32 [512, 64], P('dp'), may hold values from 0 to 63
Outputs:
- attn_out: bfloat16 [512, 64, 4096], P('dp', None, 'tensor')
- logits: float32 [512, 64, 64], P('dp')
- probe_grad: float32 [4096, 64], P('tensor')
Inputs may be any that keep to these rules, and one draw needn't show every extreme that they name: Prompt j of device i of dp, for i below 32, is paired with prompt partner_slot of it on device i + 32, and that prompt's partner_slot is j; on each device the values are a permutation. `patch_list`: each entry is (head, position). A prompt's list equals its partner's, entry for entry. Its entries are distinct, and entries k * 16 to (k + 1) * 16 - 1 name heads of the k-th block of 8 consecutive heads.
All inputs are finite; a program needn't handle non-finite values.
Results may differ from a plain program's by a relative error of at most 0.01.
Values may be sent and summed in bfloat16 or wider, within the bound.
No kernel may reach another device: no remote copies, remote signals or barrier semaphores. Data moves between devices by JAX's collectives and lax.ppermute only.
A program may use at most 128 MiB of HBM per device.

v0:
```python
import math

import jax
import jax.numpy as jnp
from jax import lax
from jax.sharding import PartitionSpec as P

DW = 4096
HDIM = 128


norm_epsilon = 1e-05


def passed_along(block, axis, distance):
    devices = range(lax.axis_size(axis))
    route = [((i - distance) % len(devices), i) for i in devices]
    return lax.ppermute(block, axis, route)


def attend(queries, attn_keys, values):
    prompt_count = queries.shape[0]
    seq_length = queries.shape[1]
    local_kv = attn_keys.shape[2] // HDIM
    local_heads = queries.shape[2] // HDIM
    group_size = local_heads // local_kv
    query_blocks = queries.reshape(prompt_count, seq_length, local_kv, group_size, HDIM)
    key_blocks = attn_keys.reshape(prompt_count, seq_length, local_kv, HDIM)
    value_blocks = values.reshape(prompt_count, seq_length, local_kv, HDIM)
    scores = jnp.einsum(
        "pqkgd,pskd->pkgqs", query_blocks, key_blocks, preferred_element_type=jnp.float32
    ) / math.sqrt(HDIM)
    causal = jnp.arange(seq_length)[:, None] >= jnp.arange(seq_length)[None, :]
    scores = jnp.where(causal, scores, -jnp.inf)
    highest = jnp.max(scores, axis=-1, keepdims=True)
    exponent = jnp.exp(scores - highest)
    weights = (exponent / jnp.sum(exponent, axis=-1, keepdims=True)).astype(jnp.bfloat16)
    mixed_rows = jnp.einsum(
        "pkgqs,pskd->pqkgd", weights, value_blocks, preferred_element_type=jnp.float32
    )
    return mixed_rows.astype(jnp.bfloat16).reshape(prompt_count, seq_length, local_heads, HDIM)


def per_device(
    residual,
    queries,
    attn_keys,
    values,
    out_weight,
    norm_gain,
    probe_weight,
    partner_slot,
    patch_list,
    concept_labels,
):
    prompt_count = residual.shape[0]
    seq_length = residual.shape[1]
    feature_count = residual.shape[2]
    token_count = prompt_count * seq_length
    heads_out = attend(queries, attn_keys, values)
    local_heads = heads_out.shape[2]
    head_ids = patch_list[..., 0] % local_heads
    pos_ids = patch_list[..., 1]
    row_ids = jnp.broadcast_to(jnp.arange(prompt_count, dtype=jnp.int32)[:, None], head_ids.shape)
    patch_mask = (
        jnp.zeros((prompt_count, seq_length, local_heads), dtype=bool)
        .at[row_ids, pos_ids, head_ids]
        .set(True)
    )
    half_way = lax.axis_size("dp") // 2
    arrived = passed_along(heads_out, "dp", half_way)
    entry_values = arrived[partner_slot][row_ids, pos_ids, head_ids]
    incoming = jnp.zeros_like(heads_out).at[row_ids, pos_ids, head_ids].set(entry_values)
    patched = jnp.where(patch_mask[..., None], incoming, heads_out)
    partial_value = jnp.dot(
        patched.reshape(token_count, -1), out_weight, preferred_element_type=jnp.float32
    )
    attn_local = lax.psum_scatter(
        partial_value.astype(jnp.bfloat16), "tensor", scatter_dimension=1, tiled=True
    )
    hidden = residual.reshape(token_count, feature_count).astype(jnp.float32) + attn_local.astype(
        jnp.float32
    )
    square_local = jnp.sum(hidden * hidden, axis=1)
    scaled = hidden * norm_gain
    square_sum = lax.psum(square_local, "tensor")
    inverse_rms = lax.rsqrt(square_sum / DW + norm_epsilon)
    normed = scaled * inverse_rms[:, None]
    logit_part = jnp.dot(
        normed, probe_weight, precision=lax.Precision.HIGHEST, preferred_element_type=jnp.float32
    )
    logits = lax.psum(logit_part.astype(jnp.bfloat16), "tensor").astype(jnp.float32)
    classes = jnp.arange(probe_weight.shape[1], dtype=jnp.int32)
    target = (concept_labels.reshape(token_count)[:, None] == classes[None, :]).astype(jnp.float32)
    error = jax.nn.sigmoid(logits) - target
    total_tokens = token_count * lax.axis_size("dp")
    grad_local = lax.dot_general(
        normed,
        error,
        (((0,), (0,)), ((), ())),
        precision=lax.Precision.HIGHEST,
        preferred_element_type=jnp.float32,
    ) / math.sqrt(total_tokens)
    probe_grad = lax.psum(grad_local, "dp")
    return (
        attn_local.reshape(prompt_count, seq_length, feature_count),
        logits.reshape(prompt_count, seq_length, -1),
        probe_grad,
    )


def solution(mesh):
    return jax.shard_map(
        per_device,
        mesh=mesh,
        in_specs=(
            P("dp", None, "tensor"),
            P("dp", None, "tensor"),
            P("dp", None, "tensor"),
            P("dp", None, "tensor"),
            P("tensor", None),
            P("tensor"),
            P("tensor", None),
            P("dp"),
            P("dp", "tensor", None),
            P("dp", None),
        ),
        out_specs=(P("dp", None, "tensor"), P("dp", None, None), P("tensor", None)),
        check_vma=False,
    )
```

profile of v0, /device:TPU:24, one launch (start us, length us, event | category | flops | bytes accessed | tf_op | source)
XLA Modules:
  0.0 812.4 jit_solution(9259078480574834374)
XLA Ops:
  7.2 0.0 copy-start
  7.2 0.0 reduce-scatter.2.cloned.1.call-start
  7.2 1.2 copy-done
  8.4 0.0 copy-start.8
  8.4 2.1 fusion.33
  10.5 0.5 fusion
  11.0 0.0 copy-done.8
  11.0 0.0 copy-start.5
  11.0 0.6 fusion.3
  11.7 0.0 copy-start.1
  11.7 0.0 copy-start.10
  11.7 3.1 collective-permute-start
  14.8 0.0 copy-done.5
  14.8 0.5 broadcast.168
  15.3 0.7 fusion.32
  16.0 0.1 reshape.81
  16.1 0.1 reshape.87
  16.2 8.5 %scatter_fusion = pred[8,64,8]{1,2,0:T(8,128)(4,1)S(1)} fusion(pred[8,64,8]{1,2,0:T(8,128)(4,1)S(1)} %broadcast_in_dim.23, s32[128]{0:T(128)S(1)} %reshape.87, pred[128]{0:T(512)(128)(4,1)S(1)} %broadcast.130), kind=kCustom, calls=%fused_computation.2 | custom fusion | bytes 1920 | tf_op jit(solution)/shard_map/scatter | solution.py:68
  24.7 0.0 copy-done.10
  24.7 0.0 copy-done.1
  24.8 13.4 %collective-permute-done = bf16[8,64,8,128]{3,1,2,0:T(8,128)(2,1)S(1)} collective-permute-done((bf16[8,64,8,128]{3,1,2,0:T(8,128)(2,1)S(1)}, bf16[8,64,8,128]{3,1,2,0:T(8,128)(2,1)S(1)}, u32[]{:S(2)}, u32[]{:S(2)}) %collective-permute-start) | collective-permute-done | bytes 1048608 | tf_op jit(solution)/shard_map/ppermute | solution.py:18
  38.2 0.7 gather_fusion
  38.9 0.7 copy.19
  39.6 1.2 gather_fusion.1
  40.9 0.1 broadcast_in_dim.27
  41.0 8.0 scatter_fusion.1
  49.0 1.8 copy_select_fusion
  50.8 0.7 copy.21
  51.5 9.4 %convolution_convert_fusion = bf16[512,4096]{1,0:T(8,128)(2,1)} fusion(bf16[1024,4096]{1,0:T(8,128)(2,1)} %param.14, bf16[64,8,8,128]{3,2,1,0:T(8,128)(2,1)S(1)} %bitcast.52), kind=kOutput, calls=%fused_computation.4 | convolution fusion | flops 4297064448 | bytes 13631488 | tf_op jit(solution)/shard_map/dot_general | solution.py:75
  60.9 0.0 copy-start.2
  60.9 0.0 reduce-scatter.2.cloned.1.call-update
  60.9 0.0 copy-start.7
  60.9 0.0 copy-start.9
  60.9 0.0 copy-start.6
  61.0 0.0 all-reduce.3.cloned.1.call-start
  61.0 49.9 %reduce-scatter.2.cloned.1.call-done = bf16[512,1024]{1,0:T(8,128)(2,1)} async-done(((bf16[512,4096]{1,0:T(8,128)(2,1)}), bf16[512,1024]{1,0:T(8,128)(2,1)}) %reduce-scatter.2.cloned.1.call-update) | async-done | bytes 1048592 | tf_op jit(solution)/shard_map/reduce_scatter | solution.py:78
  110.9 0.0 copy-done.2
  110.9 0.0 copy-start.3
  110.9 1.7 multiply_reduce_fusion
  112.7 6.8 psum.21
  119.5 0.0 copy-done.7
  119.5 0.0 copy-done.9
  119.5 0.0 copy-done.3
  119.5 3.1 fusion.5
  122.6 0.0 all-reduce.3.cloned.1.call-update
  122.6 0.0 all-reduce.5.cloned.1.call-start
  122.7 0.0 copy-done.6
  122.7 0.1 eq.17
  122.8 41.2 %all-reduce.3.cloned.1.call-done = bf16[512,64]{0,1:T(8,128)(2,1)} async-done(((bf16[512,64]{0,1:T(8,128)(2,1)}), bf16[512,64]{0,1:T(8,128)(2,1)}) %all-reduce.3.cloned.1.call-update) | async-done | bytes 65552 | tf_op jit(solution)/shard_map/psum | solution.py:92
  164.0 0.0 copy-start.4
  164.0 3.5 fusion.4
  167.5 0.0 all-reduce.5.cloned.1.call-update
  167.5 0.0 copy-done.4
  167.5 0.8 copy.26
  168.3 635.9 %all-reduce.5.cloned.1.call-done = f32[1024,64]{0,1:T(8,128)} async-done(((f32[1024,64]{0,1:T(8,128)}), f32[1024,64]{0,1:T(8,128)}) %all-reduce.5.cloned.1.call-update) | async-done | bytes 262160 | tf_op jit(solution)/shard_map/psum | solution.py:104
  804.2 1.7 copy.44
  (7 shorter events, 0.1 us)
Async XLA Ops:
  7.2 1.2 copy-start
  7.2 103.8 %reduce-scatter.2.cloned.1.call-start = ((), (), s32[]{:S(2)}) async-start(), calls=%async_computation.1 | async-start | bytes 5242880 | tf_op jit(solution)/shard_map/reduce_scatter | solution.py:78
  8.4 2.6 copy-start.8
  11.0 3.8 copy-start.5
  11.7 13.1 %copy-start.1 = (bf16[8,64,8,128]{3,1,2,0:T(8,128)(2,1)}, bf16[8,64,8,128]{3,1,2,0:T(8,128)(2,1)S(1)}, u32[]{:S(2)}) copy-start(bf16[8,64,8,128]{3,1,2,0:T(8,128)(2,1)S(1)} %fusion.3) | copy-start | bytes 3145732
  11.7 13.0 %copy-start.10 = (s32[8]{0:T(128)S(1)}, s32[8]{0:T(128)}, u32[]{:S(2)}) copy-start(s32[8]{0:T(128)} %param.17) | copy-start | bytes 100
  11.7 26.5 %collective-permute-start = (bf16[8,64,8,128]{3,1,2,0:T(8,128)(2,1)S(1)}, bf16[8,64,8,128]{3,1,2,0:T(8,128)(2,1)S(1)}, u32[]{:S(2)}, u32[]{:S(2)}) collective-permute-start(bf16[8,64,8,128]{3,1,2,0:T(8,128)(2,1)S(1)} %fusion.3), channel_id=1, source_target_pairs={{128,0},{132,4},{136,8},{140,12},{144,16},{148,20},{152,24},{156,2... | collective-permute-start | bytes 3145736 | tf_op jit(solution)/shard_map/ppermute | solution.py:18
  60.9 50.0 %copy-start.2 = (bf16[8,64,1024]{2,1,0:T(8,128)(2,1)S(1)}, bf16[8,64,1024]{2,1,0:T(8,128)(2,1)}, u32[]{:S(2)}) copy-start(bf16[8,64,1024]{2,1,0:T(8,128)(2,1)} %param.10) | copy-start | bytes 3145732
  60.9 58.5 %copy-start.7 = (f32[1024,64]{0,1:T(8,128)S(1)}, f32[1024,64]{0,1:T(8,128)}, u32[]{:S(2)}) copy-start(f32[1024,64]{0,1:T(8,128)} %param.16) | copy-start | bytes 786436
  60.9 58.5 %copy-start.9 = (f32[1024]{0:T(1024)S(1)}, f32[1024]{0:T(1024)}, u32[]{:S(2)}) copy-start(f32[1024]{0:T(1024)} %param.15) | copy-start | bytes 12292
  60.9 61.7 %copy-start.6 = (s32[8,64]{1,0:T(8,128)S(1)}, s32[8,64]{1,0:T(8,128)}, u32[]{:S(2)}) copy-start(s32[8,64]{1,0:T(8,128)} %param.19) | copy-start | bytes 6148
  61.0 103.0 %all-reduce.3.cloned.1.call-start = ((), (), s32[]{:S(2)}) async-start(), calls=%async_computation.2 | async-start | bytes 131072 | tf_op jit(solution)/shard_map/psum | solution.py:92
  110.9 8.5 %copy-start.3 = (bf16[512,1024]{1,0:T(8,128)(2,1)S(1)}, bf16[512,1024]{1,0:T(8,128)(2,1)}, u32[]{:S(2)}) copy-start(bf16[512,1024]{1,0:T(8,128)(2,1)} %reduce-scatter.2.cloned.1.call-done) | copy-start | bytes 3145732
  122.6 681.6 %all-reduce.5.cloned.1.call-start = ((), (), s32[]{:S(2)}) async-start(), calls=%async_computation.3 | async-start | bytes 524288 | tf_op jit(solution)/shard_map/psum | solution.py:104
  164.0 3.5 copy-start.4
Sparse Core Ops, SparseCore 0:
  61.0 49.8 reduce-scatter.1
  122.7 41.2 all-reduce.2
  167.6 636.5 all-reduce.4
where the time goes:
time: 822 us; the launch traced here: 812 us
  waiting for transfers between devices  741 us (90%)
  local copies, waits for them, and re-layouts  24.5 us (3%)
  matrix products  18.7 us (2%)
  between operations  14 us (2%)
    psum x1, waiting for transfers between devices, per_device(): probe_grad = lax.psum(grad_local, 'dp')  636 us
    reduce_scatter x1, waiting for transfers between devices, per_device(): lax.psum_scatter(partial_value.astype(jnp.bfloat16), 'tensor', scatter_di...  49.9 us
    psum x1, waiting for transfers between devices, per_device(): lax.psum(logit_part.astype(jnp.bfloat16), 'tensor').astype(jnp.float32)  41.2 us
  transfers between devices with their start and end apart: 4, of which 4 were waited for; matrix products, arithmetic and copies ran while one was open for 1% of the time, Pallas kernels for 0%

commit v1 on v0

--- a/solution.py
+++ b/solution.py
@@ -12,10 +12,40 @@
 norm_epsilon = 1e-05
 
 
-def passed_along(block, axis, distance):
-    devices = range(lax.axis_size(axis))
-    route = [((i - distance) % len(devices), i) for i in devices]
-    return lax.ppermute(block, axis, route)
+def exchanged(block, axis, bit):
+    count = lax.axis_size(axis)
+    return lax.ppermute(block, axis, [(i, i ^ bit) for i in range(count)])
+
+
+def butterfly_sum(block, axis, bits):
+    for bit in bits:
+        block = block + exchanged(block, axis, bit)
+    return block
+
+
+def tree_all_reduce(block, axis, halving_bits, doubling_bits):
+    position = lax.axis_index(axis)
+    kept = []
+    for bit in halving_bits:
+        half = block.shape[0] // 2
+        upper = (position // bit) % 2 == 1
+        low, high = block[:half], block[half:]
+        mine = jnp.where(upper, high, low)
+        other = jnp.where(upper, low, high)
+        block = mine + exchanged(other, axis, bit)
+        kept.append((bit, upper))
+    block = butterfly_sum(block, axis, doubling_bits)
+    for bit, upper in reversed(kept):
+        other = exchanged(block, axis, bit)
+        block = jnp.where(upper, jnp.concatenate([other, block]), jnp.concatenate([block, other]))
+    return block
+
+
+def dp_bits(count):
+    low = [1 << k for k in range(count.bit_length() - 1)]
+    if count == 64:
+        return low[:3], low[3:]
+    return [], low
 
 
 def attend(queries, attn_keys, values):
@@ -59,19 +89,30 @@
     token_count = prompt_count * seq_length
     heads_out = attend(queries, attn_keys, values)
     local_heads = heads_out.shape[2]
-    head_ids = patch_list[..., 0] % local_heads
-    pos_ids = patch_list[..., 1]
-    row_ids = jnp.broadcast_to(jnp.arange(prompt_count, dtype=jnp.int32)[:, None], head_ids.shape)
-    patch_mask = (
-        jnp.zeros((prompt_count, seq_length, local_heads), dtype=bool)
-        .at[row_ids, pos_ids, head_ids]
-        .set(True)
-    )
+    rows = seq_length * local_heads
+    flat_heads = heads_out.reshape(prompt_count, rows, HDIM)
+
+    entry_rows = patch_list[..., 1] * local_heads + patch_list[..., 0] % local_heads
+    picks = entry_rows[:, :, None] == jnp.arange(rows, dtype=jnp.int32)[None, None, :]
+    pick_values = picks.astype(jnp.bfloat16)
+    own_entries = jnp.einsum(
+        "jkr,jrd->jkd", pick_values, flat_heads, preferred_element_type=jnp.float32
+    ).astype(jnp.bfloat16)
+
     half_way = lax.axis_size("dp") // 2
-    arrived = passed_along(heads_out, "dp", half_way)
-    entry_values = arrived[partner_slot][row_ids, pos_ids, head_ids]
-    incoming = jnp.zeros_like(heads_out).at[row_ids, pos_ids, head_ids].set(entry_values)
-    patched = jnp.where(patch_mask[..., None], incoming, heads_out)
+    arrived = exchanged(own_entries, "dp", half_way)
+    slot_pick = (
+        partner_slot[:, None] == jnp.arange(prompt_count, dtype=partner_slot.dtype)[None, :]
+    ).astype(jnp.bfloat16)
+    incoming = jnp.einsum(
+        "jm,mkd->jkd", slot_pick, arrived, preferred_element_type=jnp.float32
+    ).astype(jnp.bfloat16)
+    placed = jnp.einsum(
+        "jkr,jkd->jrd", pick_values, incoming, preferred_element_type=jnp.float32
+    ).astype(jnp.bfloat16)
+    patch_mask = jnp.any(picks, axis=1)
+    patched = jnp.where(patch_mask[..., None], placed, flat_heads)
+
     partial_value = jnp.dot(
         patched.reshape(token_count, -1), out_weight, preferred_element_type=jnp.float32
     )
@@ -83,14 +124,19 @@
     )
     square_local = jnp.sum(hidden * hidden, axis=1)
     scaled = hidden * norm_gain
-    square_sum = lax.psum(square_local, "tensor")
+    raw_part = jnp.dot(
+        scaled, probe_weight, precision=lax.Precision.HIGHEST, preferred_element_type=jnp.float32
+    )
+    concepts = probe_weight.shape[1]
+    packed = jnp.concatenate([raw_part, square_local[:, None]], axis=1)
+    tensor_count = lax.axis_size("tensor")
+    packed = butterfly_sum(packed, "tensor", [1 << k for k in range(tensor_count.bit_length() - 1)])
+    raw_logits = packed[:, :concepts]
+    square_sum = packed[:, concepts]
     inverse_rms = lax.rsqrt(square_sum / DW + norm_epsilon)
+    logits = raw_logits * inverse_rms[:, None]
     normed = scaled * inverse_rms[:, None]
-    logit_part = jnp.dot(
-        normed, probe_weight, precision=lax.Precision.HIGHEST, preferred_element_type=jnp.float32
-    )
-    logits = lax.psum(logit_part.astype(jnp.bfloat16), "tensor").astype(jnp.float32)
-    classes = jnp.arange(probe_weight.shape[1], dtype=jnp.int32)
+    classes = jnp.arange(concepts, dtype=jnp.int32)
     target = (concept_labels.reshape(token_count)[:, None] == classes[None, :]).astype(jnp.float32)
     error = jax.nn.sigmoid(logits) - target
     total_tokens = token_count * lax.axis_size("dp")
@@ -101,7 +147,8 @@
         precision=lax.Precision.HIGHEST,
         preferred_element_type=jnp.float32,
     ) / math.sqrt(total_tokens)
-    probe_grad = lax.psum(grad_local, "dp")
+    halving_bits, doubling_bits = dp_bits(lax.axis_size("dp"))
+    probe_grad = tree_all_reduce(grad_local, "dp", halving_bits, doubling_bits)
     return (
         attn_local.reshape(prompt_count, seq_length, feature_count),
         logits.reshape(prompt_count, seq_length, -1),

time: 822 us -> 156 us (0.19); the launches traced: 812 us -> 155 us
  waiting for transfers between devices: 741 us -> 82.1 us
  starting transfers between devices: 3.23 us -> 30.7 us
  local copies, waits for them, and re-layouts: 24.5 us -> 3.21 us
    psum x2 -> x0, waiting for transfers between devices: 677 us -> none  [the longest x1 636 us: per_device(): probe_grad = lax.psum(grad_local, 'dp')]
    ppermute x1 -> x12, starting transfers between devices: 3.11 us -> 30.6 us  [exchanged(): return lax.ppermute(block, axis, [(i, i ^ bit) for i in range(count)])]
    ppermute x1 -> x12, waiting for transfers between devices: 13.4 us -> 32.1 us  [exchanged(): return lax.ppermute(block, axis, [(i, i ^ bit) for i in range(count)])]
    scatter x2 -> x0, local copies, waits for them, and re-layouts: 16.5 us -> none  [the longest x1 8.48 us: per_device(): patch_mask = jnp.zeros((prompt_count, seq_length, local_heads), dtype=boo...]
  transfers between devices with their start and end apart: 4 -> 13, of which waited for: 4 -> 13; matrix products, arithmetic and copies ran while one was open for 1% -> 1% of each run, Pallas kernels for 0% -> 0%
where the time goes in v1:
time: 156 us; the launch traced here: 155 us
  waiting for transfers between devices  82.1 us (53%)
  starting transfers between devices  30.7 us (20%)
  matrix products  19.5 us (12%)
  between operations  14.3 us (9%)
  other arithmetic  4.89 us (3%)
  local copies, waits for them, and re-layouts  3.21 us (2%)
    reduce_scatter x1, waiting for transfers between devices, per_device(): lax.psum_scatter(partial_value.astype(jnp.bfloat16), 'tensor', scatter_di...  50 us
    ppermute x12, waiting for transfers between devices, exchanged(): return lax.ppermute(block, axis, [(i, i ^ bit) for i in range(count)])  32.1 us
    ppermute x12, starting transfers between devices, exchanged(): return lax.ppermute(block, axis, [(i, i ^ bit) for i in range(count)])  30.6 us
    dot_general x1, matrix products, per_device(): jnp.dot(patched.reshape(token_count, -1), out_weight, preferred_element_t...  9.41 us
  transfers between devices with their start and end apart: 13, of which 13 were waited for; matrix products, arithmetic and copies ran while one was open for 1% of the time, Pallas kernels for 0%

profile of v1, /device:TPU:24, one launch (start us, length us, event | category | flops | bytes accessed | tf_op | source)
XLA Modules:
  0.0 154.6 jit_solution(15696507746703510118)
XLA Ops:
  7.2 0.0 copy-start
  7.2 0.0 reduce-scatter.2.cloned.1.call-start
  7.2 0.8 fusion.45
  8.0 0.4 copy-done
  8.4 0.0 copy-start.8
  8.4 2.1 %fusion.46 = (f32[8,8,64]{2,1,0:T(8,128)S(1)}, f32[8,1,8,64,64]{3,4,2,0,1:T(8,128)S(1)}) fusion(bf16[8,64,128]{2,1,0:T(8,128)(2,1)} %param.12, pred[64,64]{0,1:T(8,128)(4,1)S(1)} %iota_compare_fusion.5, bf16[8,64,1024]{2,1,0:T(8,128)(2,1)S(1)} %copy-done), kind=kOutput, calls=%fused_computation.70 | convolution fusion | flops 67891200 | bytes 2248704 | tf_op jit(solution)/shard_map/pqkgd,pskd->pkgqs/dot_general | solution.py:60
  10.5 0.5 fusion.6
  11.0 0.0 copy-done.8
  11.0 0.0 copy-start.7
  11.0 0.6 fusion.7
  11.7 0.7 convolution_convert_fusion.3
  12.4 3.1 %collective-permute-start = (bf16[8,16,128]{2,1,0:T(8,128)(2,1)S(1)}, bf16[8,16,128]{2,1,0:T(8,128)(2,1)S(1)}, u32[]{:S(2)}, u32[]{:S(2)}) collective-permute-start(bf16[8,16,128]{2,1,0:T(8,128)(2,1)S(1)} %convolution_convert_fusion.3), channel_id=1, source_target_pairs={{0,128},{4,132},{8,136},{12,140},{16,144},{20,148},{24,152},{28,15... | collective-permute-start | bytes 98312 | tf_op jit(solution)/shard_map/ppermute | solution.py:17
  15.5 0.1 fusion.20
  15.6 2.3 %collective-permute-done = bf16[8,16,128]{2,1,0:T(8,128)(2,1)S(1)} collective-permute-done((bf16[8,16,128]{2,1,0:T(8,128)(2,1)S(1)}, bf16[8,16,128]{2,1,0:T(8,128)(2,1)S(1)}, u32[]{:S(2)}, u32[]{:S(2)}) %collective-permute-start) | collective-permute-done | bytes 32800 | tf_op jit(solution)/shard_map/ppermute | solution.py:17
  17.9 0.0 copy-done.7
  17.9 0.2 fusion.33
  18.1 1.6 %fusion.8 = bf16[8,512,128]{2,1,0:T(8,128)(2,1)S(1)} fusion(pred[8,512]{1,0:T(8,128)(4,1)S(1)} %fusion.20, bf16[8,64,1,8,128]{4,1,3,0,2:T(8,128)(2,1)S(1)} %fusion.7, s32[8,16]{1,0:T(8,128)S(1)} %fusion.37, bf16[8,16,128]{2,0,1:T(8,128)(2,1)S(1)} %fusion.33), kind=kOutput, calls=%fused_computation.14 | convolution fusion | flops 17891328 | bytes 2134528 | tf_op jit(solution)/shard_map/jkr,jkd->jrd/dot_general | solution.py:110
  19.6 0.5 reshape.53
  20.1 9.4 %convolution_convert_fusion = bf16[512,4096]{1,0:T(8,128)(2,1)} fusion(bf16[512,1024]{1,0:T(8,128)(2,1)S(1)} %reshape.53, bf16[1024,4096]{1,0:T(8,128)(2,1)} %param.14), kind=kOutput, calls=%fused_computation | convolution fusion | flops 4297064448 | bytes 13631488 | tf_op jit(solution)/shard_map/dot_general | solution.py:116
  29.5 0.0 copy-start.1
  29.5 0.0 reduce-scatter.2.cloned.1.call-update
  29.6 0.0 copy-start.3
  29.6 0.0 copy-start.5
  29.6 50.0 %reduce-scatter.2.cloned.1.call-done = bf16[512,1024]{1,0:T(8,128)(2,1)} async-done(((bf16[512,4096]{1,0:T(8,128)(2,1)}), bf16[512,1024]{1,0:T(8,128)(2,1)}) %reduce-scatter.2.cloned.1.call-update) | async-done | bytes 1048592 | tf_op jit(solution)/shard_map/reduce_scatter | solution.py:119
  79.6 0.0 copy-done.1
  79.6 0.0 copy-start.2
  79.6 1.7 %multiply_reduce_fusion = f32[512]{0:T(512)S(1)} fusion(bf16[512,1024]{1,0:T(8,128)(2,1)} %reduce-scatter.2.cloned.1.call-done, bf16[8,64,1024]{2,1,0:T(8,128)(2,1)S(1)} %copy-done.1), kind=kLoop, calls=%fused_computation.5 | loop fusion | flops 2620928 | bytes 2099200 | tf_op jit(solution)/shard_map/reduce_sum | solution.py:125
  81.3 0.0 copy-start.6
  81.3 0.0 copy-done.3
  81.3 0.0 copy-done.5
  81.3 0.0 copy-done.2
  81.4 2.4 %fusion.4 = f32[512,64]{0,1:T(8,128)S(1)} fusion(f32[1024,64]{0,1:T(8,128)S(1)} %copy-done.3, bf16[512,1024]{1,0:T(8,128)(2,1)S(1)} %copy-done.2, bf16[512,1024]{1,0:T(8,128)(2,1)S(1)} %bitcast.55, f32[1024]{0:T(1024)S(1)} %copy-done.5), kind=kOutput, calls=%fused_computation.9 | convolution fusion | flops 404750336 | bytes 2494464 | tf_op jit(solution)/shard_map/dot_general | solution.py:127
  83.8 0.3 collective-permute-start.1
  84.0 1.2 collective-permute-done.1
  85.2 1.3 collective-permute-start.2
  86.5 0.0 copy-done.6
  86.5 0.7 eq.68
  87.2 4.2 %collective-permute-done.2 = f32[512,65]{0,1:T(8,128)} collective-permute-done((f32[512,65]{0,1:T(8,128)S(1)}, f32[512,65]{0,1:T(8,128)}, u32[]{:S(2)}, u32[]{:S(2)}) %collective-permute-start.2) | collective-permute-done | bytes 133152 | tf_op jit(solution)/shard_map/ppermute | solution.py:17
  91.4 0.9 add.67
  92.3 0.0 copy-start.4
  92.3 2.6 %fusion.9 = f32[1024,64]{0,1:T(8,128)S(1)} fusion(bf16[512,1024]{1,0:T(8,128)(2,1)S(1)} %copy-done.2, bf16[512,1024]{1,0:T(8,128)(2,1)S(1)} %bitcast.56, f32[512]{0:T(512)S(1)} %bitcast.63, f32[1024]{0:T(1024)} %param.15, s32[512]{0:T(512)} %eq.68, f32[512,65]{0,1:T(8,128)S(1)} %add.67), kind=kOutput, calls=%fused_computation.15 | convolution fusion | flops 405569536 | bytes 2500608 | tf_op jit(solution)/shard_map/dot_general | solution.py:143
  94.9 0.0 copy-done.4
  94.9 1.8 %collective-permute-start.3 = (f32[512,64]{0,1:T(8,128)S(1)}, f32[512,64]{0,1:T(8,128)S(1)}, u32[]{:S(2)}, u32[]{:S(2)}) collective-permute-start(f32[512,64]{0,1:T(8,128)S(1)} %slice_select_fusion), channel_id=1, source_target_pairs={{0,4},{4,0},{8,12},{12,8},{16,20},{20,16},{24,28},{28,24},{32,36},... | collective-permute-start | bytes 393224 | tf_op jit(solution)/shard_map/ppermute | solution.py:17
  96.7 3.4 %collective-permute-done.3 = f32[512,64]{0,1:T(8,128)S(1)} collective-permute-done((f32[512,64]{0,1:T(8,128)S(1)}, f32[512,64]{0,1:T(8,128)S(1)}, u32[]{:S(2)}, u32[]{:S(2)}) %collective-permute-start.3) | collective-permute-done | bytes 131104 | tf_op jit(solution)/shard_map/ppermute | solution.py:17
  100.2 2.6 %collective-permute-start.4 = (f32[256,64]{0,1:T(8,128)S(1)}, f32[256,64]{0,1:T(8,128)S(1)}, u32[]{:S(2)}, u32[]{:S(2)}) collective-permute-start(f32[256,64]{0,1:T(8,128)S(1)} %slice_select_fusion.1), channel_id=1, source_target_pairs={{0,8},{4,12},{8,0},{12,4},{16,24},{20,28},{24,16},{28,20},{32,40},... | collective-permute-start | bytes 196616 | tf_op jit(solution)/shard_map/ppermute | solution.py:17
  102.8 2.6 %collective-permute-done.4 = f32[256,64]{0,1:T(8,128)S(1)} collective-permute-done((f32[256,64]{0,1:T(8,128)S(1)}, f32[256,64]{0,1:T(8,128)S(1)}, u32[]{:S(2)}, u32[]{:S(2)}) %collective-permute-start.4) | collective-permute-done | bytes 65568 | tf_op jit(solution)/shard_map/ppermute | solution.py:17
  105.5 6.5 %collective-permute-start.5 = (f32[128,64]{0,1:T(8,128)S(1)}, f32[128,64]{0,1:T(8,128)S(1)}, u32[]{:S(2)}, u32[]{:S(2)}) collective-permute-start(f32[128,64]{0,1:T(8,128)S(1)} %slice_select_fusion.2), channel_id=1, source_target_pairs={{0,16},{4,20},{8,24},{12,28},{16,0},{20,4},{24,8},{28,12},{32,48},... | collective-permute-start | bytes 98312 | tf_op jit(solution)/shard_map/ppermute | solution.py:17
  112.0 2.0 %collective-permute-done.5 = f32[128,64]{0,1:T(8,128)S(1)} collective-permute-done((f32[128,64]{0,1:T(8,128)S(1)}, f32[128,64]{0,1:T(8,128)S(1)}, u32[]{:S(2)}, u32[]{:S(2)}) %collective-permute-start.5) | collective-permute-done | bytes 32800 | tf_op jit(solution)/shard_map/ppermute | solution.py:17
  114.0 1.2 collective-permute-start.6
  115.2 4.3 %collective-permute-done.6 = f32[128,64]{0,1:T(8,128)S(1)} collective-permute-done((f32[128,64]{0,1:T(8,128)S(1)}, f32[128,64]{0,1:T(8,128)S(1)}, u32[]{:S(2)}, u32[]{:S(2)}) %collective-permute-start.6) | collective-permute-done | bytes 32800 | tf_op jit(solution)/shard_map/ppermute | solution.py:17
  119.5 1.5 collective-permute-start.7
  121.0 2.5 %collective-permute-done.7 = f32[128,64]{0,1:T(8,128)S(1)} collective-permute-done((f32[128,64]{0,1:T(8,128)S(1)}, f32[128,64]{0,1:T(8,128)S(1)}, u32[]{:S(2)}, u32[]{:S(2)}) %collective-permute-start.7) | collective-permute-done | bytes 32800 | tf_op jit(solution)/shard_map/ppermute | solution.py:17
  123.4 3.0 %collective-permute-start.8 = (f32[128,64]{0,1:T(8,128)S(1)}, f32[128,64]{0,1:T(8,128)S(1)}, u32[]{:S(2)}, u32[]{:S(2)}) collective-permute-start(f32[128,64]{0,1:T(8,128)S(1)} %add.78), channel_id=1, source_target_pairs={{0,128},{4,132},{8,136},{12,140},{16,144},{20,148},{24,152},{28,15... | collective-permute-start | bytes 98312 | tf_op jit(solution)/shard_map/ppermute | solution.py:17
  126.4 2.4 %collective-permute-done.8 = f32[128,64]{0,1:T(8,128)S(1)} collective-permute-done((f32[128,64]{0,1:T(8,128)S(1)}, f32[128,64]{0,1:T(8,128)S(1)}, u32[]{:S(2)}, u32[]{:S(2)}) %collective-permute-start.8) | collective-permute-done | bytes 32800 | tf_op jit(solution)/shard_map/ppermute | solution.py:17
  128.8 5.8 %collective-permute-start.9 = (f32[128,64]{0,1:T(8,128)S(1)}, f32[128,64]{0,1:T(8,128)S(1)}, u32[]{:S(2)}, u32[]{:S(2)}) collective-permute-start(f32[128,64]{0,1:T(8,128)S(1)} %add.79), channel_id=1, source_target_pairs={{0,16},{4,20},{8,24},{12,28},{16,0},{20,4},{24,8},{28,12},{32,48},... | collective-permute-start | bytes 98312 | tf_op jit(solution)/shard_map/ppermute | solution.py:17
  134.7 2.0 %collective-permute-done.9 = f32[128,64]{0,1:T(8,128)S(1)} collective-permute-done((f32[128,64]{0,1:T(8,128)S(1)}, f32[128,64]{0,1:T(8,128)S(1)}, u32[]{:S(2)}, u32[]{:S(2)}) %collective-permute-start.9) | collective-permute-done | bytes 32800 | tf_op jit(solution)/shard_map/ppermute | solution.py:17
  136.7 2.2 %collective-permute-start.10 = (f32[256,64]{0,1:T(8,128)S(1)}, f32[256,64]{0,1:T(8,128)S(1)}, u32[]{:S(2)}, u32[]{:S(2)}) collective-permute-start(f32[256,64]{0,1:T(8,128)S(1)} %maximum_select_fusion.2), channel_id=1, source_target_pairs={{0,8},{4,12},{8,0},{12,4},{16,24},{20,28},{24,16},{28,20},{32,40},... | collective-permute-start | bytes 196616 | tf_op jit(solution)/shard_map/ppermute | solution.py:17
  138.9 3.1 %collective-permute-done.10 = f32[256,64]{0,1:T(8,128)S(1)} collective-permute-done((f32[256,64]{0,1:T(8,128)S(1)}, f32[256,64]{0,1:T(8,128)S(1)}, u32[]{:S(2)}, u32[]{:S(2)}) %collective-permute-start.10) | collective-permute-done | bytes 65568 | tf_op jit(solution)/shard_map/ppermute | solution.py:17
  142.0 1.3 collective-permute-start.11
  143.3 0.7 slice_multiply_fusion
  144.0 0.8 copy.29
  144.8 2.2 %collective-permute-done.11 = f32[512,64]{0,1:T(8,128)S(1)} collective-permute-done((f32[512,64]{0,1:T(8,128)S(1)}, f32[512,64]{0,1:T(8,128)S(1)}, u32[]{:S(2)}, u32[]{:S(2)}) %collective-permute-start.11) | collective-permute-done | bytes 131104 | tf_op jit(solution)/shard_map/ppermute | solution.py:17
  147.0 0.7 maximum_select_fusion
  (16 shorter events, 0.2 us)
Async XLA Ops:
  7.2 1.3 copy-start
  7.2 72.4 %reduce-scatter.2.cloned.1.call-start = ((), (), s32[]{:S(2)}) async-start(), calls=%async_computation.1 | async-start | bytes 5242880 | tf_op jit(solution)/shard_map/reduce_scatter | solution.py:119
  8.4 2.6 %copy-start.8 = (bf16[8,64,128]{2,1,0:T(8,128)(2,1)S(1)}, bf16[8,64,128]{2,1,0:T(8,128)(2,1)}, u32[]{:S(2)}) copy-start(bf16[8,64,128]{2,1,0:T(8,128)(2,1)} %param.13) | copy-start | bytes 393220
  11.0 6.8 %copy-start.7 = (s32[8]{0:T(128)S(1)}, s32[8]{0:T(128)}, u32[]{:S(2)}) copy-start(s32[8]{0:T(128)} %param.17) | copy-start | bytes 100
  12.4 5.5 %collective-permute-start = (bf16[8,16,128]{2,1,0:T(8,128)(2,1)S(1)}, bf16[8,16,128]{2,1,0:T(8,128)(2,1)S(1)}, u32[]{:S(2)}, u32[]{:S(2)}) collective-permute-start(bf16[8,16,128]{2,1,0:T(8,128)(2,1)S(1)} %convolution_convert_fusion.3), channel_id=1, source_target_pairs={{0,128},{4,132},{8,136},{12,140},{16,144},{20,148},{24,152},{28,15... | collective-permute-start | bytes 98312 | tf_op jit(solution)/shard_map/ppermute | solution.py:17
  29.5 50.0 %copy-start.1 = (bf16[8,64,1024]{2,1,0:T(8,128)(2,1)S(1)}, bf16[8,64,1024]{2,1,0:T(8,128)(2,1)}, u32[]{:S(2)}) copy-start(bf16[8,64,1024]{2,1,0:T(8,128)(2,1)} %param.10) | copy-start | bytes 3145732
  29.6 51.8 %copy-start.3 = (f32[1024,64]{0,1:T(8,128)S(1)}, f32[1024,64]{0,1:T(8,128)}, u32[]{:S(2)}) copy-start(f32[1024,64]{0,1:T(8,128)} %param.16) | copy-start | bytes 786436
  29.6 51.8 %copy-start.5 = (f32[1024]{0:T(1024)S(1)}, f32[1024]{0:T(1024)}, u32[]{:S(2)}) copy-start(f32[1024]{0:T(1024)} %param.15) | copy-start | bytes 12292
  79.6 1.8 %copy-start.2 = (bf16[512,1024]{1,0:T(8,128)(2,1)S(1)}, bf16[512,1024]{1,0:T(8,128)(2,1)}, u32[]{:S(2)}) copy-start(bf16[512,1024]{1,0:T(8,128)(2,1)} %reduce-scatter.2.cloned.1.call-done) | copy-start | bytes 3145732
  81.3 5.2 %copy-start.6 = (s32[8,64]{1,0:T(8,128)S(1)}, s32[8,64]{1,0:T(8,128)}, u32[]{:S(2)}) copy-start(s32[8,64]{1,0:T(8,128)} %param.19) | copy-start | bytes 6148
  83.8 1.5 collective-permute-start.1
  85.2 6.1 %collective-permute-start.2 = (f32[512,65]{0,1:T(8,128)S(1)}, f32[512,65]{0,1:T(8,128)}, u32[]{:S(2)}, u32[]{:S(2)}) collective-permute-start(f32[512,65]{0,1:T(8,128)S(1)} %fusion.44), channel_id=1, source_target_pairs={{0,2},{1,3},{2,0},{3,1},{4,6},{5,7},{6,4},{7,5},{8,10},{9,11},{10,... | collective-permute-start | bytes 399368 | tf_op jit(solution)/shard_map/ppermute | solution.py:17
  92.3 2.6 %copy-start.4 = (f32[512,1]{0,1:T(1,128)}, f32[512,1]{0,1:T(1,128)S(1)}, u32[]{:S(2)}) copy-start(f32[512,1]{0,1:T(1,128)S(1)} %fusion.41) | copy-start | bytes 6148
  94.9 5.2 %collective-permute-start.3 = (f32[512,64]{0,1:T(8,128)S(1)}, f32[512,64]{0,1:T(8,128)S(1)}, u32[]{:S(2)}, u32[]{:S(2)}) collective-permute-start(f32[512,64]{0,1:T(8,128)S(1)} %slice_select_fusion), channel_id=1, source_target_pairs={{0,4},{4,0},{8,12},{12,8},{16,20},{20,16},{24,28},{28,24},{32,36},... | collective-permute-start | bytes 393224 | tf_op jit(solution)/shard_map/ppermute | solution.py:17
  100.2 5.3 %collective-permute-start.4 = (f32[256,64]{0,1:T(8,128)S(1)}, f32[256,64]{0,1:T(8,128)S(1)}, u32[]{:S(2)}, u32[]{:S(2)}) collective-permute-start(f32[256,64]{0,1:T(8,128)S(1)} %slice_select_fusion.1), channel_id=1, source_target_pairs={{0,8},{4,12},{8,0},{12,4},{16,24},{20,28},{24,16},{28,20},{32,40},... | collective-permute-start | bytes 196616 | tf_op jit(solution)/shard_map/ppermute | solution.py:17
  105.5 8.5 %collective-permute-start.5 = (f32[128,64]{0,1:T(8,128)S(1)}, f32[128,64]{0,1:T(8,128)S(1)}, u32[]{:S(2)}, u32[]{:S(2)}) collective-permute-start(f32[128,64]{0,1:T(8,128)S(1)} %slice_select_fusion.2), channel_id=1, source_target_pairs={{0,16},{4,20},{8,24},{12,28},{16,0},{20,4},{24,8},{28,12},{32,48},... | collective-permute-start | bytes 98312 | tf_op jit(solution)/shard_map/ppermute | solution.py:17
  114.0 5.5 %collective-permute-start.6 = (f32[128,64]{0,1:T(8,128)S(1)}, f32[128,64]{0,1:T(8,128)S(1)}, u32[]{:S(2)}, u32[]{:S(2)}) collective-permute-start(f32[128,64]{0,1:T(8,128)S(1)} %select_add_fusion.2), channel_id=1, source_target_pairs={{0,32},{4,36},{8,40},{12,44},{16,48},{20,52},{24,56},{28,60},{32,0... | collective-permute-start | bytes 98312 | tf_op jit(solution)/shard_map/ppermute | solution.py:17
  119.5 3.9 %collective-permute-start.7 = (f32[128,64]{0,1:T(8,128)S(1)}, f32[128,64]{0,1:T(8,128)S(1)}, u32[]{:S(2)}, u32[]{:S(2)}) collective-permute-start(f32[128,64]{0,1:T(8,128)S(1)} %add.77), channel_id=1, source_target_pairs={{0,64},{4,68},{8,72},{12,76},{16,80},{20,84},{24,88},{28,92},{32,9... | collective-permute-start | bytes 98312 | tf_op jit(solution)/shard_map/ppermute | solution.py:17
  123.4 5.4 %collective-permute-start.8 = (f32[128,64]{0,1:T(8,128)S(1)}, f32[128,64]{0,1:T(8,128)S(1)}, u32[]{:S(2)}, u32[]{:S(2)}) collective-permute-start(f32[128,64]{0,1:T(8,128)S(1)} %add.78), channel_id=1, source_target_pairs={{0,128},{4,132},{8,136},{12,140},{16,144},{20,148},{24,152},{28,15... | collective-permute-start | bytes 98312 | tf_op jit(solution)/shard_map/ppermute | solution.py:17
  128.8 7.8 %collective-permute-start.9 = (f32[128,64]{0,1:T(8,128)S(1)}, f32[128,64]{0,1:T(8,128)S(1)}, u32[]{:S(2)}, u32[]{:S(2)}) collective-permute-start(f32[128,64]{0,1:T(8,128)S(1)} %add.79), channel_id=1, source_target_pairs={{0,16},{4,20},{8,24},{12,28},{16,0},{20,4},{24,8},{28,12},{32,48},... | collective-permute-start | bytes 98312 | tf_op jit(solution)/shard_map/ppermute | solution.py:17
  136.7 5.3 %collective-permute-start.10 = (f32[256,64]{0,1:T(8,128)S(1)}, f32[256,64]{0,1:T(8,128)S(1)}, u32[]{:S(2)}, u32[]{:S(2)}) collective-permute-start(f32[256,64]{0,1:T(8,128)S(1)} %maximum_select_fusion.2), channel_id=1, source_target_pairs={{0,8},{4,12},{8,0},{12,4},{16,24},{20,28},{24,16},{28,20},{32,40},... | collective-permute-start | bytes 196616 | tf_op jit(solution)/shard_map/ppermute | solution.py:17
  142.0 5.1 %collective-permute-start.11 = (f32[512,64]{0,1:T(8,128)S(1)}, f32[512,64]{0,1:T(8,128)S(1)}, u32[]{:S(2)}, u32[]{:S(2)}) collective-permute-start(f32[512,64]{0,1:T(8,128)S(1)} %maximum_select_fusion.1), channel_id=1, source_target_pairs={{0,4},{4,0},{8,12},{12,8},{16,20},{20,16},{24,28},{28,24},{32,36},... | collective-permute-start | bytes 393224 | tf_op jit(solution)/shard_map/ppermute | solution.py:17
Sparse Core Ops, SparseCore 0:
  29.7 49.8 reduce-scatter.1

commit v2 on v1

--- a/solution.py
+++ b/solution.py
@@ -39,6 +39,26 @@
         other = exchanged(block, axis, bit)
         block = jnp.where(upper, jnp.concatenate([other, block]), jnp.concatenate([block, other]))
     return block
+
+
+def block_reduce_scatter(partial, axis):
+    count = lax.axis_size(axis)
+    position = lax.axis_index(axis)
+    blocks = partial.reshape(partial.shape[0], count, partial.shape[1] // count)
+
+    def block(index):
+        return lax.dynamic_index_in_dim(blocks, index, 1, keepdims=False)
+
+    if count != 4:
+        total = block(position)
+        for bit in range(1, count):
+            total = total + exchanged(block(position ^ bit).astype(jnp.bfloat16), axis, bit).astype(jnp.float32)
+        return total
+    far = position ^ 2
+    far_sum = block(far) + exchanged(block(far ^ 1).astype(jnp.bfloat16), axis, 1).astype(jnp.float32)
+    from_far = exchanged(far_sum.astype(jnp.bfloat16), axis, 2)
+    near = exchanged(block(position ^ 1).astype(jnp.bfloat16), axis, 1)
+    return block(position) + near.astype(jnp.float32) + from_far.astype(jnp.float32)
 
 
 def dp_bits(count):
@@ -116,9 +136,7 @@
     partial_value = jnp.dot(
         patched.reshape(token_count, -1), out_weight, preferred_element_type=jnp.float32
     )
-    attn_local = lax.psum_scatter(
-        partial_value.astype(jnp.bfloat16), "tensor", scatter_dimension=1, tiled=True
-    )
+    attn_local = block_reduce_scatter(partial_value, "tensor").astype(jnp.bfloat16)
     hidden = residual.reshape(token_count, feature_count).astype(jnp.float32) + attn_local.astype(
         jnp.float32
     )

time: 156 us -> 140 us (0.90)
  waiting for transfers between devices: 82.1 us -> 63 us
  local copies, waits for them, and re-layouts: 3.21 us -> 19.8 us
  between operations: 14.3 us -> 0.9 us
  other arithmetic: 4.89 us -> 9.31 us
  starting transfers between devices: 30.7 us -> 28 us
    reduce_scatter x1 -> x0, waiting for transfers between devices: 50 us -> none  [per_device(): lax.psum_scatter(partial_value.astype(jnp.bfloat16), 'tensor', scatter_di...]
    ppermute x12 -> x15, waiting for transfers between devices: 32.1 us -> 63 us  [exchanged(): return lax.ppermute(block, axis, [(i, i ^ bit) for i in range(count)])]
    dot_general x0 -> x1, local copies, waits for them, and re-layouts: none -> 12 us  [per_device(): jnp.dot(patched.reshape(token_count, -1), out_weight, preferred_element_t...]
    unnamed x19 -> x23, local copies, waits for them, and re-layouts: 1.27 us -> 4.54 us
    convert_element_type x0 -> x1, other arithmetic: none -> 3.24 us  [block_reduce_scatter(): from_far = exchanged(far_sum.astype(jnp.bfloat16), axis, 2)]
    ppermute x12 -> x15, starting transfers between devices: 30.6 us -> 28 us  [exchanged(): return lax.ppermute(block, axis, [(i, i ^ bit) for i in range(count)])]
    dot_general x1, matrix products: 9.41 us -> 6.98 us  [per_device(): jnp.dot(patched.reshape(token_count, -1), out_weight, preferred_element_t...]
  transfers between devices with their start and end apart: 13 -> 15, of which waited for: 13 -> 13; matrix products, arithmetic and copies ran while one was open for 1% -> 13% of each run, Pallas kernels for 0% -> 0%
where the time goes in v2:
time: 140 us; the launch traced here: 139 us
  waiting for transfers between devices  63 us (45%)
  starting transfers between devices  28 us (20%)
  local copies, waits for them, and re-layouts  19.8 us (14%)
  matrix products  18.2 us (13%)
  other arithmetic  9.31 us (7%)
    ppermute x15, waiting for transfers between devices, exchanged(): return lax.ppermute(block, axis, [(i, i ^ bit) for i in range(count)])  63 us
    ppermute x15, starting transfers between devices, exchanged(): return lax.ppermute(block, axis, [(i, i ^ bit) for i in range(count)])  28 us
    dot_general x1, local copies, waits for them, and re-layouts, per_device(): jnp.dot(patched.reshape(token_count, -1), out_weight, preferred_element_t...  12 us
    dot_general x1, matrix products, per_device(): jnp.dot(patched.reshape(token_count, -1), out_weight, preferred_element_t...  6.98 us
    unnamed x23, local copies, waits for them, and re-layouts  4.54 us
    convert_element_type x1, other arithmetic, block_reduce_scatter(): from_far = exchanged(far_sum.astype(jnp.bfloat16), axis, 2)  3.24 us
    reduce_sum x1, other arithmetic, per_device(): square_local = jnp.sum(hidden * hidden, axis=1)  2.9 us
  transfers between devices with their start and end apart: 15, of which 13 were waited for; matrix products, arithmetic and copies ran while one was open for 13% of the time, Pallas kernels for 0%

profile of v2, /device:TPU:24, one launch (start us, length us, event | category | flops | bytes accessed | tf_op | source)
XLA Modules:
  0.0 139.2 jit_solution(7695742363548044922)
XLA Ops:
  0.6 0.0 copy-start
  0.7 0.8 fusion.51
  1.5 0.4 copy-done
  1.9 2.1 %fusion.52 = (f32[8,8,64]{2,1,0:T(8,128)S(1)}, f32[8,1,8,64,64]{3,4,2,0,1:T(8,128)S(1)}) fusion(bf16[8,64,128]{2,1,0:T(8,128)(2,1)} %param.12, pred[64,64]{0,1:T(8,128)(4,1)S(1)} %iota_compare_fusion.5, bf16[8,64,1024]{2,1,0:T(8,128)(2,1)S(1)} %copy-done), kind=kOutput, calls=%fused_computation.78 | convolution fusion | flops 67891200 | bytes 2248704 | tf_op jit(solution)/shard_map/pqkgd,pskd->pkgqs/dot_general | solution.py:80
  4.0 0.5 fusion.9
  4.5 0.0 copy-done.9
  4.5 0.6 fusion.10
  5.1 0.0 copy-start.10
  5.1 0.7 convolution_convert_fusion.2
  5.8 3.1 %collective-permute-start = (bf16[8,16,128]{2,1,0:T(8,128)(2,1)S(1)}, bf16[8,16,128]{2,1,0:T(8,128)(2,1)S(1)}, u32[]{:S(2)}, u32[]{:S(2)}) collective-permute-start(bf16[8,16,128]{2,1,0:T(8,128)(2,1)S(1)} %convolution_convert_fusion.2), channel_id=1, source_target_pairs={{0,128},{4,132},{8,136},{12,140},{16,144},{20,148},{24,152},{28,15... | collective-permute-start | bytes 98312 | tf_op jit(solution)/shard_map/ppermute | solution.py:17
  8.9 0.0 copy-done.10
  8.9 0.1 fusion.25
  9.1 0.0 copy-start.8
  9.1 12.0 %copy.31 = bf16[4096,1024]{1,0:T(8,128)(2,1)} copy(bf16[4096,1024]{0,1:T(8,128)(2,1)} %bitcast.72) | data formatting | bytes 16777216 | tf_op jit(solution)/shard_map/dot_general | solution.py:136
  21.1 0.0 collective-permute-done
  21.1 0.0 copy-done.8
  21.1 0.2 fusion.38
  21.3 2.7 %fusion.11 = bf16[8,512,128]{2,1,0:T(8,128)(2,1)S(1)} fusion(pred[8,512]{1,0:T(8,128)(4,1)S(1)} %fusion.25, bf16[8,64,1,8,128]{4,1,3,0,2:T(8,128)(2,1)} %copy-done.10, s32[8,16]{1,0:T(8,128)S(1)} %fusion.42, bf16[8,16,128]{2,0,1:T(8,128)(2,1)S(1)} %fusion.38), kind=kOutput, calls=%fused_computation.20 | convolution fusion | flops 17891328 | bytes 2134528 | tf_op jit(solution)/shard_map/jkr,jkd->jrd/dot_general | solution.py:130
  24.0 0.5 reshape.64
  24.5 7.0 %fusion.53 = f32[512,4,1024]{2,0,1:T(8,128)S(1)} fusion(bf16[512,1024,1]{1,0,2:T(8,128)(2,1)S(1)} %reshape.64, bf16[4,1024,1024]{2,1,0:T(8,128)(2,1)} %bitcast.73), kind=kOutput, calls=%fused_computation.79 | convolution fusion | flops 4294967296 | bytes 17825792 | tf_op jit(solution)/shard_map/dot_general | solution.py:136
  31.5 3.2 %copy-done.1 = f32[512,4,1024]{2,0,1:T(8,128)} copy-done((f32[512,4,1024]{2,0,1:T(8,128)}, f32[512,4,1024]{2,0,1:T(8,128)S(1)}, u32[]{:S(2)}) %copy-start.1) | copy-done | bytes 8388632
  34.8 1.3 fusion.15
  36.0 0.0 collective-permute-start.2
  36.1 0.5 collective-permute-start.1
  36.6 2.5 %collective-permute-done.2 = bf16[512,1024]{1,0:T(8,128)(2,1)} collective-permute-done((bf16[512,1024]{1,0:T(8,128)(2,1)}, bf16[512,1024]{1,0:T(8,128)(2,1)}, u32[]{:S(2)}, u32[]{:S(2)}) %collective-permute-start.2) | collective-permute-done | bytes 1048608 | tf_op jit(solution)/shard_map/ppermute | solution.py:17
  39.1 3.2 %fusion = bf16[512,1024]{1,0:T(8,128)(2,1)} fusion(bf16[512,1024]{1,0:T(8,128)(2,1)} %collective-permute-done.2, f32[512,4,1024]{2,0,1:T(8,128)} %copy-done.1, s32[]{:T(128)S(6)} %select_n.112), kind=kLoop, calls=%fused_computation.3 | loop fusion | flops 1572864 | bytes 4194308 | tf_op jit(solution)/shard_map/convert_element_type | solution.py:59
  42.3 0.7 collective-permute-start.3
  43.0 0.0 collective-permute-done.1
  43.0 24.8 %collective-permute-done.3 = bf16[512,1024]{1,0:T(8,128)(2,1)} collective-permute-done((bf16[512,1024]{1,0:T(8,128)(2,1)}, bf16[512,1024]{1,0:T(8,128)(2,1)}, u32[]{:S(2)}, u32[]{:S(2)}) %collective-permute-start.3) | collective-permute-done | bytes 1048608 | tf_op jit(solution)/shard_map/ppermute | solution.py:17
  67.8 2.9 %multiply_reduce_fusion = (f32[512]{0:T(512)S(1)}, bf16[512,1024]{1,0:T(8,128)(2,1)S(1)}) fusion(bf16[8,64,1024]{2,1,0:T(8,128)(2,1)S(1)} %copy-done.2, bf16[512,1024]{1,0:T(8,128)(2,1)} %collective-permute-done.3, bf16[512,1024]{1,0:T(8,128)(2,1)} %collective-permute-done.1, f32[512,4,1024]{2,0,1:T(8,128)} %copy-done.1, s32[]{:T(128)S(6)} %select_n.110), kind=kLoop, calls=%fused_computation.9 | loop fusion | flops 5242368 | bytes 6293508 | tf_op jit(solution)/shard_map/reduce_sum | solution.py:143
  70.7 0.0 copy-start.7
  70.7 0.0 copy-done.4
  70.7 0.0 copy-done.6
  70.8 2.4 %fusion.7 = f32[512,64]{0,1:T(8,128)S(1)} fusion(f32[1024,64]{0,1:T(8,128)S(1)} %copy-done.4, bf16[512,1024]{1,0:T(8,128)(2,1)S(1)} %get-tuple-element.10, bf16[512,1024]{1,0:T(8,128)(2,1)S(1)} %bitcast.74, f32[1024]{0:T(1024)S(1)} %copy-done.6), kind=kOutput, calls=%fused_computation.15 | convolution fusion | flops 404750336 | bytes 2494464 | tf_op jit(solution)/shard_map/dot_general | solution.py:145
  73.2 0.3 collective-permute-start.4
  73.4 1.4 collective-permute-done.4
  74.8 0.8 collective-permute-start.5
  75.7 0.7 eq.68
  76.3 4.6 %collective-permute-done.5 = f32[512,65]{0,1:T(8,128)} collective-permute-done((f32[512,65]{0,1:T(8,128)S(1)}, f32[512,65]{0,1:T(8,128)}, u32[]{:S(2)}, u32[]{:S(2)}) %collective-permute-start.5) | collective-permute-done | bytes 133152 | tf_op jit(solution)/shard_map/ppermute | solution.py:17
  80.9 0.9 add.94
  81.9 0.0 copy-start.5
  81.9 2.6 %fusion.12 = f32[1024,64]{0,1:T(8,128)S(1)} fusion(bf16[512,1024]{1,0:T(8,128)(2,1)S(1)} %get-tuple-element.10, bf16[512,1024]{1,0:T(8,128)(2,1)S(1)} %bitcast.75, f32[512]{0:T(512)S(1)} %bitcast.82, f32[1024]{0:T(1024)} %param.15, s32[512]{0:T(512)} %eq.68, f32[512,65]{0,1:T(8,128)S(1)} %add.94), kind=kOutput, calls=%fused_computation.21 | convolution fusion | flops 405569536 | bytes 2500608 | tf_op jit(solution)/shard_map/dot_general | solution.py:161
  84.5 0.0 copy-done.5
  84.5 2.0 %collective-permute-start.6 = (f32[512,64]{0,1:T(8,128)S(1)}, f32[512,64]{0,1:T(8,128)S(1)}, u32[]{:S(2)}, u32[]{:S(2)}) collective-permute-start(f32[512,64]{0,1:T(8,128)S(1)} %slice_select_fusion), channel_id=1, source_target_pairs={{0,4},{4,0},{8,12},{12,8},{16,20},{20,16},{24,28},{28,24},{32,36},... | collective-permute-start | bytes 393224 | tf_op jit(solution)/shard_map/ppermute | solution.py:17
  86.5 3.1 %collective-permute-done.6 = f32[512,64]{0,1:T(8,128)S(1)} collective-permute-done((f32[512,64]{0,1:T(8,128)S(1)}, f32[512,64]{0,1:T(8,128)S(1)}, u32[]{:S(2)}, u32[]{:S(2)}) %collective-permute-start.6) | collective-permute-done | bytes 131104 | tf_op jit(solution)/shard_map/ppermute | solution.py:17
  89.6 3.4 %collective-permute-start.7 = (f32[256,64]{0,1:T(8,128)S(1)}, f32[256,64]{0,1:T(8,128)S(1)}, u32[]{:S(2)}, u32[]{:S(2)}) collective-permute-start(f32[256,64]{0,1:T(8,128)S(1)} %slice_select_fusion.1), channel_id=1, source_target_pairs={{0,8},{4,12},{8,0},{12,4},{16,24},{20,28},{24,16},{28,20},{32,40},... | collective-permute-start | bytes 196616 | tf_op jit(solution)/shard_map/ppermute | solution.py:17
  93.0 2.2 %collective-permute-done.7 = f32[256,64]{0,1:T(8,128)S(1)} collective-permute-done((f32[256,64]{0,1:T(8,128)S(1)}, f32[256,64]{0,1:T(8,128)S(1)}, u32[]{:S(2)}, u32[]{:S(2)}) %collective-permute-start.7) | collective-permute-done | bytes 65568 | tf_op jit(solution)/shard_map/ppermute | solution.py:17
  95.2 7.6 %collective-permute-start.8 = (f32[128,64]{0,1:T(8,128)S(1)}, f32[128,64]{0,1:T(8,128)S(1)}, u32[]{:S(2)}, u32[]{:S(2)}) collective-permute-start(f32[128,64]{0,1:T(8,128)S(1)} %slice_select_fusion.2), channel_id=1, source_target_pairs={{0,16},{4,20},{8,24},{12,28},{16,0},{20,4},{24,8},{28,12},{32,48},... | collective-permute-start | bytes 98312 | tf_op jit(solution)/shard_map/ppermute | solution.py:17
  102.9 2.1 %collective-permute-done.8 = f32[128,64]{0,1:T(8,128)S(1)} collective-permute-done((f32[128,64]{0,1:T(8,128)S(1)}, f32[128,64]{0,1:T(8,128)S(1)}, u32[]{:S(2)}, u32[]{:S(2)}) %collective-permute-start.8) | collective-permute-done | bytes 32800 | tf_op jit(solution)/shard_map/ppermute | solution.py:17
  105.0 1.3 collective-permute-start.9
  106.3 4.2 %collective-permute-done.9 = f32[128,64]{0,1:T(8,128)S(1)} collective-permute-done((f32[128,64]{0,1:T(8,128)S(1)}, f32[128,64]{0,1:T(8,128)S(1)}, u32[]{:S(2)}, u32[]{:S(2)}) %collective-permute-start.9) | collective-permute-done | bytes 32800 | tf_op jit(solution)/shard_map/ppermute | solution.py:17
  110.5 0.6 collective-permute-start.10
  111.1 3.3 %collective-permute-done.10 = f32[128,64]{0,1:T(8,128)S(1)} collective-permute-done((f32[128,64]{0,1:T(8,128)S(1)}, f32[128,64]{0,1:T(8,128)S(1)}, u32[]{:S(2)}, u32[]{:S(2)}) %collective-permute-start.10) | collective-permute-done | bytes 32800 | tf_op jit(solution)/shard_map/ppermute | solution.py:17
  114.4 0.6 collective-permute-start.11
  115.0 4.8 %collective-permute-done.11 = f32[128,64]{0,1:T(8,128)S(1)} collective-permute-done((f32[128,64]{0,1:T(8,128)S(1)}, f32[128,64]{0,1:T(8,128)S(1)}, u32[]{:S(2)}, u32[]{:S(2)}) %collective-permute-start.11) | collective-permute-done | bytes 32800 | tf_op jit(solution)/shard_map/ppermute | solution.py:17
  119.9 5.7 %collective-permute-start.12 = (f32[128,64]{0,1:T(8,128)S(1)}, f32[128,64]{0,1:T(8,128)S(1)}, u32[]{:S(2)}, u32[]{:S(2)}) collective-permute-start(f32[128,64]{0,1:T(8,128)S(1)} %add.106), channel_id=1, source_target_pairs={{0,16},{4,20},{8,24},{12,28},{16,0},{20,4},{24,8},{28,12},{32,48},... | collective-permute-start | bytes 98312 | tf_op jit(solution)/shard_map/ppermute | solution.py:17
  125.5 2.1 %collective-permute-done.12 = f32[128,64]{0,1:T(8,128)S(1)} collective-permute-done((f32[128,64]{0,1:T(8,128)S(1)}, f32[128,64]{0,1:T(8,128)S(1)}, u32[]{:S(2)}, u32[]{:S(2)}) %collective-permute-start.12) | collective-permute-done | bytes 32800 | tf_op jit(solution)/shard_map/ppermute | solution.py:17
  127.7 1.3 collective-permute-start.13
  129.0 4.4 %collective-permute-done.13 = f32[256,64]{0,1:T(8,128)S(1)} collective-permute-done((f32[256,64]{0,1:T(8,128)S(1)}, f32[256,64]{0,1:T(8,128)S(1)}, u32[]{:S(2)}, u32[]{:S(2)}) %collective-permute-start.13) | collective-permute-done | bytes 65568 | tf_op jit(solution)/shard_map/ppermute | solution.py:17
  133.4 0.1 collective-permute-start.14
  133.5 0.7 slice_multiply_fusion
  134.2 0.8 copy.32
  135.0 3.4 %collective-permute-done.14 = f32[512,64]{0,1:T(8,128)S(1)} collective-permute-done((f32[512,64]{0,1:T(8,128)S(1)}, f32[512,64]{0,1:T(8,128)S(1)}, u32[]{:S(2)}, u32[]{:S(2)}) %collective-permute-start.14) | collective-permute-done | bytes 131104 | tf_op jit(solution)/shard_map/ppermute | solution.py:17
  138.5 0.7 maximum_select_fusion
  (25 shorter events, 0.2 us)
Async XLA Ops:
  0.6 1.3 copy-start
  1.9 2.6 %copy-start.9 = (bf16[8,64,128]{2,1,0:T(8,128)(2,1)S(1)}, bf16[8,64,128]{2,1,0:T(8,128)(2,1)}, u32[]{:S(2)}) copy-start(bf16[8,64,128]{2,1,0:T(8,128)(2,1)} %param.13) | copy-start | bytes 393220
  5.1 3.8 %copy-start.10 = (bf16[8,64,1,8,128]{4,1,3,0,2:T(8,128)(2,1)}, bf16[8,64,1,8,128]{4,1,3,0,2:T(8,128)(2,1)S(1)}, u32[]{:S(2)}) copy-start(bf16[8,64,1,8,128]{4,1,3,0,2:T(8,128)(2,1)S(1)} %fusion.10) | copy-start | bytes 3145732
  5.8 15.3 %collective-permute-start = (bf16[8,16,128]{2,1,0:T(8,128)(2,1)S(1)}, bf16[8,16,128]{2,1,0:T(8,128)(2,1)S(1)}, u32[]{:S(2)}, u32[]{:S(2)}) collective-permute-start(bf16[8,16,128]{2,1,0:T(8,128)(2,1)S(1)} %convolution_convert_fusion.2), channel_id=1, source_target_pairs={{0,128},{4,132},{8,136},{12,140},{16,144},{20,148},{24,152},{28,15... | collective-permute-start | bytes 98312 | tf_op jit(solution)/shard_map/ppermute | solution.py:17
  9.1 12.0 %copy-start.8 = (s32[8]{0:T(128)S(1)}, s32[8]{0:T(128)}, u32[]{:S(2)}) copy-start(s32[8]{0:T(128)} %param.17) | copy-start | bytes 100
  31.5 3.2 %copy-start.1 = (f32[512,4,1024]{2,0,1:T(8,128)}, f32[512,4,1024]{2,0,1:T(8,128)S(1)}, u32[]{:S(2)}) copy-start(f32[512,4,1024]{2,0,1:T(8,128)S(1)} %fusion.53) | copy-start | bytes 25165828
  36.0 3.0 %collective-permute-start.2 = (bf16[512,1024]{1,0:T(8,128)(2,1)}, bf16[512,1024]{1,0:T(8,128)(2,1)}, u32[]{:S(2)}, u32[]{:S(2)}) collective-permute-start(bf16[512,1024]{1,0:T(8,128)(2,1)} %get-tuple-element.12), channel_id=1, source_target_pairs={{0,1},{1,0},{2,3},{3,2},{4,5},{5,4},{6,7},{7,6},{8,9},{9,8},{10,11... | collective-permute-start | bytes 3145736 | tf_op jit(solution)/shard_map/ppermute | solution.py:17
  36.1 31.8 %copy-start.2 = (bf16[8,64,1024]{2,1,0:T(8,128)(2,1)S(1)}, bf16[8,64,1024]{2,1,0:T(8,128)(2,1)}, u32[]{:S(2)}) copy-start(bf16[8,64,1024]{2,1,0:T(8,128)(2,1)} %param.10) | copy-start | bytes 3145732
  36.1 7.0 %collective-permute-start.1 = (bf16[512,1024]{1,0:T(8,128)(2,1)S(1)}, bf16[512,1024]{1,0:T(8,128)(2,1)}, u32[]{:S(2)}, u32[]{:S(2)}) collective-permute-start(bf16[512,1024]{1,0:T(8,128)(2,1)S(1)} %get-tuple-element.11), channel_id=1, source_target_pairs={{0,1},{1,0},{2,3},{3,2},{4,5},{5,4},{6,7},{7,6},{8,9},{9,8},{10,11... | collective-permute-start | bytes 3145736 | tf_op jit(solution)/shard_map/ppermute | solution.py:17
  42.3 25.5 %collective-permute-start.3 = (bf16[512,1024]{1,0:T(8,128)(2,1)}, bf16[512,1024]{1,0:T(8,128)(2,1)}, u32[]{:S(2)}, u32[]{:S(2)}) collective-permute-start(bf16[512,1024]{1,0:T(8,128)(2,1)} %fusion), channel_id=1, source_target_pairs={{0,2},{1,3},{2,0},{3,1},{4,6},{5,7},{6,4},{7,5},{8,10},{9,11},{10,... | collective-permute-start | bytes 3145736 | tf_op jit(solution)/shard_map/ppermute | solution.py:17
  43.0 27.7 %copy-start.4 = (f32[1024,64]{0,1:T(8,128)S(1)}, f32[1024,64]{0,1:T(8,128)}, u32[]{:S(2)}) copy-start(f32[1024,64]{0,1:T(8,128)} %param.16) | copy-start | bytes 786436
  43.0 27.7 %copy-start.6 = (f32[1024]{0:T(1024)S(1)}, f32[1024]{0:T(1024)}, u32[]{:S(2)}) copy-start(f32[1024]{0:T(1024)} %param.15) | copy-start | bytes 12292
  70.7 13.7 %copy-start.3 = (bf16[512,1024]{1,0:T(8,128)(2,1)}, bf16[512,1024]{1,0:T(8,128)(2,1)S(1)}, u32[]{:S(2)}) copy-start(bf16[512,1024]{1,0:T(8,128)(2,1)S(1)} %get-tuple-element.10) | copy-start | bytes 3145732
  70.7 4.9 %copy-start.7 = (s32[8,64]{1,0:T(8,128)S(1)}, s32[8,64]{1,0:T(8,128)}, u32[]{:S(2)}) copy-start(s32[8,64]{1,0:T(8,128)} %param.19) | copy-start | bytes 6148
  73.2 1.6 %collective-permute-start.4 = (f32[512,65]{0,1:T(8,128)S(1)}, f32[512,65]{0,1:T(8,128)S(1)}, u32[]{:S(2)}, u32[]{:S(2)}) collective-permute-start(f32[512,65]{0,1:T(8,128)S(1)} %pad_maximum_fusion), channel_id=1, source_target_pairs={{0,1},{1,0},{2,3},{3,2},{4,5},{5,4},{6,7},{7,6},{8,9},{9,8},{10,11... | collective-permute-start | bytes 399368 | tf_op jit(solution)/shard_map/ppermute | solution.py:17
  74.8 6.1 %collective-permute-start.5 = (f32[512,65]{0,1:T(8,128)S(1)}, f32[512,65]{0,1:T(8,128)}, u32[]{:S(2)}, u32[]{:S(2)}) collective-permute-start(f32[512,65]{0,1:T(8,128)S(1)} %fusion.49), channel_id=1, source_target_pairs={{0,2},{1,3},{2,0},{3,1},{4,6},{5,7},{6,4},{7,5},{8,10},{9,11},{10,... | collective-permute-start | bytes 399368 | tf_op jit(solution)/shard_map/ppermute | solution.py:17
  81.9 2.6 %copy-start.5 = (f32[512,1]{0,1:T(1,128)}, f32[512,1]{0,1:T(1,128)S(1)}, u32[]{:S(2)}) copy-start(f32[512,1]{0,1:T(1,128)S(1)} %fusion.46) | copy-start | bytes 6148
  84.5 5.1 %collective-permute-start.6 = (f32[512,64]{0,1:T(8,128)S(1)}, f32[512,64]{0,1:T(8,128)S(1)}, u32[]{:S(2)}, u32[]{:S(2)}) collective-permute-start(f32[512,64]{0,1:T(8,128)S(1)} %slice_select_fusion), channel_id=1, source_target_pairs={{0,4},{4,0},{8,12},{12,8},{16,20},{20,16},{24,28},{28,24},{32,36},... | collective-permute-start | bytes 393224 | tf_op jit(solution)/shard_map/ppermute | solution.py:17
  89.6 5.6 %collective-permute-start.7 = (f32[256,64]{0,1:T(8,128)S(1)}, f32[256,64]{0,1:T(8,128)S(1)}, u32[]{:S(2)}, u32[]{:S(2)}) collective-permute-start(f32[256,64]{0,1:T(8,128)S(1)} %slice_select_fusion.1), channel_id=1, source_target_pairs={{0,8},{4,12},{8,0},{12,4},{16,24},{20,28},{24,16},{28,20},{32,40},... | collective-permute-start | bytes 196616 | tf_op jit(solution)/shard_map/ppermute | solution.py:17
  95.2 9.8 %collective-permute-start.8 = (f32[128,64]{0,1:T(8,128)S(1)}, f32[128,64]{0,1:T(8,128)S(1)}, u32[]{:S(2)}, u32[]{:S(2)}) collective-permute-start(f32[128,64]{0,1:T(8,128)S(1)} %slice_select_fusion.2), channel_id=1, source_target_pairs={{0,16},{4,20},{8,24},{12,28},{16,0},{20,4},{24,8},{28,12},{32,48},... | collective-permute-start | bytes 98312 | tf_op jit(solution)/shard_map/ppermute | solution.py:17
  105.0 5.5 %collective-permute-start.9 = (f32[128,64]{0,1:T(8,128)S(1)}, f32[128,64]{0,1:T(8,128)S(1)}, u32[]{:S(2)}, u32[]{:S(2)}) collective-permute-start(f32[128,64]{0,1:T(8,128)S(1)} %select_add_fusion.2), channel_id=1, source_target_pairs={{0,32},{4,36},{8,40},{12,44},{16,48},{20,52},{24,56},{28,60},{32,0... | collective-permute-start | bytes 98312 | tf_op jit(solution)/shard_map/ppermute | solution.py:17
  110.5 3.9 %collective-permute-start.10 = (f32[128,64]{0,1:T(8,128)S(1)}, f32[128,64]{0,1:T(8,128)S(1)}, u32[]{:S(2)}, u32[]{:S(2)}) collective-permute-start(f32[128,64]{0,1:T(8,128)S(1)} %add.104), channel_id=1, source_target_pairs={{0,64},{4,68},{8,72},{12,76},{16,80},{20,84},{24,88},{28,92},{32,9... | collective-permute-start | bytes 98312 | tf_op jit(solution)/shard_map/ppermute | solution.py:17
  114.4 5.4 %collective-permute-start.11 = (f32[128,64]{0,1:T(8,128)S(1)}, f32[128,64]{0,1:T(8,128)S(1)}, u32[]{:S(2)}, u32[]{:S(2)}) collective-permute-start(f32[128,64]{0,1:T(8,128)S(1)} %add.105), channel_id=1, source_target_pairs={{0,128},{4,132},{8,136},{12,140},{16,144},{20,148},{24,152},{28,15... | collective-permute-start | bytes 98312 | tf_op jit(solution)/shard_map/ppermute | solution.py:17
  119.9 7.8 %collective-permute-start.12 = (f32[128,64]{0,1:T(8,128)S(1)}, f32[128,64]{0,1:T(8,128)S(1)}, u32[]{:S(2)}, u32[]{:S(2)}) collective-permute-start(f32[128,64]{0,1:T(8,128)S(1)} %add.106), channel_id=1, source_target_pairs={{0,16},{4,20},{8,24},{12,28},{16,0},{20,4},{24,8},{28,12},{32,48},... | collective-permute-start | bytes 98312 | tf_op jit(solution)/shard_map/ppermute | solution.py:17
  127.7 5.7 %collective-permute-start.13 = (f32[256,64]{0,1:T(8,128)S(1)}, f32[256,64]{0,1:T(8,128)S(1)}, u32[]{:S(2)}, u32[]{:S(2)}) collective-permute-start(f32[256,64]{0,1:T(8,128)S(1)} %maximum_select_fusion.2), channel_id=1, source_target_pairs={{0,8},{4,12},{8,0},{12,4},{16,24},{20,28},{24,16},{28,20},{32,40},... | collective-permute-start | bytes 196616 | tf_op jit(solution)/shard_map/ppermute | solution.py:17
  133.4 5.1 %collective-permute-start.14 = (f32[512,64]{0,1:T(8,128)S(1)}, f32[512,64]{0,1:T(8,128)S(1)}, u32[]{:S(2)}, u32[]{:S(2)}) collective-permute-start(f32[512,64]{0,1:T(8,128)S(1)} %maximum_select_fusion.1), channel_id=1, source_target_pairs={{0,4},{4,0},{8,12},{12,8},{16,20},{20,16},{24,28},{28,24},{32,36},... | collective-permute-start | bytes 393224 | tf_op jit(solution)/shard_map/ppermute | solution.py:17

commit v3 on v2

--- a/solution.py
+++ b/solution.py
@@ -41,30 +41,34 @@
     return block
 
 
-def block_reduce_scatter(partial, axis):
+def block_reduce_scatter(heads, weight, axis):
     count = lax.axis_size(axis)
     position = lax.axis_index(axis)
-    blocks = partial.reshape(partial.shape[0], count, partial.shape[1] // count)
+    width = weight.shape[1] // count
 
     def block(index):
-        return lax.dynamic_index_in_dim(blocks, index, 1, keepdims=False)
+        columns = lax.dynamic_slice_in_dim(weight, index * width, width, axis=1)
+        return jnp.dot(heads, columns, preferred_element_type=jnp.float32)
+
+    def sent(value, bit):
+        return exchanged(value.astype(jnp.bfloat16), axis, bit).astype(jnp.float32)
 
     if count != 4:
         total = block(position)
         for bit in range(1, count):
-            total = total + exchanged(block(position ^ bit).astype(jnp.bfloat16), axis, bit).astype(jnp.float32)
+            total = total + sent(block(position ^ bit), bit)
         return total
     far = position ^ 2
-    far_sum = block(far) + exchanged(block(far ^ 1).astype(jnp.bfloat16), axis, 1).astype(jnp.float32)
-    from_far = exchanged(far_sum.astype(jnp.bfloat16), axis, 2)
-    near = exchanged(block(position ^ 1).astype(jnp.bfloat16), axis, 1)
-    return block(position) + near.astype(jnp.float32) + from_far.astype(jnp.float32)
+    from_partner = sent(block(far ^ 1), 1)
+    from_far = sent(block(far) + from_partner, 2)
+    near = sent(block(position ^ 1), 1)
+    return block(position) + near + from_far
 
 
 def dp_bits(count):
     low = [1 << k for k in range(count.bit_length() - 1)]
     if count == 64:
-        return low[:3], low[3:]
+        return low[:2], low[2:]
     return [], low
 
 
@@ -133,10 +137,9 @@
     patch_mask = jnp.any(picks, axis=1)
     patched = jnp.where(patch_mask[..., None], placed, flat_heads)
 
-    partial_value = jnp.dot(
-        patched.reshape(token_count, -1), out_weight, preferred_element_type=jnp.float32
-    )
-    attn_local = block_reduce_scatter(partial_value, "tensor").astype(jnp.bfloat16)
+    attn_local = block_reduce_scatter(
+        patched.reshape(token_count, -1), out_weight, "tensor"
+    ).astype(jnp.bfloat16)
     hidden = residual.reshape(token_count, feature_count).astype(jnp.float32) + attn_local.astype(
         jnp.float32
     )

time: 140 us -> 115 us (0.82)
  local copies, waits for them, and re-layouts: 19.8 us -> 3.26 us
  waiting for transfers between devices: 63 us -> 56.1 us
  matrix products: 18.2 us -> 23.8 us
  other arithmetic: 9.31 us -> 5.47 us
  starting transfers between devices: 28 us -> 25.3 us
    dot_general x1 -> x0, local copies, waits for them, and re-layouts: 12 us -> none  [per_device(): jnp.dot(patched.reshape(token_count, -1), out_weight, preferred_element_t...]
    ppermute x15 -> x14, waiting for transfers between devices: 63 us -> 56.1 us  [exchanged(): return lax.ppermute(block, axis, [(i, i ^ bit) for i in range(count)])]
    dot_general x1 -> x4, matrix products: 6.98 us -> 13.7 us  [block(): return jnp.dot(heads, columns, preferred_element_type=jnp.float32)]
    convert_element_type x1 -> x0, other arithmetic: 3.24 us -> none  [block_reduce_scatter(): from_far = exchanged(far_sum.astype(jnp.bfloat16), axis, 2)]
    unnamed x23 -> x19, local copies, waits for them, and re-layouts: 4.54 us -> 1.31 us
    ppermute x15 -> x14, starting transfers between devices: 28 us -> 25.3 us  [exchanged(): return lax.ppermute(block, axis, [(i, i ^ bit) for i in range(count)])]
  transfers between devices with their start and end apart: 15 -> 14, of which waited for: 13 -> 12; matrix products, arithmetic and copies ran while one was open for 13% -> 11% of each run, Pallas kernels for 0% -> 0%
where the time goes in v3:
time: 115 us
  waiting for transfers between devices  56.1 us (49%)
  starting transfers between devices  25.3 us (22%)
  matrix products  23.8 us (21%)
  other arithmetic  5.47 us (5%)
  local copies, waits for them, and re-layouts  3.26 us (3%)
    ppermute x14, waiting for transfers between devices, exchanged(): return lax.ppermute(block, axis, [(i, i ^ bit) for i in range(count)])  56.1 us
    ppermute x14, starting transfers between devices, exchanged(): return lax.ppermute(block, axis, [(i, i ^ bit) for i in range(count)])  25.3 us
    dot_general x4, matrix products, block(): return jnp.dot(heads, columns, preferred_element_type=jnp.float32)  13.7 us
    dot_general x1, matrix products, per_device(): lax.dot_general(normed, error, (((0,), (0,)), ((), ())), precision=lax.Pr...  2.55 us
    dot_general x1, matrix products, per_device(): jnp.dot(scaled, probe_weight, precision=lax.Precision.HIGHEST, preferred_...  2.39 us
    reduce_sum x1, other arithmetic, per_device(): square_local = jnp.sum(hidden * hidden, axis=1)  2.3 us
  transfers between devices with their start and end apart: 14, of which 12 were waited for; matrix products, arithmetic and copies ran while one was open for 11% of the time, Pallas kernels for 0%

profile of v3, /device:TPU:24, one launch (start us, length us, event | category | flops | bytes accessed | tf_op | source)
XLA Modules:
  0.0 114.8 jit_solution(2015846509390080279)
XLA Ops:
  0.6 0.0 copy-start
  0.7 0.8 fusion.65
  1.5 0.4 copy-done
  1.9 2.1 %fusion.66 = (f32[8,8,64]{2,1,0:T(8,128)S(1)}, f32[8,1,8,64,64]{3,4,2,0,1:T(8,128)S(1)}) fusion(bf16[8,64,128]{2,1,0:T(8,128)(2,1)} %param.12, pred[64,64]{0,1:T(8,128)(4,1)S(1)} %iota_compare_fusion.5, bf16[8,64,1024]{2,1,0:T(8,128)(2,1)S(1)} %copy-done), kind=kOutput, calls=%fused_computation.82 | convolution fusion | flops 67891200 | bytes 2248704 | tf_op jit(solution)/shard_map/pqkgd,pskd->pkgqs/dot_general | solution.py:84
  4.0 0.5 fusion.14
  4.5 0.0 copy-done.8
  4.5 0.0 copy-start.7
  4.5 0.6 fusion.23
  5.1 0.7 convolution_convert_fusion.2
  5.8 3.1 %collective-permute-start = (bf16[8,16,128]{2,1,0:T(8,128)(2,1)S(1)}, bf16[8,16,128]{2,1,0:T(8,128)(2,1)S(1)}, u32[]{:S(2)}, u32[]{:S(2)}) collective-permute-start(bf16[8,16,128]{2,1,0:T(8,128)(2,1)S(1)} %convolution_convert_fusion.2), channel_id=1, source_target_pairs={{0,128},{4,132},{8,136},{12,140},{16,144},{20,148},{24,152},{28,15... | collective-permute-start | bytes 98312 | tf_op jit(solution)/shard_map/ppermute | solution.py:17
  8.9 0.1 fusion.36
  9.1 2.3 %collective-permute-done = bf16[8,16,128]{2,1,0:T(8,128)(2,1)S(1)} collective-permute-done((bf16[8,16,128]{2,1,0:T(8,128)(2,1)S(1)}, bf16[8,16,128]{2,1,0:T(8,128)(2,1)S(1)}, u32[]{:S(2)}, u32[]{:S(2)}) %collective-permute-start) | collective-permute-done | bytes 32800 | tf_op jit(solution)/shard_map/ppermute | solution.py:17
  11.3 0.0 copy-done.7
  11.3 0.2 fusion.49
  11.5 1.6 %fusion.24 = bf16[8,512,128]{2,1,0:T(8,128)(2,1)S(1)} fusion(pred[8,512]{1,0:T(8,128)(4,1)S(1)} %fusion.36, bf16[8,64,1,8,128]{4,1,3,0,2:T(8,128)(2,1)S(1)} %fusion.23, s32[8,16]{1,0:T(8,128)S(1)} %fusion.53, bf16[8,16,128]{2,0,1:T(8,128)(2,1)S(1)} %fusion.49), kind=kOutput, calls=%fused_computation.25 | convolution fusion | flops 17891328 | bytes 2134528 | tf_op jit(solution)/shard_map/jkr,jkd->jrd/dot_general | solution.py:134
  13.1 0.5 reshape.53
  13.6 2.8 %fusion.18 = bf16[512,1024]{1,0:T(8,128)(2,1)S(1)} fusion(bf16[512,1024]{1,0:T(8,128)(2,1)S(1)} %reshape.53, bf16[1024,4096]{1,0:T(8,128)(2,1)} %param.14, s32[]{:T(128)S(6)} %select_n.87), kind=kOutput, calls=%fused_computation.21 | convolution fusion | flops 1074266112 | bytes 4194308 | tf_op jit(solution)/shard_map/dot_general | solution.py:51
  16.5 0.1 collective-permute-start.2
  16.6 3.8 %fusion.15 = bf16[512,1024]{1,0:T(8,128)(2,1)} fusion(bf16[512,1024]{1,0:T(8,128)(2,1)S(1)} %reshape.53, bf16[1024,4096]{1,0:T(8,128)(2,1)} %param.14, s32[]{:T(128)S(6)} %select_n.85), kind=kOutput, calls=%fused_computation.20 | convolution fusion | flops 1074266112 | bytes 4194308 | tf_op jit(solution)/shard_map/dot_general | solution.py:51
  20.4 0.5 collective-permute-start.1
  20.9 0.0 collective-permute-done.2
  20.9 4.1 %add_convert_fusion.1 = bf16[512,1024]{1,0:T(8,128)(2,1)} fusion(bf16[512,1024]{1,0:T(8,128)(2,1)} %collective-permute-done.2, bf16[512,1024]{1,0:T(8,128)(2,1)S(1)} %reshape.53, bf16[1024,4096]{1,0:T(8,128)(2,1)} %param.14, s32[]{:T(128)S(6)} %select_n.86), kind=kOutput, calls=%fused_computation.6 | convolution fusion | flops 1075314688 | bytes 5242884 | tf_op jit(solution)/shard_map/dot_general | solution.py:51
  25.0 0.7 collective-permute-start.3
  25.7 2.9 %fusion.8 = f32[512,1024]{1,0:T(8,128)S(1)} fusion(bf16[512,1024]{1,0:T(8,128)(2,1)S(1)} %reshape.53, bf16[1024,4096]{1,0:T(8,128)(2,1)} %param.14, s32[]{:T(128)S(6)} %select_n.84), kind=kOutput, calls=%fused_computation.13 | convolution fusion | flops 1073741824 | bytes 5242884 | tf_op jit(solution)/shard_map/dot_general | solution.py:51
  28.7 0.0 copy-start.3
  28.7 0.0 copy-start.5
  28.7 0.0 collective-permute-done.1
  28.7 21.7 %collective-permute-done.3 = bf16[512,1024]{1,0:T(8,128)(2,1)} collective-permute-done((bf16[512,1024]{1,0:T(8,128)(2,1)}, bf16[512,1024]{1,0:T(8,128)(2,1)}, u32[]{:S(2)}, u32[]{:S(2)}) %collective-permute-start.3) | collective-permute-done | bytes 1048608 | tf_op jit(solution)/shard_map/ppermute | solution.py:17
  50.4 0.0 copy-done.1
  50.4 2.3 %multiply_reduce_fusion = (f32[512]{0:T(512)S(1)}, bf16[512,1024]{1,0:T(8,128)(2,1)S(1)}) fusion(bf16[8,64,1024]{2,1,0:T(8,128)(2,1)S(1)} %copy-done.1, bf16[512,1024]{1,0:T(8,128)(2,1)} %collective-permute-done.3, f32[512,1024]{1,0:T(8,128)S(1)} %fusion.8, bf16[512,1024]{1,0:T(8,128)(2,1)} %collective-permute-done.1), kind=kLoop, calls=%fused_computation.4 | loop fusion | flops 5242368 | bytes 6293504 | tf_op jit(solution)/shard_map/reduce_sum | solution.py:146
  52.7 0.0 copy-start.6
  52.7 0.0 copy-done.3
  52.7 0.0 copy-done.5
  52.7 2.4 %fusion.12 = f32[512,64]{0,1:T(8,128)S(1)} fusion(f32[1024,64]{0,1:T(8,128)S(1)} %copy-done.3, bf16[512,1024]{1,0:T(8,128)(2,1)S(1)} %get-tuple-element.10, bf16[512,1024]{1,0:T(8,128)(2,1)S(1)} %bitcast.57, f32[1024]{0:T(1024)S(1)} %copy-done.5), kind=kOutput, calls=%fused_computation.18 | convolution fusion | flops 404750336 | bytes 2494464 | tf_op jit(solution)/shard_map/dot_general | solution.py:148
  55.2 0.1 collective-permute-start.4
  55.3 1.4 %collective-permute-done.4 = f32[512,65]{0,1:T(8,128)S(1)} collective-permute-done((f32[512,65]{0,1:T(8,128)S(1)}, f32[512,65]{0,1:T(8,128)S(1)}, u32[]{:S(2)}, u32[]{:S(2)}) %collective-permute-start.4) | collective-permute-done | bytes 133152 | tf_op jit(solution)/shard_map/ppermute | solution.py:17
  56.6 0.8 collective-permute-start.5
  57.5 0.0 copy-done.6
  57.5 0.7 eq.63
  58.1 4.6 %collective-permute-done.5 = f32[512,65]{0,1:T(8,128)} collective-permute-done((f32[512,65]{0,1:T(8,128)S(1)}, f32[512,65]{0,1:T(8,128)}, u32[]{:S(2)}, u32[]{:S(2)}) %collective-permute-start.5) | collective-permute-done | bytes 133152 | tf_op jit(solution)/shard_map/ppermute | solution.py:17
  62.7 0.9 add.89
  63.7 0.0 copy-start.4
  63.7 2.5 %fusion.25 = f32[1024,64]{0,1:T(8,128)S(1)} fusion(bf16[512,1024]{1,0:T(8,128)(2,1)S(1)} %get-tuple-element.10, bf16[512,1024]{1,0:T(8,128)(2,1)S(1)} %bitcast.58, f32[512]{0:T(512)S(1)} %bitcast.65, f32[1024]{0:T(1024)} %param.15, s32[512]{0:T(512)} %eq.63, f32[512,65]{0,1:T(8,128)S(1)} %add.89), kind=kOutput, calls=%fused_computation.26 | convolution fusion | flops 405569536 | bytes 2500608 | tf_op jit(solution)/shard_map/dot_general | solution.py:164
  66.3 0.0 copy-done.2
  66.3 0.0 copy-done.4
  66.3 2.0 %collective-permute-start.6 = (f32[512,64]{0,1:T(8,128)S(1)}, f32[512,64]{0,1:T(8,128)S(1)}, u32[]{:S(2)}, u32[]{:S(2)}) collective-permute-start(f32[512,64]{0,1:T(8,128)S(1)} %slice_select_fusion), channel_id=1, source_target_pairs={{0,4},{4,0},{8,12},{12,8},{16,20},{20,16},{24,28},{28,24},{32,36},... | collective-permute-start | bytes 393224 | tf_op jit(solution)/shard_map/ppermute | solution.py:17
  68.3 3.0 %collective-permute-done.6 = f32[512,64]{0,1:T(8,128)S(1)} collective-permute-done((f32[512,64]{0,1:T(8,128)S(1)}, f32[512,64]{0,1:T(8,128)S(1)}, u32[]{:S(2)}, u32[]{:S(2)}) %collective-permute-start.6) | collective-permute-done | bytes 131104 | tf_op jit(solution)/shard_map/ppermute | solution.py:17
  71.4 3.4 %collective-permute-start.7 = (f32[256,64]{0,1:T(8,128)S(1)}, f32[256,64]{0,1:T(8,128)S(1)}, u32[]{:S(2)}, u32[]{:S(2)}) collective-permute-start(f32[256,64]{0,1:T(8,128)S(1)} %slice_select_fusion.1), channel_id=1, source_target_pairs={{0,8},{4,12},{8,0},{12,4},{16,24},{20,28},{24,16},{28,20},{32,40},... | collective-permute-start | bytes 196616 | tf_op jit(solution)/shard_map/ppermute | solution.py:17
  74.8 2.2 %collective-permute-done.7 = f32[256,64]{0,1:T(8,128)S(1)} collective-permute-done((f32[256,64]{0,1:T(8,128)S(1)}, f32[256,64]{0,1:T(8,128)S(1)}, u32[]{:S(2)}, u32[]{:S(2)}) %collective-permute-start.7) | collective-permute-done | bytes 65568 | tf_op jit(solution)/shard_map/ppermute | solution.py:17
  77.0 7.6 %collective-permute-start.8 = (f32[256,64]{0,1:T(8,128)S(1)}, f32[256,64]{0,1:T(8,128)S(1)}, u32[]{:S(2)}, u32[]{:S(2)}) collective-permute-start(f32[256,64]{0,1:T(8,128)S(1)} %select_add_fusion.1), channel_id=1, source_target_pairs={{0,16},{4,20},{8,24},{12,28},{16,0},{20,4},{24,8},{28,12},{32,48},... | collective-permute-start | bytes 196616 | tf_op jit(solution)/shard_map/ppermute | solution.py:17
  84.7 2.8 %collective-permute-done.8 = f32[256,64]{0,1:T(8,128)S(1)} collective-permute-done((f32[256,64]{0,1:T(8,128)S(1)}, f32[256,64]{0,1:T(8,128)S(1)}, u32[]{:S(2)}, u32[]{:S(2)}) %collective-permute-start.8) | collective-permute-done | bytes 65568 | tf_op jit(solution)/shard_map/ppermute | solution.py:17
  87.5 1.3 %collective-permute-start.9 = (f32[256,64]{0,1:T(8,128)S(1)}, f32[256,64]{0,1:T(8,128)S(1)}, u32[]{:S(2)}, u32[]{:S(2)}) collective-permute-start(f32[256,64]{0,1:T(8,128)S(1)} %add.97), channel_id=1, source_target_pairs={{0,32},{4,36},{8,40},{12,44},{16,48},{20,52},{24,56},{28,60},{32,0... | collective-permute-start | bytes 196616 | tf_op jit(solution)/shard_map/ppermute | solution.py:17
  88.8 4.5 %collective-permute-done.9 = f32[256,64]{0,1:T(8,128)S(1)} collective-permute-done((f32[256,64]{0,1:T(8,128)S(1)}, f32[256,64]{0,1:T(8,128)S(1)}, u32[]{:S(2)}, u32[]{:S(2)}) %collective-permute-start.9) | collective-permute-done | bytes 65568 | tf_op jit(solution)/shard_map/ppermute | solution.py:17
  93.4 1.6 %collective-permute-start.10 = (f32[256,64]{0,1:T(8,128)S(1)}, f32[256,64]{0,1:T(8,128)S(1)}, u32[]{:S(2)}, u32[]{:S(2)}) collective-permute-start(f32[256,64]{0,1:T(8,128)S(1)} %add.98), channel_id=1, source_target_pairs={{0,64},{4,68},{8,72},{12,76},{16,80},{20,84},{24,88},{28,92},{32,9... | collective-permute-start | bytes 196616 | tf_op jit(solution)/shard_map/ppermute | solution.py:17
  95.0 2.8 %collective-permute-done.10 = f32[256,64]{0,1:T(8,128)S(1)} collective-permute-done((f32[256,64]{0,1:T(8,128)S(1)}, f32[256,64]{0,1:T(8,128)S(1)}, u32[]{:S(2)}, u32[]{:S(2)}) %collective-permute-start.10) | collective-permute-done | bytes 65568 | tf_op jit(solution)/shard_map/ppermute | solution.py:17
  97.7 3.1 %collective-permute-start.11 = (f32[256,64]{0,1:T(8,128)S(1)}, f32[256,64]{0,1:T(8,128)S(1)}, u32[]{:S(2)}, u32[]{:S(2)}) collective-permute-start(f32[256,64]{0,1:T(8,128)S(1)} %add.99), channel_id=1, source_target_pairs={{0,128},{4,132},{8,136},{12,140},{16,144},{20,148},{24,152},{28,15... | collective-permute-start | bytes 196616 | tf_op jit(solution)/shard_map/ppermute | solution.py:17
  100.9 2.7 %collective-permute-done.11 = f32[256,64]{0,1:T(8,128)S(1)} collective-permute-done((f32[256,64]{0,1:T(8,128)S(1)}, f32[256,64]{0,1:T(8,128)S(1)}, u32[]{:S(2)}, u32[]{:S(2)}) %collective-permute-start.11) | collective-permute-done | bytes 65568 | tf_op jit(solution)/shard_map/ppermute | solution.py:17
  103.6 0.8 collective-permute-start.12
  104.4 4.5 %collective-permute-done.12 = f32[256,64]{0,1:T(8,128)S(1)} collective-permute-done((f32[256,64]{0,1:T(8,128)S(1)}, f32[256,64]{0,1:T(8,128)S(1)}, u32[]{:S(2)}, u32[]{:S(2)}) %collective-permute-start.12) | collective-permute-done | bytes 65568 | tf_op jit(solution)/shard_map/ppermute | solution.py:17
  109.0 0.1 collective-permute-start.13
  109.1 0.7 slice_multiply_fusion
  109.8 0.8 copy.29
  110.6 3.4 %collective-permute-done.13 = f32[512,64]{0,1:T(8,128)S(1)} collective-permute-done((f32[512,64]{0,1:T(8,128)S(1)}, f32[512,64]{0,1:T(8,128)S(1)}, u32[]{:S(2)}, u32[]{:S(2)}) %collective-permute-start.13) | collective-permute-done | bytes 131104 | tf_op jit(solution)/shard_map/ppermute | solution.py:17
  114.0 0.7 maximum_select_fusion
  (17 shorter events, 0.2 us)
Async XLA Ops:
  0.6 1.3 %copy-start = (bf16[8,64,1024]{2,1,0:T(8,128)(2,1)S(1)}, bf16[8,64,1024]{2,1,0:T(8,128)(2,1)}, u32[]{:S(2)}) copy-start(bf16[8,64,1024]{2,1,0:T(8,128)(2,1)} %param.11) | copy-start | bytes 3145732
  1.9 2.6 %copy-start.8 = (bf16[8,64,128]{2,1,0:T(8,128)(2,1)S(1)}, bf16[8,64,128]{2,1,0:T(8,128)(2,1)}, u32[]{:S(2)}) copy-start(bf16[8,64,128]{2,1,0:T(8,128)(2,1)} %param.13) | copy-start | bytes 393220
  4.5 6.8 %copy-start.7 = (s32[8]{0:T(128)S(1)}, s32[8]{0:T(128)}, u32[]{:S(2)}) copy-start(s32[8]{0:T(128)} %param.17) | copy-start | bytes 100
  5.8 5.5 %collective-permute-start = (bf16[8,16,128]{2,1,0:T(8,128)(2,1)S(1)}, bf16[8,16,128]{2,1,0:T(8,128)(2,1)S(1)}, u32[]{:S(2)}, u32[]{:S(2)}) collective-permute-start(bf16[8,16,128]{2,1,0:T(8,128)(2,1)S(1)} %convolution_convert_fusion.2), channel_id=1, source_target_pairs={{0,128},{4,132},{8,136},{12,140},{16,144},{20,148},{24,152},{28,15... | collective-permute-start | bytes 98312 | tf_op jit(solution)/shard_map/ppermute | solution.py:17
  16.5 4.4 %collective-permute-start.2 = (bf16[512,1024]{1,0:T(8,128)(2,1)S(1)}, bf16[512,1024]{1,0:T(8,128)(2,1)}, u32[]{:S(2)}, u32[]{:S(2)}) collective-permute-start(bf16[512,1024]{1,0:T(8,128)(2,1)S(1)} %fusion.18), channel_id=1, source_target_pairs={{0,1},{1,0},{2,3},{3,2},{4,5},{5,4},{6,7},{7,6},{8,9},{9,8},{10,11... | collective-permute-start | bytes 3145736 | tf_op jit(solution)/shard_map/ppermute | solution.py:17
  20.4 8.3 %collective-permute-start.1 = (bf16[512,1024]{1,0:T(8,128)(2,1)}, bf16[512,1024]{1,0:T(8,128)(2,1)}, u32[]{:S(2)}, u32[]{:S(2)}) collective-permute-start(bf16[512,1024]{1,0:T(8,128)(2,1)} %fusion.15), channel_id=1, source_target_pairs={{0,1},{1,0},{2,3},{3,2},{4,5},{5,4},{6,7},{7,6},{8,9},{9,8},{10,11... | collective-permute-start | bytes 3145736 | tf_op jit(solution)/shard_map/ppermute | solution.py:17
  25.0 25.4 %collective-permute-start.3 = (bf16[512,1024]{1,0:T(8,128)(2,1)}, bf16[512,1024]{1,0:T(8,128)(2,1)}, u32[]{:S(2)}, u32[]{:S(2)}) collective-permute-start(bf16[512,1024]{1,0:T(8,128)(2,1)} %add_convert_fusion.1), channel_id=1, source_target_pairs={{0,2},{1,3},{2,0},{3,1},{4,6},{5,7},{6,4},{7,5},{8,10},{9,11},{10,... | collective-permute-start | bytes 3145736 | tf_op jit(solution)/shard_map/ppermute | solution.py:17
  25.7 24.7 %copy-start.1 = (bf16[8,64,1024]{2,1,0:T(8,128)(2,1)S(1)}, bf16[8,64,1024]{2,1,0:T(8,128)(2,1)}, u32[]{:S(2)}) copy-start(bf16[8,64,1024]{2,1,0:T(8,128)(2,1)} %param.10) | copy-start | bytes 3145732
  28.7 24.1 %copy-start.3 = (f32[1024,64]{0,1:T(8,128)S(1)}, f32[1024,64]{0,1:T(8,128)}, u32[]{:S(2)}) copy-start(f32[1024,64]{0,1:T(8,128)} %param.16) | copy-start | bytes 786436
  28.7 24.1 %copy-start.5 = (f32[1024]{0:T(1024)S(1)}, f32[1024]{0:T(1024)}, u32[]{:S(2)}) copy-start(f32[1024]{0:T(1024)} %param.15) | copy-start | bytes 12292
  52.7 13.6 %copy-start.2 = (bf16[512,1024]{1,0:T(8,128)(2,1)}, bf16[512,1024]{1,0:T(8,128)(2,1)S(1)}, u32[]{:S(2)}) copy-start(bf16[512,1024]{1,0:T(8,128)(2,1)S(1)} %get-tuple-element.10) | copy-start | bytes 3145732
  52.7 4.8 %copy-start.6 = (s32[8,64]{1,0:T(8,128)S(1)}, s32[8,64]{1,0:T(8,128)}, u32[]{:S(2)}) copy-start(s32[8,64]{1,0:T(8,128)} %param.19) | copy-start | bytes 6148
  55.2 1.5 %collective-permute-start.4 = (f32[512,65]{0,1:T(8,128)S(1)}, f32[512,65]{0,1:T(8,128)S(1)}, u32[]{:S(2)}, u32[]{:S(2)}) collective-permute-start(f32[512,65]{0,1:T(8,128)S(1)} %pad_maximum_fusion), channel_id=1, source_target_pairs={{0,1},{1,0},{2,3},{3,2},{4,5},{5,4},{6,7},{7,6},{8,9},{9,8},{10,11... | collective-permute-start | bytes 399368 | tf_op jit(solution)/shard_map/ppermute | solution.py:17
  56.6 6.1 %collective-permute-start.5 = (f32[512,65]{0,1:T(8,128)S(1)}, f32[512,65]{0,1:T(8,128)}, u32[]{:S(2)}, u32[]{:S(2)}) collective-permute-start(f32[512,65]{0,1:T(8,128)S(1)} %fusion.64), channel_id=1, source_target_pairs={{0,2},{1,3},{2,0},{3,1},{4,6},{5,7},{6,4},{7,5},{8,10},{9,11},{10,... | collective-permute-start | bytes 399368 | tf_op jit(solution)/shard_map/ppermute | solution.py:17
  63.7 2.6 %copy-start.4 = (f32[512,1]{0,1:T(1,128)}, f32[512,1]{0,1:T(1,128)S(1)}, u32[]{:S(2)}) copy-start(f32[512,1]{0,1:T(1,128)S(1)} %fusion.57) | copy-start | bytes 6148
  66.3 5.1 %collective-permute-start.6 = (f32[512,64]{0,1:T(8,128)S(1)}, f32[512,64]{0,1:T(8,128)S(1)}, u32[]{:S(2)}, u32[]{:S(2)}) collective-permute-start(f32[512,64]{0,1:T(8,128)S(1)} %slice_select_fusion), channel_id=1, source_target_pairs={{0,4},{4,0},{8,12},{12,8},{16,20},{20,16},{24,28},{28,24},{32,36},... | collective-permute-start | bytes 393224 | tf_op jit(solution)/shard_map/ppermute | solution.py:17
  71.4 5.6 %collective-permute-start.7 = (f32[256,64]{0,1:T(8,128)S(1)}, f32[256,64]{0,1:T(8,128)S(1)}, u32[]{:S(2)}, u32[]{:S(2)}) collective-permute-start(f32[256,64]{0,1:T(8,128)S(1)} %slice_select_fusion.1), channel_id=1, source_target_pairs={{0,8},{4,12},{8,0},{12,4},{16,24},{20,28},{24,16},{28,20},{32,40},... | collective-permute-start | bytes 196616 | tf_op jit(solution)/shard_map/ppermute | solution.py:17
  77.0 10.5 %collective-permute-start.8 = (f32[256,64]{0,1:T(8,128)S(1)}, f32[256,64]{0,1:T(8,128)S(1)}, u32[]{:S(2)}, u32[]{:S(2)}) collective-permute-start(f32[256,64]{0,1:T(8,128)S(1)} %select_add_fusion.1), channel_id=1, source_target_pairs={{0,16},{4,20},{8,24},{12,28},{16,0},{20,4},{24,8},{28,12},{32,48},... | collective-permute-start | bytes 196616 | tf_op jit(solution)/shard_map/ppermute | solution.py:17
  87.5 5.9 %collective-permute-start.9 = (f32[256,64]{0,1:T(8,128)S(1)}, f32[256,64]{0,1:T(8,128)S(1)}, u32[]{:S(2)}, u32[]{:S(2)}) collective-permute-start(f32[256,64]{0,1:T(8,128)S(1)} %add.97), channel_id=1, source_target_pairs={{0,32},{4,36},{8,40},{12,44},{16,48},{20,52},{24,56},{28,60},{32,0... | collective-permute-start | bytes 196616 | tf_op jit(solution)/shard_map/ppermute | solution.py:17
  93.4 4.4 %collective-permute-start.10 = (f32[256,64]{0,1:T(8,128)S(1)}, f32[256,64]{0,1:T(8,128)S(1)}, u32[]{:S(2)}, u32[]{:S(2)}) collective-permute-start(f32[256,64]{0,1:T(8,128)S(1)} %add.98), channel_id=1, source_target_pairs={{0,64},{4,68},{8,72},{12,76},{16,80},{20,84},{24,88},{28,92},{32,9... | collective-permute-start | bytes 196616 | tf_op jit(solution)/shard_map/ppermute | solution.py:17
  97.7 5.9 %collective-permute-start.11 = (f32[256,64]{0,1:T(8,128)S(1)}, f32[256,64]{0,1:T(8,128)S(1)}, u32[]{:S(2)}, u32[]{:S(2)}) collective-permute-start(f32[256,64]{0,1:T(8,128)S(1)} %add.99), channel_id=1, source_target_pairs={{0,128},{4,132},{8,136},{12,140},{16,144},{20,148},{24,152},{28,15... | collective-permute-start | bytes 196616 | tf_op jit(solution)/shard_map/ppermute | solution.py:17
  103.6 5.3 %collective-permute-start.12 = (f32[256,64]{0,1:T(8,128)S(1)}, f32[256,64]{0,1:T(8,128)S(1)}, u32[]{:S(2)}, u32[]{:S(2)}) collective-permute-start(f32[256,64]{0,1:T(8,128)S(1)} %add.100), channel_id=1, source_target_pairs={{0,8},{4,12},{8,0},{12,4},{16,24},{20,28},{24,16},{28,20},{32,40},... | collective-permute-start | bytes 196616 | tf_op jit(solution)/shard_map/ppermute | solution.py:17
  109.0 5.1 %collective-permute-start.13 = (f32[512,64]{0,1:T(8,128)S(1)}, f32[512,64]{0,1:T(8,128)S(1)}, u32[]{:S(2)}, u32[]{:S(2)}) collective-permute-start(f32[512,64]{0,1:T(8,128)S(1)} %maximum_select_fusion.1), channel_id=1, source_target_pairs={{0,4},{4,0},{8,12},{12,8},{16,20},{20,16},{24,28},{28,24},{32,36},... | collective-permute-start | bytes 393224 | tf_op jit(solution)/shard_map/ppermute | solution.py:17

commit v4 on v3

--- a/solution.py
+++ b/solution.py
@@ -60,7 +60,9 @@
         return total
     far = position ^ 2
     from_partner = sent(block(far ^ 1), 1)
-    from_far = sent(block(far) + from_partner, 2)
+    far_sum = (block(far) + from_partner).astype(jnp.bfloat16)
+    heads, far_sum = lax.optimization_barrier((heads, far_sum))
+    from_far = exchanged(far_sum, axis, 2).astype(jnp.float32)
     near = sent(block(position ^ 1), 1)
     return block(position) + near + from_far
 
@@ -137,37 +139,47 @@
     patch_mask = jnp.any(picks, axis=1)
     patched = jnp.where(patch_mask[..., None], placed, flat_heads)
 
-    attn_local = block_reduce_scatter(
-        patched.reshape(token_count, -1), out_weight, "tensor"
-    ).astype(jnp.bfloat16)
-    hidden = residual.reshape(token_count, feature_count).astype(jnp.float32) + attn_local.astype(
-        jnp.float32
-    )
-    square_local = jnp.sum(hidden * hidden, axis=1)
-    scaled = hidden * norm_gain
-    raw_part = jnp.dot(
-        scaled, probe_weight, precision=lax.Precision.HIGHEST, preferred_element_type=jnp.float32
-    )
+    flat_patched = patched.reshape(token_count, -1)
+    flat_residual = residual.reshape(token_count, feature_count)
+    labels = concept_labels.reshape(token_count)
     concepts = probe_weight.shape[1]
-    packed = jnp.concatenate([raw_part, square_local[:, None]], axis=1)
-    tensor_count = lax.axis_size("tensor")
-    packed = butterfly_sum(packed, "tensor", [1 << k for k in range(tensor_count.bit_length() - 1)])
-    raw_logits = packed[:, :concepts]
-    square_sum = packed[:, concepts]
-    inverse_rms = lax.rsqrt(square_sum / DW + norm_epsilon)
-    logits = raw_logits * inverse_rms[:, None]
-    normed = scaled * inverse_rms[:, None]
-    classes = jnp.arange(concepts, dtype=jnp.int32)
-    target = (concept_labels.reshape(token_count)[:, None] == classes[None, :]).astype(jnp.float32)
-    error = jax.nn.sigmoid(logits) - target
+    tensor_bits = [1 << k for k in range(lax.axis_size("tensor").bit_length() - 1)]
+    chunk_count = 2 if token_count % 2 == 0 else 1
+    chunk = token_count // chunk_count
+    attn_chunks, logit_chunks, grad_local = [], [], None
+    for index in range(chunk_count):
+        rows_here = slice(index * chunk, (index + 1) * chunk)
+        attn_local = block_reduce_scatter(flat_patched[rows_here], out_weight, "tensor").astype(
+            jnp.bfloat16
+        )
+        hidden = flat_residual[rows_here].astype(jnp.float32) + attn_local.astype(jnp.float32)
+        square_local = jnp.sum(hidden * hidden, axis=1)
+        scaled = hidden * norm_gain
+        raw_part = jnp.dot(
+            scaled, probe_weight, precision=lax.Precision.HIGHEST, preferred_element_type=jnp.float32
+        )
+        packed = jnp.concatenate([raw_part, square_local[:, None]], axis=1)
+        packed = butterfly_sum(packed, "tensor", tensor_bits)
+        inverse_rms = lax.rsqrt(packed[:, concepts] / DW + norm_epsilon)
+        logits = packed[:, :concepts] * inverse_rms[:, None]
+        normed = scaled * inverse_rms[:, None]
+        classes = jnp.arange(concepts, dtype=jnp.int32)
+        target = (labels[rows_here][:, None] == classes[None, :]).astype(jnp.float32)
+        error = jax.nn.sigmoid(logits) - target
+        grad_part = lax.dot_general(
+            normed,
+            error,
+            (((0,), (0,)), ((), ())),
+            precision=lax.Precision.HIGHEST,
+            preferred_element_type=jnp.float32,
+        )
+        grad_local = grad_part if grad_local is None else grad_local + grad_part
+        attn_chunks.append(attn_local)
+        logit_chunks.append(logits)
+    attn_local = jnp.concatenate(attn_chunks, axis=0)
+    logits = jnp.concatenate(logit_chunks, axis=0)
     total_tokens = token_count * lax.axis_size("dp")
-    grad_local = lax.dot_general(
-        normed,
-        error,
-        (((0,), (0,)), ((), ())),
-        precision=lax.Precision.HIGHEST,
-        preferred_element_type=jnp.float32,
-    ) / math.sqrt(total_tokens)
+    grad_local = grad_local / math.sqrt(total_tokens)
     halving_bits, doubling_bits = dp_bits(lax.axis_size("dp"))
     probe_grad = tree_all_reduce(grad_local, "dp", halving_bits, doubling_bits)
     return (

time: 115 us -> 112 us (0.974)
  waiting for transfers between devices: 56.1 us -> 44.6 us
  matrix products: 23.8 us -> 29.8 us
  starting transfers between devices: 25.3 us -> 28.5 us
  other arithmetic: 5.47 us -> 3.47 us
  local copies, waits for them, and re-layouts: 3.26 us -> 4.74 us
    ppermute x14 -> x19, waiting for transfers between devices: 56.1 us -> 44.6 us  [exchanged(): return lax.ppermute(block, axis, [(i, i ^ bit) for i in range(count)])]
    dot_general x4 -> x8, matrix products: 13.7 us -> 20.3 us  [block(): return jnp.dot(heads, columns, preferred_element_type=jnp.float32)]
    ppermute x14 -> x19, starting transfers between devices: 25.3 us -> 28.5 us  [exchanged(): return lax.ppermute(block, axis, [(i, i ^ bit) for i in range(count)])]
    slice x0 -> x5, local copies, waits for them, and re-layouts: none -> 2.47 us  [the longest x3 2.36 us: per_device(): flat_patched[rows_here]]
    reduce_sum x1 -> x2, other arithmetic: 2.3 us -> 0.8 us  [per_device(): square_local = jnp.sum(hidden * hidden, axis=1)]
    dot_general x1 -> x2, matrix products: 2.55 us -> 2.01 us  [per_device(): lax.dot_general(normed, error, (((0,), (0,)), ((), ())), precision=lax.Pr...]
    dot_general x1 -> x2, matrix products: 2.39 us -> 2.31 us  [per_device(): jnp.dot(scaled, probe_weight, precision=lax.Precision.HIGHEST, preferred_...]
  transfers between devices with their start and end apart: 14 -> 19, of which waited for: 12 -> 14; matrix products, arithmetic and copies ran while one was open for 11% -> 21% of each run, Pallas kernels for 0% -> 0%
where the time goes in v4:
time: 112 us
  waiting for transfers between devices  44.6 us (40%)
  matrix products  29.8 us (27%)
  starting transfers between devices  28.5 us (25%)
  local copies, waits for them, and re-layouts  4.74 us (4%)
  other arithmetic  3.47 us (3%)
    ppermute x19, waiting for transfers between devices, exchanged(): return lax.ppermute(block, axis, [(i, i ^ bit) for i in range(count)])  44.6 us
    ppermute x19, starting transfers between devices, exchanged(): return lax.ppermute(block, axis, [(i, i ^ bit) for i in range(count)])  28.5 us
    dot_general x8, matrix products, block(): return jnp.dot(heads, columns, preferred_element_type=jnp.float32)  20.3 us
    slice x3, local copies, waits for them, and re-layouts, per_device(): flat_patched[rows_here]  2.36 us
    dot_general x2, matrix products, per_device(): jnp.dot(scaled, probe_weight, precision=lax.Precision.HIGHEST, preferred_...  2.31 us
  transfers between devices with their start and end apart: 19, of which 14 were waited for; matrix products, arithmetic and copies ran while one was open for 21% of the time, Pallas kernels for 0%

profile of v4, /device:TPU:24, one launch (start us, length us, event | category | flops | bytes accessed | tf_op | source)
XLA Modules:
  0.0 112.1 jit_solution(361643706277632366)
XLA Ops:
  0.7 0.8 fusion.105
  1.5 0.4 copy-done
  1.9 2.1 %fusion.107 = (f32[8,8,64]{2,1,0:T(8,128)S(1)}, f32[8,1,8,64,64]{3,4,2,0,1:T(8,128)S(1)}) fusion(bf16[8,64,128]{2,1,0:T(8,128)(2,1)} %param.12, pred[64,64]{0,1:T(8,128)(4,1)S(1)} %iota_compare_fusion.7, bf16[8,64,1024]{2,1,0:T(8,128)(2,1)S(1)} %copy-done), kind=kOutput, calls=%fused_computation.128 | convolution fusion | flops 67891200 | bytes 2248704 | tf_op jit(solution)/shard_map/pqkgd,pskd->pkgqs/dot_general | solution.py:86
  4.0 0.5 fusion
  4.5 0.6 fusion.17
  5.2 0.7 convolution_convert_fusion.2
  5.9 3.1 %collective-permute-start = (bf16[8,16,128]{2,1,0:T(8,128)(2,1)S(1)}, bf16[8,16,128]{2,1,0:T(8,128)(2,1)S(1)}, u32[]{:S(2)}, u32[]{:S(2)}) collective-permute-start(bf16[8,16,128]{2,1,0:T(8,128)(2,1)S(1)} %convolution_convert_fusion.2), channel_id=1, source_target_pairs={{0,128},{4,132},{8,136},{12,140},{16,144},{20,148},{24,152},{28,15... | collective-permute-start | bytes 98312 | tf_op jit(solution)/shard_map/ppermute | solution.py:17
  9.0 0.1 fusion.54
  9.1 2.3 %collective-permute-done = bf16[8,16,128]{2,1,0:T(8,128)(2,1)S(1)} collective-permute-done((bf16[8,16,128]{2,1,0:T(8,128)(2,1)S(1)}, bf16[8,16,128]{2,1,0:T(8,128)(2,1)S(1)}, u32[]{:S(2)}, u32[]{:S(2)}) %collective-permute-start) | collective-permute-done | bytes 32800 | tf_op jit(solution)/shard_map/ppermute | solution.py:17
  11.4 0.2 fusion.71
  11.6 1.6 %fusion.18 = bf16[8,512,128]{2,1,0:T(8,128)(2,1)S(1)} fusion(pred[8,512]{1,0:T(8,128)(4,1)S(1)} %fusion.54, bf16[8,64,1,8,128]{4,1,3,0,2:T(8,128)(2,1)S(1)} %fusion.17, s32[8,16]{1,0:T(8,128)S(1)} %fusion.79, bf16[8,16,128]{2,0,1:T(8,128)(2,1)S(1)} %fusion.71), kind=kOutput, calls=%fused_computation.23 | convolution fusion | flops 17891328 | bytes 2134528 | tf_op jit(solution)/shard_map/jkr,jkd->jrd/dot_general | solution.py:136
  13.1 0.9 fusion.103
  14.0 0.2 slice.61
  14.3 3.2 %fusion.19 = bf16[256,1024]{1,0:T(8,128)(2,1)} fusion(bf16[256,1024]{1,0:T(8,128)(2,1)S(1)} %slice.61, bf16[1024,4096]{1,0:T(8,128)(2,1)} %param.14, s32[]{:T(128)S(6)} %select_n.89), kind=kOutput, calls=%fused_computation.24 | convolution fusion | flops 537133056 | bytes 3145732 | tf_op jit(solution)/shard_map/dot_general | solution.py:51
  17.5 0.1 fusion.104
  17.6 1.3 %slice.63 = bf16[256,1024]{1,0:T(8,128)(2,1)S(1)} reshape(bf16[4,512,128]{2,1,0:T(8,128)(2,1)} %get-tuple-element.22) | data formatting | bytes 1048576 | tf_op jit(solution)/shard_map/slice | solution.py:152
  18.9 3.1 %fusion.22 = bf16[256,1024]{1,0:T(8,128)(2,1)} fusion(bf16[256,1024]{1,0:T(8,128)(2,1)S(1)} %slice.63, bf16[1024,4096]{1,0:T(8,128)(2,1)} %param.14, s32[]{:T(128)S(6)} %select_n.89), kind=kOutput, calls=%fused_computation.25 | convolution fusion | flops 537133056 | bytes 3145732 | tf_op jit(solution)/shard_map/dot_general | solution.py:51
  22.0 0.5 collective-permute-start.4
  22.5 0.1 eq.78
  22.6 0.1 eq.82
  22.6 2.4 %add_convert_fusion.3 = bf16[256,1024]{1,0:T(8,128)(2,1)S(1)} fusion(bf16[256,1024]{1,0:T(8,128)(2,1)} %collective-permute-done.1, bf16[256,1024]{1,0:T(8,128)(2,1)S(1)} %slice.61, bf16[1024,4096]{1,0:T(8,128)(2,1)} %param.14, s32[]{:T(128)S(6)} %select_n.88), kind=kOutput, calls=%fused_computation.46 | convolution fusion | flops 537657344 | bytes 3670020 | tf_op jit(solution)/shard_map/dot_general | solution.py:51
  25.0 2.3 %fusion.25 = bf16[256,1024]{1,0:T(8,128)(2,1)S(1)} fusion(bf16[256,1024]{1,0:T(8,128)(2,1)S(1)} %slice.61, bf16[1024,4096]{1,0:T(8,128)(2,1)} %param.14, s32[]{:T(128)S(6)} %select_n.91), kind=kOutput, calls=%fused_computation.26 | convolution fusion | flops 537133056 | bytes 3145732 | tf_op jit(solution)/shard_map/dot_general | solution.py:51
  27.4 0.1 collective-permute-start.2
  27.5 0.8 collective-permute-start.3
  28.3 2.4 %add_convert_fusion.1 = bf16[256,1024]{1,0:T(8,128)(2,1)S(1)} fusion(bf16[256,1024]{1,0:T(8,128)(2,1)} %collective-permute-done.4, bf16[256,1024]{1,0:T(8,128)(2,1)S(1)} %slice.63, bf16[1024,4096]{1,0:T(8,128)(2,1)} %param.14, s32[]{:T(128)S(6)} %select_n.88), kind=kOutput, calls=%fused_computation.44 | convolution fusion | flops 537657344 | bytes 3670020 | tf_op jit(solution)/shard_map/dot_general | solution.py:51
  30.7 2.3 %fusion.28 = bf16[256,1024]{1,0:T(8,128)(2,1)S(1)} fusion(bf16[256,1024]{1,0:T(8,128)(2,1)S(1)} %slice.63, bf16[1024,4096]{1,0:T(8,128)(2,1)} %param.14, s32[]{:T(128)S(6)} %select_n.91), kind=kOutput, calls=%fused_computation.27 | convolution fusion | flops 537133056 | bytes 3145732 | tf_op jit(solution)/shard_map/dot_general | solution.py:51
  33.0 0.2 collective-permute-start.5
  33.2 1.4 %collective-permute-start.6 = (bf16[256,1024]{1,0:T(8,128)(2,1)S(1)}, bf16[256,1024]{1,0:T(8,128)(2,1)S(1)}, u32[]{:S(2)}, u32[]{:S(2)}) collective-permute-start(bf16[256,1024]{1,0:T(8,128)(2,1)S(1)} %add_convert_fusion.1), channel_id=1, source_target_pairs={{0,2},{1,3},{2,0},{3,1},{4,6},{5,7},{6,4},{7,5},{8,10},{9,11},{10,... | collective-permute-start | bytes 1572872 | tf_op jit(solution)/shard_map/ppermute | solution.py:17
  34.6 2.3 %fusion.7 = f32[256,1024]{1,0:T(8,128)S(1)} fusion(bf16[256,1024]{1,0:T(8,128)(2,1)S(1)} %slice.61, bf16[1024,4096]{1,0:T(8,128)(2,1)} %param.14, s32[]{:T(128)S(6)} %select_n.90), kind=kOutput, calls=%fused_computation.10 | convolution fusion | flops 536870912 | bytes 3670020 | tf_op jit(solution)/shard_map/dot_general | solution.py:51
  36.9 2.3 %fusion.5 = f32[256,1024]{1,0:T(8,128)S(1)} fusion(bf16[256,1024]{1,0:T(8,128)(2,1)S(1)} %slice.63, bf16[1024,4096]{1,0:T(8,128)(2,1)} %param.14, s32[]{:T(128)S(6)} %select_n.90), kind=kOutput, calls=%fused_computation.8 | convolution fusion | flops 536870912 | bytes 3670020 | tf_op jit(solution)/shard_map/dot_general | solution.py:51
  39.3 3.0 %collective-permute-done.3 = bf16[256,1024]{1,0:T(8,128)(2,1)S(1)} collective-permute-done((bf16[256,1024]{1,0:T(8,128)(2,1)S(1)}, bf16[256,1024]{1,0:T(8,128)(2,1)S(1)}, u32[]{:S(2)}, u32[]{:S(2)}) %collective-permute-start.3) | collective-permute-done | bytes 524320 | tf_op jit(solution)/shard_map/ppermute | solution.py:17
  42.3 0.4 multiply_reduce_fusion.1
  42.8 1.2 %fusion.45 = f32[256,64]{0,1:T(8,128)S(1)} fusion(f32[1024,64]{0,1:T(8,128)S(1)} %copy-done.2, bf16[256,1024]{1,0:T(8,128)(2,1)S(1)} %get-tuple-element.18, bf16[256,1024]{1,0:T(8,128)(2,1)S(1)} %bitcast.69, f32[1024]{0:T(1024)S(1)} %copy-done.3), kind=kOutput, calls=%fused_computation.50 | convolution fusion | flops 202375168 | bytes 1380352 | tf_op jit(solution)/shard_map/dot_general | solution.py:158
  43.9 0.1 collective-permute-start.7
  44.0 9.0 %collective-permute-done.6 = bf16[256,1024]{1,0:T(8,128)(2,1)S(1)} collective-permute-done((bf16[256,1024]{1,0:T(8,128)(2,1)S(1)}, bf16[256,1024]{1,0:T(8,128)(2,1)S(1)}, u32[]{:S(2)}, u32[]{:S(2)}) %collective-permute-start.6) | collective-permute-done | bytes 524320 | tf_op jit(solution)/shard_map/ppermute | solution.py:17
  53.0 0.4 multiply_reduce_fusion
  53.4 1.2 %fusion.42 = f32[256,64]{0,1:T(8,128)S(1)} fusion(f32[1024,64]{0,1:T(8,128)S(1)} %copy-done.2, bf16[256,1024]{1,0:T(8,128)(2,1)S(1)} %get-tuple-element.20, bf16[256,1024]{1,0:T(8,128)(2,1)S(1)} %bitcast.67, f32[1024]{0:T(1024)S(1)} %copy-done.3), kind=kOutput, calls=%fused_computation.49 | convolution fusion | flops 202375168 | bytes 1380352 | tf_op jit(solution)/shard_map/dot_general | solution.py:158
  54.6 0.1 collective-permute-start.9
  54.7 0.8 collective-permute-start.8
  55.5 0.4 collective-permute-done.9
  56.0 1.0 collective-permute-start.10
  56.9 3.0 %collective-permute-done.8 = f32[256,65]{0,1:T(8,128)S(1)} collective-permute-done((f32[256,65]{0,1:T(8,128)S(1)}, f32[256,65]{0,1:T(8,128)S(1)}, u32[]{:S(2)}, u32[]{:S(2)}) %collective-permute-start.8) | collective-permute-done | bytes 66592 | tf_op jit(solution)/shard_map/ppermute | solution.py:17
  60.0 1.1 collective-permute-done.10
  61.1 1.0 fusion.37
  62.1 1.0 fusion.31
  63.1 2.0 %collective-permute-start.11 = (f32[512,64]{0,1:T(8,128)S(1)}, f32[512,64]{0,1:T(8,128)S(1)}, u32[]{:S(2)}, u32[]{:S(2)}) collective-permute-start(f32[512,64]{0,1:T(8,128)S(1)} %slice_select_fusion), channel_id=1, source_target_pairs={{0,4},{4,0},{8,12},{12,8},{16,20},{20,16},{24,28},{28,24},{32,36},... | collective-permute-start | bytes 393224 | tf_op jit(solution)/shard_map/ppermute | solution.py:17
  65.1 3.3 %collective-permute-done.11 = f32[512,64]{0,1:T(8,128)S(1)} collective-permute-done((f32[512,64]{0,1:T(8,128)S(1)}, f32[512,64]{0,1:T(8,128)S(1)}, u32[]{:S(2)}, u32[]{:S(2)}) %collective-permute-start.11) | collective-permute-done | bytes 131104 | tf_op jit(solution)/shard_map/ppermute | solution.py:17
  68.5 3.4 %collective-permute-start.12 = (f32[256,64]{0,1:T(8,128)S(1)}, f32[256,64]{0,1:T(8,128)S(1)}, u32[]{:S(2)}, u32[]{:S(2)}) collective-permute-start(f32[256,64]{0,1:T(8,128)S(1)} %slice_select_fusion.1), channel_id=1, source_target_pairs={{0,8},{4,12},{8,0},{12,4},{16,24},{20,28},{24,16},{28,20},{32,40},... | collective-permute-start | bytes 196616 | tf_op jit(solution)/shard_map/ppermute | solution.py:17
  71.8 2.2 %collective-permute-done.12 = f32[256,64]{0,1:T(8,128)S(1)} collective-permute-done((f32[256,64]{0,1:T(8,128)S(1)}, f32[256,64]{0,1:T(8,128)S(1)}, u32[]{:S(2)}, u32[]{:S(2)}) %collective-permute-start.12) | collective-permute-done | bytes 65568 | tf_op jit(solution)/shard_map/ppermute | solution.py:17
  74.1 7.5 %collective-permute-start.13 = (f32[256,64]{0,1:T(8,128)S(1)}, f32[256,64]{0,1:T(8,128)S(1)}, u32[]{:S(2)}, u32[]{:S(2)}) collective-permute-start(f32[256,64]{0,1:T(8,128)S(1)} %select_add_fusion.1), channel_id=1, source_target_pairs={{0,16},{4,20},{8,24},{12,28},{16,0},{20,4},{24,8},{28,12},{32,48},... | collective-permute-start | bytes 196616 | tf_op jit(solution)/shard_map/ppermute | solution.py:17
  81.5 2.9 %collective-permute-done.13 = f32[256,64]{0,1:T(8,128)S(1)} collective-permute-done((f32[256,64]{0,1:T(8,128)S(1)}, f32[256,64]{0,1:T(8,128)S(1)}, u32[]{:S(2)}, u32[]{:S(2)}) %collective-permute-start.13) | collective-permute-done | bytes 65568 | tf_op jit(solution)/shard_map/ppermute | solution.py:17
  84.5 1.3 %collective-permute-start.14 = (f32[256,64]{0,1:T(8,128)S(1)}, f32[256,64]{0,1:T(8,128)S(1)}, u32[]{:S(2)}, u32[]{:S(2)}) collective-permute-start(f32[256,64]{0,1:T(8,128)S(1)} %add.134), channel_id=1, source_target_pairs={{0,32},{4,36},{8,40},{12,44},{16,48},{20,52},{24,56},{28,60},{32,0... | collective-permute-start | bytes 196616 | tf_op jit(solution)/shard_map/ppermute | solution.py:17
  85.8 4.5 %collective-permute-done.14 = f32[256,64]{0,1:T(8,128)S(1)} collective-permute-done((f32[256,64]{0,1:T(8,128)S(1)}, f32[256,64]{0,1:T(8,128)S(1)}, u32[]{:S(2)}, u32[]{:S(2)}) %collective-permute-start.14) | collective-permute-done | bytes 65568 | tf_op jit(solution)/shard_map/ppermute | solution.py:17
  90.4 1.6 %collective-permute-start.15 = (f32[256,64]{0,1:T(8,128)S(1)}, f32[256,64]{0,1:T(8,128)S(1)}, u32[]{:S(2)}, u32[]{:S(2)}) collective-permute-start(f32[256,64]{0,1:T(8,128)S(1)} %add.135), channel_id=1, source_target_pairs={{0,64},{4,68},{8,72},{12,76},{16,80},{20,84},{24,88},{28,92},{32,9... | collective-permute-start | bytes 196616 | tf_op jit(solution)/shard_map/ppermute | solution.py:17
  91.9 2.8 %collective-permute-done.15 = f32[256,64]{0,1:T(8,128)S(1)} collective-permute-done((f32[256,64]{0,1:T(8,128)S(1)}, f32[256,64]{0,1:T(8,128)S(1)}, u32[]{:S(2)}, u32[]{:S(2)}) %collective-permute-start.15) | collective-permute-done | bytes 65568 | tf_op jit(solution)/shard_map/ppermute | solution.py:17
  94.7 3.1 %collective-permute-start.16 = (f32[256,64]{0,1:T(8,128)S(1)}, f32[256,64]{0,1:T(8,128)S(1)}, u32[]{:S(2)}, u32[]{:S(2)}) collective-permute-start(f32[256,64]{0,1:T(8,128)S(1)} %add.136), channel_id=1, source_target_pairs={{0,128},{4,132},{8,136},{12,140},{16,144},{20,148},{24,152},{28,15... | collective-permute-start | bytes 196616 | tf_op jit(solution)/shard_map/ppermute | solution.py:17
  97.8 1.0 pad_maximum_fusion
  98.9 1.7 %collective-permute-done.16 = f32[256,64]{0,1:T(8,128)S(1)} collective-permute-done((f32[256,64]{0,1:T(8,128)S(1)}, f32[256,64]{0,1:T(8,128)S(1)}, u32[]{:S(2)}, u32[]{:S(2)}) %collective-permute-start.16) | collective-permute-done | bytes 65568 | tf_op jit(solution)/shard_map/ppermute | solution.py:17
  100.6 1.4 %collective-permute-start.17 = (f32[256,64]{0,1:T(8,128)S(1)}, f32[256,64]{0,1:T(8,128)S(1)}, u32[]{:S(2)}, u32[]{:S(2)}) collective-permute-start(f32[256,64]{0,1:T(8,128)S(1)} %add.137), channel_id=1, source_target_pairs={{0,8},{4,12},{8,0},{12,4},{16,24},{20,28},{24,16},{28,20},{32,40},... | collective-permute-start | bytes 196616 | tf_op jit(solution)/shard_map/ppermute | solution.py:17
  102.0 4.3 %collective-permute-done.17 = f32[256,64]{0,1:T(8,128)S(1)} collective-permute-done((f32[256,64]{0,1:T(8,128)S(1)}, f32[256,64]{0,1:T(8,128)S(1)}, u32[]{:S(2)}, u32[]{:S(2)}) %collective-permute-start.17) | collective-permute-done | bytes 65568 | tf_op jit(solution)/shard_map/ppermute | solution.py:17
  106.3 0.1 collective-permute-start.18
  106.4 0.8 copy.29
  107.3 4.1 %collective-permute-done.18 = f32[512,64]{0,1:T(8,128)S(1)} collective-permute-done((f32[512,64]{0,1:T(8,128)S(1)}, f32[512,64]{0,1:T(8,128)S(1)}, u32[]{:S(2)}, u32[]{:S(2)}) %collective-permute-start.18) | collective-permute-done | bytes 131104 | tf_op jit(solution)/shard_map/ppermute | solution.py:17
  111.4 0.7 maximum_select_fusion
  (42 shorter events, 0.3 us)
Async XLA Ops:
  0.6 1.3 %copy-start = (bf16[8,64,1024]{2,1,0:T(8,128)(2,1)S(1)}, bf16[8,64,1024]{2,1,0:T(8,128)(2,1)}, u32[]{:S(2)}) copy-start(bf16[8,64,1024]{2,1,0:T(8,128)(2,1)} %param.11) | copy-start | bytes 3145732
  1.9 2.6 %copy-start.6 = (bf16[8,64,128]{2,1,0:T(8,128)(2,1)S(1)}, bf16[8,64,128]{2,1,0:T(8,128)(2,1)}, u32[]{:S(2)}) copy-start(bf16[8,64,128]{2,1,0:T(8,128)(2,1)} %param.13) | copy-start | bytes 393220
  4.5 6.8 %copy-start.5 = (s32[8]{0:T(128)S(1)}, s32[8]{0:T(128)}, u32[]{:S(2)}) copy-start(s32[8]{0:T(128)} %param.17) | copy-start | bytes 100
  5.9 5.5 %collective-permute-start = (bf16[8,16,128]{2,1,0:T(8,128)(2,1)S(1)}, bf16[8,16,128]{2,1,0:T(8,128)(2,1)S(1)}, u32[]{:S(2)}, u32[]{:S(2)}) collective-permute-start(bf16[8,16,128]{2,1,0:T(8,128)(2,1)S(1)} %convolution_convert_fusion.2), channel_id=1, source_target_pairs={{0,128},{4,132},{8,136},{12,140},{16,144},{20,148},{24,152},{28,15... | collective-permute-start | bytes 98312 | tf_op jit(solution)/shard_map/ppermute | solution.py:17
  14.2 3.2 %copy-start.1 = (bf16[8,64,1024]{2,1,0:T(8,128)(2,1)S(1)}, bf16[8,64,1024]{2,1,0:T(8,128)(2,1)}, u32[]{:S(2)}) copy-start(bf16[8,64,1024]{2,1,0:T(8,128)(2,1)} %param.10) | copy-start | bytes 3145732
  17.4 5.2 %collective-permute-start.1 = (bf16[256,1024]{1,0:T(8,128)(2,1)}, bf16[256,1024]{1,0:T(8,128)(2,1)}, u32[]{:S(2)}, u32[]{:S(2)}) collective-permute-start(bf16[256,1024]{1,0:T(8,128)(2,1)} %fusion.19), channel_id=1, source_target_pairs={{0,1},{1,0},{2,3},{3,2},{4,5},{5,4},{6,7},{7,6},{8,9},{9,8},{10,11... | collective-permute-start | bytes 1572872 | tf_op jit(solution)/shard_map/ppermute | solution.py:17
  17.6 4.9 %copy-start.4 = (s32[8,64]{1,0:T(8,128)S(1)}, s32[8,64]{1,0:T(8,128)}, u32[]{:S(2)}) copy-start(s32[8,64]{1,0:T(8,128)} %param.19) | copy-start | bytes 6148
  22.0 6.3 %collective-permute-start.4 = (bf16[256,1024]{1,0:T(8,128)(2,1)}, bf16[256,1024]{1,0:T(8,128)(2,1)}, u32[]{:S(2)}, u32[]{:S(2)}) collective-permute-start(bf16[256,1024]{1,0:T(8,128)(2,1)} %fusion.22), channel_id=1, source_target_pairs={{0,1},{1,0},{2,3},{3,2},{4,5},{5,4},{6,7},{7,6},{8,9},{9,8},{10,11... | collective-permute-start | bytes 1572872 | tf_op jit(solution)/shard_map/ppermute | solution.py:17
  27.4 11.9 %collective-permute-start.2 = (bf16[256,1024]{1,0:T(8,128)(2,1)S(1)}, bf16[256,1024]{1,0:T(8,128)(2,1)S(1)}, u32[]{:S(2)}, u32[]{:S(2)}) collective-permute-start(bf16[256,1024]{1,0:T(8,128)(2,1)S(1)} %fusion.25), channel_id=1, source_target_pairs={{0,1},{1,0},{2,3},{3,2},{4,5},{5,4},{6,7},{7,6},{8,9},{9,8},{10,11... | collective-permute-start | bytes 1572872 | tf_op jit(solution)/shard_map/ppermute | solution.py:17
  27.5 14.9 %collective-permute-start.3 = (bf16[256,1024]{1,0:T(8,128)(2,1)S(1)}, bf16[256,1024]{1,0:T(8,128)(2,1)S(1)}, u32[]{:S(2)}, u32[]{:S(2)}) collective-permute-start(bf16[256,1024]{1,0:T(8,128)(2,1)S(1)} %add_convert_fusion.3), channel_id=1, source_target_pairs={{0,2},{1,3},{2,0},{3,1},{4,6},{5,7},{6,4},{7,5},{8,10},{9,11},{10,... | collective-permute-start | bytes 1572872 | tf_op jit(solution)/shard_map/ppermute | solution.py:17
  33.0 11.0 %collective-permute-start.5 = (bf16[256,1024]{1,0:T(8,128)(2,1)S(1)}, bf16[256,1024]{1,0:T(8,128)(2,1)S(1)}, u32[]{:S(2)}, u32[]{:S(2)}) collective-permute-start(bf16[256,1024]{1,0:T(8,128)(2,1)S(1)} %fusion.28), channel_id=1, source_target_pairs={{0,1},{1,0},{2,3},{3,2},{4,5},{5,4},{6,7},{7,6},{8,9},{9,8},{10,11... | collective-permute-start | bytes 1572872 | tf_op jit(solution)/shard_map/ppermute | solution.py:17
  33.2 19.8 %collective-permute-start.6 = (bf16[256,1024]{1,0:T(8,128)(2,1)S(1)}, bf16[256,1024]{1,0:T(8,128)(2,1)S(1)}, u32[]{:S(2)}, u32[]{:S(2)}) collective-permute-start(bf16[256,1024]{1,0:T(8,128)(2,1)S(1)} %add_convert_fusion.1), channel_id=1, source_target_pairs={{0,2},{1,3},{2,0},{3,1},{4,6},{5,7},{6,4},{7,5},{8,10},{9,11},{10,... | collective-permute-start | bytes 1572872 | tf_op jit(solution)/shard_map/ppermute | solution.py:17
  39.3 3.5 %copy-start.2 = (f32[1024,64]{0,1:T(8,128)S(1)}, f32[1024,64]{0,1:T(8,128)}, u32[]{:S(2)}) copy-start(f32[1024,64]{0,1:T(8,128)} %param.16) | copy-start | bytes 786436
  39.3 3.5 %copy-start.3 = (f32[1024]{0:T(1024)S(1)}, f32[1024]{0:T(1024)}, u32[]{:S(2)}) copy-start(f32[1024]{0:T(1024)} %param.15) | copy-start | bytes 12292
  43.9 10.8 %collective-permute-start.7 = (f32[256,65]{0,1:T(8,128)S(1)}, f32[256,65]{0,1:T(8,128)S(1)}, u32[]{:S(2)}, u32[]{:S(2)}) collective-permute-start(f32[256,65]{0,1:T(8,128)S(1)} %pad_maximum_fusion.2), channel_id=1, source_target_pairs={{0,1},{1,0},{2,3},{3,2},{4,5},{5,4},{6,7},{7,6},{8,9},{9,8},{10,11... | collective-permute-start | bytes 199688 | tf_op jit(solution)/shard_map/ppermute | solution.py:17
  54.6 1.4 %collective-permute-start.9 = (f32[256,65]{0,1:T(8,128)S(1)}, f32[256,65]{0,1:T(8,128)S(1)}, u32[]{:S(2)}, u32[]{:S(2)}) collective-permute-start(f32[256,65]{0,1:T(8,128)S(1)} %pad_maximum_fusion.3), channel_id=1, source_target_pairs={{0,1},{1,0},{2,3},{3,2},{4,5},{5,4},{6,7},{7,6},{8,9},{9,8},{10,11... | collective-permute-start | bytes 199688 | tf_op jit(solution)/shard_map/ppermute | solution.py:17
  54.7 5.2 %collective-permute-start.8 = (f32[256,65]{0,1:T(8,128)S(1)}, f32[256,65]{0,1:T(8,128)S(1)}, u32[]{:S(2)}, u32[]{:S(2)}) collective-permute-start(f32[256,65]{0,1:T(8,128)S(1)} %fusion.102), channel_id=1, source_target_pairs={{0,2},{1,3},{2,0},{3,1},{4,6},{5,7},{6,4},{7,5},{8,10},{9,11},{10,... | collective-permute-start | bytes 199688 | tf_op jit(solution)/shard_map/ppermute | solution.py:17
  56.0 5.1 %collective-permute-start.10 = (f32[256,65]{0,1:T(8,128)S(1)}, f32[256,65]{0,1:T(8,128)S(1)}, u32[]{:S(2)}, u32[]{:S(2)}) collective-permute-start(f32[256,65]{0,1:T(8,128)S(1)} %fusion.101), channel_id=1, source_target_pairs={{0,2},{1,3},{2,0},{3,1},{4,6},{5,7},{6,4},{7,5},{8,10},{9,11},{10,... | collective-permute-start | bytes 199688 | tf_op jit(solution)/shard_map/ppermute | solution.py:17
  63.1 5.3 %collective-permute-start.11 = (f32[512,64]{0,1:T(8,128)S(1)}, f32[512,64]{0,1:T(8,128)S(1)}, u32[]{:S(2)}, u32[]{:S(2)}) collective-permute-start(f32[512,64]{0,1:T(8,128)S(1)} %slice_select_fusion), channel_id=1, source_target_pairs={{0,4},{4,0},{8,12},{12,8},{16,20},{20,16},{24,28},{28,24},{32,36},... | collective-permute-start | bytes 393224 | tf_op jit(solution)/shard_map/ppermute | solution.py:17
  68.5 5.6 %collective-permute-start.12 = (f32[256,64]{0,1:T(8,128)S(1)}, f32[256,64]{0,1:T(8,128)S(1)}, u32[]{:S(2)}, u32[]{:S(2)}) collective-permute-start(f32[256,64]{0,1:T(8,128)S(1)} %slice_select_fusion.1), channel_id=1, source_target_pairs={{0,8},{4,12},{8,0},{12,4},{16,24},{20,28},{24,16},{28,20},{32,40},... | collective-permute-start | bytes 196616 | tf_op jit(solution)/shard_map/ppermute | solution.py:17
  74.1 10.4 %collective-permute-start.13 = (f32[256,64]{0,1:T(8,128)S(1)}, f32[256,64]{0,1:T(8,128)S(1)}, u32[]{:S(2)}, u32[]{:S(2)}) collective-permute-start(f32[256,64]{0,1:T(8,128)S(1)} %select_add_fusion.1), channel_id=1, source_target_pairs={{0,16},{4,20},{8,24},{12,28},{16,0},{20,4},{24,8},{28,12},{32,48},... | collective-permute-start | bytes 196616 | tf_op jit(solution)/shard_map/ppermute | solution.py:17
  84.5 5.9 %collective-permute-start.14 = (f32[256,64]{0,1:T(8,128)S(1)}, f32[256,64]{0,1:T(8,128)S(1)}, u32[]{:S(2)}, u32[]{:S(2)}) collective-permute-start(f32[256,64]{0,1:T(8,128)S(1)} %add.134), channel_id=1, source_target_pairs={{0,32},{4,36},{8,40},{12,44},{16,48},{20,52},{24,56},{28,60},{32,0... | collective-permute-start | bytes 196616 | tf_op jit(solution)/shard_map/ppermute | solution.py:17
  90.4 4.4 %collective-permute-start.15 = (f32[256,64]{0,1:T(8,128)S(1)}, f32[256,64]{0,1:T(8,128)S(1)}, u32[]{:S(2)}, u32[]{:S(2)}) collective-permute-start(f32[256,64]{0,1:T(8,128)S(1)} %add.135), channel_id=1, source_target_pairs={{0,64},{4,68},{8,72},{12,76},{16,80},{20,84},{24,88},{28,92},{32,9... | collective-permute-start | bytes 196616 | tf_op jit(solution)/shard_map/ppermute | solution.py:17
  94.7 5.9 %collective-permute-start.16 = (f32[256,64]{0,1:T(8,128)S(1)}, f32[256,64]{0,1:T(8,128)S(1)}, u32[]{:S(2)}, u32[]{:S(2)}) collective-permute-start(f32[256,64]{0,1:T(8,128)S(1)} %add.136), channel_id=1, source_target_pairs={{0,128},{4,132},{8,136},{12,140},{16,144},{20,148},{24,152},{28,15... | collective-permute-start | bytes 196616 | tf_op jit(solution)/shard_map/ppermute | solution.py:17
  100.6 5.7 %collective-permute-start.17 = (f32[256,64]{0,1:T(8,128)S(1)}, f32[256,64]{0,1:T(8,128)S(1)}, u32[]{:S(2)}, u32[]{:S(2)}) collective-permute-start(f32[256,64]{0,1:T(8,128)S(1)} %add.137), channel_id=1, source_target_pairs={{0,8},{4,12},{8,0},{12,4},{16,24},{20,28},{24,16},{28,20},{32,40},... | collective-permute-start | bytes 196616 | tf_op jit(solution)/shard_map/ppermute | solution.py:17
  106.3 5.1 %collective-permute-start.18 = (f32[512,64]{0,1:T(8,128)S(1)}, f32[512,64]{0,1:T(8,128)S(1)}, u32[]{:S(2)}, u32[]{:S(2)}) collective-permute-start(f32[512,64]{0,1:T(8,128)S(1)} %maximum_select_fusion.1), channel_id=1, source_target_pairs={{0,4},{4,0},{8,12},{12,8},{16,20},{20,16},{24,28},{28,24},{32,36},... | collective-permute-start | bytes 393224 | tf_op jit(solution)/shard_map/ppermute | solution.py:17

commit v5 on v4

--- a/solution.py
+++ b/solution.py
@@ -45,10 +45,10 @@
     count = lax.axis_size(axis)
     position = lax.axis_index(axis)
     width = weight.shape[1] // count
+    product = jnp.dot(heads, weight, preferred_element_type=jnp.float32)
 
     def block(index):
-        columns = lax.dynamic_slice_in_dim(weight, index * width, width, axis=1)
-        return jnp.dot(heads, columns, preferred_element_type=jnp.float32)
+        return lax.dynamic_slice_in_dim(product, index * width, width, axis=1)
 
     def sent(value, bit):
         return exchanged(value.astype(jnp.bfloat16), axis, bit).astype(jnp.float32)
@@ -61,7 +61,6 @@
     far = position ^ 2
     from_partner = sent(block(far ^ 1), 1)
     far_sum = (block(far) + from_partner).astype(jnp.bfloat16)
-    heads, far_sum = lax.optimization_barrier((heads, far_sum))
     from_far = exchanged(far_sum, axis, 2).astype(jnp.float32)
     near = sent(block(position ^ 1), 1)
     return block(position) + near + from_far

time: 112 us -> 119 us (1.062)
  matrix products: 29.8 us -> 20.9 us
  other arithmetic: 3.47 us -> 10.4 us
  waiting for transfers between devices: 44.6 us -> 50.1 us
  local copies, waits for them, and re-layouts: 4.74 us -> 8.09 us
    dot_general x8 -> x2, matrix products: 20.3 us -> 11.4 us  [block_reduce_scatter(): product = jnp.dot(heads, weight, preferred_element_type=jnp.float32)]
    ppermute x19, waiting for transfers between devices: 44.6 us -> 50.1 us  [exchanged(): return lax.ppermute(block, axis, [(i, i ^ bit) for i in range(count)])]
    convert_element_type x0 -> x2, other arithmetic: none -> 4.49 us  [block_reduce_scatter(): far_sum = (block(far) + from_partner).astype(jnp.bfloat16)]
    unnamed x15 -> x21, local copies, waits for them, and re-layouts: 1.3 us -> 4.16 us
    reduce_sum x2, other arithmetic: 0.8 us -> 3.26 us  [per_device(): square_local = jnp.sum(hidden * hidden, axis=1)]
    convert_element_type x0 -> x2, local copies, waits for them, and re-layouts: none -> 2.33 us  [sent(): return exchanged(value.astype(jnp.bfloat16), axis, bit).astype(jnp.float32)]
    slice x3, local copies, waits for them, and re-layouts: 2.36 us -> 0.52 us  [per_device(): flat_patched[rows_here]]
  transfers between devices with their start and end apart: 19 -> 19, of which waited for: 14 -> 14; matrix products, arithmetic and copies ran while one was open for 21% -> 16% of each run, Pallas kernels for 0% -> 0%
where the time goes in v5:
time: 119 us
  waiting for transfers between devices  50.1 us (42%)
  starting transfers between devices  28.2 us (24%)
  matrix products  20.9 us (18%)
  other arithmetic  10.4 us (9%)
  local copies, waits for them, and re-layouts  8.09 us (7%)
    ppermute x19, waiting for transfers between devices, exchanged(): return lax.ppermute(block, axis, [(i, i ^ bit) for i in range(count)])  50.1 us
    ppermute x19, starting transfers between devices, exchanged(): return lax.ppermute(block, axis, [(i, i ^ bit) for i in range(count)])  28.2 us
    dot_general x2, matrix products, block_reduce_scatter(): product = jnp.dot(heads, weight, preferred_element_type=jnp.float32)  11.4 us
    convert_element_type x2, other arithmetic, block_reduce_scatter(): far_sum = (block(far) + from_partner).astype(jnp.bfloat16)  4.49 us
    unnamed x21, local copies, waits for them, and re-layouts  4.16 us
    reduce_sum x2, other arithmetic, per_device(): square_local = jnp.sum(hidden * hidden, axis=1)  3.26 us
  transfers between devices with their start and end apart: 19, of which 14 were waited for; matrix products, arithmetic and copies ran while one was open for 16% of the time, Pallas kernels for 0%

profile of v5, /device:TPU:24, one launch (start us, length us, event | category | flops | bytes accessed | tf_op | source)
XLA Modules:
  0.0 118.7 jit_solution(3211587705515799445)
XLA Ops:
  0.6 0.0 copy-start
  0.7 0.8 fusion.65
  1.5 0.4 copy-done
  1.9 2.1 %fusion.67 = (f32[8,8,64]{2,1,0:T(8,128)S(1)}, f32[8,1,8,64,64]{3,4,2,0,1:T(8,128)S(1)}) fusion(bf16[8,64,128]{2,1,0:T(8,128)(2,1)} %param.12, pred[64,64]{0,1:T(8,128)(4,1)S(1)} %iota_compare_fusion.7, bf16[8,64,1024]{2,1,0:T(8,128)(2,1)S(1)} %copy-done), kind=kOutput, calls=%fused_computation.104 | convolution fusion | flops 67891200 | bytes 2248704 | tf_op jit(solution)/shard_map/pqkgd,pskd->pkgqs/dot_general | solution.py:85
  4.0 0.5 fusion
  4.5 0.0 copy-start.8
  4.5 0.6 fusion.1
  5.2 0.7 convolution_convert_fusion.2
  5.9 3.1 %collective-permute-start = (bf16[8,16,128]{2,1,0:T(8,128)(2,1)S(1)}, bf16[8,16,128]{2,1,0:T(8,128)(2,1)S(1)}, u32[]{:S(2)}, u32[]{:S(2)}) collective-permute-start(bf16[8,16,128]{2,1,0:T(8,128)(2,1)S(1)} %convolution_convert_fusion.2), channel_id=1, source_target_pairs={{0,128},{4,132},{8,136},{12,140},{16,144},{20,148},{24,152},{28,15... | collective-permute-start | bytes 98312 | tf_op jit(solution)/shard_map/ppermute | solution.py:17
  9.0 0.1 fusion.26
  9.1 2.2 %collective-permute-done = bf16[8,16,128]{2,1,0:T(8,128)(2,1)S(1)} collective-permute-done((bf16[8,16,128]{2,1,0:T(8,128)(2,1)S(1)}, bf16[8,16,128]{2,1,0:T(8,128)(2,1)S(1)}, u32[]{:S(2)}, u32[]{:S(2)}) %collective-permute-start) | collective-permute-done | bytes 32800 | tf_op jit(solution)/shard_map/ppermute | solution.py:17
  11.4 0.2 fusion.43
  11.6 1.6 %fusion.2 = bf16[8,512,128]{2,1,0:T(8,128)(2,1)S(1)} fusion(pred[8,512]{1,0:T(8,128)(4,1)S(1)} %fusion.26, bf16[8,64,1,8,128]{4,1,3,0,2:T(8,128)(2,1)S(1)} %fusion.1, s32[8,16]{1,0:T(8,128)S(1)} %fusion.51, bf16[8,16,128]{2,0,1:T(8,128)(2,1)S(1)} %fusion.43), kind=kOutput, calls=%fused_computation.7 | convolution fusion | flops 17891328 | bytes 2134528 | tf_op jit(solution)/shard_map/jkr,jkd->jrd/dot_general | solution.py:135
  13.1 0.1 fusion.63
  13.2 0.2 slice.61
  13.5 5.7 %fusion.68 = f32[256,4096]{1,0:T(8,128)S(1)} fusion(bf16[256,1024]{1,0:T(8,128)(2,1)S(1)} %slice.61, bf16[1024,4096]{1,0:T(8,128)(2,1)} %param.14), kind=kOutput, calls=%fused_computation.105 | convolution fusion | flops 2147483648 | bytes 13107200 | tf_op jit(solution)/shard_map/dot_general | solution.py:48
  19.2 1.9 %copy-done.2 = f32[256,4096]{1,0:T(8,128)} copy-done((f32[256,4096]{1,0:T(8,128)}, f32[256,4096]{1,0:T(8,128)S(1)}, u32[]{:S(2)}) %copy-start.2) | copy-done | bytes 4194328
  21.1 1.2 %dynamic-slice_convert_fusion.3 = (bf16[256,1024]{1,0:T(8,128)(2,1)}, bf16[256,1024]{1,0:T(8,128)(2,1)}) fusion(f32[256,4096]{1,0:T(8,128)S(1)} %fusion.68, s32[]{:T(128)S(6)} %select_n.89, s32[]{:T(128)S(6)} %select_n.91), kind=kLoop, calls=%fused_computation.30 | loop fusion | bytes 2097160 | tf_op jit(solution)/shard_map/convert_element_type | solution.py:54
  22.3 0.5 collective-permute-start.1
  22.8 0.2 slice.63
  23.1 5.7 %fusion.69 = f32[256,4096]{1,0:T(8,128)S(1)} fusion(bf16[256,1024]{1,0:T(8,128)(2,1)S(1)} %slice.63, bf16[1024,4096]{1,0:T(8,128)(2,1)} %param.14), kind=kOutput, calls=%fused_computation.106 | convolution fusion | flops 2147483648 | bytes 13107200 | tf_op jit(solution)/shard_map/dot_general | solution.py:48
  28.8 1.1 dynamic-slice_convert_fusion.1
  30.0 3.0 %add_convert_fusion.3 = bf16[256,1024]{1,0:T(8,128)(2,1)} fusion(bf16[256,1024]{1,0:T(8,128)(2,1)S(1)} %collective-permute-done.2, f32[256,4096]{1,0:T(8,128)} %copy-done.2, s32[]{:T(128)S(6)} %select_n.90), kind=kLoop, calls=%fused_computation.28 | loop fusion | flops 786432 | bytes 2097156 | tf_op jit(solution)/shard_map/convert_element_type | solution.py:63
  32.9 0.7 collective-permute-start.3
  33.7 0.1 eq.78
  33.7 0.1 eq.82
  33.8 0.1 fusion.64
  33.9 0.9 copy-done.5
  34.9 1.5 %add_convert_fusion.1 = bf16[256,1024]{1,0:T(8,128)(2,1)S(1)} fusion(bf16[256,1024]{1,0:T(8,128)(2,1)} %collective-permute-done.5, f32[256,4096]{1,0:T(8,128)} %copy-done.1, s32[]{:T(128)S(6)} %select_n.90), kind=kLoop, calls=%fused_computation.24 | loop fusion | flops 786432 | bytes 2097156 | tf_op jit(solution)/shard_map/convert_element_type | solution.py:63
  36.4 1.6 %collective-permute-start.6 = (bf16[256,1024]{1,0:T(8,128)(2,1)S(1)}, bf16[256,1024]{1,0:T(8,128)(2,1)S(1)}, u32[]{:S(2)}, u32[]{:S(2)}) collective-permute-start(bf16[256,1024]{1,0:T(8,128)(2,1)S(1)} %add_convert_fusion.1), channel_id=1, source_target_pairs={{0,2},{1,3},{2,0},{3,1},{4,6},{5,7},{6,4},{7,5},{8,10},{9,11},{10,... | collective-permute-start | bytes 1572872 | tf_op jit(solution)/shard_map/ppermute | solution.py:17
  38.0 9.9 %collective-permute-done.3 = bf16[256,1024]{1,0:T(8,128)(2,1)S(1)} collective-permute-done((bf16[256,1024]{1,0:T(8,128)(2,1)}, bf16[256,1024]{1,0:T(8,128)(2,1)S(1)}, u32[]{:S(2)}, u32[]{:S(2)}) %collective-permute-start.3) | collective-permute-done | bytes 524320 | tf_op jit(solution)/shard_map/ppermute | solution.py:17
  47.9 1.6 %multiply_reduce_fusion.1 = (f32[256]{0:T(256)S(1)}, bf16[256,1024]{1,0:T(8,128)(2,1)S(1)}) fusion(bf16[4,64,1024]{2,1,0:T(8,128)(2,1)S(1)} %get-tuple-element.19, bf16[256,1024]{1,0:T(8,128)(2,1)S(1)} %collective-permute-done.3, bf16[256,1024]{1,0:T(8,128)(2,1)S(1)} %collective-permute-done.1, f32[256,4096]{1,0:T(8,128)} %copy-done.2, s32[]{:T(128)S(6)} %select_n.88), kind=kLoop, calls=%fused_computation.22 | loop fusion | flops 2621184 | bytes 3146756 | tf_op jit(solution)/shard_map/reduce_sum | solution.py:155
  49.6 1.2 fusion.17
  50.7 0.1 collective-permute-start.7
  50.8 7.6 %collective-permute-done.6 = bf16[256,1024]{1,0:T(8,128)(2,1)S(1)} collective-permute-done((bf16[256,1024]{1,0:T(8,128)(2,1)S(1)}, bf16[256,1024]{1,0:T(8,128)(2,1)S(1)}, u32[]{:S(2)}, u32[]{:S(2)}) %collective-permute-start.6) | collective-permute-done | bytes 524320 | tf_op jit(solution)/shard_map/ppermute | solution.py:17
  58.4 1.6 %multiply_reduce_fusion = (f32[256]{0:T(256)S(1)}, bf16[256,1024]{1,0:T(8,128)(2,1)S(1)}) fusion(bf16[4,64,1024]{2,1,0:T(8,128)(2,1)S(1)} %get-tuple-element.20, bf16[256,1024]{1,0:T(8,128)(2,1)S(1)} %collective-permute-done.6, bf16[256,1024]{1,0:T(8,128)(2,1)S(1)} %collective-permute-done.4, f32[256,4096]{1,0:T(8,128)} %copy-done.1, s32[]{:T(128)S(6)} %select_n.88), kind=kLoop, calls=%fused_computation.21 | loop fusion | flops 2621184 | bytes 3146756 | tf_op jit(solution)/shard_map/reduce_sum | solution.py:155
  60.0 1.2 fusion.14
  61.2 0.1 collective-permute-start.9
  61.3 0.8 collective-permute-start.8
  62.2 0.4 collective-permute-done.9
  62.6 1.0 collective-permute-start.10
  63.5 3.0 %collective-permute-done.8 = f32[256,65]{0,1:T(8,128)S(1)} collective-permute-done((f32[256,65]{0,1:T(8,128)S(1)}, f32[256,65]{0,1:T(8,128)S(1)}, u32[]{:S(2)}, u32[]{:S(2)}) %collective-permute-start.8) | collective-permute-done | bytes 66592 | tf_op jit(solution)/shard_map/ppermute | solution.py:17
  66.6 1.1 collective-permute-done.10
  67.7 1.0 fusion.9
  68.7 1.0 fusion.3
  69.8 2.0 %collective-permute-start.11 = (f32[512,64]{0,1:T(8,128)S(1)}, f32[512,64]{0,1:T(8,128)S(1)}, u32[]{:S(2)}, u32[]{:S(2)}) collective-permute-start(f32[512,64]{0,1:T(8,128)S(1)} %slice_select_fusion), channel_id=1, source_target_pairs={{0,4},{4,0},{8,12},{12,8},{16,20},{20,16},{24,28},{28,24},{32,36},... | collective-permute-start | bytes 393224 | tf_op jit(solution)/shard_map/ppermute | solution.py:17
  71.8 3.3 %collective-permute-done.11 = f32[512,64]{0,1:T(8,128)S(1)} collective-permute-done((f32[512,64]{0,1:T(8,128)S(1)}, f32[512,64]{0,1:T(8,128)S(1)}, u32[]{:S(2)}, u32[]{:S(2)}) %collective-permute-start.11) | collective-permute-done | bytes 131104 | tf_op jit(solution)/shard_map/ppermute | solution.py:17
  75.1 3.4 %collective-permute-start.12 = (f32[256,64]{0,1:T(8,128)S(1)}, f32[256,64]{0,1:T(8,128)S(1)}, u32[]{:S(2)}, u32[]{:S(2)}) collective-permute-start(f32[256,64]{0,1:T(8,128)S(1)} %slice_select_fusion.1), channel_id=1, source_target_pairs={{0,8},{4,12},{8,0},{12,4},{16,24},{20,28},{24,16},{28,20},{32,40},... | collective-permute-start | bytes 196616 | tf_op jit(solution)/shard_map/ppermute | solution.py:17
  78.5 2.2 %collective-permute-done.12 = f32[256,64]{0,1:T(8,128)S(1)} collective-permute-done((f32[256,64]{0,1:T(8,128)S(1)}, f32[256,64]{0,1:T(8,128)S(1)}, u32[]{:S(2)}, u32[]{:S(2)}) %collective-permute-start.12) | collective-permute-done | bytes 65568 | tf_op jit(solution)/shard_map/ppermute | solution.py:17
  80.7 7.5 %collective-permute-start.13 = (f32[256,64]{0,1:T(8,128)S(1)}, f32[256,64]{0,1:T(8,128)S(1)}, u32[]{:S(2)}, u32[]{:S(2)}) collective-permute-start(f32[256,64]{0,1:T(8,128)S(1)} %select_add_fusion.1), channel_id=1, source_target_pairs={{0,16},{4,20},{8,24},{12,28},{16,0},{20,4},{24,8},{28,12},{32,48},... | collective-permute-start | bytes 196616 | tf_op jit(solution)/shard_map/ppermute | solution.py:17
  88.2 2.9 %collective-permute-done.13 = f32[256,64]{0,1:T(8,128)S(1)} collective-permute-done((f32[256,64]{0,1:T(8,128)S(1)}, f32[256,64]{0,1:T(8,128)S(1)}, u32[]{:S(2)}, u32[]{:S(2)}) %collective-permute-start.13) | collective-permute-done | bytes 65568 | tf_op jit(solution)/shard_map/ppermute | solution.py:17
  91.1 1.3 %collective-permute-start.14 = (f32[256,64]{0,1:T(8,128)S(1)}, f32[256,64]{0,1:T(8,128)S(1)}, u32[]{:S(2)}, u32[]{:S(2)}) collective-permute-start(f32[256,64]{0,1:T(8,128)S(1)} %add.134), channel_id=1, source_target_pairs={{0,32},{4,36},{8,40},{12,44},{16,48},{20,52},{24,56},{28,60},{32,0... | collective-permute-start | bytes 196616 | tf_op jit(solution)/shard_map/ppermute | solution.py:17
  92.4 4.5 %collective-permute-done.14 = f32[256,64]{0,1:T(8,128)S(1)} collective-permute-done((f32[256,64]{0,1:T(8,128)S(1)}, f32[256,64]{0,1:T(8,128)S(1)}, u32[]{:S(2)}, u32[]{:S(2)}) %collective-permute-start.14) | collective-permute-done | bytes 65568 | tf_op jit(solution)/shard_map/ppermute | solution.py:17
  97.0 1.6 %collective-permute-start.15 = (f32[256,64]{0,1:T(8,128)S(1)}, f32[256,64]{0,1:T(8,128)S(1)}, u32[]{:S(2)}, u32[]{:S(2)}) collective-permute-start(f32[256,64]{0,1:T(8,128)S(1)} %add.135), channel_id=1, source_target_pairs={{0,64},{4,68},{8,72},{12,76},{16,80},{20,84},{24,88},{28,92},{32,9... | collective-permute-start | bytes 196616 | tf_op jit(solution)/shard_map/ppermute | solution.py:17
  98.6 2.8 %collective-permute-done.15 = f32[256,64]{0,1:T(8,128)S(1)} collective-permute-done((f32[256,64]{0,1:T(8,128)S(1)}, f32[256,64]{0,1:T(8,128)S(1)}, u32[]{:S(2)}, u32[]{:S(2)}) %collective-permute-start.15) | collective-permute-done | bytes 65568 | tf_op jit(solution)/shard_map/ppermute | solution.py:17
  101.4 3.1 %collective-permute-start.16 = (f32[256,64]{0,1:T(8,128)S(1)}, f32[256,64]{0,1:T(8,128)S(1)}, u32[]{:S(2)}, u32[]{:S(2)}) collective-permute-start(f32[256,64]{0,1:T(8,128)S(1)} %add.136), channel_id=1, source_target_pairs={{0,128},{4,132},{8,136},{12,140},{16,144},{20,148},{24,152},{28,15... | collective-permute-start | bytes 196616 | tf_op jit(solution)/shard_map/ppermute | solution.py:17
  104.5 1.0 pad_maximum_fusion
  105.5 1.7 %collective-permute-done.16 = f32[256,64]{0,1:T(8,128)S(1)} collective-permute-done((f32[256,64]{0,1:T(8,128)S(1)}, f32[256,64]{0,1:T(8,128)S(1)}, u32[]{:S(2)}, u32[]{:S(2)}) %collective-permute-start.16) | collective-permute-done | bytes 65568 | tf_op jit(solution)/shard_map/ppermute | solution.py:17
  107.2 1.4 %collective-permute-start.17 = (f32[256,64]{0,1:T(8,128)S(1)}, f32[256,64]{0,1:T(8,128)S(1)}, u32[]{:S(2)}, u32[]{:S(2)}) collective-permute-start(f32[256,64]{0,1:T(8,128)S(1)} %add.137), channel_id=1, source_target_pairs={{0,8},{4,12},{8,0},{12,4},{16,24},{20,28},{24,16},{28,20},{32,40},... | collective-permute-start | bytes 196616 | tf_op jit(solution)/shard_map/ppermute | solution.py:17
  108.6 4.3 %collective-permute-done.17 = f32[256,64]{0,1:T(8,128)S(1)} collective-permute-done((f32[256,64]{0,1:T(8,128)S(1)}, f32[256,64]{0,1:T(8,128)S(1)}, u32[]{:S(2)}, u32[]{:S(2)}) %collective-permute-start.17) | collective-permute-done | bytes 65568 | tf_op jit(solution)/shard_map/ppermute | solution.py:17
  112.9 0.1 collective-permute-start.18
  113.1 0.8 copy.29
  113.9 4.1 %collective-permute-done.18 = f32[512,64]{0,1:T(8,128)S(1)} collective-permute-done((f32[512,64]{0,1:T(8,128)S(1)}, f32[512,64]{0,1:T(8,128)S(1)}, u32[]{:S(2)}, u32[]{:S(2)}) %collective-permute-start.18) | collective-permute-done | bytes 131104 | tf_op jit(solution)/shard_map/ppermute | solution.py:17
  118.0 0.7 maximum_select_fusion
  (46 shorter events, 0.3 us)
Async XLA Ops:
  0.6 1.3 %copy-start = (bf16[8,64,1024]{2,1,0:T(8,128)(2,1)S(1)}, bf16[8,64,1024]{2,1,0:T(8,128)(2,1)}, u32[]{:S(2)}) copy-start(bf16[8,64,1024]{2,1,0:T(8,128)(2,1)} %param.11) | copy-start | bytes 3145732
  1.9 2.6 %copy-start.9 = (bf16[8,64,128]{2,1,0:T(8,128)(2,1)S(1)}, bf16[8,64,128]{2,1,0:T(8,128)(2,1)}, u32[]{:S(2)}) copy-start(bf16[8,64,128]{2,1,0:T(8,128)(2,1)} %param.13) | copy-start | bytes 393220
  4.5 6.8 %copy-start.8 = (s32[8]{0:T(128)S(1)}, s32[8]{0:T(128)}, u32[]{:S(2)}) copy-start(s32[8]{0:T(128)} %param.17) | copy-start | bytes 100
  5.9 5.5 %collective-permute-start = (bf16[8,16,128]{2,1,0:T(8,128)(2,1)S(1)}, bf16[8,16,128]{2,1,0:T(8,128)(2,1)S(1)}, u32[]{:S(2)}, u32[]{:S(2)}) collective-permute-start(bf16[8,16,128]{2,1,0:T(8,128)(2,1)S(1)} %convolution_convert_fusion.2), channel_id=1, source_target_pairs={{0,128},{4,132},{8,136},{12,140},{16,144},{20,148},{24,152},{28,15... | collective-permute-start | bytes 98312 | tf_op jit(solution)/shard_map/ppermute | solution.py:17
  19.2 1.9 %copy-start.2 = (f32[256,4096]{1,0:T(8,128)}, f32[256,4096]{1,0:T(8,128)S(1)}, u32[]{:S(2)}) copy-start(f32[256,4096]{1,0:T(8,128)S(1)} %fusion.68) | copy-start | bytes 12582916
  22.3 7.6 %collective-permute-start.2 = (bf16[256,1024]{1,0:T(8,128)(2,1)}, bf16[256,1024]{1,0:T(8,128)(2,1)S(1)}, u32[]{:S(2)}, u32[]{:S(2)}) collective-permute-start(bf16[256,1024]{1,0:T(8,128)(2,1)} %get-tuple-element.14), channel_id=1, source_target_pairs={{0,1},{1,0},{2,3},{3,2},{4,5},{5,4},{6,7},{7,6},{8,9},{9,8},{10,11... | collective-permute-start | bytes 1572872 | tf_op jit(solution)/shard_map/ppermute | solution.py:17
  22.3 15.7 %collective-permute-start.1 = (bf16[256,1024]{1,0:T(8,128)(2,1)}, bf16[256,1024]{1,0:T(8,128)(2,1)S(1)}, u32[]{:S(2)}, u32[]{:S(2)}) collective-permute-start(bf16[256,1024]{1,0:T(8,128)(2,1)} %get-tuple-element.13), channel_id=1, source_target_pairs={{0,1},{1,0},{2,3},{3,2},{4,5},{5,4},{6,7},{7,6},{8,9},{9,8},{10,11... | collective-permute-start | bytes 1572872 | tf_op jit(solution)/shard_map/ppermute | solution.py:17
  28.8 4.1 %copy-start.1 = (f32[256,4096]{1,0:T(8,128)}, f32[256,4096]{1,0:T(8,128)S(1)}, u32[]{:S(2)}) copy-start(f32[256,4096]{1,0:T(8,128)S(1)} %fusion.69) | copy-start | bytes 12582916
  28.8 4.9 %copy-start.7 = (s32[8,64]{1,0:T(8,128)S(1)}, s32[8,64]{1,0:T(8,128)}, u32[]{:S(2)}) copy-start(s32[8,64]{1,0:T(8,128)} %param.19) | copy-start | bytes 6148
  28.8 5.0 %copy-start.3 = (bf16[8,64,1024]{2,1,0:T(8,128)(2,1)S(1)}, bf16[8,64,1024]{2,1,0:T(8,128)(2,1)}, u32[]{:S(2)}) copy-start(bf16[8,64,1024]{2,1,0:T(8,128)(2,1)} %param.10) | copy-start | bytes 3145732
  29.9 4.9 %collective-permute-start.5 = (bf16[256,1024]{1,0:T(8,128)(2,1)}, bf16[256,1024]{1,0:T(8,128)(2,1)}, u32[]{:S(2)}, u32[]{:S(2)}) collective-permute-start(bf16[256,1024]{1,0:T(8,128)(2,1)} %get-tuple-element.16), channel_id=1, source_target_pairs={{0,1},{1,0},{2,3},{3,2},{4,5},{5,4},{6,7},{7,6},{8,9},{9,8},{10,11... | collective-permute-start | bytes 1572872 | tf_op jit(solution)/shard_map/ppermute | solution.py:17
  32.9 15.0 %collective-permute-start.3 = (bf16[256,1024]{1,0:T(8,128)(2,1)}, bf16[256,1024]{1,0:T(8,128)(2,1)S(1)}, u32[]{:S(2)}, u32[]{:S(2)}) collective-permute-start(bf16[256,1024]{1,0:T(8,128)(2,1)} %add_convert_fusion.3), channel_id=1, source_target_pairs={{0,2},{1,3},{2,0},{3,1},{4,6},{5,7},{6,4},{7,5},{8,10},{9,11},{10,... | collective-permute-start | bytes 1572872 | tf_op jit(solution)/shard_map/ppermute | solution.py:17
  33.8 1.0 copy-start.5
  34.9 16.0 %collective-permute-start.4 = (bf16[256,1024]{1,0:T(8,128)(2,1)S(1)}, bf16[256,1024]{1,0:T(8,128)(2,1)S(1)}, u32[]{:S(2)}, u32[]{:S(2)}) collective-permute-start(bf16[256,1024]{1,0:T(8,128)(2,1)S(1)} %copy-done.5), channel_id=1, source_target_pairs={{0,1},{1,0},{2,3},{3,2},{4,5},{5,4},{6,7},{7,6},{8,9},{9,8},{10,11... | collective-permute-start | bytes 1572872 | tf_op jit(solution)/shard_map/ppermute | solution.py:17
  36.4 13.1 %copy-start.4 = (f32[1024,64]{0,1:T(8,128)S(1)}, f32[1024,64]{0,1:T(8,128)}, u32[]{:S(2)}) copy-start(f32[1024,64]{0,1:T(8,128)} %param.16) | copy-start | bytes 786436
  36.4 13.1 %copy-start.6 = (f32[1024]{0:T(1024)S(1)}, f32[1024]{0:T(1024)}, u32[]{:S(2)}) copy-start(f32[1024]{0:T(1024)} %param.15) | copy-start | bytes 12292
  36.4 21.9 %collective-permute-start.6 = (bf16[256,1024]{1,0:T(8,128)(2,1)S(1)}, bf16[256,1024]{1,0:T(8,128)(2,1)S(1)}, u32[]{:S(2)}, u32[]{:S(2)}) collective-permute-start(bf16[256,1024]{1,0:T(8,128)(2,1)S(1)} %add_convert_fusion.1), channel_id=1, source_target_pairs={{0,2},{1,3},{2,0},{3,1},{4,6},{5,7},{6,4},{7,5},{8,10},{9,11},{10,... | collective-permute-start | bytes 1572872 | tf_op jit(solution)/shard_map/ppermute | solution.py:17
  50.7 10.6 %collective-permute-start.7 = (f32[256,65]{0,1:T(8,128)S(1)}, f32[256,65]{0,1:T(8,128)S(1)}, u32[]{:S(2)}, u32[]{:S(2)}) collective-permute-start(f32[256,65]{0,1:T(8,128)S(1)} %pad_maximum_fusion.2), channel_id=1, source_target_pairs={{0,1},{1,0},{2,3},{3,2},{4,5},{5,4},{6,7},{7,6},{8,9},{9,8},{10,11... | collective-permute-start | bytes 199688 | tf_op jit(solution)/shard_map/ppermute | solution.py:17
  61.2 1.4 %collective-permute-start.9 = (f32[256,65]{0,1:T(8,128)S(1)}, f32[256,65]{0,1:T(8,128)S(1)}, u32[]{:S(2)}, u32[]{:S(2)}) collective-permute-start(f32[256,65]{0,1:T(8,128)S(1)} %pad_maximum_fusion.3), channel_id=1, source_target_pairs={{0,1},{1,0},{2,3},{3,2},{4,5},{5,4},{6,7},{7,6},{8,9},{9,8},{10,11... | collective-permute-start | bytes 199688 | tf_op jit(solution)/shard_map/ppermute | solution.py:17
  61.3 5.2 %collective-permute-start.8 = (f32[256,65]{0,1:T(8,128)S(1)}, f32[256,65]{0,1:T(8,128)S(1)}, u32[]{:S(2)}, u32[]{:S(2)}) collective-permute-start(f32[256,65]{0,1:T(8,128)S(1)} %fusion.62), channel_id=1, source_target_pairs={{0,2},{1,3},{2,0},{3,1},{4,6},{5,7},{6,4},{7,5},{8,10},{9,11},{10,... | collective-permute-start | bytes 199688 | tf_op jit(solution)/shard_map/ppermute | solution.py:17
  62.6 5.1 %collective-permute-start.10 = (f32[256,65]{0,1:T(8,128)S(1)}, f32[256,65]{0,1:T(8,128)S(1)}, u32[]{:S(2)}, u32[]{:S(2)}) collective-permute-start(f32[256,65]{0,1:T(8,128)S(1)} %fusion.61), channel_id=1, source_target_pairs={{0,2},{1,3},{2,0},{3,1},{4,6},{5,7},{6,4},{7,5},{8,10},{9,11},{10,... | collective-permute-start | bytes 199688 | tf_op jit(solution)/shard_map/ppermute | solution.py:17
  69.8 5.3 %collective-permute-start.11 = (f32[512,64]{0,1:T(8,128)S(1)}, f32[512,64]{0,1:T(8,128)S(1)}, u32[]{:S(2)}, u32[]{:S(2)}) collective-permute-start(f32[512,64]{0,1:T(8,128)S(1)} %slice_select_fusion), channel_id=1, source_target_pairs={{0,4},{4,0},{8,12},{12,8},{16,20},{20,16},{24,28},{28,24},{32,36},... | collective-permute-start | bytes 393224 | tf_op jit(solution)/shard_map/ppermute | solution.py:17
  75.1 5.6 %collective-permute-start.12 = (f32[256,64]{0,1:T(8,128)S(1)}, f32[256,64]{0,1:T(8,128)S(1)}, u32[]{:S(2)}, u32[]{:S(2)}) collective-permute-start(f32[256,64]{0,1:T(8,128)S(1)} %slice_select_fusion.1), channel_id=1, source_target_pairs={{0,8},{4,12},{8,0},{12,4},{16,24},{20,28},{24,16},{28,20},{32,40},... | collective-permute-start | bytes 196616 | tf_op jit(solution)/shard_map/ppermute | solution.py:17
  80.7 10.4 %collective-permute-start.13 = (f32[256,64]{0,1:T(8,128)S(1)}, f32[256,64]{0,1:T(8,128)S(1)}, u32[]{:S(2)}, u32[]{:S(2)}) collective-permute-start(f32[256,64]{0,1:T(8,128)S(1)} %select_add_fusion.1), channel_id=1, source_target_pairs={{0,16},{4,20},{8,24},{12,28},{16,0},{20,4},{24,8},{28,12},{32,48},... | collective-permute-start | bytes 196616 | tf_op jit(solution)/shard_map/ppermute | solution.py:17
  91.1 5.9 %collective-permute-start.14 = (f32[256,64]{0,1:T(8,128)S(1)}, f32[256,64]{0,1:T(8,128)S(1)}, u32[]{:S(2)}, u32[]{:S(2)}) collective-permute-start(f32[256,64]{0,1:T(8,128)S(1)} %add.134), channel_id=1, source_target_pairs={{0,32},{4,36},{8,40},{12,44},{16,48},{20,52},{24,56},{28,60},{32,0... | collective-permute-start | bytes 196616 | tf_op jit(solution)/shard_map/ppermute | solution.py:17
  97.0 4.4 %collective-permute-start.15 = (f32[256,64]{0,1:T(8,128)S(1)}, f32[256,64]{0,1:T(8,128)S(1)}, u32[]{:S(2)}, u32[]{:S(2)}) collective-permute-start(f32[256,64]{0,1:T(8,128)S(1)} %add.135), channel_id=1, source_target_pairs={{0,64},{4,68},{8,72},{12,76},{16,80},{20,84},{24,88},{28,92},{32,9... | collective-permute-start | bytes 196616 | tf_op jit(solution)/shard_map/ppermute | solution.py:17
  101.4 5.9 %collective-permute-start.16 = (f32[256,64]{0,1:T(8,128)S(1)}, f32[256,64]{0,1:T(8,128)S(1)}, u32[]{:S(2)}, u32[]{:S(2)}) collective-permute-start(f32[256,64]{0,1:T(8,128)S(1)} %add.136), channel_id=1, source_target_pairs={{0,128},{4,132},{8,136},{12,140},{16,144},{20,148},{24,152},{28,15... | collective-permute-start | bytes 196616 | tf_op jit(solution)/shard_map/ppermute | solution.py:17
  107.2 5.7 %collective-permute-start.17 = (f32[256,64]{0,1:T(8,128)S(1)}, f32[256,64]{0,1:T(8,128)S(1)}, u32[]{:S(2)}, u32[]{:S(2)}) collective-permute-start(f32[256,64]{0,1:T(8,128)S(1)} %add.137), channel_id=1, source_target_pairs={{0,8},{4,12},{8,0},{12,4},{16,24},{20,28},{24,16},{28,20},{32,40},... | collective-permute-start | bytes 196616 | tf_op jit(solution)/shard_map/ppermute | solution.py:17
  112.9 5.1 %collective-permute-start.18 = (f32[512,64]{0,1:T(8,128)S(1)}, f32[512,64]{0,1:T(8,128)S(1)}, u32[]{:S(2)}, u32[]{:S(2)}) collective-permute-start(f32[512,64]{0,1:T(8,128)S(1)} %maximum_select_fusion.1), channel_id=1, source_target_pairs={{0,4},{4,0},{8,12},{12,8},{16,20},{20,16},{24,28},{28,24},{32,36},... | collective-permute-start | bytes 393224 | tf_op jit(solution)/shard_map/ppermute | solution.py:17

commit v6 on v5

--- a/solution.py
+++ b/solution.py
@@ -41,29 +41,38 @@
     return block
 
 
-def block_reduce_scatter(heads, weight, axis):
+def far_half(heads, weight, axis, after=None):
     count = lax.axis_size(axis)
     position = lax.axis_index(axis)
     width = weight.shape[1] // count
-    product = jnp.dot(heads, weight, preferred_element_type=jnp.float32)
+    if after is not None:
+        heads, _ = lax.optimization_barrier((heads, after))
 
     def block(index):
-        return lax.dynamic_slice_in_dim(product, index * width, width, axis=1)
+        columns = lax.dynamic_slice_in_dim(weight, index * width, width, axis=1)
+        return jnp.dot(heads, columns, preferred_element_type=jnp.float32)
 
     def sent(value, bit):
         return exchanged(value.astype(jnp.bfloat16), axis, bit).astype(jnp.float32)
 
-    if count != 4:
-        total = block(position)
-        for bit in range(1, count):
-            total = total + sent(block(position ^ bit), bit)
-        return total
     far = position ^ 2
     from_partner = sent(block(far ^ 1), 1)
     far_sum = (block(far) + from_partner).astype(jnp.bfloat16)
-    from_far = exchanged(far_sum, axis, 2).astype(jnp.float32)
-    near = sent(block(position ^ 1), 1)
-    return block(position) + near + from_far
+    heads, far_sum = lax.optimization_barrier((heads, far_sum))
+    return heads, far_sum, exchanged(far_sum, axis, 2)
+
+
+def near_half(heads, weight, axis, from_far):
+    count = lax.axis_size(axis)
+    position = lax.axis_index(axis)
+    width = weight.shape[1] // count
+
+    def block(index):
+        columns = lax.dynamic_slice_in_dim(weight, index * width, width, axis=1)
+        return jnp.dot(heads, columns, preferred_element_type=jnp.float32)
+
+    near = exchanged(block(position ^ 1).astype(jnp.bfloat16), axis, 1).astype(jnp.float32)
+    return block(position) + near + from_far.astype(jnp.float32)
 
 
 def dp_bits(count):
@@ -145,12 +154,20 @@
     tensor_bits = [1 << k for k in range(lax.axis_size("tensor").bit_length() - 1)]
     chunk_count = 2 if token_count % 2 == 0 else 1
     chunk = token_count // chunk_count
+    halves, sent_block = [], None
+    for index in range(chunk_count):
+        rows_here = slice(index * chunk, (index + 1) * chunk)
+        heads_here, sent_block, from_far = far_half(
+            flat_patched[rows_here], out_weight, "tensor", sent_block
+        )
+        halves.append((heads_here, sent_block, from_far))
     attn_chunks, logit_chunks, grad_local = [], [], None
     for index in range(chunk_count):
         rows_here = slice(index * chunk, (index + 1) * chunk)
-        attn_local = block_reduce_scatter(flat_patched[rows_here], out_weight, "tensor").astype(
-            jnp.bfloat16
-        )
+        heads_here, _, from_far = halves[index]
+        if index + 1 < chunk_count:
+            from_far, _ = lax.optimization_barrier((from_far, halves[index + 1][1]))
+        attn_local = near_half(heads_here, out_weight, "tensor", from_far).astype(jnp.bfloat16)
         hidden = flat_residual[rows_here].astype(jnp.float32) + attn_local.astype(jnp.float32)
         square_local = jnp.sum(hidden * hidden, axis=1)
         scaled = hidden * norm_gain

time: 119 us -> 112 us (0.941)
  matrix products: 20.9 us -> 32 us
  waiting for transfers between devices: 50.1 us -> 39.7 us
  other arithmetic: 10.4 us -> 5.33 us
  local copies, waits for them, and re-layouts: 8.09 us -> 5.99 us
    dot_general x2 -> x8, matrix products: 11.4 us -> 22.6 us  [block(): return jnp.dot(heads, columns, preferred_element_type=jnp.float32)]
    ppermute x19, waiting for transfers between devices: 50.1 us -> 39.7 us  [exchanged(): return lax.ppermute(block, axis, [(i, i ^ bit) for i in range(count)])]
    convert_element_type x2 -> x0, other arithmetic: 4.49 us -> none  [block_reduce_scatter(): far_sum = (block(far) + from_partner).astype(jnp.bfloat16)]
    unnamed x21 -> x19, local copies, waits for them, and re-layouts: 4.16 us -> 1.3 us
    eq x2, local copies, waits for them, and re-layouts: 0.16 us -> 2.68 us  [per_device(): labels[rows_here][:, None] == classes[None, :]]
    convert_element_type x2 -> x0, local copies, waits for them, and re-layouts: 2.33 us -> none  [sent(): return exchanged(value.astype(jnp.bfloat16), axis, bit).astype(jnp.float32)]
    reduce_sum x2, other arithmetic: 3.26 us -> 2.02 us  [per_device(): square_local = jnp.sum(hidden * hidden, axis=1)]
  transfers between devices with their start and end apart: 19 -> 19, of which waited for: 14 -> 14; matrix products, arithmetic and copies ran while one was open for 16% -> 20% of each run, Pallas kernels for 0% -> 0%
where the time goes in v6:
time: 112 us
  waiting for transfers between devices  39.7 us (35%)
  matrix products  32 us (29%)
  starting transfers between devices  28 us (25%)
  local copies, waits for them, and re-layouts  5.99 us (5%)
  other arithmetic  5.33 us (5%)
    ppermute x19, waiting for transfers between devices, exchanged(): return lax.ppermute(block, axis, [(i, i ^ bit) for i in range(count)])  39.7 us
    ppermute x19, starting transfers between devices, exchanged(): return lax.ppermute(block, axis, [(i, i ^ bit) for i in range(count)])  28 us
    dot_general x8, matrix products, block(): return jnp.dot(heads, columns, preferred_element_type=jnp.float32)  22.6 us
    eq x2, local copies, waits for them, and re-layouts, per_device(): labels[rows_here][:, None] == classes[None, :]  2.68 us
    dot_general x2, matrix products, per_device(): jnp.dot(scaled, probe_weight, precision=lax.Precision.HIGHEST, preferred_...  2.32 us
  transfers between devices with their start and end apart: 19, of which 14 were waited for; matrix products, arithmetic and copies ran while one was open for 20% of the time, Pallas kernels for 0%

profile of v6, /device:TPU:24, one launch (start us, length us, event | category | flops | bytes accessed | tf_op | source)
XLA Modules:
  0.0 112.0 jit_solution(9215475834442421712)
XLA Ops:
  0.7 0.8 fusion.105
  1.5 0.4 copy-done
  1.9 2.1 %fusion.107 = (f32[8,8,64]{2,1,0:T(8,128)S(1)}, f32[8,1,8,64,64]{3,4,2,0,1:T(8,128)S(1)}) fusion(bf16[8,64,128]{2,1,0:T(8,128)(2,1)} %param.12, pred[64,64]{0,1:T(8,128)(4,1)S(1)} %iota_compare_fusion.7, bf16[8,64,1024]{2,1,0:T(8,128)(2,1)S(1)} %copy-done), kind=kOutput, calls=%fused_computation.128 | convolution fusion | flops 67891200 | bytes 2248704 | tf_op jit(solution)/shard_map/pqkgd,pskd->pkgqs/dot_general | solution.py:94
  4.0 0.5 fusion
  4.5 0.6 fusion.17
  5.2 0.7 convolution_convert_fusion.2
  5.9 3.1 %collective-permute-start = (bf16[8,16,128]{2,1,0:T(8,128)(2,1)S(1)}, bf16[8,16,128]{2,1,0:T(8,128)(2,1)S(1)}, u32[]{:S(2)}, u32[]{:S(2)}) collective-permute-start(bf16[8,16,128]{2,1,0:T(8,128)(2,1)S(1)} %convolution_convert_fusion.2), channel_id=1, source_target_pairs={{0,128},{4,132},{8,136},{12,140},{16,144},{20,148},{24,152},{28,15... | collective-permute-start | bytes 98312 | tf_op jit(solution)/shard_map/ppermute | solution.py:17
  9.0 0.1 fusion.54
  9.1 2.3 %collective-permute-done = bf16[8,16,128]{2,1,0:T(8,128)(2,1)S(1)} collective-permute-done((bf16[8,16,128]{2,1,0:T(8,128)(2,1)S(1)}, bf16[8,16,128]{2,1,0:T(8,128)(2,1)S(1)}, u32[]{:S(2)}, u32[]{:S(2)}) %collective-permute-start) | collective-permute-done | bytes 32800 | tf_op jit(solution)/shard_map/ppermute | solution.py:17
  11.4 0.2 fusion.71
  11.6 1.5 %fusion.18 = bf16[8,512,128]{2,1,0:T(8,128)(2,1)S(1)} fusion(pred[8,512]{1,0:T(8,128)(4,1)S(1)} %fusion.54, bf16[8,64,1,8,128]{4,1,3,0,2:T(8,128)(2,1)S(1)} %fusion.17, s32[8,16]{1,0:T(8,128)S(1)} %fusion.79, bf16[8,16,128]{2,0,1:T(8,128)(2,1)S(1)} %fusion.71), kind=kOutput, calls=%fused_computation.23 | convolution fusion | flops 17891328 | bytes 2134528 | tf_op jit(solution)/shard_map/jkr,jkd->jrd/dot_general | solution.py:144
  13.2 0.2 slice.61
  13.4 3.1 %fusion.19 = bf16[256,1024]{1,0:T(8,128)(2,1)} fusion(bf16[256,1024]{1,0:T(8,128)(2,1)S(1)} %slice.61, bf16[1024,4096]{1,0:T(8,128)(2,1)} %param.14, s32[]{:T(128)S(6)} %select_n.89), kind=kOutput, calls=%fused_computation.24 | convolution fusion | flops 537133056 | bytes 3145732 | tf_op jit(solution)/shard_map/dot_general | solution.py:53
  16.5 0.2 slice.63
  16.7 1.9 %collective-permute-done.1 = bf16[256,1024]{1,0:T(8,128)(2,1)S(1)} collective-permute-done((bf16[256,1024]{1,0:T(8,128)(2,1)}, bf16[256,1024]{1,0:T(8,128)(2,1)S(1)}, u32[]{:S(2)}, u32[]{:S(2)}) %collective-permute-start.1) | collective-permute-done | bytes 524320 | tf_op jit(solution)/shard_map/ppermute | solution.py:17
  18.6 3.1 %add_convert_fusion.3 = bf16[256,1024]{1,0:T(8,128)(2,1)} fusion(bf16[256,1024]{1,0:T(8,128)(2,1)S(1)} %collective-permute-done.1, bf16[256,1024]{1,0:T(8,128)(2,1)S(1)} %slice.61, bf16[1024,4096]{1,0:T(8,128)(2,1)} %param.14, s32[]{:T(128)S(6)} %select_n.88), kind=kOutput, calls=%fused_computation.46 | convolution fusion | flops 537657344 | bytes 3670020 | tf_op jit(solution)/shard_map/dot_general | solution.py:53
  21.7 3.2 %fusion.22 = bf16[256,1024]{1,0:T(8,128)(2,1)} fusion(bf16[256,1024]{1,0:T(8,128)(2,1)S(1)} %slice.63, bf16[1024,4096]{1,0:T(8,128)(2,1)} %param.14, s32[]{:T(128)S(6)} %select_n.89), kind=kOutput, calls=%fused_computation.25 | convolution fusion | flops 537133056 | bytes 3145732 | tf_op jit(solution)/shard_map/dot_general | solution.py:53
  24.9 0.1 collective-permute-start.4
  25.0 0.1 fusion.103
  25.2 0.8 collective-permute-start.3
  26.0 2.3 %fusion.25 = bf16[256,1024]{1,0:T(8,128)(2,1)S(1)} fusion(bf16[256,1024]{1,0:T(8,128)(2,1)S(1)} %slice.61, bf16[1024,4096]{1,0:T(8,128)(2,1)} %param.14, s32[]{:T(128)S(6)} %select_n.91), kind=kOutput, calls=%fused_computation.26 | convolution fusion | flops 537133056 | bytes 3145732 | tf_op jit(solution)/shard_map/dot_general | solution.py:72
  28.3 0.2 collective-permute-start.2
  28.5 2.3 %fusion.7 = f32[256,1024]{1,0:T(8,128)S(1)} fusion(bf16[256,1024]{1,0:T(8,128)(2,1)S(1)} %slice.61, bf16[1024,4096]{1,0:T(8,128)(2,1)} %param.14, s32[]{:T(128)S(6)} %select_n.90), kind=kOutput, calls=%fused_computation.10 | convolution fusion | flops 536870912 | bytes 3670020 | tf_op jit(solution)/shard_map/dot_general | solution.py:72
  30.8 3.2 %add_convert_fusion.2 = bf16[256,1024]{1,0:T(8,128)(2,1)} fusion(bf16[256,1024]{1,0:T(8,128)(2,1)} %collective-permute-done.4, bf16[256,1024]{1,0:T(8,128)(2,1)S(1)} %slice.63, bf16[1024,4096]{1,0:T(8,128)(2,1)} %param.14, s32[]{:T(128)S(6)} %select_n.88), kind=kOutput, calls=%fused_computation.45 | convolution fusion | flops 537657344 | bytes 3670020 | tf_op jit(solution)/shard_map/dot_general | solution.py:53
  34.0 1.3 %collective-permute-start.6 = (bf16[256,1024]{1,0:T(8,128)(2,1)}, bf16[256,1024]{1,0:T(8,128)(2,1)}, u32[]{:S(2)}, u32[]{:S(2)}) collective-permute-start(bf16[256,1024]{1,0:T(8,128)(2,1)} %add_convert_fusion.2), channel_id=1, source_target_pairs={{0,2},{1,3},{2,0},{3,1},{4,6},{5,7},{6,4},{7,5},{8,10},{9,11},{10,... | collective-permute-start | bytes 1572872 | tf_op jit(solution)/shard_map/ppermute | solution.py:17
  35.3 5.0 %collective-permute-done.3 = bf16[256,1024]{1,0:T(8,128)(2,1)S(1)} collective-permute-done((bf16[256,1024]{1,0:T(8,128)(2,1)}, bf16[256,1024]{1,0:T(8,128)(2,1)S(1)}, u32[]{:S(2)}, u32[]{:S(2)}) %collective-permute-start.3) | collective-permute-done | bytes 524320 | tf_op jit(solution)/shard_map/ppermute | solution.py:17
  40.3 0.4 multiply_reduce_fusion.1
  40.7 1.2 %fusion.45 = f32[256,64]{0,1:T(8,128)S(1)} fusion(f32[1024,64]{0,1:T(8,128)S(1)} %copy-done.2, bf16[256,1024]{1,0:T(8,128)(2,1)S(1)} %get-tuple-element.22, bf16[256,1024]{1,0:T(8,128)(2,1)S(1)} %bitcast.69, f32[1024]{0:T(1024)S(1)} %copy-done.3), kind=kOutput, calls=%fused_computation.50 | convolution fusion | flops 202375168 | bytes 1380352 | tf_op jit(solution)/shard_map/dot_general | solution.py:174
  41.8 0.6 pad_maximum_fusion.2
  42.5 3.1 %fusion.28 = bf16[256,1024]{1,0:T(8,128)(2,1)} fusion(bf16[256,1024]{1,0:T(8,128)(2,1)S(1)} %slice.63, bf16[1024,4096]{1,0:T(8,128)(2,1)} %param.14, s32[]{:T(128)S(6)} %select_n.91), kind=kOutput, calls=%fused_computation.27 | convolution fusion | flops 537133056 | bytes 3145732 | tf_op jit(solution)/shard_map/dot_general | solution.py:72
  45.6 0.5 collective-permute-start.5
  46.1 0.6 fusion.106
  46.7 1.3 %eq.78 = s32[256]{0:T(256)} reshape(s32[4,64]{1,0:T(4,128)} %get-tuple-element.32) | data formatting | bytes 2048 | tf_op jit(solution)/shard_map/eq | solution.py:183
  48.0 1.3 %eq.82 = s32[256]{0:T(256)} reshape(s32[4,64]{1,0:T(4,128)} %get-tuple-element.31) | data formatting | bytes 2048 | tf_op jit(solution)/shard_map/eq | solution.py:183
  49.4 0.8 collective-permute-start.8
  50.2 2.3 %fusion.5 = f32[256,1024]{1,0:T(8,128)S(1)} fusion(bf16[256,1024]{1,0:T(8,128)(2,1)S(1)} %slice.63, bf16[1024,4096]{1,0:T(8,128)(2,1)} %param.14, s32[]{:T(128)S(6)} %select_n.90), kind=kOutput, calls=%fused_computation.8 | convolution fusion | flops 536870912 | bytes 3670020 | tf_op jit(solution)/shard_map/dot_general | solution.py:72
  52.5 1.3 %collective-permute-done.8 = f32[256,65]{0,1:T(8,128)S(1)} collective-permute-done((f32[256,65]{0,1:T(8,128)S(1)}, f32[256,65]{0,1:T(8,128)S(1)}, u32[]{:S(2)}, u32[]{:S(2)}) %collective-permute-start.8) | collective-permute-done | bytes 66592 | tf_op jit(solution)/shard_map/ppermute | solution.py:17
  53.9 1.6 %multiply_reduce_fusion = (f32[256]{0:T(256)S(1)}, bf16[256,1024]{1,0:T(8,128)(2,1)S(1)}) fusion(bf16[4,64,1024]{2,1,0:T(8,128)(2,1)S(1)} %get-tuple-element.26, bf16[256,1024]{1,0:T(8,128)(2,1)} %collective-permute-done.6, f32[256,1024]{1,0:T(8,128)S(1)} %fusion.5, bf16[256,1024]{1,0:T(8,128)(2,1)} %collective-permute-done.5), kind=kLoop, calls=%fused_computation.41 | loop fusion | flops 2621184 | bytes 3146752 | tf_op jit(solution)/shard_map/reduce_sum | solution.py:172
  55.5 1.2 %fusion.42 = f32[256,64]{0,1:T(8,128)S(1)} fusion(f32[1024,64]{0,1:T(8,128)S(1)} %copy-done.2, bf16[256,1024]{1,0:T(8,128)(2,1)S(1)} %get-tuple-element.24, bf16[256,1024]{1,0:T(8,128)(2,1)S(1)} %bitcast.67, f32[1024]{0:T(1024)S(1)} %copy-done.3), kind=kOutput, calls=%fused_computation.49 | convolution fusion | flops 202375168 | bytes 1380352 | tf_op jit(solution)/shard_map/dot_general | solution.py:174
  56.7 0.1 collective-permute-start.9
  56.8 1.2 %collective-permute-done.9 = f32[256,65]{0,1:T(8,128)S(1)} collective-permute-done((f32[256,65]{0,1:T(8,128)S(1)}, f32[256,65]{0,1:T(8,128)S(1)}, u32[]{:S(2)}, u32[]{:S(2)}) %collective-permute-start.9) | collective-permute-done | bytes 66592 | tf_op jit(solution)/shard_map/ppermute | solution.py:17
  58.1 0.8 collective-permute-start.10
  58.9 1.0 fusion.37
  59.9 2.6 %collective-permute-done.10 = f32[256,65]{0,1:T(8,128)S(1)} collective-permute-done((f32[256,65]{0,1:T(8,128)S(1)}, f32[256,65]{0,1:T(8,128)S(1)}, u32[]{:S(2)}, u32[]{:S(2)}) %collective-permute-start.10) | collective-permute-done | bytes 66592 | tf_op jit(solution)/shard_map/ppermute | solution.py:17
  62.5 1.0 fusion.31
  63.6 2.0 %collective-permute-start.11 = (f32[512,64]{0,1:T(8,128)S(1)}, f32[512,64]{0,1:T(8,128)S(1)}, u32[]{:S(2)}, u32[]{:S(2)}) collective-permute-start(f32[512,64]{0,1:T(8,128)S(1)} %slice_select_fusion), channel_id=1, source_target_pairs={{0,4},{4,0},{8,12},{12,8},{16,20},{20,16},{24,28},{28,24},{32,36},... | collective-permute-start | bytes 393224 | tf_op jit(solution)/shard_map/ppermute | solution.py:17
  65.6 3.1 %collective-permute-done.11 = f32[512,64]{0,1:T(8,128)S(1)} collective-permute-done((f32[512,64]{0,1:T(8,128)S(1)}, f32[512,64]{0,1:T(8,128)S(1)}, u32[]{:S(2)}, u32[]{:S(2)}) %collective-permute-start.11) | collective-permute-done | bytes 131104 | tf_op jit(solution)/shard_map/ppermute | solution.py:17
  68.7 3.4 %collective-permute-start.12 = (f32[256,64]{0,1:T(8,128)S(1)}, f32[256,64]{0,1:T(8,128)S(1)}, u32[]{:S(2)}, u32[]{:S(2)}) collective-permute-start(f32[256,64]{0,1:T(8,128)S(1)} %slice_select_fusion.1), channel_id=1, source_target_pairs={{0,8},{4,12},{8,0},{12,4},{16,24},{20,28},{24,16},{28,20},{32,40},... | collective-permute-start | bytes 196616 | tf_op jit(solution)/shard_map/ppermute | solution.py:17
  72.0 2.2 %collective-permute-done.12 = f32[256,64]{0,1:T(8,128)S(1)} collective-permute-done((f32[256,64]{0,1:T(8,128)S(1)}, f32[256,64]{0,1:T(8,128)S(1)}, u32[]{:S(2)}, u32[]{:S(2)}) %collective-permute-start.12) | collective-permute-done | bytes 65568 | tf_op jit(solution)/shard_map/ppermute | solution.py:17
  74.3 7.6 %collective-permute-start.13 = (f32[256,64]{0,1:T(8,128)S(1)}, f32[256,64]{0,1:T(8,128)S(1)}, u32[]{:S(2)}, u32[]{:S(2)}) collective-permute-start(f32[256,64]{0,1:T(8,128)S(1)} %select_add_fusion.1), channel_id=1, source_target_pairs={{0,16},{4,20},{8,24},{12,28},{16,0},{20,4},{24,8},{28,12},{32,48},... | collective-permute-start | bytes 196616 | tf_op jit(solution)/shard_map/ppermute | solution.py:17
  81.9 2.5 %collective-permute-done.13 = f32[256,64]{0,1:T(8,128)S(1)} collective-permute-done((f32[256,64]{0,1:T(8,128)S(1)}, f32[256,64]{0,1:T(8,128)S(1)}, u32[]{:S(2)}, u32[]{:S(2)}) %collective-permute-start.13) | collective-permute-done | bytes 65568 | tf_op jit(solution)/shard_map/ppermute | solution.py:17
  84.5 1.3 %collective-permute-start.14 = (f32[256,64]{0,1:T(8,128)S(1)}, f32[256,64]{0,1:T(8,128)S(1)}, u32[]{:S(2)}, u32[]{:S(2)}) collective-permute-start(f32[256,64]{0,1:T(8,128)S(1)} %add.134), channel_id=1, source_target_pairs={{0,32},{4,36},{8,40},{12,44},{16,48},{20,52},{24,56},{28,60},{32,0... | collective-permute-start | bytes 196616 | tf_op jit(solution)/shard_map/ppermute | solution.py:17
  85.8 4.5 %collective-permute-done.14 = f32[256,64]{0,1:T(8,128)S(1)} collective-permute-done((f32[256,64]{0,1:T(8,128)S(1)}, f32[256,64]{0,1:T(8,128)S(1)}, u32[]{:S(2)}, u32[]{:S(2)}) %collective-permute-start.14) | collective-permute-done | bytes 65568 | tf_op jit(solution)/shard_map/ppermute | solution.py:17
  90.4 1.6 %collective-permute-start.15 = (f32[256,64]{0,1:T(8,128)S(1)}, f32[256,64]{0,1:T(8,128)S(1)}, u32[]{:S(2)}, u32[]{:S(2)}) collective-permute-start(f32[256,64]{0,1:T(8,128)S(1)} %add.135), channel_id=1, source_target_pairs={{0,64},{4,68},{8,72},{12,76},{16,80},{20,84},{24,88},{28,92},{32,9... | collective-permute-start | bytes 196616 | tf_op jit(solution)/shard_map/ppermute | solution.py:17
  91.9 2.8 %collective-permute-done.15 = f32[256,64]{0,1:T(8,128)S(1)} collective-permute-done((f32[256,64]{0,1:T(8,128)S(1)}, f32[256,64]{0,1:T(8,128)S(1)}, u32[]{:S(2)}, u32[]{:S(2)}) %collective-permute-start.15) | collective-permute-done | bytes 65568 | tf_op jit(solution)/shard_map/ppermute | solution.py:17
  94.7 3.1 %collective-permute-start.16 = (f32[256,64]{0,1:T(8,128)S(1)}, f32[256,64]{0,1:T(8,128)S(1)}, u32[]{:S(2)}, u32[]{:S(2)}) collective-permute-start(f32[256,64]{0,1:T(8,128)S(1)} %add.136), channel_id=1, source_target_pairs={{0,128},{4,132},{8,136},{12,140},{16,144},{20,148},{24,152},{28,15... | collective-permute-start | bytes 196616 | tf_op jit(solution)/shard_map/ppermute | solution.py:17
  97.9 2.7 %collective-permute-done.16 = f32[256,64]{0,1:T(8,128)S(1)} collective-permute-done((f32[256,64]{0,1:T(8,128)S(1)}, f32[256,64]{0,1:T(8,128)S(1)}, u32[]{:S(2)}, u32[]{:S(2)}) %collective-permute-start.16) | collective-permute-done | bytes 65568 | tf_op jit(solution)/shard_map/ppermute | solution.py:17
  100.6 1.1 collective-permute-start.17
  101.7 1.0 pad_maximum_fusion
  102.7 3.5 %collective-permute-done.17 = f32[256,64]{0,1:T(8,128)S(1)} collective-permute-done((f32[256,64]{0,1:T(8,128)S(1)}, f32[256,64]{0,1:T(8,128)S(1)}, u32[]{:S(2)}, u32[]{:S(2)}) %collective-permute-start.17) | collective-permute-done | bytes 65568 | tf_op jit(solution)/shard_map/ppermute | solution.py:17
  106.2 0.1 collective-permute-start.18
  106.4 0.8 copy.29
  107.2 4.1 %collective-permute-done.18 = f32[512,64]{0,1:T(8,128)S(1)} collective-permute-done((f32[512,64]{0,1:T(8,128)S(1)}, f32[512,64]{0,1:T(8,128)S(1)}, u32[]{:S(2)}, u32[]{:S(2)}) %collective-permute-start.18) | collective-permute-done | bytes 131104 | tf_op jit(solution)/shard_map/ppermute | solution.py:17
  111.3 0.7 maximum_select_fusion
  (46 shorter events, 0.4 us)
Async XLA Ops:
  0.6 1.3 %copy-start = (bf16[8,64,1024]{2,1,0:T(8,128)(2,1)S(1)}, bf16[8,64,1024]{2,1,0:T(8,128)(2,1)}, u32[]{:S(2)}) copy-start(bf16[8,64,1024]{2,1,0:T(8,128)(2,1)} %param.11) | copy-start | bytes 3145732
  1.9 2.6 %copy-start.8 = (bf16[8,64,128]{2,1,0:T(8,128)(2,1)S(1)}, bf16[8,64,128]{2,1,0:T(8,128)(2,1)}, u32[]{:S(2)}) copy-start(bf16[8,64,128]{2,1,0:T(8,128)(2,1)} %param.13) | copy-start | bytes 393220
  4.5 6.9 %copy-start.7 = (s32[8]{0:T(128)S(1)}, s32[8]{0:T(128)}, u32[]{:S(2)}) copy-start(s32[8]{0:T(128)} %param.17) | copy-start | bytes 100
  5.9 5.5 %collective-permute-start = (bf16[8,16,128]{2,1,0:T(8,128)(2,1)S(1)}, bf16[8,16,128]{2,1,0:T(8,128)(2,1)S(1)}, u32[]{:S(2)}, u32[]{:S(2)}) collective-permute-start(bf16[8,16,128]{2,1,0:T(8,128)(2,1)S(1)} %convolution_convert_fusion.2), channel_id=1, source_target_pairs={{0,128},{4,132},{8,136},{12,140},{16,144},{20,148},{24,152},{28,15... | collective-permute-start | bytes 98312 | tf_op jit(solution)/shard_map/ppermute | solution.py:17
  16.5 2.1 %collective-permute-start.1 = (bf16[256,1024]{1,0:T(8,128)(2,1)}, bf16[256,1024]{1,0:T(8,128)(2,1)S(1)}, u32[]{:S(2)}, u32[]{:S(2)}) collective-permute-start(bf16[256,1024]{1,0:T(8,128)(2,1)} %fusion.19), channel_id=1, source_target_pairs={{0,1},{1,0},{2,3},{3,2},{4,5},{5,4},{6,7},{7,6},{8,9},{9,8},{10,11... | collective-permute-start | bytes 1572872 | tf_op jit(solution)/shard_map/ppermute | solution.py:17
  21.7 3.3 %copy-start.1 = (bf16[8,64,1024]{2,1,0:T(8,128)(2,1)S(1)}, bf16[8,64,1024]{2,1,0:T(8,128)(2,1)}, u32[]{:S(2)}) copy-start(bf16[8,64,1024]{2,1,0:T(8,128)(2,1)} %param.10) | copy-start | bytes 3145732
  24.9 5.9 %collective-permute-start.4 = (bf16[256,1024]{1,0:T(8,128)(2,1)}, bf16[256,1024]{1,0:T(8,128)(2,1)}, u32[]{:S(2)}, u32[]{:S(2)}) collective-permute-start(bf16[256,1024]{1,0:T(8,128)(2,1)} %fusion.22), channel_id=1, source_target_pairs={{0,1},{1,0},{2,3},{3,2},{4,5},{5,4},{6,7},{7,6},{8,9},{9,8},{10,11... | collective-permute-start | bytes 1572872 | tf_op jit(solution)/shard_map/ppermute | solution.py:17
  25.2 15.1 %collective-permute-start.3 = (bf16[256,1024]{1,0:T(8,128)(2,1)}, bf16[256,1024]{1,0:T(8,128)(2,1)S(1)}, u32[]{:S(2)}, u32[]{:S(2)}) collective-permute-start(bf16[256,1024]{1,0:T(8,128)(2,1)} %add_convert_fusion.3), channel_id=1, source_target_pairs={{0,2},{1,3},{2,0},{3,1},{4,6},{5,7},{6,4},{7,5},{8,10},{9,11},{10,... | collective-permute-start | bytes 1572872 | tf_op jit(solution)/shard_map/ppermute | solution.py:17
  28.3 12.0 %collective-permute-start.2 = (bf16[256,1024]{1,0:T(8,128)(2,1)S(1)}, bf16[256,1024]{1,0:T(8,128)(2,1)S(1)}, u32[]{:S(2)}, u32[]{:S(2)}) collective-permute-start(bf16[256,1024]{1,0:T(8,128)(2,1)S(1)} %fusion.25), channel_id=1, source_target_pairs={{0,1},{1,0},{2,3},{3,2},{4,5},{5,4},{6,7},{7,6},{8,9},{9,8},{10,11... | collective-permute-start | bytes 1572872 | tf_op jit(solution)/shard_map/ppermute | solution.py:17
  34.0 6.7 %copy-start.2 = (f32[1024,64]{0,1:T(8,128)S(1)}, f32[1024,64]{0,1:T(8,128)}, u32[]{:S(2)}) copy-start(f32[1024,64]{0,1:T(8,128)} %param.16) | copy-start | bytes 786436
  34.0 6.7 %copy-start.3 = (f32[1024]{0:T(1024)S(1)}, f32[1024]{0:T(1024)}, u32[]{:S(2)}) copy-start(f32[1024]{0:T(1024)} %param.15) | copy-start | bytes 12292
  34.0 19.9 %collective-permute-start.6 = (bf16[256,1024]{1,0:T(8,128)(2,1)}, bf16[256,1024]{1,0:T(8,128)(2,1)}, u32[]{:S(2)}, u32[]{:S(2)}) collective-permute-start(bf16[256,1024]{1,0:T(8,128)(2,1)} %add_convert_fusion.2), channel_id=1, source_target_pairs={{0,2},{1,3},{2,0},{3,1},{4,6},{5,7},{6,4},{7,5},{8,10},{9,11},{10,... | collective-permute-start | bytes 1572872 | tf_op jit(solution)/shard_map/ppermute | solution.py:17
  41.8 4.3 %copy-start.4 = (s32[8,64]{1,0:T(8,128)S(1)}, s32[8,64]{1,0:T(8,128)}, u32[]{:S(2)}) copy-start(s32[8,64]{1,0:T(8,128)} %param.19) | copy-start | bytes 6148
  42.5 6.9 %collective-permute-start.7 = (f32[256,65]{0,1:T(8,128)}, f32[256,65]{0,1:T(8,128)S(1)}, u32[]{:S(2)}, u32[]{:S(2)}) collective-permute-start(f32[256,65]{0,1:T(8,128)} %pad_maximum_fusion.2), channel_id=1, source_target_pairs={{0,1},{1,0},{2,3},{3,2},{4,5},{5,4},{6,7},{7,6},{8,9},{9,8},{10,11... | collective-permute-start | bytes 199688 | tf_op jit(solution)/shard_map/ppermute | solution.py:17
  45.6 8.3 %collective-permute-start.5 = (bf16[256,1024]{1,0:T(8,128)(2,1)}, bf16[256,1024]{1,0:T(8,128)(2,1)}, u32[]{:S(2)}, u32[]{:S(2)}) collective-permute-start(bf16[256,1024]{1,0:T(8,128)(2,1)} %fusion.28), channel_id=1, source_target_pairs={{0,1},{1,0},{2,3},{3,2},{4,5},{5,4},{6,7},{7,6},{8,9},{9,8},{10,11... | collective-permute-start | bytes 1572872 | tf_op jit(solution)/shard_map/ppermute | solution.py:17
  49.4 4.4 %collective-permute-start.8 = (f32[256,65]{0,1:T(8,128)S(1)}, f32[256,65]{0,1:T(8,128)S(1)}, u32[]{:S(2)}, u32[]{:S(2)}) collective-permute-start(f32[256,65]{0,1:T(8,128)S(1)} %fusion.102), channel_id=1, source_target_pairs={{0,2},{1,3},{2,0},{3,1},{4,6},{5,7},{6,4},{7,5},{8,10},{9,11},{10,... | collective-permute-start | bytes 199688 | tf_op jit(solution)/shard_map/ppermute | solution.py:17
  53.9 5.0 %copy-start.6 = (s32[256]{0:T(256)S(1)}, s32[256]{0:T(256)}, u32[]{:S(2)}) copy-start(s32[256]{0:T(256)} %eq.78) | copy-start | bytes 3076
  55.5 7.0 %copy-start.5 = (s32[256]{0:T(256)S(1)}, s32[256]{0:T(256)}, u32[]{:S(2)}) copy-start(s32[256]{0:T(256)} %eq.82) | copy-start | bytes 3076
  56.7 1.4 %collective-permute-start.9 = (f32[256,65]{0,1:T(8,128)S(1)}, f32[256,65]{0,1:T(8,128)S(1)}, u32[]{:S(2)}, u32[]{:S(2)}) collective-permute-start(f32[256,65]{0,1:T(8,128)S(1)} %pad_maximum_fusion.3), channel_id=1, source_target_pairs={{0,1},{1,0},{2,3},{3,2},{4,5},{5,4},{6,7},{7,6},{8,9},{9,8},{10,11... | collective-permute-start | bytes 199688 | tf_op jit(solution)/shard_map/ppermute | solution.py:17
  58.1 4.4 %collective-permute-start.10 = (f32[256,65]{0,1:T(8,128)S(1)}, f32[256,65]{0,1:T(8,128)S(1)}, u32[]{:S(2)}, u32[]{:S(2)}) collective-permute-start(f32[256,65]{0,1:T(8,128)S(1)} %fusion.101), channel_id=1, source_target_pairs={{0,2},{1,3},{2,0},{3,1},{4,6},{5,7},{6,4},{7,5},{8,10},{9,11},{10,... | collective-permute-start | bytes 199688 | tf_op jit(solution)/shard_map/ppermute | solution.py:17
  63.6 5.1 %collective-permute-start.11 = (f32[512,64]{0,1:T(8,128)S(1)}, f32[512,64]{0,1:T(8,128)S(1)}, u32[]{:S(2)}, u32[]{:S(2)}) collective-permute-start(f32[512,64]{0,1:T(8,128)S(1)} %slice_select_fusion), channel_id=1, source_target_pairs={{0,4},{4,0},{8,12},{12,8},{16,20},{20,16},{24,28},{28,24},{32,36},... | collective-permute-start | bytes 393224 | tf_op jit(solution)/shard_map/ppermute | solution.py:17
  68.7 5.6 %collective-permute-start.12 = (f32[256,64]{0,1:T(8,128)S(1)}, f32[256,64]{0,1:T(8,128)S(1)}, u32[]{:S(2)}, u32[]{:S(2)}) collective-permute-start(f32[256,64]{0,1:T(8,128)S(1)} %slice_select_fusion.1), channel_id=1, source_target_pairs={{0,8},{4,12},{8,0},{12,4},{16,24},{20,28},{24,16},{28,20},{32,40},... | collective-permute-start | bytes 196616 | tf_op jit(solution)/shard_map/ppermute | solution.py:17
  74.3 10.2 %collective-permute-start.13 = (f32[256,64]{0,1:T(8,128)S(1)}, f32[256,64]{0,1:T(8,128)S(1)}, u32[]{:S(2)}, u32[]{:S(2)}) collective-permute-start(f32[256,64]{0,1:T(8,128)S(1)} %select_add_fusion.1), channel_id=1, source_target_pairs={{0,16},{4,20},{8,24},{12,28},{16,0},{20,4},{24,8},{28,12},{32,48},... | collective-permute-start | bytes 196616 | tf_op jit(solution)/shard_map/ppermute | solution.py:17
  84.5 5.9 %collective-permute-start.14 = (f32[256,64]{0,1:T(8,128)S(1)}, f32[256,64]{0,1:T(8,128)S(1)}, u32[]{:S(2)}, u32[]{:S(2)}) collective-permute-start(f32[256,64]{0,1:T(8,128)S(1)} %add.134), channel_id=1, source_target_pairs={{0,32},{4,36},{8,40},{12,44},{16,48},{20,52},{24,56},{28,60},{32,0... | collective-permute-start | bytes 196616 | tf_op jit(solution)/shard_map/ppermute | solution.py:17
  90.4 4.4 %collective-permute-start.15 = (f32[256,64]{0,1:T(8,128)S(1)}, f32[256,64]{0,1:T(8,128)S(1)}, u32[]{:S(2)}, u32[]{:S(2)}) collective-permute-start(f32[256,64]{0,1:T(8,128)S(1)} %add.135), channel_id=1, source_target_pairs={{0,64},{4,68},{8,72},{12,76},{16,80},{20,84},{24,88},{28,92},{32,9... | collective-permute-start | bytes 196616 | tf_op jit(solution)/shard_map/ppermute | solution.py:17
  94.7 5.9 %collective-permute-start.16 = (f32[256,64]{0,1:T(8,128)S(1)}, f32[256,64]{0,1:T(8,128)S(1)}, u32[]{:S(2)}, u32[]{:S(2)}) collective-permute-start(f32[256,64]{0,1:T(8,128)S(1)} %add.136), channel_id=1, source_target_pairs={{0,128},{4,132},{8,136},{12,140},{16,144},{20,148},{24,152},{28,15... | collective-permute-start | bytes 196616 | tf_op jit(solution)/shard_map/ppermute | solution.py:17
  100.6 5.6 %collective-permute-start.17 = (f32[256,64]{0,1:T(8,128)S(1)}, f32[256,64]{0,1:T(8,128)S(1)}, u32[]{:S(2)}, u32[]{:S(2)}) collective-permute-start(f32[256,64]{0,1:T(8,128)S(1)} %add.137), channel_id=1, source_target_pairs={{0,8},{4,12},{8,0},{12,4},{16,24},{20,28},{24,16},{28,20},{32,40},... | collective-permute-start | bytes 196616 | tf_op jit(solution)/shard_map/ppermute | solution.py:17
  106.2 5.1 %collective-permute-start.18 = (f32[512,64]{0,1:T(8,128)S(1)}, f32[512,64]{0,1:T(8,128)S(1)}, u32[]{:S(2)}, u32[]{:S(2)}) collective-permute-start(f32[512,64]{0,1:T(8,128)S(1)} %maximum_select_fusion.1), channel_id=1, source_target_pairs={{0,4},{4,0},{8,12},{12,8},{16,20},{20,16},{24,28},{28,24},{32,36},... | collective-permute-start | bytes 393224 | tf_op jit(solution)/shard_map/ppermute | solution.py:17

commit v7 on v6

--- a/solution.py
+++ b/solution.py
@@ -105,6 +105,39 @@
     return mixed_rows.astype(jnp.bfloat16).reshape(prompt_count, seq_length, local_heads, HDIM)
 
 
+def attend_rows(queries, attn_keys, values, pick_values, head_ids, pos_ids):
+    prompt_count = queries.shape[0]
+    seq_length = queries.shape[1]
+    local_kv = attn_keys.shape[2] // HDIM
+    local_heads = queries.shape[2] // HDIM
+    group_size = local_heads // local_kv
+    query_rows = jnp.einsum(
+        "jkr,jrd->jkd",
+        pick_values,
+        queries.reshape(prompt_count, seq_length * local_heads, HDIM),
+        preferred_element_type=jnp.float32,
+    ).astype(queries.dtype)
+    key_blocks = attn_keys.reshape(prompt_count, seq_length, local_kv, HDIM)
+    value_blocks = values.reshape(prompt_count, seq_length, local_kv, HDIM)
+    kv_pick = (
+        (head_ids // group_size)[:, :, None] == jnp.arange(local_kv, dtype=head_ids.dtype)[None, None, :]
+    ).astype(jnp.float32)
+    all_scores = jnp.einsum(
+        "jkd,jsvd->jksv", query_rows, key_blocks, preferred_element_type=jnp.float32
+    )
+    scores = jnp.sum(all_scores * kv_pick[:, :, None, :], axis=-1) / math.sqrt(HDIM)
+    causal = jnp.arange(seq_length)[None, None, :] <= pos_ids[:, :, None]
+    scores = jnp.where(causal, scores, -jnp.inf)
+    highest = jnp.max(scores, axis=-1, keepdims=True)
+    exponent = jnp.exp(scores - highest)
+    weights = (exponent / jnp.sum(exponent, axis=-1, keepdims=True)).astype(jnp.bfloat16)
+    all_rows = jnp.einsum(
+        "jks,jsvd->jkvd", weights, value_blocks, preferred_element_type=jnp.float32
+    )
+    mixed = jnp.sum(all_rows * kv_pick[..., None], axis=2)
+    return mixed.astype(jnp.bfloat16)
+
+
 def per_device(
     residual,
     queries,
@@ -121,17 +154,17 @@
     seq_length = residual.shape[1]
     feature_count = residual.shape[2]
     token_count = prompt_count * seq_length
-    heads_out = attend(queries, attn_keys, values)
-    local_heads = heads_out.shape[2]
+    local_heads = queries.shape[2] // HDIM
     rows = seq_length * local_heads
-    flat_heads = heads_out.reshape(prompt_count, rows, HDIM)
 
     entry_rows = patch_list[..., 1] * local_heads + patch_list[..., 0] % local_heads
     picks = entry_rows[:, :, None] == jnp.arange(rows, dtype=jnp.int32)[None, None, :]
     pick_values = picks.astype(jnp.bfloat16)
-    own_entries = jnp.einsum(
-        "jkr,jrd->jkd", pick_values, flat_heads, preferred_element_type=jnp.float32
-    ).astype(jnp.bfloat16)
+    own_entries = attend_rows(
+        queries, attn_keys, values, pick_values, patch_list[..., 0] % local_heads, patch_list[..., 1]
+    )
+    heads_out = attend(queries, attn_keys, values)
+    flat_heads = heads_out.reshape(prompt_count, rows, HDIM)
 
     half_way = lax.axis_size("dp") // 2
     arrived = exchanged(own_entries, "dp", half_way)

time: 112 us -> 108 us (0.964)
  matrix products: 32 us -> 29.4 us
  waiting for transfers between devices: 39.7 us -> 37.4 us
  local copies, waits for them, and re-layouts: 5.99 us -> 7.11 us
    ppermute x19, waiting for transfers between devices: 39.7 us -> 37.4 us  [exchanged(): return lax.ppermute(block, axis, [(i, i ^ bit) for i in range(count)])]
    dot_general x8, matrix products: 22.6 us -> 20.9 us  [block(): return jnp.dot(heads, columns, preferred_element_type=jnp.float32)]
    reshape x0 -> x1, local copies, waits for them, and re-layouts: none -> 1.52 us  [attend_rows(): queries.reshape(prompt_count, seq_length * local_heads, HDIM)]
    reduce_sum x2, other arithmetic: 2.02 us -> 0.79 us  [per_device(): square_local = jnp.sum(hidden * hidden, axis=1)]
  transfers between devices with their start and end apart: 19 -> 19, of which waited for: 14 -> 13; matrix products, arithmetic and copies ran while one was open for 20% -> 23% of each run, Pallas kernels for 0% -> 0%
where the time goes in v7:
time: 108 us; the launch traced here: 107 us
  waiting for transfers between devices  37.4 us (35%)
  matrix products  29.4 us (27%)
  starting transfers between devices  27.8 us (26%)
  local copies, waits for them, and re-layouts  7.11 us (7%)
  other arithmetic  4.32 us (4%)
  between operations  1.08 us (1%)
    ppermute x19, waiting for transfers between devices, exchanged(): return lax.ppermute(block, axis, [(i, i ^ bit) for i in range(count)])  37.4 us
    ppermute x19, starting transfers between devices, exchanged(): return lax.ppermute(block, axis, [(i, i ^ bit) for i in range(count)])  27.8 us
    dot_general x8, matrix products, block(): return jnp.dot(heads, columns, preferred_element_type=jnp.float32)  20.9 us
    eq x2, local copies, waits for them, and re-layouts, per_device(): labels[rows_here][:, None] == classes[None, :]  2.66 us
    dot_general x2, matrix products, per_device(): jnp.dot(scaled, probe_weight, precision=lax.Precision.HIGHEST, preferred_...  2.32 us
  transfers between devices with their start and end apart: 19, of which 13 were waited for; matrix products, arithmetic and copies ran while one was open for 23% of the time, Pallas kernels for 0%

profile of v7, /device:TPU:24, one launch (start us, length us, event | category | flops | bytes accessed | tf_op | source)
XLA Modules:
  0.0 107.1 jit_solution(2535515014832105958)
XLA Ops:
  0.7 0.8 fusion.113
  1.6 1.5 %reshape.87 = bf16[8,512,128]{2,1,0:T(8,128)(2,1)S(1)} reshape(bf16[8,64,1024]{2,1,0:T(8,128)(2,1)} %param.11) | data formatting | bytes 2097152 | tf_op jit(solution)/shard_map/reshape | solution.py:117
  3.1 0.4 fusion.36
  3.5 0.2 fusion.116
  3.7 0.3 fusion.37
  4.0 3.1 %collective-permute-start = (bf16[8,16,128]{2,1,0:T(8,128)(2,1)S(1)}, bf16[8,16,128]{2,1,0:T(8,128)(2,1)S(1)}, u32[]{:S(2)}, u32[]{:S(2)}) collective-permute-start(bf16[8,16,128]{2,1,0:T(8,128)(2,1)S(1)} %fusion.37), channel_id=1, source_target_pairs={{0,128},{4,132},{8,136},{12,140},{16,144},{20,148},{24,152},{28,15... | collective-permute-start | bytes 98312 | tf_op jit(solution)/shard_map/ppermute | solution.py:17
  7.1 1.1 %fusion.115 = (f32[8,8,64]{2,1,0:T(8,128)S(1)}, f32[8,1,8,64,64]{3,4,2,0,1:T(8,128)S(1)}) fusion(bf16[8,64,128]{2,1,0:T(8,128)(2,1)S(1)} %copy-done.3, pred[64,64]{0,1:T(8,128)(4,1)S(1)} %iota_compare_fusion.9, bf16[8,64,1024]{2,1,0:T(8,128)(2,1)S(1)} %copy-done.1), kind=kOutput, calls=%fused_computation.146 | convolution fusion | flops 67891200 | bytes 2248704 | tf_op jit(solution)/shard_map/pqkgd,pskd->pkgqs/dot_general | solution.py:94
  8.3 0.5 fusion.1
  8.8 0.6 fusion.19
  9.5 0.1 fusion.58
  9.6 0.2 fusion.76
  9.8 1.5 %fusion.18 = bf16[8,512,128]{2,1,0:T(8,128)(2,1)S(1)} fusion(bf16[8,64,1,8,128]{4,1,3,0,2:T(8,128)(2,1)S(1)} %fusion.19, pred[8,512]{1,0:T(8,128)(4,1)S(1)} %fusion.58, s32[8,16]{1,0:T(8,128)S(1)} %add_bitcast_fusion, bf16[8,16,128]{2,0,1:T(8,128)(2,1)S(1)} %fusion.76), kind=kOutput, calls=%fused_computation.23 | convolution fusion | flops 17891328 | bytes 2134528 | tf_op jit(solution)/shard_map/jkr,jkd->jrd/dot_general | solution.py:177
  11.4 0.2 slice.63
  11.6 2.3 %fusion.20 = bf16[256,1024]{1,0:T(8,128)(2,1)S(1)} fusion(bf16[256,1024]{1,0:T(8,128)(2,1)S(1)} %slice.63, bf16[1024,4096]{1,0:T(8,128)(2,1)} %param.14, s32[]{:T(128)S(6)} %select_n.104), kind=kOutput, calls=%fused_computation.25 | convolution fusion | flops 537133056 | bytes 3145732 | tf_op jit(solution)/shard_map/dot_general | solution.py:53
  14.1 0.2 slice.65
  14.3 1.7 %collective-permute-done.1 = bf16[256,1024]{1,0:T(8,128)(2,1)S(1)} collective-permute-done((bf16[256,1024]{1,0:T(8,128)(2,1)S(1)}, bf16[256,1024]{1,0:T(8,128)(2,1)S(1)}, u32[]{:S(2)}, u32[]{:S(2)}) %collective-permute-start.1) | collective-permute-done | bytes 524320 | tf_op jit(solution)/shard_map/ppermute | solution.py:17
  16.0 2.3 %add_convert_fusion.3 = bf16[256,1024]{1,0:T(8,128)(2,1)S(1)} fusion(bf16[256,1024]{1,0:T(8,128)(2,1)S(1)} %collective-permute-done.1, bf16[256,1024]{1,0:T(8,128)(2,1)S(1)} %slice.63, bf16[1024,4096]{1,0:T(8,128)(2,1)} %param.14, s32[]{:T(128)S(6)} %select_n.103), kind=kOutput, calls=%fused_computation.53 | convolution fusion | flops 537657344 | bytes 3670020 | tf_op jit(solution)/shard_map/dot_general | solution.py:53
  18.3 3.2 %fusion.23 = bf16[256,1024]{1,0:T(8,128)(2,1)} fusion(bf16[256,1024]{1,0:T(8,128)(2,1)S(1)} %slice.65, bf16[1024,4096]{1,0:T(8,128)(2,1)} %param.14, s32[]{:T(128)S(6)} %select_n.104), kind=kOutput, calls=%fused_computation.26 | convolution fusion | flops 537133056 | bytes 3145732 | tf_op jit(solution)/shard_map/dot_general | solution.py:53
  21.5 0.1 collective-permute-start.4
  21.6 0.1 fusion.111
  21.7 0.8 collective-permute-start.3
  22.5 2.3 %fusion.26 = bf16[256,1024]{1,0:T(8,128)(2,1)S(1)} fusion(bf16[256,1024]{1,0:T(8,128)(2,1)S(1)} %slice.63, bf16[1024,4096]{1,0:T(8,128)(2,1)} %param.14, s32[]{:T(128)S(6)} %select_n.106), kind=kOutput, calls=%fused_computation.27 | convolution fusion | flops 537133056 | bytes 3145732 | tf_op jit(solution)/shard_map/dot_general | solution.py:72
  24.9 0.2 collective-permute-start.2
  25.0 2.3 %fusion.8 = f32[256,1024]{1,0:T(8,128)S(1)} fusion(bf16[256,1024]{1,0:T(8,128)(2,1)S(1)} %slice.63, bf16[1024,4096]{1,0:T(8,128)(2,1)} %param.14, s32[]{:T(128)S(6)} %select_n.105), kind=kOutput, calls=%fused_computation.11 | convolution fusion | flops 536870912 | bytes 3670020 | tf_op jit(solution)/shard_map/dot_general | solution.py:72
  27.3 3.1 %add_convert_fusion.2 = bf16[256,1024]{1,0:T(8,128)(2,1)} fusion(bf16[256,1024]{1,0:T(8,128)(2,1)S(1)} %collective-permute-done.4, bf16[256,1024]{1,0:T(8,128)(2,1)S(1)} %slice.65, bf16[1024,4096]{1,0:T(8,128)(2,1)} %param.14, s32[]{:T(128)S(6)} %select_n.103), kind=kOutput, calls=%fused_computation.52 | convolution fusion | flops 537657344 | bytes 3670020 | tf_op jit(solution)/shard_map/dot_general | solution.py:53
  30.5 1.3 %collective-permute-start.6 = (bf16[256,1024]{1,0:T(8,128)(2,1)}, bf16[256,1024]{1,0:T(8,128)(2,1)S(1)}, u32[]{:S(2)}, u32[]{:S(2)}) collective-permute-start(bf16[256,1024]{1,0:T(8,128)(2,1)} %add_convert_fusion.2), channel_id=1, source_target_pairs={{0,2},{1,3},{2,0},{3,1},{4,6},{5,7},{6,4},{7,5},{8,10},{9,11},{10,... | collective-permute-start | bytes 1572872 | tf_op jit(solution)/shard_map/ppermute | solution.py:17
  31.7 4.9 %collective-permute-done.3 = bf16[256,1024]{1,0:T(8,128)(2,1)S(1)} collective-permute-done((bf16[256,1024]{1,0:T(8,128)(2,1)S(1)}, bf16[256,1024]{1,0:T(8,128)(2,1)S(1)}, u32[]{:S(2)}, u32[]{:S(2)}) %collective-permute-start.3) | collective-permute-done | bytes 524320 | tf_op jit(solution)/shard_map/ppermute | solution.py:17
  36.6 0.4 multiply_reduce_fusion.1
  37.0 1.2 %fusion.50 = f32[256,64]{0,1:T(8,128)S(1)} fusion(f32[1024,64]{0,1:T(8,128)S(1)} %copy-done, bf16[256,1024]{1,0:T(8,128)(2,1)S(1)} %get-tuple-element.19, bf16[256,1024]{1,0:T(8,128)(2,1)S(1)} %bitcast.76, f32[1024]{0:T(1024)S(1)} %copy-done.4), kind=kOutput, calls=%fused_computation.57 | convolution fusion | flops 202375168 | bytes 1380352 | tf_op jit(solution)/shard_map/dot_general | solution.py:207
  38.2 0.6 pad_maximum_fusion.2
  38.8 3.1 %fusion.29 = bf16[256,1024]{1,0:T(8,128)(2,1)} fusion(bf16[256,1024]{1,0:T(8,128)(2,1)S(1)} %slice.65, bf16[1024,4096]{1,0:T(8,128)(2,1)} %param.14, s32[]{:T(128)S(6)} %select_n.106), kind=kOutput, calls=%fused_computation.28 | convolution fusion | flops 537133056 | bytes 3145732 | tf_op jit(solution)/shard_map/dot_general | solution.py:72
  41.9 0.5 collective-permute-start.5
  42.5 0.6 fusion.114
  43.0 1.3 %eq.86 = s32[256]{0:T(256)} reshape(s32[4,64]{1,0:T(4,128)} %get-tuple-element.29) | data formatting | bytes 2048 | tf_op jit(solution)/shard_map/eq | solution.py:216
  44.4 1.3 %eq.90 = s32[256]{0:T(256)} reshape(s32[4,64]{1,0:T(4,128)} %get-tuple-element.28) | data formatting | bytes 2048 | tf_op jit(solution)/shard_map/eq | solution.py:216
  45.7 0.8 collective-permute-start.8
  46.5 2.3 %fusion.6 = f32[256,1024]{1,0:T(8,128)S(1)} fusion(bf16[256,1024]{1,0:T(8,128)(2,1)S(1)} %slice.65, bf16[1024,4096]{1,0:T(8,128)(2,1)} %param.14, s32[]{:T(128)S(6)} %select_n.105), kind=kOutput, calls=%fused_computation.9 | convolution fusion | flops 536870912 | bytes 3670020 | tf_op jit(solution)/shard_map/dot_general | solution.py:72
  48.8 1.3 %collective-permute-done.8 = f32[256,65]{0,1:T(8,128)S(1)} collective-permute-done((f32[256,65]{0,1:T(8,128)S(1)}, f32[256,65]{0,1:T(8,128)S(1)}, u32[]{:S(2)}, u32[]{:S(2)}) %collective-permute-start.8) | collective-permute-done | bytes 66592 | tf_op jit(solution)/shard_map/ppermute | solution.py:17
  50.2 0.4 multiply_reduce_fusion
  50.6 1.2 %fusion.47 = f32[256,64]{0,1:T(8,128)S(1)} fusion(f32[1024,64]{0,1:T(8,128)S(1)} %copy-done, bf16[256,1024]{1,0:T(8,128)(2,1)S(1)} %get-tuple-element.21, bf16[256,1024]{1,0:T(8,128)(2,1)S(1)} %bitcast.74, f32[1024]{0:T(1024)S(1)} %copy-done.4), kind=kOutput, calls=%fused_computation.56 | convolution fusion | flops 202375168 | bytes 1380352 | tf_op jit(solution)/shard_map/dot_general | solution.py:207
  51.9 1.2 %collective-permute-done.9 = f32[256,65]{0,1:T(8,128)S(1)} collective-permute-done((f32[256,65]{0,1:T(8,128)S(1)}, f32[256,65]{0,1:T(8,128)S(1)}, u32[]{:S(2)}, u32[]{:S(2)}) %collective-permute-start.9) | collective-permute-done | bytes 66592 | tf_op jit(solution)/shard_map/ppermute | solution.py:17
  53.1 0.8 collective-permute-start.10
  54.0 1.0 fusion.42
  55.0 2.6 %collective-permute-done.10 = f32[256,65]{0,1:T(8,128)S(1)} collective-permute-done((f32[256,65]{0,1:T(8,128)S(1)}, f32[256,65]{0,1:T(8,128)S(1)}, u32[]{:S(2)}, u32[]{:S(2)}) %collective-permute-start.10) | collective-permute-done | bytes 66592 | tf_op jit(solution)/shard_map/ppermute | solution.py:17
  57.6 1.0 fusion.32
  58.7 2.0 %collective-permute-start.11 = (f32[512,64]{0,1:T(8,128)S(1)}, f32[512,64]{0,1:T(8,128)S(1)}, u32[]{:S(2)}, u32[]{:S(2)}) collective-permute-start(f32[512,64]{0,1:T(8,128)S(1)} %slice_select_fusion), channel_id=1, source_target_pairs={{0,4},{4,0},{8,12},{12,8},{16,20},{20,16},{24,28},{28,24},{32,36},... | collective-permute-start | bytes 393224 | tf_op jit(solution)/shard_map/ppermute | solution.py:17
  60.7 3.1 %collective-permute-done.11 = f32[512,64]{0,1:T(8,128)S(1)} collective-permute-done((f32[512,64]{0,1:T(8,128)S(1)}, f32[512,64]{0,1:T(8,128)S(1)}, u32[]{:S(2)}, u32[]{:S(2)}) %collective-permute-start.11) | collective-permute-done | bytes 131104 | tf_op jit(solution)/shard_map/ppermute | solution.py:17
  63.8 3.4 %collective-permute-start.12 = (f32[256,64]{0,1:T(8,128)S(1)}, f32[256,64]{0,1:T(8,128)S(1)}, u32[]{:S(2)}, u32[]{:S(2)}) collective-permute-start(f32[256,64]{0,1:T(8,128)S(1)} %slice_select_fusion.1), channel_id=1, source_target_pairs={{0,8},{4,12},{8,0},{12,4},{16,24},{20,28},{24,16},{28,20},{32,40},... | collective-permute-start | bytes 196616 | tf_op jit(solution)/shard_map/ppermute | solution.py:17
  67.1 2.2 %collective-permute-done.12 = f32[256,64]{0,1:T(8,128)S(1)} collective-permute-done((f32[256,64]{0,1:T(8,128)S(1)}, f32[256,64]{0,1:T(8,128)S(1)}, u32[]{:S(2)}, u32[]{:S(2)}) %collective-permute-start.12) | collective-permute-done | bytes 65568 | tf_op jit(solution)/shard_map/ppermute | solution.py:17
  69.4 7.6 %collective-permute-start.13 = (f32[256,64]{0,1:T(8,128)S(1)}, f32[256,64]{0,1:T(8,128)S(1)}, u32[]{:S(2)}, u32[]{:S(2)}) collective-permute-start(f32[256,64]{0,1:T(8,128)S(1)} %select_add_fusion.1), channel_id=1, source_target_pairs={{0,16},{4,20},{8,24},{12,28},{16,0},{20,4},{24,8},{28,12},{32,48},... | collective-permute-start | bytes 196616 | tf_op jit(solution)/shard_map/ppermute | solution.py:17
  77.0 2.6 %collective-permute-done.13 = f32[256,64]{0,1:T(8,128)S(1)} collective-permute-done((f32[256,64]{0,1:T(8,128)S(1)}, f32[256,64]{0,1:T(8,128)S(1)}, u32[]{:S(2)}, u32[]{:S(2)}) %collective-permute-start.13) | collective-permute-done | bytes 65568 | tf_op jit(solution)/shard_map/ppermute | solution.py:17
  79.6 1.3 %collective-permute-start.14 = (f32[256,64]{0,1:T(8,128)S(1)}, f32[256,64]{0,1:T(8,128)S(1)}, u32[]{:S(2)}, u32[]{:S(2)}) collective-permute-start(f32[256,64]{0,1:T(8,128)S(1)} %add.139), channel_id=1, source_target_pairs={{0,32},{4,36},{8,40},{12,44},{16,48},{20,52},{24,56},{28,60},{32,0... | collective-permute-start | bytes 196616 | tf_op jit(solution)/shard_map/ppermute | solution.py:17
  80.9 4.5 %collective-permute-done.14 = f32[256,64]{0,1:T(8,128)S(1)} collective-permute-done((f32[256,64]{0,1:T(8,128)S(1)}, f32[256,64]{0,1:T(8,128)S(1)}, u32[]{:S(2)}, u32[]{:S(2)}) %collective-permute-start.14) | collective-permute-done | bytes 65568 | tf_op jit(solution)/shard_map/ppermute | solution.py:17
  85.5 1.5 %collective-permute-start.15 = (f32[256,64]{0,1:T(8,128)S(1)}, f32[256,64]{0,1:T(8,128)S(1)}, u32[]{:S(2)}, u32[]{:S(2)}) collective-permute-start(f32[256,64]{0,1:T(8,128)S(1)} %add.140), channel_id=1, source_target_pairs={{0,64},{4,68},{8,72},{12,76},{16,80},{20,84},{24,88},{28,92},{32,9... | collective-permute-start | bytes 196616 | tf_op jit(solution)/shard_map/ppermute | solution.py:17
  86.9 2.9 %collective-permute-done.15 = f32[256,64]{0,1:T(8,128)S(1)} collective-permute-done((f32[256,64]{0,1:T(8,128)S(1)}, f32[256,64]{0,1:T(8,128)S(1)}, u32[]{:S(2)}, u32[]{:S(2)}) %collective-permute-start.15) | collective-permute-done | bytes 65568 | tf_op jit(solution)/shard_map/ppermute | solution.py:17
  89.8 3.0 %collective-permute-start.16 = (f32[256,64]{0,1:T(8,128)S(1)}, f32[256,64]{0,1:T(8,128)S(1)}, u32[]{:S(2)}, u32[]{:S(2)}) collective-permute-start(f32[256,64]{0,1:T(8,128)S(1)} %add.141), channel_id=1, source_target_pairs={{0,128},{4,132},{8,136},{12,140},{16,144},{20,148},{24,152},{28,15... | collective-permute-start | bytes 196616 | tf_op jit(solution)/shard_map/ppermute | solution.py:17
  92.8 2.9 %collective-permute-done.16 = f32[256,64]{0,1:T(8,128)S(1)} collective-permute-done((f32[256,64]{0,1:T(8,128)S(1)}, f32[256,64]{0,1:T(8,128)S(1)}, u32[]{:S(2)}, u32[]{:S(2)}) %collective-permute-start.16) | collective-permute-done | bytes 65568 | tf_op jit(solution)/shard_map/ppermute | solution.py:17
  95.7 1.1 %collective-permute-start.17 = (f32[256,64]{0,1:T(8,128)S(1)}, f32[256,64]{0,1:T(8,128)S(1)}, u32[]{:S(2)}, u32[]{:S(2)}) collective-permute-start(f32[256,64]{0,1:T(8,128)S(1)} %add.142), channel_id=1, source_target_pairs={{0,8},{4,12},{8,0},{12,4},{16,24},{20,28},{24,16},{28,20},{32,40},... | collective-permute-start | bytes 196616 | tf_op jit(solution)/shard_map/ppermute | solution.py:17
  96.8 1.0 pad_maximum_fusion
  97.8 3.5 %collective-permute-done.17 = f32[256,64]{0,1:T(8,128)S(1)} collective-permute-done((f32[256,64]{0,1:T(8,128)S(1)}, f32[256,64]{0,1:T(8,128)S(1)}, u32[]{:S(2)}, u32[]{:S(2)}) %collective-permute-start.17) | collective-permute-done | bytes 65568 | tf_op jit(solution)/shard_map/ppermute | solution.py:17
  101.3 0.1 collective-permute-start.18
  101.5 0.8 copy.24
  102.3 4.1 %collective-permute-done.18 = f32[512,64]{0,1:T(8,128)S(1)} collective-permute-done((f32[512,64]{0,1:T(8,128)S(1)}, f32[512,64]{0,1:T(8,128)S(1)}, u32[]{:S(2)}, u32[]{:S(2)}) %collective-permute-start.18) | collective-permute-done | bytes 131104 | tf_op jit(solution)/shard_map/ppermute | solution.py:17
  106.4 0.7 maximum_select_fusion
  (52 shorter events, 0.6 us)
Async XLA Ops:
  0.6 36.4 %copy-start = (f32[1024,64]{0,1:T(8,128)S(1)}, f32[1024,64]{0,1:T(8,128)}, u32[]{:S(2)}) copy-start(f32[1024,64]{0,1:T(8,128)} %param.16) | copy-start | bytes 786436
  0.6 6.5 %copy-start.1 = (bf16[8,64,1024]{2,1,0:T(8,128)(2,1)S(1)}, bf16[8,64,1024]{2,1,0:T(8,128)(2,1)}, u32[]{:S(2)}) copy-start(bf16[8,64,1024]{2,1,0:T(8,128)(2,1)} %param.11) | copy-start | bytes 3145732
  0.7 2.4 %copy-start.3 = (bf16[8,64,128]{2,1,0:T(8,128)(2,1)S(1)}, bf16[8,64,128]{2,1,0:T(8,128)(2,1)}, u32[]{:S(2)}) copy-start(bf16[8,64,128]{2,1,0:T(8,128)(2,1)} %param.12) | copy-start | bytes 393220
  0.7 3.0 %copy-start.9 = (bf16[8,64,128]{2,1,0:T(8,128)(2,1)S(1)}, bf16[8,64,128]{2,1,0:T(8,128)(2,1)}, u32[]{:S(2)}) copy-start(bf16[8,64,128]{2,1,0:T(8,128)(2,1)} %param.13) | copy-start | bytes 393220
  4.0 5.6 %collective-permute-start = (bf16[8,16,128]{2,1,0:T(8,128)(2,1)S(1)}, bf16[8,16,128]{2,1,0:T(8,128)(2,1)S(1)}, u32[]{:S(2)}, u32[]{:S(2)}) collective-permute-start(bf16[8,16,128]{2,1,0:T(8,128)(2,1)S(1)} %fusion.37), channel_id=1, source_target_pairs={{0,128},{4,132},{8,136},{12,140},{16,144},{20,148},{24,152},{28,15... | collective-permute-start | bytes 98312 | tf_op jit(solution)/shard_map/ppermute | solution.py:17
  8.8 0.8 copy-start.8
  14.0 2.0 %collective-permute-start.1 = (bf16[256,1024]{1,0:T(8,128)(2,1)S(1)}, bf16[256,1024]{1,0:T(8,128)(2,1)S(1)}, u32[]{:S(2)}, u32[]{:S(2)}) collective-permute-start(bf16[256,1024]{1,0:T(8,128)(2,1)S(1)} %fusion.20), channel_id=1, source_target_pairs={{0,1},{1,0},{2,3},{3,2},{4,5},{5,4},{6,7},{7,6},{8,9},{9,8},{10,11... | collective-permute-start | bytes 1572872 | tf_op jit(solution)/shard_map/ppermute | solution.py:17
  18.3 3.3 %copy-start.2 = (bf16[8,64,1024]{2,1,0:T(8,128)(2,1)S(1)}, bf16[8,64,1024]{2,1,0:T(8,128)(2,1)}, u32[]{:S(2)}) copy-start(bf16[8,64,1024]{2,1,0:T(8,128)(2,1)} %param.10) | copy-start | bytes 3145732
  21.5 5.9 %collective-permute-start.4 = (bf16[256,1024]{1,0:T(8,128)(2,1)}, bf16[256,1024]{1,0:T(8,128)(2,1)S(1)}, u32[]{:S(2)}, u32[]{:S(2)}) collective-permute-start(bf16[256,1024]{1,0:T(8,128)(2,1)} %fusion.23), channel_id=1, source_target_pairs={{0,1},{1,0},{2,3},{3,2},{4,5},{5,4},{6,7},{7,6},{8,9},{9,8},{10,11... | collective-permute-start | bytes 1572872 | tf_op jit(solution)/shard_map/ppermute | solution.py:17
  21.7 14.9 %collective-permute-start.3 = (bf16[256,1024]{1,0:T(8,128)(2,1)S(1)}, bf16[256,1024]{1,0:T(8,128)(2,1)S(1)}, u32[]{:S(2)}, u32[]{:S(2)}) collective-permute-start(bf16[256,1024]{1,0:T(8,128)(2,1)S(1)} %add_convert_fusion.3), channel_id=1, source_target_pairs={{0,2},{1,3},{2,0},{3,1},{4,6},{5,7},{6,4},{7,5},{8,10},{9,11},{10,... | collective-permute-start | bytes 1572872 | tf_op jit(solution)/shard_map/ppermute | solution.py:17
  24.9 11.7 %collective-permute-start.2 = (bf16[256,1024]{1,0:T(8,128)(2,1)S(1)}, bf16[256,1024]{1,0:T(8,128)(2,1)S(1)}, u32[]{:S(2)}, u32[]{:S(2)}) collective-permute-start(bf16[256,1024]{1,0:T(8,128)(2,1)S(1)} %fusion.26), channel_id=1, source_target_pairs={{0,1},{1,0},{2,3},{3,2},{4,5},{5,4},{6,7},{7,6},{8,9},{9,8},{10,11... | collective-permute-start | bytes 1572872 | tf_op jit(solution)/shard_map/ppermute | solution.py:17
  30.5 6.6 %copy-start.4 = (f32[1024]{0:T(1024)S(1)}, f32[1024]{0:T(1024)}, u32[]{:S(2)}) copy-start(f32[1024]{0:T(1024)} %param.15) | copy-start | bytes 12292
  30.5 19.7 %collective-permute-start.6 = (bf16[256,1024]{1,0:T(8,128)(2,1)}, bf16[256,1024]{1,0:T(8,128)(2,1)S(1)}, u32[]{:S(2)}, u32[]{:S(2)}) collective-permute-start(bf16[256,1024]{1,0:T(8,128)(2,1)} %add_convert_fusion.2), channel_id=1, source_target_pairs={{0,2},{1,3},{2,0},{3,1},{4,6},{5,7},{6,4},{7,5},{8,10},{9,11},{10,... | collective-permute-start | bytes 1572872 | tf_op jit(solution)/shard_map/ppermute | solution.py:17
  38.2 4.3 %copy-start.5 = (s32[8,64]{1,0:T(8,128)S(1)}, s32[8,64]{1,0:T(8,128)}, u32[]{:S(2)}) copy-start(s32[8,64]{1,0:T(8,128)} %param.19) | copy-start | bytes 6148
  38.8 6.9 %collective-permute-start.7 = (f32[256,65]{0,1:T(8,128)}, f32[256,65]{0,1:T(8,128)S(1)}, u32[]{:S(2)}, u32[]{:S(2)}) collective-permute-start(f32[256,65]{0,1:T(8,128)} %pad_maximum_fusion.2), channel_id=1, source_target_pairs={{0,1},{1,0},{2,3},{3,2},{4,5},{5,4},{6,7},{7,6},{8,9},{9,8},{10,11... | collective-permute-start | bytes 199688 | tf_op jit(solution)/shard_map/ppermute | solution.py:17
  41.9 8.2 %collective-permute-start.5 = (bf16[256,1024]{1,0:T(8,128)(2,1)}, bf16[256,1024]{1,0:T(8,128)(2,1)S(1)}, u32[]{:S(2)}, u32[]{:S(2)}) collective-permute-start(bf16[256,1024]{1,0:T(8,128)(2,1)} %fusion.29), channel_id=1, source_target_pairs={{0,1},{1,0},{2,3},{3,2},{4,5},{5,4},{6,7},{7,6},{8,9},{9,8},{10,11... | collective-permute-start | bytes 1572872 | tf_op jit(solution)/shard_map/ppermute | solution.py:17
  45.7 4.4 %collective-permute-start.8 = (f32[256,65]{0,1:T(8,128)S(1)}, f32[256,65]{0,1:T(8,128)S(1)}, u32[]{:S(2)}, u32[]{:S(2)}) collective-permute-start(f32[256,65]{0,1:T(8,128)S(1)} %fusion.110), channel_id=1, source_target_pairs={{0,2},{1,3},{2,0},{3,1},{4,6},{5,7},{6,4},{7,5},{8,10},{9,11},{10,... | collective-permute-start | bytes 199688 | tf_op jit(solution)/shard_map/ppermute | solution.py:17
  50.2 3.8 %copy-start.7 = (s32[256]{0:T(256)S(1)}, s32[256]{0:T(256)}, u32[]{:S(2)}) copy-start(s32[256]{0:T(256)} %eq.86) | copy-start | bytes 3076
  50.6 7.0 %copy-start.6 = (s32[256]{0:T(256)S(1)}, s32[256]{0:T(256)}, u32[]{:S(2)}) copy-start(s32[256]{0:T(256)} %eq.90) | copy-start | bytes 3076
  51.8 1.4 %collective-permute-start.9 = (f32[256,65]{0,1:T(8,128)S(1)}, f32[256,65]{0,1:T(8,128)S(1)}, u32[]{:S(2)}, u32[]{:S(2)}) collective-permute-start(f32[256,65]{0,1:T(8,128)S(1)} %pad_maximum_fusion.3), channel_id=1, source_target_pairs={{0,1},{1,0},{2,3},{3,2},{4,5},{5,4},{6,7},{7,6},{8,9},{9,8},{10,11... | collective-permute-start | bytes 199688 | tf_op jit(solution)/shard_map/ppermute | solution.py:17
  53.1 4.4 %collective-permute-start.10 = (f32[256,65]{0,1:T(8,128)S(1)}, f32[256,65]{0,1:T(8,128)S(1)}, u32[]{:S(2)}, u32[]{:S(2)}) collective-permute-start(f32[256,65]{0,1:T(8,128)S(1)} %fusion.109), channel_id=1, source_target_pairs={{0,2},{1,3},{2,0},{3,1},{4,6},{5,7},{6,4},{7,5},{8,10},{9,11},{10,... | collective-permute-start | bytes 199688 | tf_op jit(solution)/shard_map/ppermute | solution.py:17
  58.7 5.1 %collective-permute-start.11 = (f32[512,64]{0,1:T(8,128)S(1)}, f32[512,64]{0,1:T(8,128)S(1)}, u32[]{:S(2)}, u32[]{:S(2)}) collective-permute-start(f32[512,64]{0,1:T(8,128)S(1)} %slice_select_fusion), channel_id=1, source_target_pairs={{0,4},{4,0},{8,12},{12,8},{16,20},{20,16},{24,28},{28,24},{32,36},... | collective-permute-start | bytes 393224 | tf_op jit(solution)/shard_map/ppermute | solution.py:17
  63.8 5.6 %collective-permute-start.12 = (f32[256,64]{0,1:T(8,128)S(1)}, f32[256,64]{0,1:T(8,128)S(1)}, u32[]{:S(2)}, u32[]{:S(2)}) collective-permute-start(f32[256,64]{0,1:T(8,128)S(1)} %slice_select_fusion.1), channel_id=1, source_target_pairs={{0,8},{4,12},{8,0},{12,4},{16,24},{20,28},{24,16},{28,20},{32,40},... | collective-permute-start | bytes 196616 | tf_op jit(solution)/shard_map/ppermute | solution.py:17
  69.4 10.2 %collective-permute-start.13 = (f32[256,64]{0,1:T(8,128)S(1)}, f32[256,64]{0,1:T(8,128)S(1)}, u32[]{:S(2)}, u32[]{:S(2)}) collective-permute-start(f32[256,64]{0,1:T(8,128)S(1)} %select_add_fusion.1), channel_id=1, source_target_pairs={{0,16},{4,20},{8,24},{12,28},{16,0},{20,4},{24,8},{28,12},{32,48},... | collective-permute-start | bytes 196616 | tf_op jit(solution)/shard_map/ppermute | solution.py:17
  79.6 5.9 %collective-permute-start.14 = (f32[256,64]{0,1:T(8,128)S(1)}, f32[256,64]{0,1:T(8,128)S(1)}, u32[]{:S(2)}, u32[]{:S(2)}) collective-permute-start(f32[256,64]{0,1:T(8,128)S(1)} %add.139), channel_id=1, source_target_pairs={{0,32},{4,36},{8,40},{12,44},{16,48},{20,52},{24,56},{28,60},{32,0... | collective-permute-start | bytes 196616 | tf_op jit(solution)/shard_map/ppermute | solution.py:17
  85.5 4.4 %collective-permute-start.15 = (f32[256,64]{0,1:T(8,128)S(1)}, f32[256,64]{0,1:T(8,128)S(1)}, u32[]{:S(2)}, u32[]{:S(2)}) collective-permute-start(f32[256,64]{0,1:T(8,128)S(1)} %add.140), channel_id=1, source_target_pairs={{0,64},{4,68},{8,72},{12,76},{16,80},{20,84},{24,88},{28,92},{32,9... | collective-permute-start | bytes 196616 | tf_op jit(solution)/shard_map/ppermute | solution.py:17
  89.8 5.9 %collective-permute-start.16 = (f32[256,64]{0,1:T(8,128)S(1)}, f32[256,64]{0,1:T(8,128)S(1)}, u32[]{:S(2)}, u32[]{:S(2)}) collective-permute-start(f32[256,64]{0,1:T(8,128)S(1)} %add.141), channel_id=1, source_target_pairs={{0,128},{4,132},{8,136},{12,140},{16,144},{20,148},{24,152},{28,15... | collective-permute-start | bytes 196616 | tf_op jit(solution)/shard_map/ppermute | solution.py:17
  95.7 5.6 %collective-permute-start.17 = (f32[256,64]{0,1:T(8,128)S(1)}, f32[256,64]{0,1:T(8,128)S(1)}, u32[]{:S(2)}, u32[]{:S(2)}) collective-permute-start(f32[256,64]{0,1:T(8,128)S(1)} %add.142), channel_id=1, source_target_pairs={{0,8},{4,12},{8,0},{12,4},{16,24},{20,28},{24,16},{28,20},{32,40},... | collective-permute-start | bytes 196616 | tf_op jit(solution)/shard_map/ppermute | solution.py:17
  101.3 5.1 %collective-permute-start.18 = (f32[512,64]{0,1:T(8,128)S(1)}, f32[512,64]{0,1:T(8,128)S(1)}, u32[]{:S(2)}, u32[]{:S(2)}) collective-permute-start(f32[512,64]{0,1:T(8,128)S(1)} %maximum_select_fusion.1), channel_id=1, source_target_pairs={{0,4},{4,0},{8,12},{12,8},{16,20},{20,16},{24,28},{28,24},{32,36},... | collective-permute-start | bytes 393224 | tf_op jit(solution)/shard_map/ppermute | solution.py:17

commit v8 on v7

--- a/solution.py
+++ b/solution.py
@@ -105,16 +105,25 @@
     return mixed_rows.astype(jnp.bfloat16).reshape(prompt_count, seq_length, local_heads, HDIM)
 
 
-def attend_rows(queries, attn_keys, values, pick_values, head_ids, pos_ids):
+def attend_rows(queries, attn_keys, values, head_ids, pos_ids):
     prompt_count = queries.shape[0]
     seq_length = queries.shape[1]
     local_kv = attn_keys.shape[2] // HDIM
     local_heads = queries.shape[2] // HDIM
     group_size = local_heads // local_kv
+    pos_pick = (
+        pos_ids[:, :, None] == jnp.arange(seq_length, dtype=pos_ids.dtype)[None, None, :]
+    ).astype(queries.dtype)
+    head_pick = (
+        head_ids[:, :, None] == jnp.arange(local_heads, dtype=head_ids.dtype)[None, None, :]
+    ).astype(queries.dtype)
+    query_lines = jnp.einsum(
+        "jks,jsf->jkf", pos_pick, queries, preferred_element_type=jnp.float32
+    ).astype(queries.dtype)
     query_rows = jnp.einsum(
-        "jkr,jrd->jkd",
-        pick_values,
-        queries.reshape(prompt_count, seq_length * local_heads, HDIM),
+        "jkh,jkhd->jkd",
+        head_pick,
+        query_lines.reshape(prompt_count, -1, local_heads, HDIM),
         preferred_element_type=jnp.float32,
     ).astype(queries.dtype)
     key_blocks = attn_keys.reshape(prompt_count, seq_length, local_kv, HDIM)
@@ -161,7 +170,7 @@
     picks = entry_rows[:, :, None] == jnp.arange(rows, dtype=jnp.int32)[None, None, :]
     pick_values = picks.astype(jnp.bfloat16)
     own_entries = attend_rows(
-        queries, attn_keys, values, pick_values, patch_list[..., 0] % local_heads, patch_list[..., 1]
+        queries, attn_keys, values, patch_list[..., 0] % local_heads, patch_list[..., 1]
     )
     heads_out = attend(queries, attn_keys, values)
     flat_heads = heads_out.reshape(prompt_count, rows, HDIM)

time: 108 us -> 110 us (1.019)
  matrix products: 29.4 us -> 31.5 us
  other arithmetic: 4.32 us -> 5.62 us
  local copies, waits for them, and re-layouts: 7.11 us -> 5.96 us
    dot_general x8, matrix products: 20.9 us -> 22.6 us  [block(): return jnp.dot(heads, columns, preferred_element_type=jnp.float32)]
    reshape x1 -> x0, local copies, waits for them, and re-layouts: 1.52 us -> none  [attend_rows(): queries.reshape(prompt_count, seq_length * local_heads, HDIM)]
    reduce_sum x2, other arithmetic: 0.79 us -> 2.02 us  [per_device(): square_local = jnp.sum(hidden * hidden, axis=1)]
  transfers between devices with their start and end apart: 19 -> 19, of which waited for: 13 -> 13; matrix products, arithmetic and copies ran while one was open for 23% -> 22% of each run, Pallas kernels for 0% -> 0%
where the time goes in v8:
time: 110 us
  waiting for transfers between devices  37.7 us (34%)
  matrix products  31.5 us (29%)
  starting transfers between devices  27.8 us (25%)
  local copies, waits for them, and re-layouts  5.96 us (5%)
  other arithmetic  5.62 us (5%)
    ppermute x19, waiting for transfers between devices, exchanged(): return lax.ppermute(block, axis, [(i, i ^ bit) for i in range(count)])  37.7 us
    ppermute x19, starting transfers between devices, exchanged(): return lax.ppermute(block, axis, [(i, i ^ bit) for i in range(count)])  27.8 us
    dot_general x8, matrix products, block(): return jnp.dot(heads, columns, preferred_element_type=jnp.float32)  22.6 us
    eq x2, local copies, waits for them, and re-layouts, per_device(): labels[rows_here][:, None] == classes[None, :]  2.71 us
    dot_general x2, matrix products, per_device(): jnp.dot(scaled, probe_weight, precision=lax.Precision.HIGHEST, preferred_...  2.31 us
  transfers between devices with their start and end apart: 19, of which 13 were waited for; matrix products, arithmetic and copies ran while one was open for 22% of the time, Pallas kernels for 0%

profile of v8, /device:TPU:24, one launch (start us, length us, event | category | flops | bytes accessed | tf_op | source)
XLA Modules:
  0.0 109.6 jit_solution(935312312040918422)
XLA Ops:
  0.7 0.8 fusion.118
  1.6 0.3 copy-done
  1.9 0.3 convolution_convert_fusion.2
  2.3 0.3 fusion.58
  2.6 0.2 fusion.36
  2.7 0.2 fusion.121
  2.9 0.3 fusion.37
  3.2 3.1 %collective-permute-start = (bf16[8,16,128]{2,1,0:T(8,128)(2,1)S(1)}, bf16[8,16,128]{2,1,0:T(8,128)(2,1)S(1)}, u32[]{:S(2)}, u32[]{:S(2)}) collective-permute-start(bf16[8,16,128]{2,1,0:T(8,128)(2,1)S(1)} %fusion.37), channel_id=1, source_target_pairs={{0,128},{4,132},{8,136},{12,140},{16,144},{20,148},{24,152},{28,15... | collective-permute-start | bytes 98312 | tf_op jit(solution)/shard_map/ppermute | solution.py:17
  6.3 1.1 %fusion.120 = (f32[8,8,64]{2,1,0:T(8,128)S(1)}, f32[8,1,8,64,64]{3,4,2,0,1:T(8,128)S(1)}) fusion(bf16[8,64,128]{2,1,0:T(8,128)(2,1)S(1)} %copy-done.3, pred[64,64]{0,1:T(8,128)(4,1)S(1)} %iota_compare_fusion.10, bf16[8,64,1024]{2,1,0:T(8,128)(2,1)S(1)} %copy-done), kind=kOutput, calls=%fused_computation.154 | convolution fusion | flops 67891200 | bytes 2248704 | tf_op jit(solution)/shard_map/pqkgd,pskd->pkgqs/dot_general | solution.py:94
  7.5 0.5 fusion.1
  8.0 0.6 fusion.19
  8.7 0.1 fusion.60
  8.8 0.2 fusion.78
  9.0 1.6 %fusion.18 = bf16[8,512,128]{2,1,0:T(8,128)(2,1)S(1)} fusion(bf16[8,64,1,8,128]{4,1,3,0,2:T(8,128)(2,1)S(1)} %fusion.19, pred[8,512]{1,0:T(8,128)(4,1)S(1)} %fusion.60, s32[8,16]{1,0:T(8,128)S(1)} %get-tuple-element.31, bf16[8,16,128]{2,0,1:T(8,128)(2,1)S(1)} %fusion.78), kind=kOutput, calls=%fused_computation.23 | convolution fusion | flops 17891328 | bytes 2134528 | tf_op jit(solution)/shard_map/jkr,jkd->jrd/dot_general | solution.py:186
  10.7 0.2 slice.63
  10.9 3.1 %fusion.20 = bf16[256,1024]{1,0:T(8,128)(2,1)} fusion(bf16[256,1024]{1,0:T(8,128)(2,1)S(1)} %slice.63, bf16[1024,4096]{1,0:T(8,128)(2,1)} %param.14, s32[]{:T(128)S(6)} %select_n.105), kind=kOutput, calls=%fused_computation.25 | convolution fusion | flops 537133056 | bytes 3145732 | tf_op jit(solution)/shard_map/dot_general | solution.py:53
  14.0 0.2 slice.65
  14.3 1.9 %collective-permute-done.1 = bf16[256,1024]{1,0:T(8,128)(2,1)S(1)} collective-permute-done((bf16[256,1024]{1,0:T(8,128)(2,1)}, bf16[256,1024]{1,0:T(8,128)(2,1)S(1)}, u32[]{:S(2)}, u32[]{:S(2)}) %collective-permute-start.1) | collective-permute-done | bytes 524320 | tf_op jit(solution)/shard_map/ppermute | solution.py:17
  16.1 3.1 %add_convert_fusion.3 = bf16[256,1024]{1,0:T(8,128)(2,1)} fusion(bf16[256,1024]{1,0:T(8,128)(2,1)S(1)} %collective-permute-done.1, bf16[256,1024]{1,0:T(8,128)(2,1)S(1)} %slice.63, bf16[1024,4096]{1,0:T(8,128)(2,1)} %param.14, s32[]{:T(128)S(6)} %select_n.104), kind=kOutput, calls=%fused_computation.53 | convolution fusion | flops 537657344 | bytes 3670020 | tf_op jit(solution)/shard_map/dot_general | solution.py:53
  19.2 3.2 %fusion.23 = bf16[256,1024]{1,0:T(8,128)(2,1)} fusion(bf16[256,1024]{1,0:T(8,128)(2,1)S(1)} %slice.65, bf16[1024,4096]{1,0:T(8,128)(2,1)} %param.14, s32[]{:T(128)S(6)} %select_n.105), kind=kOutput, calls=%fused_computation.26 | convolution fusion | flops 537133056 | bytes 3145732 | tf_op jit(solution)/shard_map/dot_general | solution.py:53
  22.4 0.1 collective-permute-start.4
  22.7 0.8 collective-permute-start.3
  23.5 2.3 %fusion.26 = bf16[256,1024]{1,0:T(8,128)(2,1)S(1)} fusion(bf16[256,1024]{1,0:T(8,128)(2,1)S(1)} %slice.63, bf16[1024,4096]{1,0:T(8,128)(2,1)} %param.14, s32[]{:T(128)S(6)} %select_n.107), kind=kOutput, calls=%fused_computation.27 | convolution fusion | flops 537133056 | bytes 3145732 | tf_op jit(solution)/shard_map/dot_general | solution.py:72
  25.8 0.2 collective-permute-start.2
  26.0 2.3 %fusion.8 = f32[256,1024]{1,0:T(8,128)S(1)} fusion(bf16[256,1024]{1,0:T(8,128)(2,1)S(1)} %slice.63, bf16[1024,4096]{1,0:T(8,128)(2,1)} %param.14, s32[]{:T(128)S(6)} %select_n.106), kind=kOutput, calls=%fused_computation.11 | convolution fusion | flops 536870912 | bytes 3670020 | tf_op jit(solution)/shard_map/dot_general | solution.py:72
  28.3 3.2 %add_convert_fusion.2 = bf16[256,1024]{1,0:T(8,128)(2,1)} fusion(bf16[256,1024]{1,0:T(8,128)(2,1)} %collective-permute-done.4, bf16[256,1024]{1,0:T(8,128)(2,1)S(1)} %slice.65, bf16[1024,4096]{1,0:T(8,128)(2,1)} %param.14, s32[]{:T(128)S(6)} %select_n.104), kind=kOutput, calls=%fused_computation.52 | convolution fusion | flops 537657344 | bytes 3670020 | tf_op jit(solution)/shard_map/dot_general | solution.py:53
  31.5 1.3 %collective-permute-start.6 = (bf16[256,1024]{1,0:T(8,128)(2,1)}, bf16[256,1024]{1,0:T(8,128)(2,1)}, u32[]{:S(2)}, u32[]{:S(2)}) collective-permute-start(bf16[256,1024]{1,0:T(8,128)(2,1)} %add_convert_fusion.2), channel_id=1, source_target_pairs={{0,2},{1,3},{2,0},{3,1},{4,6},{5,7},{6,4},{7,5},{8,10},{9,11},{10,... | collective-permute-start | bytes 1572872 | tf_op jit(solution)/shard_map/ppermute | solution.py:17
  32.8 5.0 %collective-permute-done.3 = bf16[256,1024]{1,0:T(8,128)(2,1)S(1)} collective-permute-done((bf16[256,1024]{1,0:T(8,128)(2,1)}, bf16[256,1024]{1,0:T(8,128)(2,1)S(1)}, u32[]{:S(2)}, u32[]{:S(2)}) %collective-permute-start.3) | collective-permute-done | bytes 524320 | tf_op jit(solution)/shard_map/ppermute | solution.py:17
  37.8 0.4 multiply_reduce_fusion.1
  38.2 1.2 %fusion.50 = f32[256,64]{0,1:T(8,128)S(1)} fusion(f32[1024,64]{0,1:T(8,128)S(1)} %copy-done.2, bf16[256,1024]{1,0:T(8,128)(2,1)S(1)} %get-tuple-element.19, bf16[256,1024]{1,0:T(8,128)(2,1)S(1)} %bitcast.90, f32[1024]{0:T(1024)S(1)} %copy-done.4), kind=kOutput, calls=%fused_computation.57 | convolution fusion | flops 202375168 | bytes 1380352 | tf_op jit(solution)/shard_map/dot_general | solution.py:216
  39.4 0.6 pad_maximum_fusion.2
  40.0 3.1 %fusion.29 = bf16[256,1024]{1,0:T(8,128)(2,1)} fusion(bf16[256,1024]{1,0:T(8,128)(2,1)S(1)} %slice.65, bf16[1024,4096]{1,0:T(8,128)(2,1)} %param.14, s32[]{:T(128)S(6)} %select_n.107), kind=kOutput, calls=%fused_computation.28 | convolution fusion | flops 537133056 | bytes 3145732 | tf_op jit(solution)/shard_map/dot_general | solution.py:72
  43.1 0.5 collective-permute-start.5
  43.6 0.6 fusion.119
  44.2 1.4 %eq.115 = s32[256]{0:T(256)} reshape(s32[4,64]{1,0:T(4,128)} %get-tuple-element.29) | data formatting | bytes 2048 | tf_op jit(solution)/shard_map/eq | solution.py:225
  45.6 1.4 %eq.119 = s32[256]{0:T(256)} reshape(s32[4,64]{1,0:T(4,128)} %get-tuple-element.28) | data formatting | bytes 2048 | tf_op jit(solution)/shard_map/eq | solution.py:225
  47.0 0.8 collective-permute-start.8
  47.8 2.3 %fusion.6 = f32[256,1024]{1,0:T(8,128)S(1)} fusion(bf16[256,1024]{1,0:T(8,128)(2,1)S(1)} %slice.65, bf16[1024,4096]{1,0:T(8,128)(2,1)} %param.14, s32[]{:T(128)S(6)} %select_n.106), kind=kOutput, calls=%fused_computation.9 | convolution fusion | flops 536870912 | bytes 3670020 | tf_op jit(solution)/shard_map/dot_general | solution.py:72
  50.1 1.3 %collective-permute-done.8 = f32[256,65]{0,1:T(8,128)S(1)} collective-permute-done((f32[256,65]{0,1:T(8,128)S(1)}, f32[256,65]{0,1:T(8,128)S(1)}, u32[]{:S(2)}, u32[]{:S(2)}) %collective-permute-start.8) | collective-permute-done | bytes 66592 | tf_op jit(solution)/shard_map/ppermute | solution.py:17
  51.5 1.6 %multiply_reduce_fusion = (f32[256]{0:T(256)S(1)}, bf16[256,1024]{1,0:T(8,128)(2,1)S(1)}) fusion(bf16[4,64,1024]{2,1,0:T(8,128)(2,1)S(1)} %get-tuple-element.23, bf16[256,1024]{1,0:T(8,128)(2,1)} %collective-permute-done.6, f32[256,1024]{1,0:T(8,128)S(1)} %fusion.6, bf16[256,1024]{1,0:T(8,128)(2,1)} %collective-permute-done.5), kind=kLoop, calls=%fused_computation.48 | loop fusion | flops 2621184 | bytes 3146752 | tf_op jit(solution)/shard_map/reduce_sum | solution.py:214
  53.1 1.2 %fusion.47 = f32[256,64]{0,1:T(8,128)S(1)} fusion(f32[1024,64]{0,1:T(8,128)S(1)} %copy-done.2, bf16[256,1024]{1,0:T(8,128)(2,1)S(1)} %get-tuple-element.21, bf16[256,1024]{1,0:T(8,128)(2,1)S(1)} %bitcast.88, f32[1024]{0:T(1024)S(1)} %copy-done.4), kind=kOutput, calls=%fused_computation.56 | convolution fusion | flops 202375168 | bytes 1380352 | tf_op jit(solution)/shard_map/dot_general | solution.py:216
  54.4 1.2 %collective-permute-done.9 = f32[256,65]{0,1:T(8,128)S(1)} collective-permute-done((f32[256,65]{0,1:T(8,128)S(1)}, f32[256,65]{0,1:T(8,128)S(1)}, u32[]{:S(2)}, u32[]{:S(2)}) %collective-permute-start.9) | collective-permute-done | bytes 66592 | tf_op jit(solution)/shard_map/ppermute | solution.py:17
  55.6 0.8 collective-permute-start.10
  56.5 1.0 fusion.42
  57.5 2.6 %collective-permute-done.10 = f32[256,65]{0,1:T(8,128)S(1)} collective-permute-done((f32[256,65]{0,1:T(8,128)S(1)}, f32[256,65]{0,1:T(8,128)S(1)}, u32[]{:S(2)}, u32[]{:S(2)}) %collective-permute-start.10) | collective-permute-done | bytes 66592 | tf_op jit(solution)/shard_map/ppermute | solution.py:17
  60.1 1.0 fusion.32
  61.1 2.0 %collective-permute-start.11 = (f32[512,64]{0,1:T(8,128)S(1)}, f32[512,64]{0,1:T(8,128)S(1)}, u32[]{:S(2)}, u32[]{:S(2)}) collective-permute-start(f32[512,64]{0,1:T(8,128)S(1)} %slice_select_fusion), channel_id=1, source_target_pairs={{0,4},{4,0},{8,12},{12,8},{16,20},{20,16},{24,28},{28,24},{32,36},... | collective-permute-start | bytes 393224 | tf_op jit(solution)/shard_map/ppermute | solution.py:17
  63.2 3.0 %collective-permute-done.11 = f32[512,64]{0,1:T(8,128)S(1)} collective-permute-done((f32[512,64]{0,1:T(8,128)S(1)}, f32[512,64]{0,1:T(8,128)S(1)}, u32[]{:S(2)}, u32[]{:S(2)}) %collective-permute-start.11) | collective-permute-done | bytes 131104 | tf_op jit(solution)/shard_map/ppermute | solution.py:17
  66.2 3.4 %collective-permute-start.12 = (f32[256,64]{0,1:T(8,128)S(1)}, f32[256,64]{0,1:T(8,128)S(1)}, u32[]{:S(2)}, u32[]{:S(2)}) collective-permute-start(f32[256,64]{0,1:T(8,128)S(1)} %slice_select_fusion.1), channel_id=1, source_target_pairs={{0,8},{4,12},{8,0},{12,4},{16,24},{20,28},{24,16},{28,20},{32,40},... | collective-permute-start | bytes 196616 | tf_op jit(solution)/shard_map/ppermute | solution.py:17
  69.6 2.2 %collective-permute-done.12 = f32[256,64]{0,1:T(8,128)S(1)} collective-permute-done((f32[256,64]{0,1:T(8,128)S(1)}, f32[256,64]{0,1:T(8,128)S(1)}, u32[]{:S(2)}, u32[]{:S(2)}) %collective-permute-start.12) | collective-permute-done | bytes 65568 | tf_op jit(solution)/shard_map/ppermute | solution.py:17
  71.9 7.6 %collective-permute-start.13 = (f32[256,64]{0,1:T(8,128)S(1)}, f32[256,64]{0,1:T(8,128)S(1)}, u32[]{:S(2)}, u32[]{:S(2)}) collective-permute-start(f32[256,64]{0,1:T(8,128)S(1)} %select_add_fusion.1), channel_id=1, source_target_pairs={{0,16},{4,20},{8,24},{12,28},{16,0},{20,4},{24,8},{28,12},{32,48},... | collective-permute-start | bytes 196616 | tf_op jit(solution)/shard_map/ppermute | solution.py:17
  79.5 2.5 %collective-permute-done.13 = f32[256,64]{0,1:T(8,128)S(1)} collective-permute-done((f32[256,64]{0,1:T(8,128)S(1)}, f32[256,64]{0,1:T(8,128)S(1)}, u32[]{:S(2)}, u32[]{:S(2)}) %collective-permute-start.13) | collective-permute-done | bytes 65568 | tf_op jit(solution)/shard_map/ppermute | solution.py:17
  82.1 1.3 %collective-permute-start.14 = (f32[256,64]{0,1:T(8,128)S(1)}, f32[256,64]{0,1:T(8,128)S(1)}, u32[]{:S(2)}, u32[]{:S(2)}) collective-permute-start(f32[256,64]{0,1:T(8,128)S(1)} %add.140), channel_id=1, source_target_pairs={{0,32},{4,36},{8,40},{12,44},{16,48},{20,52},{24,56},{28,60},{32,0... | collective-permute-start | bytes 196616 | tf_op jit(solution)/shard_map/ppermute | solution.py:17
  83.4 4.5 %collective-permute-done.14 = f32[256,64]{0,1:T(8,128)S(1)} collective-permute-done((f32[256,64]{0,1:T(8,128)S(1)}, f32[256,64]{0,1:T(8,128)S(1)}, u32[]{:S(2)}, u32[]{:S(2)}) %collective-permute-start.14) | collective-permute-done | bytes 65568 | tf_op jit(solution)/shard_map/ppermute | solution.py:17
  87.9 1.5 %collective-permute-start.15 = (f32[256,64]{0,1:T(8,128)S(1)}, f32[256,64]{0,1:T(8,128)S(1)}, u32[]{:S(2)}, u32[]{:S(2)}) collective-permute-start(f32[256,64]{0,1:T(8,128)S(1)} %add.141), channel_id=1, source_target_pairs={{0,64},{4,68},{8,72},{12,76},{16,80},{20,84},{24,88},{28,92},{32,9... | collective-permute-start | bytes 196616 | tf_op jit(solution)/shard_map/ppermute | solution.py:17
  89.4 2.9 %collective-permute-done.15 = f32[256,64]{0,1:T(8,128)S(1)} collective-permute-done((f32[256,64]{0,1:T(8,128)S(1)}, f32[256,64]{0,1:T(8,128)S(1)}, u32[]{:S(2)}, u32[]{:S(2)}) %collective-permute-start.15) | collective-permute-done | bytes 65568 | tf_op jit(solution)/shard_map/ppermute | solution.py:17
  92.3 3.0 %collective-permute-start.16 = (f32[256,64]{0,1:T(8,128)S(1)}, f32[256,64]{0,1:T(8,128)S(1)}, u32[]{:S(2)}, u32[]{:S(2)}) collective-permute-start(f32[256,64]{0,1:T(8,128)S(1)} %add.142), channel_id=1, source_target_pairs={{0,128},{4,132},{8,136},{12,140},{16,144},{20,148},{24,152},{28,15... | collective-permute-start | bytes 196616 | tf_op jit(solution)/shard_map/ppermute | solution.py:17
  95.3 2.9 %collective-permute-done.16 = f32[256,64]{0,1:T(8,128)S(1)} collective-permute-done((f32[256,64]{0,1:T(8,128)S(1)}, f32[256,64]{0,1:T(8,128)S(1)}, u32[]{:S(2)}, u32[]{:S(2)}) %collective-permute-start.16) | collective-permute-done | bytes 65568 | tf_op jit(solution)/shard_map/ppermute | solution.py:17
  98.2 1.1 %collective-permute-start.17 = (f32[256,64]{0,1:T(8,128)S(1)}, f32[256,64]{0,1:T(8,128)S(1)}, u32[]{:S(2)}, u32[]{:S(2)}) collective-permute-start(f32[256,64]{0,1:T(8,128)S(1)} %add.143), channel_id=1, source_target_pairs={{0,8},{4,12},{8,0},{12,4},{16,24},{20,28},{24,16},{28,20},{32,40},... | collective-permute-start | bytes 196616 | tf_op jit(solution)/shard_map/ppermute | solution.py:17
  99.3 1.0 pad_maximum_fusion
  100.3 3.5 %collective-permute-done.17 = f32[256,64]{0,1:T(8,128)S(1)} collective-permute-done((f32[256,64]{0,1:T(8,128)S(1)}, f32[256,64]{0,1:T(8,128)S(1)}, u32[]{:S(2)}, u32[]{:S(2)}) %collective-permute-start.17) | collective-permute-done | bytes 65568 | tf_op jit(solution)/shard_map/ppermute | solution.py:17
  104.0 0.8 copy.26
  104.8 4.1 %collective-permute-done.18 = f32[512,64]{0,1:T(8,128)S(1)} collective-permute-done((f32[512,64]{0,1:T(8,128)S(1)}, f32[512,64]{0,1:T(8,128)S(1)}, u32[]{:S(2)}, u32[]{:S(2)}) %collective-permute-start.18) | collective-permute-done | bytes 131104 | tf_op jit(solution)/shard_map/ppermute | solution.py:17
  108.9 0.7 maximum_select_fusion
  (55 shorter events, 0.8 us)
Async XLA Ops:
  0.6 1.3 %copy-start = (bf16[8,64,1024]{2,1,0:T(8,128)(2,1)S(1)}, bf16[8,64,1024]{2,1,0:T(8,128)(2,1)}, u32[]{:S(2)}) copy-start(bf16[8,64,1024]{2,1,0:T(8,128)(2,1)} %param.11) | copy-start | bytes 3145732
  0.6 1.9 %copy-start.3 = (bf16[8,64,128]{2,1,0:T(8,128)(2,1)S(1)}, bf16[8,64,128]{2,1,0:T(8,128)(2,1)}, u32[]{:S(2)}) copy-start(bf16[8,64,128]{2,1,0:T(8,128)(2,1)} %param.12) | copy-start | bytes 393220
  0.7 2.3 %copy-start.9 = (bf16[8,64,128]{2,1,0:T(8,128)(2,1)S(1)}, bf16[8,64,128]{2,1,0:T(8,128)(2,1)}, u32[]{:S(2)}) copy-start(bf16[8,64,128]{2,1,0:T(8,128)(2,1)} %param.13) | copy-start | bytes 393220
  3.2 5.6 %collective-permute-start = (bf16[8,16,128]{2,1,0:T(8,128)(2,1)S(1)}, bf16[8,16,128]{2,1,0:T(8,128)(2,1)S(1)}, u32[]{:S(2)}, u32[]{:S(2)}) collective-permute-start(bf16[8,16,128]{2,1,0:T(8,128)(2,1)S(1)} %fusion.37), channel_id=1, source_target_pairs={{0,128},{4,132},{8,136},{12,140},{16,144},{20,148},{24,152},{28,15... | collective-permute-start | bytes 98312 | tf_op jit(solution)/shard_map/ppermute | solution.py:17
  8.0 0.8 copy-start.8
  14.0 2.1 %collective-permute-start.1 = (bf16[256,1024]{1,0:T(8,128)(2,1)}, bf16[256,1024]{1,0:T(8,128)(2,1)S(1)}, u32[]{:S(2)}, u32[]{:S(2)}) collective-permute-start(bf16[256,1024]{1,0:T(8,128)(2,1)} %fusion.20), channel_id=1, source_target_pairs={{0,1},{1,0},{2,3},{3,2},{4,5},{5,4},{6,7},{7,6},{8,9},{9,8},{10,11... | collective-permute-start | bytes 1572872 | tf_op jit(solution)/shard_map/ppermute | solution.py:17
  19.2 3.3 %copy-start.1 = (bf16[8,64,1024]{2,1,0:T(8,128)(2,1)S(1)}, bf16[8,64,1024]{2,1,0:T(8,128)(2,1)}, u32[]{:S(2)}) copy-start(bf16[8,64,1024]{2,1,0:T(8,128)(2,1)} %param.10) | copy-start | bytes 3145732
  22.4 5.9 %collective-permute-start.4 = (bf16[256,1024]{1,0:T(8,128)(2,1)}, bf16[256,1024]{1,0:T(8,128)(2,1)}, u32[]{:S(2)}, u32[]{:S(2)}) collective-permute-start(bf16[256,1024]{1,0:T(8,128)(2,1)} %fusion.23), channel_id=1, source_target_pairs={{0,1},{1,0},{2,3},{3,2},{4,5},{5,4},{6,7},{7,6},{8,9},{9,8},{10,11... | collective-permute-start | bytes 1572872 | tf_op jit(solution)/shard_map/ppermute | solution.py:17
  22.7 15.1 %collective-permute-start.3 = (bf16[256,1024]{1,0:T(8,128)(2,1)}, bf16[256,1024]{1,0:T(8,128)(2,1)S(1)}, u32[]{:S(2)}, u32[]{:S(2)}) collective-permute-start(bf16[256,1024]{1,0:T(8,128)(2,1)} %add_convert_fusion.3), channel_id=1, source_target_pairs={{0,2},{1,3},{2,0},{3,1},{4,6},{5,7},{6,4},{7,5},{8,10},{9,11},{10,... | collective-permute-start | bytes 1572872 | tf_op jit(solution)/shard_map/ppermute | solution.py:17
  25.8 12.0 %collective-permute-start.2 = (bf16[256,1024]{1,0:T(8,128)(2,1)S(1)}, bf16[256,1024]{1,0:T(8,128)(2,1)S(1)}, u32[]{:S(2)}, u32[]{:S(2)}) collective-permute-start(bf16[256,1024]{1,0:T(8,128)(2,1)S(1)} %fusion.26), channel_id=1, source_target_pairs={{0,1},{1,0},{2,3},{3,2},{4,5},{5,4},{6,7},{7,6},{8,9},{9,8},{10,11... | collective-permute-start | bytes 1572872 | tf_op jit(solution)/shard_map/ppermute | solution.py:17
  31.5 6.7 %copy-start.2 = (f32[1024,64]{0,1:T(8,128)S(1)}, f32[1024,64]{0,1:T(8,128)}, u32[]{:S(2)}) copy-start(f32[1024,64]{0,1:T(8,128)} %param.16) | copy-start | bytes 786436
  31.5 6.7 %copy-start.4 = (f32[1024]{0:T(1024)S(1)}, f32[1024]{0:T(1024)}, u32[]{:S(2)}) copy-start(f32[1024]{0:T(1024)} %param.15) | copy-start | bytes 12292
  31.5 19.9 %collective-permute-start.6 = (bf16[256,1024]{1,0:T(8,128)(2,1)}, bf16[256,1024]{1,0:T(8,128)(2,1)}, u32[]{:S(2)}, u32[]{:S(2)}) collective-permute-start(bf16[256,1024]{1,0:T(8,128)(2,1)} %add_convert_fusion.2), channel_id=1, source_target_pairs={{0,2},{1,3},{2,0},{3,1},{4,6},{5,7},{6,4},{7,5},{8,10},{9,11},{10,... | collective-permute-start | bytes 1572872 | tf_op jit(solution)/shard_map/ppermute | solution.py:17
  39.4 4.3 %copy-start.5 = (s32[8,64]{1,0:T(8,128)S(1)}, s32[8,64]{1,0:T(8,128)}, u32[]{:S(2)}) copy-start(s32[8,64]{1,0:T(8,128)} %param.19) | copy-start | bytes 6148
  40.0 7.0 %collective-permute-start.7 = (f32[256,65]{0,1:T(8,128)}, f32[256,65]{0,1:T(8,128)S(1)}, u32[]{:S(2)}, u32[]{:S(2)}) collective-permute-start(f32[256,65]{0,1:T(8,128)} %pad_maximum_fusion.2), channel_id=1, source_target_pairs={{0,1},{1,0},{2,3},{3,2},{4,5},{5,4},{6,7},{7,6},{8,9},{9,8},{10,11... | collective-permute-start | bytes 199688 | tf_op jit(solution)/shard_map/ppermute | solution.py:17
  43.1 8.3 %collective-permute-start.5 = (bf16[256,1024]{1,0:T(8,128)(2,1)}, bf16[256,1024]{1,0:T(8,128)(2,1)}, u32[]{:S(2)}, u32[]{:S(2)}) collective-permute-start(bf16[256,1024]{1,0:T(8,128)(2,1)} %fusion.29), channel_id=1, source_target_pairs={{0,1},{1,0},{2,3},{3,2},{4,5},{5,4},{6,7},{7,6},{8,9},{9,8},{10,11... | collective-permute-start | bytes 1572872 | tf_op jit(solution)/shard_map/ppermute | solution.py:17
  47.0 4.4 %collective-permute-start.8 = (f32[256,65]{0,1:T(8,128)S(1)}, f32[256,65]{0,1:T(8,128)S(1)}, u32[]{:S(2)}, u32[]{:S(2)}) collective-permute-start(f32[256,65]{0,1:T(8,128)S(1)} %fusion.115), channel_id=1, source_target_pairs={{0,2},{1,3},{2,0},{3,1},{4,6},{5,7},{6,4},{7,5},{8,10},{9,11},{10,... | collective-permute-start | bytes 199688 | tf_op jit(solution)/shard_map/ppermute | solution.py:17
  51.4 5.0 %copy-start.7 = (s32[256]{0:T(256)S(1)}, s32[256]{0:T(256)}, u32[]{:S(2)}) copy-start(s32[256]{0:T(256)} %eq.115) | copy-start | bytes 3076
  53.1 7.0 %copy-start.6 = (s32[256]{0:T(256)S(1)}, s32[256]{0:T(256)}, u32[]{:S(2)}) copy-start(s32[256]{0:T(256)} %eq.119) | copy-start | bytes 3076
  54.3 1.4 %collective-permute-start.9 = (f32[256,65]{0,1:T(8,128)S(1)}, f32[256,65]{0,1:T(8,128)S(1)}, u32[]{:S(2)}, u32[]{:S(2)}) collective-permute-start(f32[256,65]{0,1:T(8,128)S(1)} %pad_maximum_fusion.3), channel_id=1, source_target_pairs={{0,1},{1,0},{2,3},{3,2},{4,5},{5,4},{6,7},{7,6},{8,9},{9,8},{10,11... | collective-permute-start | bytes 199688 | tf_op jit(solution)/shard_map/ppermute | solution.py:17
  55.6 4.4 %collective-permute-start.10 = (f32[256,65]{0,1:T(8,128)S(1)}, f32[256,65]{0,1:T(8,128)S(1)}, u32[]{:S(2)}, u32[]{:S(2)}) collective-permute-start(f32[256,65]{0,1:T(8,128)S(1)} %fusion.114), channel_id=1, source_target_pairs={{0,2},{1,3},{2,0},{3,1},{4,6},{5,7},{6,4},{7,5},{8,10},{9,11},{10,... | collective-permute-start | bytes 199688 | tf_op jit(solution)/shard_map/ppermute | solution.py:17
  61.1 5.1 %collective-permute-start.11 = (f32[512,64]{0,1:T(8,128)S(1)}, f32[512,64]{0,1:T(8,128)S(1)}, u32[]{:S(2)}, u32[]{:S(2)}) collective-permute-start(f32[512,64]{0,1:T(8,128)S(1)} %slice_select_fusion), channel_id=1, source_target_pairs={{0,4},{4,0},{8,12},{12,8},{16,20},{20,16},{24,28},{28,24},{32,36},... | collective-permute-start | bytes 393224 | tf_op jit(solution)/shard_map/ppermute | solution.py:17
  66.2 5.6 %collective-permute-start.12 = (f32[256,64]{0,1:T(8,128)S(1)}, f32[256,64]{0,1:T(8,128)S(1)}, u32[]{:S(2)}, u32[]{:S(2)}) collective-permute-start(f32[256,64]{0,1:T(8,128)S(1)} %slice_select_fusion.1), channel_id=1, source_target_pairs={{0,8},{4,12},{8,0},{12,4},{16,24},{20,28},{24,16},{28,20},{32,40},... | collective-permute-start | bytes 196616 | tf_op jit(solution)/shard_map/ppermute | solution.py:17
  71.9 10.2 %collective-permute-start.13 = (f32[256,64]{0,1:T(8,128)S(1)}, f32[256,64]{0,1:T(8,128)S(1)}, u32[]{:S(2)}, u32[]{:S(2)}) collective-permute-start(f32[256,64]{0,1:T(8,128)S(1)} %select_add_fusion.1), channel_id=1, source_target_pairs={{0,16},{4,20},{8,24},{12,28},{16,0},{20,4},{24,8},{28,12},{32,48},... | collective-permute-start | bytes 196616 | tf_op jit(solution)/shard_map/ppermute | solution.py:17
  82.1 5.9 %collective-permute-start.14 = (f32[256,64]{0,1:T(8,128)S(1)}, f32[256,64]{0,1:T(8,128)S(1)}, u32[]{:S(2)}, u32[]{:S(2)}) collective-permute-start(f32[256,64]{0,1:T(8,128)S(1)} %add.140), channel_id=1, source_target_pairs={{0,32},{4,36},{8,40},{12,44},{16,48},{20,52},{24,56},{28,60},{32,0... | collective-permute-start | bytes 196616 | tf_op jit(solution)/shard_map/ppermute | solution.py:17
  87.9 4.4 %collective-permute-start.15 = (f32[256,64]{0,1:T(8,128)S(1)}, f32[256,64]{0,1:T(8,128)S(1)}, u32[]{:S(2)}, u32[]{:S(2)}) collective-permute-start(f32[256,64]{0,1:T(8,128)S(1)} %add.141), channel_id=1, source_target_pairs={{0,64},{4,68},{8,72},{12,76},{16,80},{20,84},{24,88},{28,92},{32,9... | collective-permute-start | bytes 196616 | tf_op jit(solution)/shard_map/ppermute | solution.py:17
  92.3 5.9 %collective-permute-start.16 = (f32[256,64]{0,1:T(8,128)S(1)}, f32[256,64]{0,1:T(8,128)S(1)}, u32[]{:S(2)}, u32[]{:S(2)}) collective-permute-start(f32[256,64]{0,1:T(8,128)S(1)} %add.142), channel_id=1, source_target_pairs={{0,128},{4,132},{8,136},{12,140},{16,144},{20,148},{24,152},{28,15... | collective-permute-start | bytes 196616 | tf_op jit(solution)/shard_map/ppermute | solution.py:17
  98.2 5.6 %collective-permute-start.17 = (f32[256,64]{0,1:T(8,128)S(1)}, f32[256,64]{0,1:T(8,128)S(1)}, u32[]{:S(2)}, u32[]{:S(2)}) collective-permute-start(f32[256,64]{0,1:T(8,128)S(1)} %add.143), channel_id=1, source_target_pairs={{0,8},{4,12},{8,0},{12,4},{16,24},{20,28},{24,16},{28,20},{32,40},... | collective-permute-start | bytes 196616 | tf_op jit(solution)/shard_map/ppermute | solution.py:17
  103.8 5.1 %collective-permute-start.18 = (f32[512,64]{0,1:T(8,128)S(1)}, f32[512,64]{0,1:T(8,128)S(1)}, u32[]{:S(2)}, u32[]{:S(2)}) collective-permute-start(f32[512,64]{0,1:T(8,128)S(1)} %maximum_select_fusion.1), channel_id=1, source_target_pairs={{0,4},{4,0},{8,12},{12,8},{16,20},{20,16},{24,28},{28,24},{32,36},... | collective-permute-start | bytes 393224 | tf_op jit(solution)/shard_map/ppermute | solution.py:17

commit v9 on v7

--- a/solution.py
+++ b/solution.py
@@ -56,10 +56,11 @@
         return exchanged(value.astype(jnp.bfloat16), axis, bit).astype(jnp.float32)
 
     far = position ^ 2
-    from_partner = sent(block(far ^ 1), 1)
+    partner_share = block(far ^ 1).astype(jnp.bfloat16)
+    from_partner = exchanged(partner_share, axis, 1).astype(jnp.float32)
     far_sum = (block(far) + from_partner).astype(jnp.bfloat16)
     heads, far_sum = lax.optimization_barrier((heads, far_sum))
-    return heads, far_sum, exchanged(far_sum, axis, 2)
+    return heads, partner_share, exchanged(far_sum, axis, 2)
 
 
 def near_half(heads, weight, axis, from_far):

time: 108 us -> 105 us (0.972)
  local copies, waits for them, and re-layouts: 7.11 us -> 4.03 us
  waiting for transfers between devices: 37.4 us -> 39.7 us
  matrix products: 29.4 us -> 28 us
    eq x2, local copies, waits for them, and re-layouts: 2.66 us -> 0.16 us  [per_device(): labels[rows_here][:, None] == classes[None, :]]
    ppermute x19, waiting for transfers between devices: 37.4 us -> 39.7 us  [exchanged(): return lax.ppermute(block, axis, [(i, i ^ bit) for i in range(count)])]
    dot_general x8, matrix products: 20.9 us -> 19.5 us  [block(): return jnp.dot(heads, columns, preferred_element_type=jnp.float32)]
where the time goes in v9:
time: 105 us
  waiting for transfers between devices  39.7 us (38%)
  starting transfers between devices  28.4 us (27%)
  matrix products  28 us (27%)
  local copies, waits for them, and re-layouts  4.03 us (4%)
  other arithmetic  3.69 us (4%)
  between operations  1.08 us (1%)
    ppermute x19, waiting for transfers between devices, exchanged(): return lax.ppermute(block, axis, [(i, i ^ bit) for i in range(count)])  39.7 us
    ppermute x19, starting transfers between devices, exchanged(): return lax.ppermute(block, axis, [(i, i ^ bit) for i in range(count)])  28.4 us
    dot_general x8, matrix products, block(): return jnp.dot(heads, columns, preferred_element_type=jnp.float32)  19.5 us
    dot_general x2, matrix products, per_device(): jnp.dot(scaled, probe_weight, precision=lax.Precision.HIGHEST, preferred_...  2.31 us
  transfers between devices with their start and end apart: 19, of which 13 were waited for; matrix products, arithmetic and copies ran while one was open for 23% of the time, Pallas kernels for 0%

profile of v9, /device:TPU:24, one launch (start us, length us, event | category | flops | bytes accessed | tf_op | source)
XLA Modules:
  0.0 104.8 jit_solution(1055321937366976752)
XLA Ops:
  0.7 0.8 fusion.113
  1.6 1.5 %reshape.87 = bf16[8,512,128]{2,1,0:T(8,128)(2,1)S(1)} reshape(bf16[8,64,1024]{2,1,0:T(8,128)(2,1)} %param.11) | data formatting | bytes 2097152 | tf_op jit(solution)/shard_map/reshape | solution.py:118
  3.1 0.4 fusion.36
  3.5 0.2 fusion.116
  3.7 0.3 fusion.37
  4.0 3.1 %collective-permute-start = (bf16[8,16,128]{2,1,0:T(8,128)(2,1)S(1)}, bf16[8,16,128]{2,1,0:T(8,128)(2,1)S(1)}, u32[]{:S(2)}, u32[]{:S(2)}) collective-permute-start(bf16[8,16,128]{2,1,0:T(8,128)(2,1)S(1)} %fusion.37), channel_id=1, source_target_pairs={{0,128},{4,132},{8,136},{12,140},{16,144},{20,148},{24,152},{28,15... | collective-permute-start | bytes 98312 | tf_op jit(solution)/shard_map/ppermute | solution.py:17
  7.1 1.1 %fusion.115 = (f32[8,8,64]{2,1,0:T(8,128)S(1)}, f32[8,1,8,64,64]{3,4,2,0,1:T(8,128)S(1)}) fusion(bf16[8,64,128]{2,1,0:T(8,128)(2,1)S(1)} %copy-done.3, pred[64,64]{0,1:T(8,128)(4,1)S(1)} %iota_compare_fusion.9, bf16[8,64,1024]{2,1,0:T(8,128)(2,1)S(1)} %copy-done.1), kind=kOutput, calls=%fused_computation.146 | convolution fusion | flops 67891200 | bytes 2248704 | tf_op jit(solution)/shard_map/pqkgd,pskd->pkgqs/dot_general | solution.py:95
  8.3 0.5 fusion.1
  8.8 0.6 fusion.19
  9.5 0.1 fusion.58
  9.6 0.2 fusion.76
  9.8 1.5 %fusion.18 = bf16[8,512,128]{2,1,0:T(8,128)(2,1)S(1)} fusion(bf16[8,64,1,8,128]{4,1,3,0,2:T(8,128)(2,1)S(1)} %fusion.19, pred[8,512]{1,0:T(8,128)(4,1)S(1)} %fusion.58, s32[8,16]{1,0:T(8,128)S(1)} %add_bitcast_fusion, bf16[8,16,128]{2,0,1:T(8,128)(2,1)S(1)} %fusion.76), kind=kOutput, calls=%fused_computation.23 | convolution fusion | flops 17891328 | bytes 2134528 | tf_op jit(solution)/shard_map/jkr,jkd->jrd/dot_general | solution.py:178
  11.4 0.2 slice.63
  11.7 3.2 %fusion.20 = bf16[256,1024]{1,0:T(8,128)(2,1)} fusion(bf16[256,1024]{1,0:T(8,128)(2,1)S(1)} %slice.63, bf16[1024,4096]{1,0:T(8,128)(2,1)} %param.14, s32[]{:T(128)S(6)} %select_n.104), kind=kOutput, calls=%fused_computation.25 | convolution fusion | flops 537133056 | bytes 3145732 | tf_op jit(solution)/shard_map/dot_general | solution.py:53
  14.9 0.1 fusion.111
  15.0 0.2 slice.65
  15.2 2.3 %fusion.23 = bf16[256,1024]{1,0:T(8,128)(2,1)S(1)} fusion(bf16[256,1024]{1,0:T(8,128)(2,1)S(1)} %slice.65, bf16[1024,4096]{1,0:T(8,128)(2,1)} %param.14, s32[]{:T(128)S(6)} %select_n.104), kind=kOutput, calls=%fused_computation.26 | convolution fusion | flops 537133056 | bytes 3145732 | tf_op jit(solution)/shard_map/dot_general | solution.py:53
  17.5 0.6 collective-permute-start.4
  18.1 0.1 eq.86
  18.2 0.1 eq.90
  18.3 2.4 %add_convert_fusion.3 = bf16[256,1024]{1,0:T(8,128)(2,1)S(1)} fusion(bf16[256,1024]{1,0:T(8,128)(2,1)} %collective-permute-done.1, bf16[256,1024]{1,0:T(8,128)(2,1)S(1)} %slice.63, bf16[1024,4096]{1,0:T(8,128)(2,1)} %param.14, s32[]{:T(128)S(6)} %select_n.103), kind=kOutput, calls=%fused_computation.53 | convolution fusion | flops 537657344 | bytes 3670020 | tf_op jit(solution)/shard_map/dot_general | solution.py:53
  20.7 0.8 collective-permute-start.3
  21.5 2.3 %fusion.26 = bf16[256,1024]{1,0:T(8,128)(2,1)S(1)} fusion(bf16[256,1024]{1,0:T(8,128)(2,1)S(1)} %slice.63, bf16[1024,4096]{1,0:T(8,128)(2,1)} %param.14, s32[]{:T(128)S(6)} %select_n.106), kind=kOutput, calls=%fused_computation.27 | convolution fusion | flops 537133056 | bytes 3145732 | tf_op jit(solution)/shard_map/dot_general | solution.py:73
  23.8 0.1 collective-permute-start.2
  23.9 2.4 %add_convert_fusion.1 = bf16[256,1024]{1,0:T(8,128)(2,1)S(1)} fusion(bf16[256,1024]{1,0:T(8,128)(2,1)} %collective-permute-done.4, bf16[256,1024]{1,0:T(8,128)(2,1)S(1)} %slice.65, bf16[1024,4096]{1,0:T(8,128)(2,1)} %param.14, s32[]{:T(128)S(6)} %select_n.103), kind=kOutput, calls=%fused_computation.51 | convolution fusion | flops 537657344 | bytes 3670020 | tf_op jit(solution)/shard_map/dot_general | solution.py:53
  26.3 2.3 %fusion.29 = bf16[256,1024]{1,0:T(8,128)(2,1)S(1)} fusion(bf16[256,1024]{1,0:T(8,128)(2,1)S(1)} %slice.65, bf16[1024,4096]{1,0:T(8,128)(2,1)} %param.14, s32[]{:T(128)S(6)} %select_n.106), kind=kOutput, calls=%fused_computation.28 | convolution fusion | flops 537133056 | bytes 3145732 | tf_op jit(solution)/shard_map/dot_general | solution.py:73
  28.7 0.6 collective-permute-start.5
  29.2 1.3 %collective-permute-start.6 = (bf16[256,1024]{1,0:T(8,128)(2,1)S(1)}, bf16[256,1024]{1,0:T(8,128)(2,1)S(1)}, u32[]{:S(2)}, u32[]{:S(2)}) collective-permute-start(bf16[256,1024]{1,0:T(8,128)(2,1)S(1)} %add_convert_fusion.1), channel_id=1, source_target_pairs={{0,2},{1,3},{2,0},{3,1},{4,6},{5,7},{6,4},{7,5},{8,10},{9,11},{10,... | collective-permute-start | bytes 1572872 | tf_op jit(solution)/shard_map/ppermute | solution.py:17
  30.5 2.3 %fusion.8 = f32[256,1024]{1,0:T(8,128)S(1)} fusion(bf16[256,1024]{1,0:T(8,128)(2,1)S(1)} %slice.63, bf16[1024,4096]{1,0:T(8,128)(2,1)} %param.14, s32[]{:T(128)S(6)} %select_n.105), kind=kOutput, calls=%fused_computation.11 | convolution fusion | flops 536870912 | bytes 3670020 | tf_op jit(solution)/shard_map/dot_general | solution.py:73
  32.8 2.3 %fusion.6 = f32[256,1024]{1,0:T(8,128)S(1)} fusion(bf16[256,1024]{1,0:T(8,128)(2,1)S(1)} %slice.65, bf16[1024,4096]{1,0:T(8,128)(2,1)} %param.14, s32[]{:T(128)S(6)} %select_n.105), kind=kOutput, calls=%fused_computation.9 | convolution fusion | flops 536870912 | bytes 3670020 | tf_op jit(solution)/shard_map/dot_general | solution.py:73
  35.1 0.4 collective-permute-done.3
  35.6 0.4 multiply_reduce_fusion.1
  36.0 1.2 %fusion.50 = f32[256,64]{0,1:T(8,128)S(1)} fusion(f32[1024,64]{0,1:T(8,128)S(1)} %copy-done, bf16[256,1024]{1,0:T(8,128)(2,1)S(1)} %get-tuple-element.19, bf16[256,1024]{1,0:T(8,128)(2,1)S(1)} %bitcast.76, f32[1024]{0:T(1024)S(1)} %copy-done.4), kind=kOutput, calls=%fused_computation.57 | convolution fusion | flops 202375168 | bytes 1380352 | tf_op jit(solution)/shard_map/dot_general | solution.py:208
  37.2 0.1 collective-permute-start.7
  37.3 8.6 %collective-permute-done.6 = bf16[256,1024]{1,0:T(8,128)(2,1)S(1)} collective-permute-done((bf16[256,1024]{1,0:T(8,128)(2,1)S(1)}, bf16[256,1024]{1,0:T(8,128)(2,1)S(1)}, u32[]{:S(2)}, u32[]{:S(2)}) %collective-permute-start.6) | collective-permute-done | bytes 524320 | tf_op jit(solution)/shard_map/ppermute | solution.py:17
  45.9 0.4 multiply_reduce_fusion
  46.3 1.2 %fusion.47 = f32[256,64]{0,1:T(8,128)S(1)} fusion(f32[1024,64]{0,1:T(8,128)S(1)} %copy-done, bf16[256,1024]{1,0:T(8,128)(2,1)S(1)} %get-tuple-element.21, bf16[256,1024]{1,0:T(8,128)(2,1)S(1)} %bitcast.74, f32[1024]{0:T(1024)S(1)} %copy-done.4), kind=kOutput, calls=%fused_computation.56 | convolution fusion | flops 202375168 | bytes 1380352 | tf_op jit(solution)/shard_map/dot_general | solution.py:208
  47.5 0.1 collective-permute-start.9
  47.6 0.8 collective-permute-start.8
  48.4 0.4 collective-permute-done.9
  48.8 1.0 collective-permute-start.10
  49.8 3.0 %collective-permute-done.8 = f32[256,65]{0,1:T(8,128)S(1)} collective-permute-done((f32[256,65]{0,1:T(8,128)S(1)}, f32[256,65]{0,1:T(8,128)S(1)}, u32[]{:S(2)}, u32[]{:S(2)}) %collective-permute-start.8) | collective-permute-done | bytes 66592 | tf_op jit(solution)/shard_map/ppermute | solution.py:17
  52.8 1.1 %collective-permute-done.10 = f32[256,65]{0,1:T(8,128)S(1)} collective-permute-done((f32[256,65]{0,1:T(8,128)S(1)}, f32[256,65]{0,1:T(8,128)S(1)}, u32[]{:S(2)}, u32[]{:S(2)}) %collective-permute-start.10) | collective-permute-done | bytes 66592 | tf_op jit(solution)/shard_map/ppermute | solution.py:17
  53.9 1.0 fusion.42
  55.0 1.0 fusion.32
  56.0 2.0 %collective-permute-start.11 = (f32[512,64]{0,1:T(8,128)S(1)}, f32[512,64]{0,1:T(8,128)S(1)}, u32[]{:S(2)}, u32[]{:S(2)}) collective-permute-start(f32[512,64]{0,1:T(8,128)S(1)} %slice_select_fusion), channel_id=1, source_target_pairs={{0,4},{4,0},{8,12},{12,8},{16,20},{20,16},{24,28},{28,24},{32,36},... | collective-permute-start | bytes 393224 | tf_op jit(solution)/shard_map/ppermute | solution.py:17
  58.0 3.3 %collective-permute-done.11 = f32[512,64]{0,1:T(8,128)S(1)} collective-permute-done((f32[512,64]{0,1:T(8,128)S(1)}, f32[512,64]{0,1:T(8,128)S(1)}, u32[]{:S(2)}, u32[]{:S(2)}) %collective-permute-start.11) | collective-permute-done | bytes 131104 | tf_op jit(solution)/shard_map/ppermute | solution.py:17
  61.3 3.4 %collective-permute-start.12 = (f32[256,64]{0,1:T(8,128)S(1)}, f32[256,64]{0,1:T(8,128)S(1)}, u32[]{:S(2)}, u32[]{:S(2)}) collective-permute-start(f32[256,64]{0,1:T(8,128)S(1)} %slice_select_fusion.1), channel_id=1, source_target_pairs={{0,8},{4,12},{8,0},{12,4},{16,24},{20,28},{24,16},{28,20},{32,40},... | collective-permute-start | bytes 196616 | tf_op jit(solution)/shard_map/ppermute | solution.py:17
  64.7 2.2 %collective-permute-done.12 = f32[256,64]{0,1:T(8,128)S(1)} collective-permute-done((f32[256,64]{0,1:T(8,128)S(1)}, f32[256,64]{0,1:T(8,128)S(1)}, u32[]{:S(2)}, u32[]{:S(2)}) %collective-permute-start.12) | collective-permute-done | bytes 65568 | tf_op jit(solution)/shard_map/ppermute | solution.py:17
  67.0 7.5 %collective-permute-start.13 = (f32[256,64]{0,1:T(8,128)S(1)}, f32[256,64]{0,1:T(8,128)S(1)}, u32[]{:S(2)}, u32[]{:S(2)}) collective-permute-start(f32[256,64]{0,1:T(8,128)S(1)} %select_add_fusion.1), channel_id=1, source_target_pairs={{0,16},{4,20},{8,24},{12,28},{16,0},{20,4},{24,8},{28,12},{32,48},... | collective-permute-start | bytes 196616 | tf_op jit(solution)/shard_map/ppermute | solution.py:17
  74.4 2.9 %collective-permute-done.13 = f32[256,64]{0,1:T(8,128)S(1)} collective-permute-done((f32[256,64]{0,1:T(8,128)S(1)}, f32[256,64]{0,1:T(8,128)S(1)}, u32[]{:S(2)}, u32[]{:S(2)}) %collective-permute-start.13) | collective-permute-done | bytes 65568 | tf_op jit(solution)/shard_map/ppermute | solution.py:17
  77.4 1.3 %collective-permute-start.14 = (f32[256,64]{0,1:T(8,128)S(1)}, f32[256,64]{0,1:T(8,128)S(1)}, u32[]{:S(2)}, u32[]{:S(2)}) collective-permute-start(f32[256,64]{0,1:T(8,128)S(1)} %add.139), channel_id=1, source_target_pairs={{0,32},{4,36},{8,40},{12,44},{16,48},{20,52},{24,56},{28,60},{32,0... | collective-permute-start | bytes 196616 | tf_op jit(solution)/shard_map/ppermute | solution.py:17
  78.7 4.5 %collective-permute-done.14 = f32[256,64]{0,1:T(8,128)S(1)} collective-permute-done((f32[256,64]{0,1:T(8,128)S(1)}, f32[256,64]{0,1:T(8,128)S(1)}, u32[]{:S(2)}, u32[]{:S(2)}) %collective-permute-start.14) | collective-permute-done | bytes 65568 | tf_op jit(solution)/shard_map/ppermute | solution.py:17
  83.2 1.4 %collective-permute-start.15 = (f32[256,64]{0,1:T(8,128)S(1)}, f32[256,64]{0,1:T(8,128)S(1)}, u32[]{:S(2)}, u32[]{:S(2)}) collective-permute-start(f32[256,64]{0,1:T(8,128)S(1)} %add.140), channel_id=1, source_target_pairs={{0,64},{4,68},{8,72},{12,76},{16,80},{20,84},{24,88},{28,92},{32,9... | collective-permute-start | bytes 196616 | tf_op jit(solution)/shard_map/ppermute | solution.py:17
  84.7 2.9 %collective-permute-done.15 = f32[256,64]{0,1:T(8,128)S(1)} collective-permute-done((f32[256,64]{0,1:T(8,128)S(1)}, f32[256,64]{0,1:T(8,128)S(1)}, u32[]{:S(2)}, u32[]{:S(2)}) %collective-permute-start.15) | collective-permute-done | bytes 65568 | tf_op jit(solution)/shard_map/ppermute | solution.py:17
  87.6 3.0 %collective-permute-start.16 = (f32[256,64]{0,1:T(8,128)S(1)}, f32[256,64]{0,1:T(8,128)S(1)}, u32[]{:S(2)}, u32[]{:S(2)}) collective-permute-start(f32[256,64]{0,1:T(8,128)S(1)} %add.141), channel_id=1, source_target_pairs={{0,128},{4,132},{8,136},{12,140},{16,144},{20,148},{24,152},{28,15... | collective-permute-start | bytes 196616 | tf_op jit(solution)/shard_map/ppermute | solution.py:17
  90.6 1.0 pad_maximum_fusion
  91.6 1.8 %collective-permute-done.16 = f32[256,64]{0,1:T(8,128)S(1)} collective-permute-done((f32[256,64]{0,1:T(8,128)S(1)}, f32[256,64]{0,1:T(8,128)S(1)}, u32[]{:S(2)}, u32[]{:S(2)}) %collective-permute-start.16) | collective-permute-done | bytes 65568 | tf_op jit(solution)/shard_map/ppermute | solution.py:17
  93.5 1.3 %collective-permute-start.17 = (f32[256,64]{0,1:T(8,128)S(1)}, f32[256,64]{0,1:T(8,128)S(1)}, u32[]{:S(2)}, u32[]{:S(2)}) collective-permute-start(f32[256,64]{0,1:T(8,128)S(1)} %add.142), channel_id=1, source_target_pairs={{0,8},{4,12},{8,0},{12,4},{16,24},{20,28},{24,16},{28,20},{32,40},... | collective-permute-start | bytes 196616 | tf_op jit(solution)/shard_map/ppermute | solution.py:17
  94.8 4.3 %collective-permute-done.17 = f32[256,64]{0,1:T(8,128)S(1)} collective-permute-done((f32[256,64]{0,1:T(8,128)S(1)}, f32[256,64]{0,1:T(8,128)S(1)}, u32[]{:S(2)}, u32[]{:S(2)}) %collective-permute-start.17) | collective-permute-done | bytes 65568 | tf_op jit(solution)/shard_map/ppermute | solution.py:17
  99.1 0.1 collective-permute-start.18
  99.2 0.8 copy.24
  100.0 4.1 %collective-permute-done.18 = f32[512,64]{0,1:T(8,128)S(1)} collective-permute-done((f32[512,64]{0,1:T(8,128)S(1)}, f32[512,64]{0,1:T(8,128)S(1)}, u32[]{:S(2)}, u32[]{:S(2)}) %collective-permute-start.18) | collective-permute-done | bytes 131104 | tf_op jit(solution)/shard_map/ppermute | solution.py:17
  104.1 0.7 maximum_select_fusion
  (48 shorter events, 0.4 us)
Async XLA Ops:
  0.6 35.3 %copy-start = (f32[1024,64]{0,1:T(8,128)S(1)}, f32[1024,64]{0,1:T(8,128)}, u32[]{:S(2)}) copy-start(f32[1024,64]{0,1:T(8,128)} %param.16) | copy-start | bytes 786436
  0.6 6.5 %copy-start.1 = (bf16[8,64,1024]{2,1,0:T(8,128)(2,1)S(1)}, bf16[8,64,1024]{2,1,0:T(8,128)(2,1)}, u32[]{:S(2)}) copy-start(bf16[8,64,1024]{2,1,0:T(8,128)(2,1)} %param.11) | copy-start | bytes 3145732
  0.7 2.4 %copy-start.3 = (bf16[8,64,128]{2,1,0:T(8,128)(2,1)S(1)}, bf16[8,64,128]{2,1,0:T(8,128)(2,1)}, u32[]{:S(2)}) copy-start(bf16[8,64,128]{2,1,0:T(8,128)(2,1)} %param.12) | copy-start | bytes 393220
  0.7 3.0 %copy-start.7 = (bf16[8,64,128]{2,1,0:T(8,128)(2,1)S(1)}, bf16[8,64,128]{2,1,0:T(8,128)(2,1)}, u32[]{:S(2)}) copy-start(bf16[8,64,128]{2,1,0:T(8,128)(2,1)} %param.13) | copy-start | bytes 393220
  4.0 5.6 %collective-permute-start = (bf16[8,16,128]{2,1,0:T(8,128)(2,1)S(1)}, bf16[8,16,128]{2,1,0:T(8,128)(2,1)S(1)}, u32[]{:S(2)}, u32[]{:S(2)}) collective-permute-start(bf16[8,16,128]{2,1,0:T(8,128)(2,1)S(1)} %fusion.37), channel_id=1, source_target_pairs={{0,128},{4,132},{8,136},{12,140},{16,144},{20,148},{24,152},{28,15... | collective-permute-start | bytes 98312 | tf_op jit(solution)/shard_map/ppermute | solution.py:17
  8.8 0.8 copy-start.6
  11.6 3.2 %copy-start.2 = (bf16[8,64,1024]{2,1,0:T(8,128)(2,1)S(1)}, bf16[8,64,1024]{2,1,0:T(8,128)(2,1)}, u32[]{:S(2)}) copy-start(bf16[8,64,1024]{2,1,0:T(8,128)(2,1)} %param.10) | copy-start | bytes 3145732
  14.8 3.4 %collective-permute-start.1 = (bf16[256,1024]{1,0:T(8,128)(2,1)}, bf16[256,1024]{1,0:T(8,128)(2,1)}, u32[]{:S(2)}, u32[]{:S(2)}) collective-permute-start(bf16[256,1024]{1,0:T(8,128)(2,1)} %fusion.20), channel_id=1, source_target_pairs={{0,1},{1,0},{2,3},{3,2},{4,5},{5,4},{6,7},{7,6},{8,9},{9,8},{10,11... | collective-permute-start | bytes 1572872 | tf_op jit(solution)/shard_map/ppermute | solution.py:17
  15.0 3.2 %copy-start.5 = (s32[8,64]{1,0:T(8,128)S(1)}, s32[8,64]{1,0:T(8,128)}, u32[]{:S(2)}) copy-start(s32[8,64]{1,0:T(8,128)} %param.19) | copy-start | bytes 6148
  17.5 6.4 %collective-permute-start.4 = (bf16[256,1024]{1,0:T(8,128)(2,1)S(1)}, bf16[256,1024]{1,0:T(8,128)(2,1)}, u32[]{:S(2)}, u32[]{:S(2)}) collective-permute-start(bf16[256,1024]{1,0:T(8,128)(2,1)S(1)} %fusion.23), channel_id=1, source_target_pairs={{0,1},{1,0},{2,3},{3,2},{4,5},{5,4},{6,7},{7,6},{8,9},{9,8},{10,11... | collective-permute-start | bytes 1572872 | tf_op jit(solution)/shard_map/ppermute | solution.py:17
  20.7 14.9 %collective-permute-start.3 = (bf16[256,1024]{1,0:T(8,128)(2,1)S(1)}, bf16[256,1024]{1,0:T(8,128)(2,1)S(1)}, u32[]{:S(2)}, u32[]{:S(2)}) collective-permute-start(bf16[256,1024]{1,0:T(8,128)(2,1)S(1)} %add_convert_fusion.3), channel_id=1, source_target_pairs={{0,2},{1,3},{2,0},{3,1},{4,6},{5,7},{6,4},{7,5},{8,10},{9,11},{10,... | collective-permute-start | bytes 1572872 | tf_op jit(solution)/shard_map/ppermute | solution.py:17
  23.8 11.7 %collective-permute-start.2 = (bf16[256,1024]{1,0:T(8,128)(2,1)S(1)}, bf16[256,1024]{1,0:T(8,128)(2,1)S(1)}, u32[]{:S(2)}, u32[]{:S(2)}) collective-permute-start(bf16[256,1024]{1,0:T(8,128)(2,1)S(1)} %fusion.26), channel_id=1, source_target_pairs={{0,1},{1,0},{2,3},{3,2},{4,5},{5,4},{6,7},{7,6},{8,9},{9,8},{10,11... | collective-permute-start | bytes 1572872 | tf_op jit(solution)/shard_map/ppermute | solution.py:17
  28.7 8.6 %collective-permute-start.5 = (bf16[256,1024]{1,0:T(8,128)(2,1)S(1)}, bf16[256,1024]{1,0:T(8,128)(2,1)S(1)}, u32[]{:S(2)}, u32[]{:S(2)}) collective-permute-start(bf16[256,1024]{1,0:T(8,128)(2,1)S(1)} %fusion.29), channel_id=1, source_target_pairs={{0,1},{1,0},{2,3},{3,2},{4,5},{5,4},{6,7},{7,6},{8,9},{9,8},{10,11... | collective-permute-start | bytes 1572872 | tf_op jit(solution)/shard_map/ppermute | solution.py:17
  29.2 16.7 %collective-permute-start.6 = (bf16[256,1024]{1,0:T(8,128)(2,1)S(1)}, bf16[256,1024]{1,0:T(8,128)(2,1)S(1)}, u32[]{:S(2)}, u32[]{:S(2)}) collective-permute-start(bf16[256,1024]{1,0:T(8,128)(2,1)S(1)} %add_convert_fusion.1), channel_id=1, source_target_pairs={{0,2},{1,3},{2,0},{3,1},{4,6},{5,7},{6,4},{7,5},{8,10},{9,11},{10,... | collective-permute-start | bytes 1572872 | tf_op jit(solution)/shard_map/ppermute | solution.py:17
  35.1 0.9 copy-start.4
  37.2 10.4 %collective-permute-start.7 = (f32[256,65]{0,1:T(8,128)S(1)}, f32[256,65]{0,1:T(8,128)S(1)}, u32[]{:S(2)}, u32[]{:S(2)}) collective-permute-start(f32[256,65]{0,1:T(8,128)S(1)} %pad_maximum_fusion.2), channel_id=1, source_target_pairs={{0,1},{1,0},{2,3},{3,2},{4,5},{5,4},{6,7},{7,6},{8,9},{9,8},{10,11... | collective-permute-start | bytes 199688 | tf_op jit(solution)/shard_map/ppermute | solution.py:17
  47.5 1.4 %collective-permute-start.9 = (f32[256,65]{0,1:T(8,128)S(1)}, f32[256,65]{0,1:T(8,128)S(1)}, u32[]{:S(2)}, u32[]{:S(2)}) collective-permute-start(f32[256,65]{0,1:T(8,128)S(1)} %pad_maximum_fusion.3), channel_id=1, source_target_pairs={{0,1},{1,0},{2,3},{3,2},{4,5},{5,4},{6,7},{7,6},{8,9},{9,8},{10,11... | collective-permute-start | bytes 199688 | tf_op jit(solution)/shard_map/ppermute | solution.py:17
  47.6 5.2 %collective-permute-start.8 = (f32[256,65]{0,1:T(8,128)S(1)}, f32[256,65]{0,1:T(8,128)S(1)}, u32[]{:S(2)}, u32[]{:S(2)}) collective-permute-start(f32[256,65]{0,1:T(8,128)S(1)} %fusion.110), channel_id=1, source_target_pairs={{0,2},{1,3},{2,0},{3,1},{4,6},{5,7},{6,4},{7,5},{8,10},{9,11},{10,... | collective-permute-start | bytes 199688 | tf_op jit(solution)/shard_map/ppermute | solution.py:17
  48.8 5.1 %collective-permute-start.10 = (f32[256,65]{0,1:T(8,128)S(1)}, f32[256,65]{0,1:T(8,128)S(1)}, u32[]{:S(2)}, u32[]{:S(2)}) collective-permute-start(f32[256,65]{0,1:T(8,128)S(1)} %fusion.109), channel_id=1, source_target_pairs={{0,2},{1,3},{2,0},{3,1},{4,6},{5,7},{6,4},{7,5},{8,10},{9,11},{10,... | collective-permute-start | bytes 199688 | tf_op jit(solution)/shard_map/ppermute | solution.py:17
  56.0 5.3 %collective-permute-start.11 = (f32[512,64]{0,1:T(8,128)S(1)}, f32[512,64]{0,1:T(8,128)S(1)}, u32[]{:S(2)}, u32[]{:S(2)}) collective-permute-start(f32[512,64]{0,1:T(8,128)S(1)} %slice_select_fusion), channel_id=1, source_target_pairs={{0,4},{4,0},{8,12},{12,8},{16,20},{20,16},{24,28},{28,24},{32,36},... | collective-permute-start | bytes 393224 | tf_op jit(solution)/shard_map/ppermute | solution.py:17
  61.3 5.6 %collective-permute-start.12 = (f32[256,64]{0,1:T(8,128)S(1)}, f32[256,64]{0,1:T(8,128)S(1)}, u32[]{:S(2)}, u32[]{:S(2)}) collective-permute-start(f32[256,64]{0,1:T(8,128)S(1)} %slice_select_fusion.1), channel_id=1, source_target_pairs={{0,8},{4,12},{8,0},{12,4},{16,24},{20,28},{24,16},{28,20},{32,40},... | collective-permute-start | bytes 196616 | tf_op jit(solution)/shard_map/ppermute | solution.py:17
  67.0 10.4 %collective-permute-start.13 = (f32[256,64]{0,1:T(8,128)S(1)}, f32[256,64]{0,1:T(8,128)S(1)}, u32[]{:S(2)}, u32[]{:S(2)}) collective-permute-start(f32[256,64]{0,1:T(8,128)S(1)} %select_add_fusion.1), channel_id=1, source_target_pairs={{0,16},{4,20},{8,24},{12,28},{16,0},{20,4},{24,8},{28,12},{32,48},... | collective-permute-start | bytes 196616 | tf_op jit(solution)/shard_map/ppermute | solution.py:17
  77.4 5.9 %collective-permute-start.14 = (f32[256,64]{0,1:T(8,128)S(1)}, f32[256,64]{0,1:T(8,128)S(1)}, u32[]{:S(2)}, u32[]{:S(2)}) collective-permute-start(f32[256,64]{0,1:T(8,128)S(1)} %add.139), channel_id=1, source_target_pairs={{0,32},{4,36},{8,40},{12,44},{16,48},{20,52},{24,56},{28,60},{32,0... | collective-permute-start | bytes 196616 | tf_op jit(solution)/shard_map/ppermute | solution.py:17
  83.2 4.4 %collective-permute-start.15 = (f32[256,64]{0,1:T(8,128)S(1)}, f32[256,64]{0,1:T(8,128)S(1)}, u32[]{:S(2)}, u32[]{:S(2)}) collective-permute-start(f32[256,64]{0,1:T(8,128)S(1)} %add.140), channel_id=1, source_target_pairs={{0,64},{4,68},{8,72},{12,76},{16,80},{20,84},{24,88},{28,92},{32,9... | collective-permute-start | bytes 196616 | tf_op jit(solution)/shard_map/ppermute | solution.py:17
  87.6 5.9 %collective-permute-start.16 = (f32[256,64]{0,1:T(8,128)S(1)}, f32[256,64]{0,1:T(8,128)S(1)}, u32[]{:S(2)}, u32[]{:S(2)}) collective-permute-start(f32[256,64]{0,1:T(8,128)S(1)} %add.141), channel_id=1, source_target_pairs={{0,128},{4,132},{8,136},{12,140},{16,144},{20,148},{24,152},{28,15... | collective-permute-start | bytes 196616 | tf_op jit(solution)/shard_map/ppermute | solution.py:17
  93.5 5.6 %collective-permute-start.17 = (f32[256,64]{0,1:T(8,128)S(1)}, f32[256,64]{0,1:T(8,128)S(1)}, u32[]{:S(2)}, u32[]{:S(2)}) collective-permute-start(f32[256,64]{0,1:T(8,128)S(1)} %add.142), channel_id=1, source_target_pairs={{0,8},{4,12},{8,0},{12,4},{16,24},{20,28},{24,16},{28,20},{32,40},... | collective-permute-start | bytes 196616 | tf_op jit(solution)/shard_map/ppermute | solution.py:17
  99.1 5.1 %collective-permute-start.18 = (f32[512,64]{0,1:T(8,128)S(1)}, f32[512,64]{0,1:T(8,128)S(1)}, u32[]{:S(2)}, u32[]{:S(2)}) collective-permute-start(f32[512,64]{0,1:T(8,128)S(1)} %maximum_select_fusion.1), channel_id=1, source_target_pairs={{0,4},{4,0},{8,12},{12,8},{16,20},{20,16},{24,28},{28,24},{32,36},... | collective-permute-start | bytes 393224 | tf_op jit(solution)/shard_map/ppermute | solution.py:17

commit v10 on v9

--- a/solution.py
+++ b/solution.py
@@ -195,12 +195,14 @@
             flat_patched[rows_here], out_weight, "tensor", sent_block
         )
         halves.append((heads_here, sent_block, from_far))
-    attn_chunks, logit_chunks, grad_local = [], [], None
+    attn_chunks, logit_chunks, grad_local, summed = [], [], None, None
     for index in range(chunk_count):
         rows_here = slice(index * chunk, (index + 1) * chunk)
         heads_here, _, from_far = halves[index]
         if index + 1 < chunk_count:
             from_far, _ = lax.optimization_barrier((from_far, halves[index + 1][1]))
+        if summed is not None:
+            from_far, _ = lax.optimization_barrier((from_far, summed))
         attn_local = near_half(heads_here, out_weight, "tensor", from_far).astype(jnp.bfloat16)
         hidden = flat_residual[rows_here].astype(jnp.float32) + attn_local.astype(jnp.float32)
         square_local = jnp.sum(hidden * hidden, axis=1)
@@ -210,6 +212,7 @@
         )
         packed = jnp.concatenate([raw_part, square_local[:, None]], axis=1)
         packed = butterfly_sum(packed, "tensor", tensor_bits)
+        summed = packed
         inverse_rms = lax.rsqrt(packed[:, concepts] / DW + norm_epsilon)
         logits = packed[:, :concepts] * inverse_rms[:, None]
         normed = scaled * inverse_rms[:, None]

time: 105 us -> 105 us (level)
  waiting for transfers between devices: 39.7 us -> 34.3 us
  local copies, waits for them, and re-layouts: 4.03 us -> 7.08 us
  matrix products: 28 us -> 30.4 us
    ppermute x19, waiting for transfers between devices: 39.7 us -> 34.3 us  [exchanged(): return lax.ppermute(block, axis, [(i, i ^ bit) for i in range(count)])]
    eq x2, local copies, waits for them, and re-layouts: 0.16 us -> 2.66 us  [per_device(): labels[rows_here][:, None] == classes[None, :]]
    dot_general x8, matrix products: 19.5 us -> 21.9 us  [block(): return jnp.dot(heads, columns, preferred_element_type=jnp.float32)]
  transfers between devices with their start and end apart: 19 -> 19, of which waited for: 13 -> 12; matrix products, arithmetic and copies ran while one was open for 23% -> 28% of each run, Pallas kernels for 0% -> 0%
where the time goes in v10:
time: 105 us
  waiting for transfers between devices  34.3 us (33%)
  matrix products  30.4 us (29%)
  starting transfers between devices  27.7 us (26%)
  local copies, waits for them, and re-layouts  7.08 us (7%)
  other arithmetic  4.33 us (4%)
  between operations  1.06 us (1%)
    ppermute x19, waiting for transfers between devices, exchanged(): return lax.ppermute(block, axis, [(i, i ^ bit) for i in range(count)])  34.3 us
    ppermute x19, starting transfers between devices, exchanged(): return lax.ppermute(block, axis, [(i, i ^ bit) for i in range(count)])  27.7 us
    dot_general x8, matrix products, block(): return jnp.dot(heads, columns, preferred_element_type=jnp.float32)  21.9 us
    eq x2, local copies, waits for them, and re-layouts, per_device(): labels[rows_here][:, None] == classes[None, :]  2.66 us
    dot_general x2, matrix products, per_device(): jnp.dot(scaled, probe_weight, precision=lax.Precision.HIGHEST, preferred_...  2.31 us
  transfers between devices with their start and end apart: 19, of which 12 were waited for; matrix products, arithmetic and copies ran while one was open for 28% of the time, Pallas kernels for 0%

profile of v10, /device:TPU:24, one launch (start us, length us, event | category | flops | bytes accessed | tf_op | source)
XLA Modules:
  0.0 104.9 jit_solution(14036615440132018377)
XLA Ops:
  0.7 0.8 fusion.113
  1.6 1.5 %reshape.87 = bf16[8,512,128]{2,1,0:T(8,128)(2,1)S(1)} reshape(bf16[8,64,1024]{2,1,0:T(8,128)(2,1)} %param.11) | data formatting | bytes 2097152 | tf_op jit(solution)/shard_map/reshape | solution.py:118
  3.1 0.4 fusion.36
  3.5 0.2 fusion.116
  3.7 0.3 fusion.37
  4.0 3.1 %collective-permute-start = (bf16[8,16,128]{2,1,0:T(8,128)(2,1)S(1)}, bf16[8,16,128]{2,1,0:T(8,128)(2,1)S(1)}, u32[]{:S(2)}, u32[]{:S(2)}) collective-permute-start(bf16[8,16,128]{2,1,0:T(8,128)(2,1)S(1)} %fusion.37), channel_id=1, source_target_pairs={{0,128},{4,132},{8,136},{12,140},{16,144},{20,148},{24,152},{28,15... | collective-permute-start | bytes 98312 | tf_op jit(solution)/shard_map/ppermute | solution.py:17
  7.1 1.1 %fusion.115 = (f32[8,8,64]{2,1,0:T(8,128)S(1)}, f32[8,1,8,64,64]{3,4,2,0,1:T(8,128)S(1)}) fusion(bf16[8,64,128]{2,1,0:T(8,128)(2,1)S(1)} %copy-done.3, pred[64,64]{0,1:T(8,128)(4,1)S(1)} %iota_compare_fusion.9, bf16[8,64,1024]{2,1,0:T(8,128)(2,1)S(1)} %copy-done.1), kind=kOutput, calls=%fused_computation.146 | convolution fusion | flops 67891200 | bytes 2248704 | tf_op jit(solution)/shard_map/pqkgd,pskd->pkgqs/dot_general | solution.py:95
  8.3 0.5 fusion.1
  8.8 0.6 fusion.19
  9.5 0.1 fusion.58
  9.6 0.2 fusion.76
  9.8 1.5 %fusion.18 = bf16[8,512,128]{2,1,0:T(8,128)(2,1)S(1)} fusion(bf16[8,64,1,8,128]{4,1,3,0,2:T(8,128)(2,1)S(1)} %fusion.19, pred[8,512]{1,0:T(8,128)(4,1)S(1)} %fusion.58, s32[8,16]{1,0:T(8,128)S(1)} %add_bitcast_fusion, bf16[8,16,128]{2,0,1:T(8,128)(2,1)S(1)} %fusion.76), kind=kOutput, calls=%fused_computation.23 | convolution fusion | flops 17891328 | bytes 2134528 | tf_op jit(solution)/shard_map/jkr,jkd->jrd/dot_general | solution.py:178
  11.3 0.1 fusion.112
  11.4 0.2 slice.63
  11.6 3.1 %fusion.20 = bf16[256,1024]{1,0:T(8,128)(2,1)} fusion(bf16[256,1024]{1,0:T(8,128)(2,1)S(1)} %slice.63, bf16[1024,4096]{1,0:T(8,128)(2,1)} %param.14, s32[]{:T(128)S(6)} %select_n.104), kind=kOutput, calls=%fused_computation.25 | convolution fusion | flops 537133056 | bytes 3145732 | tf_op jit(solution)/shard_map/dot_general | solution.py:53
  14.8 0.2 slice.65
  15.0 3.2 %fusion.23 = bf16[256,1024]{1,0:T(8,128)(2,1)} fusion(bf16[256,1024]{1,0:T(8,128)(2,1)S(1)} %slice.65, bf16[1024,4096]{1,0:T(8,128)(2,1)} %param.14, s32[]{:T(128)S(6)} %select_n.104), kind=kOutput, calls=%fused_computation.26 | convolution fusion | flops 537133056 | bytes 3145732 | tf_op jit(solution)/shard_map/dot_general | solution.py:53
  18.2 0.5 collective-permute-start.4
  18.8 2.4 %add_convert_fusion.3 = bf16[256,1024]{1,0:T(8,128)(2,1)S(1)} fusion(bf16[256,1024]{1,0:T(8,128)(2,1)} %collective-permute-done.1, bf16[256,1024]{1,0:T(8,128)(2,1)S(1)} %slice.63, bf16[1024,4096]{1,0:T(8,128)(2,1)} %param.14, s32[]{:T(128)S(6)} %select_n.103), kind=kOutput, calls=%fused_computation.53 | convolution fusion | flops 537657344 | bytes 3670020 | tf_op jit(solution)/shard_map/dot_general | solution.py:53
  21.2 0.8 collective-permute-start.3
  22.0 2.3 %fusion.26 = bf16[256,1024]{1,0:T(8,128)(2,1)S(1)} fusion(bf16[256,1024]{1,0:T(8,128)(2,1)S(1)} %slice.63, bf16[1024,4096]{1,0:T(8,128)(2,1)} %param.14, s32[]{:T(128)S(6)} %select_n.106), kind=kOutput, calls=%fused_computation.27 | convolution fusion | flops 537133056 | bytes 3145732 | tf_op jit(solution)/shard_map/dot_general | solution.py:73
  24.3 0.1 collective-permute-start.2
  24.4 3.2 %add_convert_fusion.1 = bf16[256,1024]{1,0:T(8,128)(2,1)} fusion(bf16[256,1024]{1,0:T(8,128)(2,1)} %collective-permute-done.4, bf16[256,1024]{1,0:T(8,128)(2,1)S(1)} %slice.65, bf16[1024,4096]{1,0:T(8,128)(2,1)} %param.14, s32[]{:T(128)S(6)} %select_n.103), kind=kOutput, calls=%fused_computation.51 | convolution fusion | flops 537657344 | bytes 3670020 | tf_op jit(solution)/shard_map/dot_general | solution.py:53
  27.6 1.3 %collective-permute-start.6 = (bf16[256,1024]{1,0:T(8,128)(2,1)}, bf16[256,1024]{1,0:T(8,128)(2,1)S(1)}, u32[]{:S(2)}, u32[]{:S(2)}) collective-permute-start(bf16[256,1024]{1,0:T(8,128)(2,1)} %add_convert_fusion.1), channel_id=1, source_target_pairs={{0,2},{1,3},{2,0},{3,1},{4,6},{5,7},{6,4},{7,5},{8,10},{9,11},{10,... | collective-permute-start | bytes 1572872 | tf_op jit(solution)/shard_map/ppermute | solution.py:17
  28.9 3.1 %fusion.29 = bf16[256,1024]{1,0:T(8,128)(2,1)} fusion(bf16[256,1024]{1,0:T(8,128)(2,1)S(1)} %slice.65, bf16[1024,4096]{1,0:T(8,128)(2,1)} %param.14, s32[]{:T(128)S(6)} %select_n.106), kind=kOutput, calls=%fused_computation.28 | convolution fusion | flops 537133056 | bytes 3145732 | tf_op jit(solution)/shard_map/dot_general | solution.py:73
  32.0 0.2 collective-permute-start.5
  32.2 2.3 %fusion.8 = f32[256,1024]{1,0:T(8,128)S(1)} fusion(bf16[256,1024]{1,0:T(8,128)(2,1)S(1)} %slice.63, bf16[1024,4096]{1,0:T(8,128)(2,1)} %param.14, s32[]{:T(128)S(6)} %select_n.105), kind=kOutput, calls=%fused_computation.11 | convolution fusion | flops 536870912 | bytes 3670020 | tf_op jit(solution)/shard_map/dot_general | solution.py:73
  34.5 1.5 %collective-permute-done.3 = bf16[256,1024]{1,0:T(8,128)(2,1)S(1)} collective-permute-done((bf16[256,1024]{1,0:T(8,128)(2,1)S(1)}, bf16[256,1024]{1,0:T(8,128)(2,1)S(1)}, u32[]{:S(2)}, u32[]{:S(2)}) %collective-permute-start.3) | collective-permute-done | bytes 524320 | tf_op jit(solution)/shard_map/ppermute | solution.py:17
  36.1 0.4 multiply_reduce_fusion.1
  36.5 1.2 %fusion.50 = f32[256,64]{0,1:T(8,128)S(1)} fusion(f32[1024,64]{0,1:T(8,128)S(1)} %copy-done, bf16[256,1024]{1,0:T(8,128)(2,1)S(1)} %get-tuple-element.23, bf16[256,1024]{1,0:T(8,128)(2,1)S(1)} %bitcast.76, f32[1024]{0:T(1024)S(1)} %copy-done.4), kind=kOutput, calls=%fused_computation.57 | convolution fusion | flops 202375168 | bytes 1380352 | tf_op jit(solution)/shard_map/dot_general | solution.py:210
  37.6 0.6 pad_maximum_fusion.2
  38.3 0.6 fusion.114
  38.9 1.3 %eq.86 = s32[256]{0:T(256)} reshape(s32[4,64]{1,0:T(4,128)} %get-tuple-element.31) | data formatting | bytes 2048 | tf_op jit(solution)/shard_map/eq | solution.py:220
  40.2 1.3 %eq.90 = s32[256]{0:T(256)} reshape(s32[4,64]{1,0:T(4,128)} %get-tuple-element.30) | data formatting | bytes 2048 | tf_op jit(solution)/shard_map/eq | solution.py:220
  41.6 0.8 collective-permute-start.8
  42.4 2.3 %fusion.6 = f32[256,1024]{1,0:T(8,128)S(1)} fusion(bf16[256,1024]{1,0:T(8,128)(2,1)S(1)} %slice.65, bf16[1024,4096]{1,0:T(8,128)(2,1)} %param.14, s32[]{:T(128)S(6)} %select_n.105), kind=kOutput, calls=%fused_computation.9 | convolution fusion | flops 536870912 | bytes 3670020 | tf_op jit(solution)/shard_map/dot_general | solution.py:73
  44.7 3.2 %collective-permute-done.8 = f32[256,65]{0,1:T(8,128)S(1)} collective-permute-done((f32[256,65]{0,1:T(8,128)S(1)}, f32[256,65]{0,1:T(8,128)S(1)}, u32[]{:S(2)}, u32[]{:S(2)}) %collective-permute-start.8) | collective-permute-done | bytes 66592 | tf_op jit(solution)/shard_map/ppermute | solution.py:17
  48.0 0.4 multiply_reduce_fusion
  48.4 1.2 %fusion.47 = f32[256,64]{0,1:T(8,128)S(1)} fusion(f32[1024,64]{0,1:T(8,128)S(1)} %copy-done, bf16[256,1024]{1,0:T(8,128)(2,1)S(1)} %get-tuple-element.21, bf16[256,1024]{1,0:T(8,128)(2,1)S(1)} %bitcast.74, f32[1024]{0:T(1024)S(1)} %copy-done.4), kind=kOutput, calls=%fused_computation.56 | convolution fusion | flops 202375168 | bytes 1380352 | tf_op jit(solution)/shard_map/dot_general | solution.py:210
  49.5 0.1 collective-permute-start.9
  49.6 1.2 %collective-permute-done.9 = f32[256,65]{0,1:T(8,128)S(1)} collective-permute-done((f32[256,65]{0,1:T(8,128)S(1)}, f32[256,65]{0,1:T(8,128)S(1)}, u32[]{:S(2)}, u32[]{:S(2)}) %collective-permute-start.9) | collective-permute-done | bytes 66592 | tf_op jit(solution)/shard_map/ppermute | solution.py:17
  50.9 0.8 collective-permute-start.10
  51.7 1.0 fusion.42
  52.7 2.6 %collective-permute-done.10 = f32[256,65]{0,1:T(8,128)S(1)} collective-permute-done((f32[256,65]{0,1:T(8,128)S(1)}, f32[256,65]{0,1:T(8,128)S(1)}, u32[]{:S(2)}, u32[]{:S(2)}) %collective-permute-start.10) | collective-permute-done | bytes 66592 | tf_op jit(solution)/shard_map/ppermute | solution.py:17
  55.4 1.0 fusion.32
  56.4 2.0 %collective-permute-start.11 = (f32[512,64]{0,1:T(8,128)S(1)}, f32[512,64]{0,1:T(8,128)S(1)}, u32[]{:S(2)}, u32[]{:S(2)}) collective-permute-start(f32[512,64]{0,1:T(8,128)S(1)} %slice_select_fusion), channel_id=1, source_target_pairs={{0,4},{4,0},{8,12},{12,8},{16,20},{20,16},{24,28},{28,24},{32,36},... | collective-permute-start | bytes 393224 | tf_op jit(solution)/shard_map/ppermute | solution.py:17
  58.4 3.0 %collective-permute-done.11 = f32[512,64]{0,1:T(8,128)S(1)} collective-permute-done((f32[512,64]{0,1:T(8,128)S(1)}, f32[512,64]{0,1:T(8,128)S(1)}, u32[]{:S(2)}, u32[]{:S(2)}) %collective-permute-start.11) | collective-permute-done | bytes 131104 | tf_op jit(solution)/shard_map/ppermute | solution.py:17
  61.5 3.4 %collective-permute-start.12 = (f32[256,64]{0,1:T(8,128)S(1)}, f32[256,64]{0,1:T(8,128)S(1)}, u32[]{:S(2)}, u32[]{:S(2)}) collective-permute-start(f32[256,64]{0,1:T(8,128)S(1)} %slice_select_fusion.1), channel_id=1, source_target_pairs={{0,8},{4,12},{8,0},{12,4},{16,24},{20,28},{24,16},{28,20},{32,40},... | collective-permute-start | bytes 196616 | tf_op jit(solution)/shard_map/ppermute | solution.py:17
  64.9 2.2 %collective-permute-done.12 = f32[256,64]{0,1:T(8,128)S(1)} collective-permute-done((f32[256,64]{0,1:T(8,128)S(1)}, f32[256,64]{0,1:T(8,128)S(1)}, u32[]{:S(2)}, u32[]{:S(2)}) %collective-permute-start.12) | collective-permute-done | bytes 65568 | tf_op jit(solution)/shard_map/ppermute | solution.py:17
  67.1 7.6 %collective-permute-start.13 = (f32[256,64]{0,1:T(8,128)S(1)}, f32[256,64]{0,1:T(8,128)S(1)}, u32[]{:S(2)}, u32[]{:S(2)}) collective-permute-start(f32[256,64]{0,1:T(8,128)S(1)} %select_add_fusion.1), channel_id=1, source_target_pairs={{0,16},{4,20},{8,24},{12,28},{16,0},{20,4},{24,8},{28,12},{32,48},... | collective-permute-start | bytes 196616 | tf_op jit(solution)/shard_map/ppermute | solution.py:17
  74.8 2.6 %collective-permute-done.13 = f32[256,64]{0,1:T(8,128)S(1)} collective-permute-done((f32[256,64]{0,1:T(8,128)S(1)}, f32[256,64]{0,1:T(8,128)S(1)}, u32[]{:S(2)}, u32[]{:S(2)}) %collective-permute-start.13) | collective-permute-done | bytes 65568 | tf_op jit(solution)/shard_map/ppermute | solution.py:17
  77.3 1.3 %collective-permute-start.14 = (f32[256,64]{0,1:T(8,128)S(1)}, f32[256,64]{0,1:T(8,128)S(1)}, u32[]{:S(2)}, u32[]{:S(2)}) collective-permute-start(f32[256,64]{0,1:T(8,128)S(1)} %add.139), channel_id=1, source_target_pairs={{0,32},{4,36},{8,40},{12,44},{16,48},{20,52},{24,56},{28,60},{32,0... | collective-permute-start | bytes 196616 | tf_op jit(solution)/shard_map/ppermute | solution.py:17
  78.7 4.5 %collective-permute-done.14 = f32[256,64]{0,1:T(8,128)S(1)} collective-permute-done((f32[256,64]{0,1:T(8,128)S(1)}, f32[256,64]{0,1:T(8,128)S(1)}, u32[]{:S(2)}, u32[]{:S(2)}) %collective-permute-start.14) | collective-permute-done | bytes 65568 | tf_op jit(solution)/shard_map/ppermute | solution.py:17
  83.2 1.4 %collective-permute-start.15 = (f32[256,64]{0,1:T(8,128)S(1)}, f32[256,64]{0,1:T(8,128)S(1)}, u32[]{:S(2)}, u32[]{:S(2)}) collective-permute-start(f32[256,64]{0,1:T(8,128)S(1)} %add.140), channel_id=1, source_target_pairs={{0,64},{4,68},{8,72},{12,76},{16,80},{20,84},{24,88},{28,92},{32,9... | collective-permute-start | bytes 196616 | tf_op jit(solution)/shard_map/ppermute | solution.py:17
  84.7 2.9 %collective-permute-done.15 = f32[256,64]{0,1:T(8,128)S(1)} collective-permute-done((f32[256,64]{0,1:T(8,128)S(1)}, f32[256,64]{0,1:T(8,128)S(1)}, u32[]{:S(2)}, u32[]{:S(2)}) %collective-permute-start.15) | collective-permute-done | bytes 65568 | tf_op jit(solution)/shard_map/ppermute | solution.py:17
  87.6 3.0 %collective-permute-start.16 = (f32[256,64]{0,1:T(8,128)S(1)}, f32[256,64]{0,1:T(8,128)S(1)}, u32[]{:S(2)}, u32[]{:S(2)}) collective-permute-start(f32[256,64]{0,1:T(8,128)S(1)} %add.141), channel_id=1, source_target_pairs={{0,128},{4,132},{8,136},{12,140},{16,144},{20,148},{24,152},{28,15... | collective-permute-start | bytes 196616 | tf_op jit(solution)/shard_map/ppermute | solution.py:17
  90.6 2.9 %collective-permute-done.16 = f32[256,64]{0,1:T(8,128)S(1)} collective-permute-done((f32[256,64]{0,1:T(8,128)S(1)}, f32[256,64]{0,1:T(8,128)S(1)}, u32[]{:S(2)}, u32[]{:S(2)}) %collective-permute-start.16) | collective-permute-done | bytes 65568 | tf_op jit(solution)/shard_map/ppermute | solution.py:17
  93.4 1.1 %collective-permute-start.17 = (f32[256,64]{0,1:T(8,128)S(1)}, f32[256,64]{0,1:T(8,128)S(1)}, u32[]{:S(2)}, u32[]{:S(2)}) collective-permute-start(f32[256,64]{0,1:T(8,128)S(1)} %add.142), channel_id=1, source_target_pairs={{0,8},{4,12},{8,0},{12,4},{16,24},{20,28},{24,16},{28,20},{32,40},... | collective-permute-start | bytes 196616 | tf_op jit(solution)/shard_map/ppermute | solution.py:17
  94.5 1.0 pad_maximum_fusion
  95.6 3.5 %collective-permute-done.17 = f32[256,64]{0,1:T(8,128)S(1)} collective-permute-done((f32[256,64]{0,1:T(8,128)S(1)}, f32[256,64]{0,1:T(8,128)S(1)}, u32[]{:S(2)}, u32[]{:S(2)}) %collective-permute-start.17) | collective-permute-done | bytes 65568 | tf_op jit(solution)/shard_map/ppermute | solution.py:17
  99.1 0.1 collective-permute-start.18
  99.2 0.8 copy.24
  100.1 4.1 %collective-permute-done.18 = f32[512,64]{0,1:T(8,128)S(1)} collective-permute-done((f32[512,64]{0,1:T(8,128)S(1)}, f32[512,64]{0,1:T(8,128)S(1)}, u32[]{:S(2)}, u32[]{:S(2)}) %collective-permute-start.18) | collective-permute-done | bytes 131104 | tf_op jit(solution)/shard_map/ppermute | solution.py:17
  104.1 0.7 maximum_select_fusion
  (52 shorter events, 0.4 us)
Async XLA Ops:
  0.6 35.8 %copy-start = (f32[1024,64]{0,1:T(8,128)S(1)}, f32[1024,64]{0,1:T(8,128)}, u32[]{:S(2)}) copy-start(f32[1024,64]{0,1:T(8,128)} %param.16) | copy-start | bytes 786436
  0.6 6.5 %copy-start.1 = (bf16[8,64,1024]{2,1,0:T(8,128)(2,1)S(1)}, bf16[8,64,1024]{2,1,0:T(8,128)(2,1)}, u32[]{:S(2)}) copy-start(bf16[8,64,1024]{2,1,0:T(8,128)(2,1)} %param.11) | copy-start | bytes 3145732
  0.7 2.4 %copy-start.3 = (bf16[8,64,128]{2,1,0:T(8,128)(2,1)S(1)}, bf16[8,64,128]{2,1,0:T(8,128)(2,1)}, u32[]{:S(2)}) copy-start(bf16[8,64,128]{2,1,0:T(8,128)(2,1)} %param.12) | copy-start | bytes 393220
  0.7 3.0 %copy-start.9 = (bf16[8,64,128]{2,1,0:T(8,128)(2,1)S(1)}, bf16[8,64,128]{2,1,0:T(8,128)(2,1)}, u32[]{:S(2)}) copy-start(bf16[8,64,128]{2,1,0:T(8,128)(2,1)} %param.13) | copy-start | bytes 393220
  4.0 5.6 %collective-permute-start = (bf16[8,16,128]{2,1,0:T(8,128)(2,1)S(1)}, bf16[8,16,128]{2,1,0:T(8,128)(2,1)S(1)}, u32[]{:S(2)}, u32[]{:S(2)}) collective-permute-start(bf16[8,16,128]{2,1,0:T(8,128)(2,1)S(1)} %fusion.37), channel_id=1, source_target_pairs={{0,128},{4,132},{8,136},{12,140},{16,144},{20,148},{24,152},{28,15... | collective-permute-start | bytes 98312 | tf_op jit(solution)/shard_map/ppermute | solution.py:17
  8.8 0.8 copy-start.8
  14.7 4.0 %collective-permute-start.1 = (bf16[256,1024]{1,0:T(8,128)(2,1)}, bf16[256,1024]{1,0:T(8,128)(2,1)}, u32[]{:S(2)}, u32[]{:S(2)}) collective-permute-start(bf16[256,1024]{1,0:T(8,128)(2,1)} %fusion.20), channel_id=1, source_target_pairs={{0,1},{1,0},{2,3},{3,2},{4,5},{5,4},{6,7},{7,6},{8,9},{9,8},{10,11... | collective-permute-start | bytes 1572872 | tf_op jit(solution)/shard_map/ppermute | solution.py:17
  14.8 3.9 %copy-start.2 = (bf16[8,64,1024]{2,1,0:T(8,128)(2,1)S(1)}, bf16[8,64,1024]{2,1,0:T(8,128)(2,1)}, u32[]{:S(2)}) copy-start(bf16[8,64,1024]{2,1,0:T(8,128)(2,1)} %param.10) | copy-start | bytes 3145732
  18.2 6.2 %collective-permute-start.4 = (bf16[256,1024]{1,0:T(8,128)(2,1)}, bf16[256,1024]{1,0:T(8,128)(2,1)}, u32[]{:S(2)}, u32[]{:S(2)}) collective-permute-start(bf16[256,1024]{1,0:T(8,128)(2,1)} %fusion.23), channel_id=1, source_target_pairs={{0,1},{1,0},{2,3},{3,2},{4,5},{5,4},{6,7},{7,6},{8,9},{9,8},{10,11... | collective-permute-start | bytes 1572872 | tf_op jit(solution)/shard_map/ppermute | solution.py:17
  21.2 14.9 %collective-permute-start.3 = (bf16[256,1024]{1,0:T(8,128)(2,1)S(1)}, bf16[256,1024]{1,0:T(8,128)(2,1)S(1)}, u32[]{:S(2)}, u32[]{:S(2)}) collective-permute-start(bf16[256,1024]{1,0:T(8,128)(2,1)S(1)} %add_convert_fusion.3), channel_id=1, source_target_pairs={{0,2},{1,3},{2,0},{3,1},{4,6},{5,7},{6,4},{7,5},{8,10},{9,11},{10,... | collective-permute-start | bytes 1572872 | tf_op jit(solution)/shard_map/ppermute | solution.py:17
  24.3 11.8 %collective-permute-start.2 = (bf16[256,1024]{1,0:T(8,128)(2,1)S(1)}, bf16[256,1024]{1,0:T(8,128)(2,1)S(1)}, u32[]{:S(2)}, u32[]{:S(2)}) collective-permute-start(bf16[256,1024]{1,0:T(8,128)(2,1)S(1)} %fusion.26), channel_id=1, source_target_pairs={{0,1},{1,0},{2,3},{3,2},{4,5},{5,4},{6,7},{7,6},{8,9},{9,8},{10,11... | collective-permute-start | bytes 1572872 | tf_op jit(solution)/shard_map/ppermute | solution.py:17
  27.6 20.3 %collective-permute-start.6 = (bf16[256,1024]{1,0:T(8,128)(2,1)}, bf16[256,1024]{1,0:T(8,128)(2,1)S(1)}, u32[]{:S(2)}, u32[]{:S(2)}) collective-permute-start(bf16[256,1024]{1,0:T(8,128)(2,1)} %add_convert_fusion.1), channel_id=1, source_target_pairs={{0,2},{1,3},{2,0},{3,1},{4,6},{5,7},{6,4},{7,5},{8,10},{9,11},{10,... | collective-permute-start | bytes 1572872 | tf_op jit(solution)/shard_map/ppermute | solution.py:17
  32.0 15.9 %collective-permute-start.5 = (bf16[256,1024]{1,0:T(8,128)(2,1)}, bf16[256,1024]{1,0:T(8,128)(2,1)S(1)}, u32[]{:S(2)}, u32[]{:S(2)}) collective-permute-start(bf16[256,1024]{1,0:T(8,128)(2,1)} %fusion.29), channel_id=1, source_target_pairs={{0,1},{1,0},{2,3},{3,2},{4,5},{5,4},{6,7},{7,6},{8,9},{9,8},{10,11... | collective-permute-start | bytes 1572872 | tf_op jit(solution)/shard_map/ppermute | solution.py:17
  34.5 2.0 %copy-start.4 = (f32[1024]{0:T(1024)S(1)}, f32[1024]{0:T(1024)}, u32[]{:S(2)}) copy-start(f32[1024]{0:T(1024)} %param.15) | copy-start | bytes 12292
  36.1 2.2 %copy-start.5 = (s32[8,64]{1,0:T(8,128)S(1)}, s32[8,64]{1,0:T(8,128)}, u32[]{:S(2)}) copy-start(s32[8,64]{1,0:T(8,128)} %param.19) | copy-start | bytes 6148
  38.3 3.3 %collective-permute-start.7 = (f32[256,65]{0,1:T(8,128)}, f32[256,65]{0,1:T(8,128)S(1)}, u32[]{:S(2)}, u32[]{:S(2)}) collective-permute-start(f32[256,65]{0,1:T(8,128)} %pad_maximum_fusion.2), channel_id=1, source_target_pairs={{0,1},{1,0},{2,3},{3,2},{4,5},{5,4},{6,7},{7,6},{8,9},{9,8},{10,11... | collective-permute-start | bytes 199688 | tf_op jit(solution)/shard_map/ppermute | solution.py:17
  41.6 6.4 %collective-permute-start.8 = (f32[256,65]{0,1:T(8,128)S(1)}, f32[256,65]{0,1:T(8,128)S(1)}, u32[]{:S(2)}, u32[]{:S(2)}) collective-permute-start(f32[256,65]{0,1:T(8,128)S(1)} %fusion.110), channel_id=1, source_target_pairs={{0,2},{1,3},{2,0},{3,1},{4,6},{5,7},{6,4},{7,5},{8,10},{9,11},{10,... | collective-permute-start | bytes 199688 | tf_op jit(solution)/shard_map/ppermute | solution.py:17
  47.9 3.8 %copy-start.7 = (s32[256]{0:T(256)S(1)}, s32[256]{0:T(256)}, u32[]{:S(2)}) copy-start(s32[256]{0:T(256)} %eq.86) | copy-start | bytes 3076
  48.3 7.0 %copy-start.6 = (s32[256]{0:T(256)S(1)}, s32[256]{0:T(256)}, u32[]{:S(2)}) copy-start(s32[256]{0:T(256)} %eq.90) | copy-start | bytes 3076
  49.5 1.4 %collective-permute-start.9 = (f32[256,65]{0,1:T(8,128)S(1)}, f32[256,65]{0,1:T(8,128)S(1)}, u32[]{:S(2)}, u32[]{:S(2)}) collective-permute-start(f32[256,65]{0,1:T(8,128)S(1)} %pad_maximum_fusion.3), channel_id=1, source_target_pairs={{0,1},{1,0},{2,3},{3,2},{4,5},{5,4},{6,7},{7,6},{8,9},{9,8},{10,11... | collective-permute-start | bytes 199688 | tf_op jit(solution)/shard_map/ppermute | solution.py:17
  50.9 4.4 %collective-permute-start.10 = (f32[256,65]{0,1:T(8,128)S(1)}, f32[256,65]{0,1:T(8,128)S(1)}, u32[]{:S(2)}, u32[]{:S(2)}) collective-permute-start(f32[256,65]{0,1:T(8,128)S(1)} %fusion.109), channel_id=1, source_target_pairs={{0,2},{1,3},{2,0},{3,1},{4,6},{5,7},{6,4},{7,5},{8,10},{9,11},{10,... | collective-permute-start | bytes 199688 | tf_op jit(solution)/shard_map/ppermute | solution.py:17
  56.4 5.1 %collective-permute-start.11 = (f32[512,64]{0,1:T(8,128)S(1)}, f32[512,64]{0,1:T(8,128)S(1)}, u32[]{:S(2)}, u32[]{:S(2)}) collective-permute-start(f32[512,64]{0,1:T(8,128)S(1)} %slice_select_fusion), channel_id=1, source_target_pairs={{0,4},{4,0},{8,12},{12,8},{16,20},{20,16},{24,28},{28,24},{32,36},... | collective-permute-start | bytes 393224 | tf_op jit(solution)/shard_map/ppermute | solution.py:17
  61.5 5.6 %collective-permute-start.12 = (f32[256,64]{0,1:T(8,128)S(1)}, f32[256,64]{0,1:T(8,128)S(1)}, u32[]{:S(2)}, u32[]{:S(2)}) collective-permute-start(f32[256,64]{0,1:T(8,128)S(1)} %slice_select_fusion.1), channel_id=1, source_target_pairs={{0,8},{4,12},{8,0},{12,4},{16,24},{20,28},{24,16},{28,20},{32,40},... | collective-permute-start | bytes 196616 | tf_op jit(solution)/shard_map/ppermute | solution.py:17
  67.1 10.2 %collective-permute-start.13 = (f32[256,64]{0,1:T(8,128)S(1)}, f32[256,64]{0,1:T(8,128)S(1)}, u32[]{:S(2)}, u32[]{:S(2)}) collective-permute-start(f32[256,64]{0,1:T(8,128)S(1)} %select_add_fusion.1), channel_id=1, source_target_pairs={{0,16},{4,20},{8,24},{12,28},{16,0},{20,4},{24,8},{28,12},{32,48},... | collective-permute-start | bytes 196616 | tf_op jit(solution)/shard_map/ppermute | solution.py:17
  77.3 5.9 %collective-permute-start.14 = (f32[256,64]{0,1:T(8,128)S(1)}, f32[256,64]{0,1:T(8,128)S(1)}, u32[]{:S(2)}, u32[]{:S(2)}) collective-permute-start(f32[256,64]{0,1:T(8,128)S(1)} %add.139), channel_id=1, source_target_pairs={{0,32},{4,36},{8,40},{12,44},{16,48},{20,52},{24,56},{28,60},{32,0... | collective-permute-start | bytes 196616 | tf_op jit(solution)/shard_map/ppermute | solution.py:17
  83.2 4.4 %collective-permute-start.15 = (f32[256,64]{0,1:T(8,128)S(1)}, f32[256,64]{0,1:T(8,128)S(1)}, u32[]{:S(2)}, u32[]{:S(2)}) collective-permute-start(f32[256,64]{0,1:T(8,128)S(1)} %add.140), channel_id=1, source_target_pairs={{0,64},{4,68},{8,72},{12,76},{16,80},{20,84},{24,88},{28,92},{32,9... | collective-permute-start | bytes 196616 | tf_op jit(solution)/shard_map/ppermute | solution.py:17
  87.6 5.9 %collective-permute-start.16 = (f32[256,64]{0,1:T(8,128)S(1)}, f32[256,64]{0,1:T(8,128)S(1)}, u32[]{:S(2)}, u32[]{:S(2)}) collective-permute-start(f32[256,64]{0,1:T(8,128)S(1)} %add.141), channel_id=1, source_target_pairs={{0,128},{4,132},{8,136},{12,140},{16,144},{20,148},{24,152},{28,15... | collective-permute-start | bytes 196616 | tf_op jit(solution)/shard_map/ppermute | solution.py:17
  93.4 5.6 %collective-permute-start.17 = (f32[256,64]{0,1:T(8,128)S(1)}, f32[256,64]{0,1:T(8,128)S(1)}, u32[]{:S(2)}, u32[]{:S(2)}) collective-permute-start(f32[256,64]{0,1:T(8,128)S(1)} %add.142), channel_id=1, source_target_pairs={{0,8},{4,12},{8,0},{12,4},{16,24},{20,28},{24,16},{28,20},{32,40},... | collective-permute-start | bytes 196616 | tf_op jit(solution)/shard_map/ppermute | solution.py:17
  99.1 5.1 %collective-permute-start.18 = (f32[512,64]{0,1:T(8,128)S(1)}, f32[512,64]{0,1:T(8,128)S(1)}, u32[]{:S(2)}, u32[]{:S(2)}) collective-permute-start(f32[512,64]{0,1:T(8,128)S(1)} %maximum_select_fusion.1), channel_id=1, source_target_pairs={{0,4},{4,0},{8,12},{12,8},{16,20},{20,16},{24,28},{28,24},{32,36},... | collective-permute-start | bytes 393224 | tf_op jit(solution)/shard_map/ppermute | solution.py:17

commit v11 on v9

--- a/solution.py
+++ b/solution.py
@@ -206,7 +206,7 @@
         square_local = jnp.sum(hidden * hidden, axis=1)
         scaled = hidden * norm_gain
         raw_part = jnp.dot(
-            scaled, probe_weight, precision=lax.Precision.HIGHEST, preferred_element_type=jnp.float32
+            scaled, probe_weight, precision=lax.Precision.HIGH, preferred_element_type=jnp.float32
         )
         packed = jnp.concatenate([raw_part, square_local[:, None]], axis=1)
         packed = butterfly_sum(packed, "tensor", tensor_bits)
@@ -220,7 +220,7 @@
             normed,
             error,
             (((0,), (0,)), ((), ())),
-            precision=lax.Precision.HIGHEST,
+            precision=lax.Precision.HIGH,
             preferred_element_type=jnp.float32,
         )
         grad_local = grad_part if grad_local is None else grad_local + grad_part

time: 105 us -> 104 us (level)
  matrix products: 28 us -> 26.2 us
where the time goes in v11:
time: 104 us
  waiting for transfers between devices  40.1 us (39%)
  starting transfers between devices  28.4 us (27%)
  matrix products  26.2 us (25%)
  local copies, waits for them, and re-layouts  4.03 us (4%)
  other arithmetic  3.69 us (4%)
  between operations  1.08 us (1%)
    ppermute x19, waiting for transfers between devices, exchanged(): return lax.ppermute(block, axis, [(i, i ^ bit) for i in range(count)])  40.1 us
    ppermute x19, starting transfers between devices, exchanged(): return lax.ppermute(block, axis, [(i, i ^ bit) for i in range(count)])  28.4 us
    dot_general x8, matrix products, block(): return jnp.dot(heads, columns, preferred_element_type=jnp.float32)  19.5 us
  transfers between devices with their start and end apart: 19, of which 13 were waited for; matrix products, arithmetic and copies ran while one was open for 23% of the time, Pallas kernels for 0%

profile of v11, /device:TPU:24, one launch (start us, length us, event | category | flops | bytes accessed | tf_op | source)
XLA Modules:
  0.0 103.6 jit_solution(9763441367907487820)
XLA Ops:
  0.7 0.8 fusion.113
  1.6 1.5 %reshape.87 = bf16[8,512,128]{2,1,0:T(8,128)(2,1)S(1)} reshape(bf16[8,64,1024]{2,1,0:T(8,128)(2,1)} %param.11) | data formatting | bytes 2097152 | tf_op jit(solution)/shard_map/reshape | solution.py:118
  3.1 0.4 fusion.36
  3.5 0.2 fusion.116
  3.7 0.3 fusion.37
  4.0 3.1 %collective-permute-start = (bf16[8,16,128]{2,1,0:T(8,128)(2,1)S(1)}, bf16[8,16,128]{2,1,0:T(8,128)(2,1)S(1)}, u32[]{:S(2)}, u32[]{:S(2)}) collective-permute-start(bf16[8,16,128]{2,1,0:T(8,128)(2,1)S(1)} %fusion.37), channel_id=1, source_target_pairs={{0,128},{4,132},{8,136},{12,140},{16,144},{20,148},{24,152},{28,15... | collective-permute-start | bytes 98312 | tf_op jit(solution)/shard_map/ppermute | solution.py:17
  7.1 1.1 %fusion.115 = (f32[8,8,64]{2,1,0:T(8,128)S(1)}, f32[8,1,8,64,64]{3,4,2,0,1:T(8,128)S(1)}) fusion(bf16[8,64,128]{2,1,0:T(8,128)(2,1)S(1)} %copy-done.3, pred[64,64]{0,1:T(8,128)(4,1)S(1)} %iota_compare_fusion.9, bf16[8,64,1024]{2,1,0:T(8,128)(2,1)S(1)} %copy-done.1), kind=kOutput, calls=%fused_computation.146 | convolution fusion | flops 67891200 | bytes 2248704 | tf_op jit(solution)/shard_map/pqkgd,pskd->pkgqs/dot_general | solution.py:95
  8.3 0.5 fusion.1
  8.8 0.6 fusion.19
  9.5 0.1 fusion.58
  9.6 0.2 fusion.76
  9.8 1.5 %fusion.18 = bf16[8,512,128]{2,1,0:T(8,128)(2,1)S(1)} fusion(bf16[8,64,1,8,128]{4,1,3,0,2:T(8,128)(2,1)S(1)} %fusion.19, pred[8,512]{1,0:T(8,128)(4,1)S(1)} %fusion.58, s32[8,16]{1,0:T(8,128)S(1)} %add_bitcast_fusion, bf16[8,16,128]{2,0,1:T(8,128)(2,1)S(1)} %fusion.76), kind=kOutput, calls=%fused_computation.23 | convolution fusion | flops 17891328 | bytes 2134528 | tf_op jit(solution)/shard_map/jkr,jkd->jrd/dot_general | solution.py:178
  11.4 0.2 slice.63
  11.7 3.2 %fusion.20 = bf16[256,1024]{1,0:T(8,128)(2,1)} fusion(bf16[256,1024]{1,0:T(8,128)(2,1)S(1)} %slice.63, bf16[1024,4096]{1,0:T(8,128)(2,1)} %param.14, s32[]{:T(128)S(6)} %select_n.104), kind=kOutput, calls=%fused_computation.25 | convolution fusion | flops 537133056 | bytes 3145732 | tf_op jit(solution)/shard_map/dot_general | solution.py:53
  14.9 0.1 fusion.111
  15.0 0.2 slice.65
  15.2 2.3 %fusion.23 = bf16[256,1024]{1,0:T(8,128)(2,1)S(1)} fusion(bf16[256,1024]{1,0:T(8,128)(2,1)S(1)} %slice.65, bf16[1024,4096]{1,0:T(8,128)(2,1)} %param.14, s32[]{:T(128)S(6)} %select_n.104), kind=kOutput, calls=%fused_computation.26 | convolution fusion | flops 537133056 | bytes 3145732 | tf_op jit(solution)/shard_map/dot_general | solution.py:53
  17.5 0.6 collective-permute-start.4
  18.1 0.1 eq.86
  18.2 0.1 eq.90
  18.3 2.4 %add_convert_fusion.3 = bf16[256,1024]{1,0:T(8,128)(2,1)S(1)} fusion(bf16[256,1024]{1,0:T(8,128)(2,1)} %collective-permute-done.1, bf16[256,1024]{1,0:T(8,128)(2,1)S(1)} %slice.63, bf16[1024,4096]{1,0:T(8,128)(2,1)} %param.14, s32[]{:T(128)S(6)} %select_n.103), kind=kOutput, calls=%fused_computation.53 | convolution fusion | flops 537657344 | bytes 3670020 | tf_op jit(solution)/shard_map/dot_general | solution.py:53
  20.7 0.8 collective-permute-start.3
  21.5 2.3 %fusion.26 = bf16[256,1024]{1,0:T(8,128)(2,1)S(1)} fusion(bf16[256,1024]{1,0:T(8,128)(2,1)S(1)} %slice.63, bf16[1024,4096]{1,0:T(8,128)(2,1)} %param.14, s32[]{:T(128)S(6)} %select_n.106), kind=kOutput, calls=%fused_computation.27 | convolution fusion | flops 537133056 | bytes 3145732 | tf_op jit(solution)/shard_map/dot_general | solution.py:73
  23.8 0.1 collective-permute-start.2
  23.9 2.4 %add_convert_fusion.1 = bf16[256,1024]{1,0:T(8,128)(2,1)S(1)} fusion(bf16[256,1024]{1,0:T(8,128)(2,1)} %collective-permute-done.4, bf16[256,1024]{1,0:T(8,128)(2,1)S(1)} %slice.65, bf16[1024,4096]{1,0:T(8,128)(2,1)} %param.14, s32[]{:T(128)S(6)} %select_n.103), kind=kOutput, calls=%fused_computation.51 | convolution fusion | flops 537657344 | bytes 3670020 | tf_op jit(solution)/shard_map/dot_general | solution.py:53
  26.3 2.3 %fusion.29 = bf16[256,1024]{1,0:T(8,128)(2,1)S(1)} fusion(bf16[256,1024]{1,0:T(8,128)(2,1)S(1)} %slice.65, bf16[1024,4096]{1,0:T(8,128)(2,1)} %param.14, s32[]{:T(128)S(6)} %select_n.106), kind=kOutput, calls=%fused_computation.28 | convolution fusion | flops 537133056 | bytes 3145732 | tf_op jit(solution)/shard_map/dot_general | solution.py:73
  28.7 0.6 collective-permute-start.5
  29.2 1.3 %collective-permute-start.6 = (bf16[256,1024]{1,0:T(8,128)(2,1)S(1)}, bf16[256,1024]{1,0:T(8,128)(2,1)S(1)}, u32[]{:S(2)}, u32[]{:S(2)}) collective-permute-start(bf16[256,1024]{1,0:T(8,128)(2,1)S(1)} %add_convert_fusion.1), channel_id=1, source_target_pairs={{0,2},{1,3},{2,0},{3,1},{4,6},{5,7},{6,4},{7,5},{8,10},{9,11},{10,... | collective-permute-start | bytes 1572872 | tf_op jit(solution)/shard_map/ppermute | solution.py:17
  30.5 2.3 %fusion.8 = f32[256,1024]{1,0:T(8,128)S(1)} fusion(bf16[256,1024]{1,0:T(8,128)(2,1)S(1)} %slice.63, bf16[1024,4096]{1,0:T(8,128)(2,1)} %param.14, s32[]{:T(128)S(6)} %select_n.105), kind=kOutput, calls=%fused_computation.11 | convolution fusion | flops 536870912 | bytes 3670020 | tf_op jit(solution)/shard_map/dot_general | solution.py:73
  32.8 2.3 %fusion.6 = f32[256,1024]{1,0:T(8,128)S(1)} fusion(bf16[256,1024]{1,0:T(8,128)(2,1)S(1)} %slice.65, bf16[1024,4096]{1,0:T(8,128)(2,1)} %param.14, s32[]{:T(128)S(6)} %select_n.105), kind=kOutput, calls=%fused_computation.9 | convolution fusion | flops 536870912 | bytes 3670020 | tf_op jit(solution)/shard_map/dot_general | solution.py:73
  35.1 0.4 collective-permute-done.3
  35.6 0.4 multiply_reduce_fusion.1
  36.0 0.7 fusion.50
  36.7 0.1 collective-permute-start.7
  36.8 9.1 %collective-permute-done.6 = bf16[256,1024]{1,0:T(8,128)(2,1)S(1)} collective-permute-done((bf16[256,1024]{1,0:T(8,128)(2,1)S(1)}, bf16[256,1024]{1,0:T(8,128)(2,1)S(1)}, u32[]{:S(2)}, u32[]{:S(2)}) %collective-permute-start.6) | collective-permute-done | bytes 524320 | tf_op jit(solution)/shard_map/ppermute | solution.py:17
  45.9 0.4 multiply_reduce_fusion
  46.3 0.7 fusion.47
  47.0 0.1 collective-permute-start.9
  47.1 0.8 collective-permute-start.8
  48.0 0.4 collective-permute-done.9
  48.4 1.0 collective-permute-start.10
  49.3 3.0 %collective-permute-done.8 = f32[256,65]{0,1:T(8,128)S(1)} collective-permute-done((f32[256,65]{0,1:T(8,128)S(1)}, f32[256,65]{0,1:T(8,128)S(1)}, u32[]{:S(2)}, u32[]{:S(2)}) %collective-permute-start.8) | collective-permute-done | bytes 66592 | tf_op jit(solution)/shard_map/ppermute | solution.py:17
  52.4 1.1 %collective-permute-done.10 = f32[256,65]{0,1:T(8,128)S(1)} collective-permute-done((f32[256,65]{0,1:T(8,128)S(1)}, f32[256,65]{0,1:T(8,128)S(1)}, u32[]{:S(2)}, u32[]{:S(2)}) %collective-permute-start.10) | collective-permute-done | bytes 66592 | tf_op jit(solution)/shard_map/ppermute | solution.py:17
  53.5 0.6 fusion.42
  54.1 0.6 fusion.32
  54.7 2.0 %collective-permute-start.11 = (f32[512,64]{0,1:T(8,128)S(1)}, f32[512,64]{0,1:T(8,128)S(1)}, u32[]{:S(2)}, u32[]{:S(2)}) collective-permute-start(f32[512,64]{0,1:T(8,128)S(1)} %slice_select_fusion), channel_id=1, source_target_pairs={{0,4},{4,0},{8,12},{12,8},{16,20},{20,16},{24,28},{28,24},{32,36},... | collective-permute-start | bytes 393224 | tf_op jit(solution)/shard_map/ppermute | solution.py:17
  56.7 3.3 %collective-permute-done.11 = f32[512,64]{0,1:T(8,128)S(1)} collective-permute-done((f32[512,64]{0,1:T(8,128)S(1)}, f32[512,64]{0,1:T(8,128)S(1)}, u32[]{:S(2)}, u32[]{:S(2)}) %collective-permute-start.11) | collective-permute-done | bytes 131104 | tf_op jit(solution)/shard_map/ppermute | solution.py:17
  60.1 3.4 %collective-permute-start.12 = (f32[256,64]{0,1:T(8,128)S(1)}, f32[256,64]{0,1:T(8,128)S(1)}, u32[]{:S(2)}, u32[]{:S(2)}) collective-permute-start(f32[256,64]{0,1:T(8,128)S(1)} %slice_select_fusion.1), channel_id=1, source_target_pairs={{0,8},{4,12},{8,0},{12,4},{16,24},{20,28},{24,16},{28,20},{32,40},... | collective-permute-start | bytes 196616 | tf_op jit(solution)/shard_map/ppermute | solution.py:17
  63.4 2.2 %collective-permute-done.12 = f32[256,64]{0,1:T(8,128)S(1)} collective-permute-done((f32[256,64]{0,1:T(8,128)S(1)}, f32[256,64]{0,1:T(8,128)S(1)}, u32[]{:S(2)}, u32[]{:S(2)}) %collective-permute-start.12) | collective-permute-done | bytes 65568 | tf_op jit(solution)/shard_map/ppermute | solution.py:17
  65.7 7.5 %collective-permute-start.13 = (f32[256,64]{0,1:T(8,128)S(1)}, f32[256,64]{0,1:T(8,128)S(1)}, u32[]{:S(2)}, u32[]{:S(2)}) collective-permute-start(f32[256,64]{0,1:T(8,128)S(1)} %select_add_fusion.1), channel_id=1, source_target_pairs={{0,16},{4,20},{8,24},{12,28},{16,0},{20,4},{24,8},{28,12},{32,48},... | collective-permute-start | bytes 196616 | tf_op jit(solution)/shard_map/ppermute | solution.py:17
  73.1 2.9 %collective-permute-done.13 = f32[256,64]{0,1:T(8,128)S(1)} collective-permute-done((f32[256,64]{0,1:T(8,128)S(1)}, f32[256,64]{0,1:T(8,128)S(1)}, u32[]{:S(2)}, u32[]{:S(2)}) %collective-permute-start.13) | collective-permute-done | bytes 65568 | tf_op jit(solution)/shard_map/ppermute | solution.py:17
  76.1 1.3 %collective-permute-start.14 = (f32[256,64]{0,1:T(8,128)S(1)}, f32[256,64]{0,1:T(8,128)S(1)}, u32[]{:S(2)}, u32[]{:S(2)}) collective-permute-start(f32[256,64]{0,1:T(8,128)S(1)} %add.139), channel_id=1, source_target_pairs={{0,32},{4,36},{8,40},{12,44},{16,48},{20,52},{24,56},{28,60},{32,0... | collective-permute-start | bytes 196616 | tf_op jit(solution)/shard_map/ppermute | solution.py:17
  77.4 4.5 %collective-permute-done.14 = f32[256,64]{0,1:T(8,128)S(1)} collective-permute-done((f32[256,64]{0,1:T(8,128)S(1)}, f32[256,64]{0,1:T(8,128)S(1)}, u32[]{:S(2)}, u32[]{:S(2)}) %collective-permute-start.14) | collective-permute-done | bytes 65568 | tf_op jit(solution)/shard_map/ppermute | solution.py:17
  82.0 1.4 %collective-permute-start.15 = (f32[256,64]{0,1:T(8,128)S(1)}, f32[256,64]{0,1:T(8,128)S(1)}, u32[]{:S(2)}, u32[]{:S(2)}) collective-permute-start(f32[256,64]{0,1:T(8,128)S(1)} %add.140), channel_id=1, source_target_pairs={{0,64},{4,68},{8,72},{12,76},{16,80},{20,84},{24,88},{28,92},{32,9... | collective-permute-start | bytes 196616 | tf_op jit(solution)/shard_map/ppermute | solution.py:17
  83.4 2.9 %collective-permute-done.15 = f32[256,64]{0,1:T(8,128)S(1)} collective-permute-done((f32[256,64]{0,1:T(8,128)S(1)}, f32[256,64]{0,1:T(8,128)S(1)}, u32[]{:S(2)}, u32[]{:S(2)}) %collective-permute-start.15) | collective-permute-done | bytes 65568 | tf_op jit(solution)/shard_map/ppermute | solution.py:17
  86.3 3.0 %collective-permute-start.16 = (f32[256,64]{0,1:T(8,128)S(1)}, f32[256,64]{0,1:T(8,128)S(1)}, u32[]{:S(2)}, u32[]{:S(2)}) collective-permute-start(f32[256,64]{0,1:T(8,128)S(1)} %add.141), channel_id=1, source_target_pairs={{0,128},{4,132},{8,136},{12,140},{16,144},{20,148},{24,152},{28,15... | collective-permute-start | bytes 196616 | tf_op jit(solution)/shard_map/ppermute | solution.py:17
  89.3 1.0 %pad_maximum_fusion = bf16[512,1024]{1,0:T(8,128)(2,1)} fusion(bf16[256,1024]{1,0:T(8,128)(2,1)S(1)} %get-tuple-element.21, bf16[256,1024]{1,0:T(8,128)(2,1)S(1)} %get-tuple-element.19), kind=kLoop, calls=%fused_computation.41 | loop fusion | flops 2097152 | bytes 2097152 | tf_op jit(solution)/shard_map/concatenate | solution.py:229
  90.4 1.8 %collective-permute-done.16 = f32[256,64]{0,1:T(8,128)S(1)} collective-permute-done((f32[256,64]{0,1:T(8,128)S(1)}, f32[256,64]{0,1:T(8,128)S(1)}, u32[]{:S(2)}, u32[]{:S(2)}) %collective-permute-start.16) | collective-permute-done | bytes 65568 | tf_op jit(solution)/shard_map/ppermute | solution.py:17
  92.2 1.3 %collective-permute-start.17 = (f32[256,64]{0,1:T(8,128)S(1)}, f32[256,64]{0,1:T(8,128)S(1)}, u32[]{:S(2)}, u32[]{:S(2)}) collective-permute-start(f32[256,64]{0,1:T(8,128)S(1)} %add.142), channel_id=1, source_target_pairs={{0,8},{4,12},{8,0},{12,4},{16,24},{20,28},{24,16},{28,20},{32,40},... | collective-permute-start | bytes 196616 | tf_op jit(solution)/shard_map/ppermute | solution.py:17
  93.5 4.3 %collective-permute-done.17 = f32[256,64]{0,1:T(8,128)S(1)} collective-permute-done((f32[256,64]{0,1:T(8,128)S(1)}, f32[256,64]{0,1:T(8,128)S(1)}, u32[]{:S(2)}, u32[]{:S(2)}) %collective-permute-start.17) | collective-permute-done | bytes 65568 | tf_op jit(solution)/shard_map/ppermute | solution.py:17
  97.8 0.1 collective-permute-start.18
  97.9 0.8 copy.24
  98.8 4.1 %collective-permute-done.18 = f32[512,64]{0,1:T(8,128)S(1)} collective-permute-done((f32[512,64]{0,1:T(8,128)S(1)}, f32[512,64]{0,1:T(8,128)S(1)}, u32[]{:S(2)}, u32[]{:S(2)}) %collective-permute-start.18) | collective-permute-done | bytes 131104 | tf_op jit(solution)/shard_map/ppermute | solution.py:17
  102.8 0.7 maximum_select_fusion
  (48 shorter events, 0.4 us)
Async XLA Ops:
  0.6 35.3 %copy-start = (f32[1024,64]{0,1:T(8,128)S(1)}, f32[1024,64]{0,1:T(8,128)}, u32[]{:S(2)}) copy-start(f32[1024,64]{0,1:T(8,128)} %param.16) | copy-start | bytes 786436
  0.6 6.5 %copy-start.1 = (bf16[8,64,1024]{2,1,0:T(8,128)(2,1)S(1)}, bf16[8,64,1024]{2,1,0:T(8,128)(2,1)}, u32[]{:S(2)}) copy-start(bf16[8,64,1024]{2,1,0:T(8,128)(2,1)} %param.11) | copy-start | bytes 3145732
  0.7 2.4 %copy-start.3 = (bf16[8,64,128]{2,1,0:T(8,128)(2,1)S(1)}, bf16[8,64,128]{2,1,0:T(8,128)(2,1)}, u32[]{:S(2)}) copy-start(bf16[8,64,128]{2,1,0:T(8,128)(2,1)} %param.12) | copy-start | bytes 393220
  0.7 3.0 %copy-start.7 = (bf16[8,64,128]{2,1,0:T(8,128)(2,1)S(1)}, bf16[8,64,128]{2,1,0:T(8,128)(2,1)}, u32[]{:S(2)}) copy-start(bf16[8,64,128]{2,1,0:T(8,128)(2,1)} %param.13) | copy-start | bytes 393220
  4.0 5.6 %collective-permute-start = (bf16[8,16,128]{2,1,0:T(8,128)(2,1)S(1)}, bf16[8,16,128]{2,1,0:T(8,128)(2,1)S(1)}, u32[]{:S(2)}, u32[]{:S(2)}) collective-permute-start(bf16[8,16,128]{2,1,0:T(8,128)(2,1)S(1)} %fusion.37), channel_id=1, source_target_pairs={{0,128},{4,132},{8,136},{12,140},{16,144},{20,148},{24,152},{28,15... | collective-permute-start | bytes 98312 | tf_op jit(solution)/shard_map/ppermute | solution.py:17
  8.8 0.8 copy-start.6
  11.6 3.2 %copy-start.2 = (bf16[8,64,1024]{2,1,0:T(8,128)(2,1)S(1)}, bf16[8,64,1024]{2,1,0:T(8,128)(2,1)}, u32[]{:S(2)}) copy-start(bf16[8,64,1024]{2,1,0:T(8,128)(2,1)} %param.10) | copy-start | bytes 3145732
  14.8 3.4 %collective-permute-start.1 = (bf16[256,1024]{1,0:T(8,128)(2,1)}, bf16[256,1024]{1,0:T(8,128)(2,1)}, u32[]{:S(2)}, u32[]{:S(2)}) collective-permute-start(bf16[256,1024]{1,0:T(8,128)(2,1)} %fusion.20), channel_id=1, source_target_pairs={{0,1},{1,0},{2,3},{3,2},{4,5},{5,4},{6,7},{7,6},{8,9},{9,8},{10,11... | collective-permute-start | bytes 1572872 | tf_op jit(solution)/shard_map/ppermute | solution.py:17
  15.0 3.2 %copy-start.5 = (s32[8,64]{1,0:T(8,128)S(1)}, s32[8,64]{1,0:T(8,128)}, u32[]{:S(2)}) copy-start(s32[8,64]{1,0:T(8,128)} %param.19) | copy-start | bytes 6148
  17.5 6.4 %collective-permute-start.4 = (bf16[256,1024]{1,0:T(8,128)(2,1)S(1)}, bf16[256,1024]{1,0:T(8,128)(2,1)}, u32[]{:S(2)}, u32[]{:S(2)}) collective-permute-start(bf16[256,1024]{1,0:T(8,128)(2,1)S(1)} %fusion.23), channel_id=1, source_target_pairs={{0,1},{1,0},{2,3},{3,2},{4,5},{5,4},{6,7},{7,6},{8,9},{9,8},{10,11... | collective-permute-start | bytes 1572872 | tf_op jit(solution)/shard_map/ppermute | solution.py:17
  20.7 14.9 %collective-permute-start.3 = (bf16[256,1024]{1,0:T(8,128)(2,1)S(1)}, bf16[256,1024]{1,0:T(8,128)(2,1)S(1)}, u32[]{:S(2)}, u32[]{:S(2)}) collective-permute-start(bf16[256,1024]{1,0:T(8,128)(2,1)S(1)} %add_convert_fusion.3), channel_id=1, source_target_pairs={{0,2},{1,3},{2,0},{3,1},{4,6},{5,7},{6,4},{7,5},{8,10},{9,11},{10,... | collective-permute-start | bytes 1572872 | tf_op jit(solution)/shard_map/ppermute | solution.py:17
  23.8 11.7 %collective-permute-start.2 = (bf16[256,1024]{1,0:T(8,128)(2,1)S(1)}, bf16[256,1024]{1,0:T(8,128)(2,1)S(1)}, u32[]{:S(2)}, u32[]{:S(2)}) collective-permute-start(bf16[256,1024]{1,0:T(8,128)(2,1)S(1)} %fusion.26), channel_id=1, source_target_pairs={{0,1},{1,0},{2,3},{3,2},{4,5},{5,4},{6,7},{7,6},{8,9},{9,8},{10,11... | collective-permute-start | bytes 1572872 | tf_op jit(solution)/shard_map/ppermute | solution.py:17
  28.7 8.1 %collective-permute-start.5 = (bf16[256,1024]{1,0:T(8,128)(2,1)S(1)}, bf16[256,1024]{1,0:T(8,128)(2,1)S(1)}, u32[]{:S(2)}, u32[]{:S(2)}) collective-permute-start(bf16[256,1024]{1,0:T(8,128)(2,1)S(1)} %fusion.29), channel_id=1, source_target_pairs={{0,1},{1,0},{2,3},{3,2},{4,5},{5,4},{6,7},{7,6},{8,9},{9,8},{10,11... | collective-permute-start | bytes 1572872 | tf_op jit(solution)/shard_map/ppermute | solution.py:17
  29.2 16.7 %collective-permute-start.6 = (bf16[256,1024]{1,0:T(8,128)(2,1)S(1)}, bf16[256,1024]{1,0:T(8,128)(2,1)S(1)}, u32[]{:S(2)}, u32[]{:S(2)}) collective-permute-start(bf16[256,1024]{1,0:T(8,128)(2,1)S(1)} %add_convert_fusion.1), channel_id=1, source_target_pairs={{0,2},{1,3},{2,0},{3,1},{4,6},{5,7},{6,4},{7,5},{8,10},{9,11},{10,... | collective-permute-start | bytes 1572872 | tf_op jit(solution)/shard_map/ppermute | solution.py:17
  35.1 0.9 copy-start.4
  36.7 10.4 %collective-permute-start.7 = (f32[256,65]{0,1:T(8,128)S(1)}, f32[256,65]{0,1:T(8,128)S(1)}, u32[]{:S(2)}, u32[]{:S(2)}) collective-permute-start(f32[256,65]{0,1:T(8,128)S(1)} %pad_maximum_fusion.2), channel_id=1, source_target_pairs={{0,1},{1,0},{2,3},{3,2},{4,5},{5,4},{6,7},{7,6},{8,9},{9,8},{10,11... | collective-permute-start | bytes 199688 | tf_op jit(solution)/shard_map/ppermute | solution.py:17
  47.0 1.4 %collective-permute-start.9 = (f32[256,65]{0,1:T(8,128)S(1)}, f32[256,65]{0,1:T(8,128)S(1)}, u32[]{:S(2)}, u32[]{:S(2)}) collective-permute-start(f32[256,65]{0,1:T(8,128)S(1)} %pad_maximum_fusion.3), channel_id=1, source_target_pairs={{0,1},{1,0},{2,3},{3,2},{4,5},{5,4},{6,7},{7,6},{8,9},{9,8},{10,11... | collective-permute-start | bytes 199688 | tf_op jit(solution)/shard_map/ppermute | solution.py:17
  47.1 5.2 %collective-permute-start.8 = (f32[256,65]{0,1:T(8,128)S(1)}, f32[256,65]{0,1:T(8,128)S(1)}, u32[]{:S(2)}, u32[]{:S(2)}) collective-permute-start(f32[256,65]{0,1:T(8,128)S(1)} %fusion.110), channel_id=1, source_target_pairs={{0,2},{1,3},{2,0},{3,1},{4,6},{5,7},{6,4},{7,5},{8,10},{9,11},{10,... | collective-permute-start | bytes 199688 | tf_op jit(solution)/shard_map/ppermute | solution.py:17
  48.4 5.1 %collective-permute-start.10 = (f32[256,65]{0,1:T(8,128)S(1)}, f32[256,65]{0,1:T(8,128)S(1)}, u32[]{:S(2)}, u32[]{:S(2)}) collective-permute-start(f32[256,65]{0,1:T(8,128)S(1)} %fusion.109), channel_id=1, source_target_pairs={{0,2},{1,3},{2,0},{3,1},{4,6},{5,7},{6,4},{7,5},{8,10},{9,11},{10,... | collective-permute-start | bytes 199688 | tf_op jit(solution)/shard_map/ppermute | solution.py:17
  54.7 5.3 %collective-permute-start.11 = (f32[512,64]{0,1:T(8,128)S(1)}, f32[512,64]{0,1:T(8,128)S(1)}, u32[]{:S(2)}, u32[]{:S(2)}) collective-permute-start(f32[512,64]{0,1:T(8,128)S(1)} %slice_select_fusion), channel_id=1, source_target_pairs={{0,4},{4,0},{8,12},{12,8},{16,20},{20,16},{24,28},{28,24},{32,36},... | collective-permute-start | bytes 393224 | tf_op jit(solution)/shard_map/ppermute | solution.py:17
  60.1 5.6 %collective-permute-start.12 = (f32[256,64]{0,1:T(8,128)S(1)}, f32[256,64]{0,1:T(8,128)S(1)}, u32[]{:S(2)}, u32[]{:S(2)}) collective-permute-start(f32[256,64]{0,1:T(8,128)S(1)} %slice_select_fusion.1), channel_id=1, source_target_pairs={{0,8},{4,12},{8,0},{12,4},{16,24},{20,28},{24,16},{28,20},{32,40},... | collective-permute-start | bytes 196616 | tf_op jit(solution)/shard_map/ppermute | solution.py:17
  65.7 10.4 %collective-permute-start.13 = (f32[256,64]{0,1:T(8,128)S(1)}, f32[256,64]{0,1:T(8,128)S(1)}, u32[]{:S(2)}, u32[]{:S(2)}) collective-permute-start(f32[256,64]{0,1:T(8,128)S(1)} %select_add_fusion.1), channel_id=1, source_target_pairs={{0,16},{4,20},{8,24},{12,28},{16,0},{20,4},{24,8},{28,12},{32,48},... | collective-permute-start | bytes 196616 | tf_op jit(solution)/shard_map/ppermute | solution.py:17
  76.1 5.9 %collective-permute-start.14 = (f32[256,64]{0,1:T(8,128)S(1)}, f32[256,64]{0,1:T(8,128)S(1)}, u32[]{:S(2)}, u32[]{:S(2)}) collective-permute-start(f32[256,64]{0,1:T(8,128)S(1)} %add.139), channel_id=1, source_target_pairs={{0,32},{4,36},{8,40},{12,44},{16,48},{20,52},{24,56},{28,60},{32,0... | collective-permute-start | bytes 196616 | tf_op jit(solution)/shard_map/ppermute | solution.py:17
  82.0 4.4 %collective-permute-start.15 = (f32[256,64]{0,1:T(8,128)S(1)}, f32[256,64]{0,1:T(8,128)S(1)}, u32[]{:S(2)}, u32[]{:S(2)}) collective-permute-start(f32[256,64]{0,1:T(8,128)S(1)} %add.140), channel_id=1, source_target_pairs={{0,64},{4,68},{8,72},{12,76},{16,80},{20,84},{24,88},{28,92},{32,9... | collective-permute-start | bytes 196616 | tf_op jit(solution)/shard_map/ppermute | solution.py:17
  86.3 5.9 %collective-permute-start.16 = (f32[256,64]{0,1:T(8,128)S(1)}, f32[256,64]{0,1:T(8,128)S(1)}, u32[]{:S(2)}, u32[]{:S(2)}) collective-permute-start(f32[256,64]{0,1:T(8,128)S(1)} %add.141), channel_id=1, source_target_pairs={{0,128},{4,132},{8,136},{12,140},{16,144},{20,148},{24,152},{28,15... | collective-permute-start | bytes 196616 | tf_op jit(solution)/shard_map/ppermute | solution.py:17
  92.2 5.6 %collective-permute-start.17 = (f32[256,64]{0,1:T(8,128)S(1)}, f32[256,64]{0,1:T(8,128)S(1)}, u32[]{:S(2)}, u32[]{:S(2)}) collective-permute-start(f32[256,64]{0,1:T(8,128)S(1)} %add.142), channel_id=1, source_target_pairs={{0,8},{4,12},{8,0},{12,4},{16,24},{20,28},{24,16},{28,20},{32,40},... | collective-permute-start | bytes 196616 | tf_op jit(solution)/shard_map/ppermute | solution.py:17
  97.8 5.1 %collective-permute-start.18 = (f32[512,64]{0,1:T(8,128)S(1)}, f32[512,64]{0,1:T(8,128)S(1)}, u32[]{:S(2)}, u32[]{:S(2)}) collective-permute-start(f32[512,64]{0,1:T(8,128)S(1)} %maximum_select_fusion.1), channel_id=1, source_target_pairs={{0,4},{4,0},{8,12},{12,8},{16,20},{20,16},{24,28},{28,24},{32,36},... | collective-permute-start | bytes 393224 | tf_op jit(solution)/shard_map/ppermute | solution.py:17

commit v12 on v11

--- a/solution.py
+++ b/solution.py
@@ -79,7 +79,7 @@
 def dp_bits(count):
     low = [1 << k for k in range(count.bit_length() - 1)]
     if count == 64:
-        return low[:2], low[2:]
+        return [low[0], low[4]], [low[1], low[2], low[3], low[5]]
     return [], low
 
 
@@ -175,24 +175,32 @@
     incoming = jnp.einsum(
         "jm,mkd->jkd", slot_pick, arrived, preferred_element_type=jnp.float32
     ).astype(jnp.bfloat16)
-    placed = jnp.einsum(
-        "jkr,jkd->jrd", pick_values, incoming, preferred_element_type=jnp.float32
-    ).astype(jnp.bfloat16)
     patch_mask = jnp.any(picks, axis=1)
-    patched = jnp.where(patch_mask[..., None], placed, flat_heads)
-
-    flat_patched = patched.reshape(token_count, -1)
     flat_residual = residual.reshape(token_count, feature_count)
+    chunk_count = 2 if prompt_count % 2 == 0 else 1
+    chunk = token_count // chunk_count
+    prompts_per_chunk = prompt_count // chunk_count
+    patched_chunks = []
+    for index in range(chunk_count):
+        prompts_here = slice(index * prompts_per_chunk, (index + 1) * prompts_per_chunk)
+        placed = jnp.einsum(
+            "jkr,jkd->jrd",
+            pick_values[prompts_here],
+            incoming[prompts_here],
+            preferred_element_type=jnp.float32,
+        ).astype(jnp.bfloat16)
+        patched_here = jnp.where(
+            patch_mask[prompts_here][..., None], placed, flat_heads[prompts_here]
+        )
+        patched_chunks.append(patched_here.reshape(chunk, -1))
     labels = concept_labels.reshape(token_count)
     concepts = probe_weight.shape[1]
     tensor_bits = [1 << k for k in range(lax.axis_size("tensor").bit_length() - 1)]
-    chunk_count = 2 if token_count % 2 == 0 else 1
-    chunk = token_count // chunk_count
     halves, sent_block = [], None
     for index in range(chunk_count):
         rows_here = slice(index * chunk, (index + 1) * chunk)
         heads_here, sent_block, from_far = far_half(
-            flat_patched[rows_here], out_weight, "tensor", sent_block
+            patched_chunks[index], out_weight, "tensor", sent_block
         )
         halves.append((heads_here, sent_block, from_far))
     attn_chunks, logit_chunks, grad_local = [], [], None

time: 104 us -> 103 us (level)
  starting transfers between devices: 28.4 us -> 26 us
  local copies, waits for them, and re-layouts: 4.03 us -> 5.25 us
    ppermute x19, starting transfers between devices: 28.4 us -> 26 us  [exchanged(): return lax.ppermute(block, axis, [(i, i ^ bit) for i in range(count)])]
    unnamed x17, local copies, waits for them, and re-layouts: 0.89 us -> 1.98 us
  transfers between devices with their start and end apart: 19 -> 19, of which waited for: 13 -> 13; matrix products, arithmetic and copies ran while one was open for 23% -> 24% of each run, Pallas kernels for 0% -> 0%
where the time goes in v12:
time: 103 us
  waiting for transfers between devices  40.7 us (40%)
  matrix products  26.2 us (25%)
  starting transfers between devices  26 us (25%)
  local copies, waits for them, and re-layouts  5.25 us (5%)
  other arithmetic  3.76 us (4%)
  between operations  1.08 us (1%)
    ppermute x19, waiting for transfers between devices, exchanged(): return lax.ppermute(block, axis, [(i, i ^ bit) for i in range(count)])  40.7 us
    ppermute x19, starting transfers between devices, exchanged(): return lax.ppermute(block, axis, [(i, i ^ bit) for i in range(count)])  26 us
    dot_general x8, matrix products, block(): return jnp.dot(heads, columns, preferred_element_type=jnp.float32)  19.4 us
  transfers between devices with their start and end apart: 19, of which 13 were waited for; matrix products, arithmetic and copies ran while one was open for 24% of the time, Pallas kernels for 0%

profile of v12, /device:TPU:24, one launch (start us, length us, event | category | flops | bytes accessed | tf_op | source)
XLA Modules:
  0.0 103.0 jit_solution(15502401422939164274)
XLA Ops:
  0.7 0.8 fusion.117
  1.6 1.5 %reshape.93 = bf16[8,512,128]{2,1,0:T(8,128)(2,1)S(1)} reshape(bf16[8,64,1024]{2,1,0:T(8,128)(2,1)} %param.11) | data formatting | bytes 2097152 | tf_op jit(solution)/shard_map/reshape | solution.py:118
  3.2 0.4 fusion.37
  3.6 0.2 fusion.121
  3.8 0.3 fusion.78
  4.2 3.1 %collective-permute-start = (bf16[8,16,128]{2,0,1:T(8,128)(2,1)S(1)}, bf16[8,16,128]{2,0,1:T(8,128)(2,1)S(1)}, u32[]{:S(2)}, u32[]{:S(2)}) collective-permute-start(bf16[8,16,128]{2,0,1:T(8,128)(2,1)S(1)} %fusion.65), channel_id=1, source_target_pairs={{0,128},{4,132},{8,136},{12,140},{16,144},{20,148},{24,152},{28,15... | collective-permute-start | bytes 98312 | tf_op jit(solution)/shard_map/ppermute | solution.py:17
  7.3 0.1 fusion.58
  7.4 1.1 %fusion.120 = (f32[8,8,64]{2,1,0:T(8,128)S(1)}, f32[8,1,8,64,64]{3,4,2,0,1:T(8,128)S(1)}) fusion(bf16[8,64,128]{2,1,0:T(8,128)(2,1)S(1)} %copy-done.3, pred[64,64]{0,1:T(8,128)(4,1)S(1)} %iota_compare_fusion.10, bf16[8,64,1024]{2,1,0:T(8,128)(2,1)S(1)} %copy-done.1), kind=kOutput, calls=%fused_computation.152 | convolution fusion | flops 67891200 | bytes 2248704 | tf_op jit(solution)/shard_map/pqkgd,pskd->pkgqs/dot_general | solution.py:95
  8.6 0.5 fusion.1
  9.1 0.6 fusion.18
  9.8 0.1 fusion.115
  9.9 1.1 %copy-done.2 = bf16[8,64,1024]{2,1,0:T(8,128)(2,1)S(1)} copy-done((bf16[8,64,1024]{2,1,0:T(8,128)(2,1)S(1)}, bf16[8,64,1024]{2,1,0:T(8,128)(2,1)}, u32[]{:S(2)}) %copy-start.2) | copy-done | bytes 1048600
  11.0 0.1 fusion.114
  11.1 0.2 convolution_convert_fusion.3
  11.3 0.8 fusion.31
  12.1 0.2 reshape.96
  12.4 3.1 %fusion.19 = bf16[256,1024]{1,0:T(8,128)(2,1)} fusion(bf16[256,1024]{1,0:T(8,128)(2,1)S(1)} %reshape.96, bf16[1024,4096]{1,0:T(8,128)(2,1)} %param.14, s32[]{:T(128)S(6)} %select_n.107), kind=kOutput, calls=%fused_computation.23 | convolution fusion | flops 537133056 | bytes 3145732 | tf_op jit(solution)/shard_map/dot_general | solution.py:53
  15.5 0.8 fusion.32
  16.3 0.2 reshape.97
  16.5 2.3 %fusion.22 = bf16[256,1024]{1,0:T(8,128)(2,1)S(1)} fusion(bf16[256,1024]{1,0:T(8,128)(2,1)S(1)} %reshape.97, bf16[1024,4096]{1,0:T(8,128)(2,1)} %param.14, s32[]{:T(128)S(6)} %select_n.107), kind=kOutput, calls=%fused_computation.24 | convolution fusion | flops 537133056 | bytes 3145732 | tf_op jit(solution)/shard_map/dot_general | solution.py:53
  18.8 0.6 collective-permute-start.4
  19.6 2.4 %add_convert_fusion.3 = bf16[256,1024]{1,0:T(8,128)(2,1)S(1)} fusion(bf16[256,1024]{1,0:T(8,128)(2,1)} %collective-permute-done.1, bf16[256,1024]{1,0:T(8,128)(2,1)S(1)} %reshape.96, bf16[1024,4096]{1,0:T(8,128)(2,1)} %param.14, s32[]{:T(128)S(6)} %select_n.106), kind=kOutput, calls=%fused_computation.54 | convolution fusion | flops 537657344 | bytes 3670020 | tf_op jit(solution)/shard_map/dot_general | solution.py:53
  22.0 0.8 collective-permute-start.3
  22.8 2.3 %fusion.25 = bf16[256,1024]{1,0:T(8,128)(2,1)S(1)} fusion(bf16[256,1024]{1,0:T(8,128)(2,1)S(1)} %reshape.96, bf16[1024,4096]{1,0:T(8,128)(2,1)} %param.14, s32[]{:T(128)S(6)} %select_n.109), kind=kOutput, calls=%fused_computation.25 | convolution fusion | flops 537133056 | bytes 3145732 | tf_op jit(solution)/shard_map/dot_general | solution.py:73
  25.1 0.1 collective-permute-start.2
  25.2 2.4 %add_convert_fusion.1 = bf16[256,1024]{1,0:T(8,128)(2,1)S(1)} fusion(bf16[256,1024]{1,0:T(8,128)(2,1)} %collective-permute-done.4, bf16[256,1024]{1,0:T(8,128)(2,1)S(1)} %reshape.97, bf16[1024,4096]{1,0:T(8,128)(2,1)} %param.14, s32[]{:T(128)S(6)} %select_n.106), kind=kOutput, calls=%fused_computation.52 | convolution fusion | flops 537657344 | bytes 3670020 | tf_op jit(solution)/shard_map/dot_general | solution.py:53
  27.6 2.3 %fusion.28 = bf16[256,1024]{1,0:T(8,128)(2,1)S(1)} fusion(bf16[256,1024]{1,0:T(8,128)(2,1)S(1)} %reshape.97, bf16[1024,4096]{1,0:T(8,128)(2,1)} %param.14, s32[]{:T(128)S(6)} %select_n.109), kind=kOutput, calls=%fused_computation.26 | convolution fusion | flops 537133056 | bytes 3145732 | tf_op jit(solution)/shard_map/dot_general | solution.py:73
  29.9 0.6 collective-permute-start.5
  30.5 1.3 %collective-permute-start.6 = (bf16[256,1024]{1,0:T(8,128)(2,1)S(1)}, bf16[256,1024]{1,0:T(8,128)(2,1)S(1)}, u32[]{:S(2)}, u32[]{:S(2)}) collective-permute-start(bf16[256,1024]{1,0:T(8,128)(2,1)S(1)} %add_convert_fusion.1), channel_id=1, source_target_pairs={{0,2},{1,3},{2,0},{3,1},{4,6},{5,7},{6,4},{7,5},{8,10},{9,11},{10,... | collective-permute-start | bytes 1572872 | tf_op jit(solution)/shard_map/ppermute | solution.py:17
  31.8 2.3 %fusion.8 = f32[256,1024]{1,0:T(8,128)S(1)} fusion(bf16[256,1024]{1,0:T(8,128)(2,1)S(1)} %reshape.96, bf16[1024,4096]{1,0:T(8,128)(2,1)} %param.14, s32[]{:T(128)S(6)} %select_n.108), kind=kOutput, calls=%fused_computation.11 | convolution fusion | flops 536870912 | bytes 3670020 | tf_op jit(solution)/shard_map/dot_general | solution.py:73
  34.1 2.3 %fusion.6 = f32[256,1024]{1,0:T(8,128)S(1)} fusion(bf16[256,1024]{1,0:T(8,128)(2,1)S(1)} %reshape.97, bf16[1024,4096]{1,0:T(8,128)(2,1)} %param.14, s32[]{:T(128)S(6)} %select_n.108), kind=kOutput, calls=%fused_computation.9 | convolution fusion | flops 536870912 | bytes 3670020 | tf_op jit(solution)/shard_map/dot_general | solution.py:73
  36.4 0.4 collective-permute-done.3
  36.9 0.4 multiply_reduce_fusion.1
  37.3 0.7 fusion.50
  38.1 9.1 %collective-permute-done.6 = bf16[256,1024]{1,0:T(8,128)(2,1)S(1)} collective-permute-done((bf16[256,1024]{1,0:T(8,128)(2,1)S(1)}, bf16[256,1024]{1,0:T(8,128)(2,1)S(1)}, u32[]{:S(2)}, u32[]{:S(2)}) %collective-permute-start.6) | collective-permute-done | bytes 524320 | tf_op jit(solution)/shard_map/ppermute | solution.py:17
  47.2 0.4 multiply_reduce_fusion
  47.6 0.7 fusion.47
  48.3 0.1 collective-permute-start.9
  48.4 0.8 collective-permute-start.8
  49.2 0.4 collective-permute-done.9
  49.6 1.0 collective-permute-start.10
  50.6 3.0 %collective-permute-done.8 = f32[256,65]{0,1:T(8,128)S(1)} collective-permute-done((f32[256,65]{0,1:T(8,128)S(1)}, f32[256,65]{0,1:T(8,128)S(1)}, u32[]{:S(2)}, u32[]{:S(2)}) %collective-permute-start.8) | collective-permute-done | bytes 66592 | tf_op jit(solution)/shard_map/ppermute | solution.py:17
  53.7 1.1 %collective-permute-done.10 = f32[256,65]{0,1:T(8,128)S(1)} collective-permute-done((f32[256,65]{0,1:T(8,128)S(1)}, f32[256,65]{0,1:T(8,128)S(1)}, u32[]{:S(2)}, u32[]{:S(2)}) %collective-permute-start.10) | collective-permute-done | bytes 66592 | tf_op jit(solution)/shard_map/ppermute | solution.py:17
  54.8 0.6 fusion.42
  55.4 0.6 fusion.33
  56.0 2.0 %collective-permute-start.11 = (f32[512,64]{0,1:T(8,128)S(1)}, f32[512,64]{0,1:T(8,128)S(1)}, u32[]{:S(2)}, u32[]{:S(2)}) collective-permute-start(f32[512,64]{0,1:T(8,128)S(1)} %slice_select_fusion), channel_id=1, source_target_pairs={{0,4},{4,0},{8,12},{12,8},{16,20},{20,16},{24,28},{28,24},{32,36},... | collective-permute-start | bytes 393224 | tf_op jit(solution)/shard_map/ppermute | solution.py:17
  58.0 3.3 %collective-permute-done.11 = f32[512,64]{0,1:T(8,128)S(1)} collective-permute-done((f32[512,64]{0,1:T(8,128)S(1)}, f32[512,64]{0,1:T(8,128)S(1)}, u32[]{:S(2)}, u32[]{:S(2)}) %collective-permute-start.11) | collective-permute-done | bytes 131104 | tf_op jit(solution)/shard_map/ppermute | solution.py:17
  61.4 0.7 collective-permute-start.12
  62.0 3.7 %collective-permute-done.12 = f32[256,64]{0,1:T(8,128)S(1)} collective-permute-done((f32[256,64]{0,1:T(8,128)S(1)}, f32[256,64]{0,1:T(8,128)S(1)}, u32[]{:S(2)}, u32[]{:S(2)}) %collective-permute-start.12) | collective-permute-done | bytes 65568 | tf_op jit(solution)/shard_map/ppermute | solution.py:17
  65.7 3.3 %collective-permute-start.13 = (f32[256,64]{0,1:T(8,128)S(1)}, f32[256,64]{0,1:T(8,128)S(1)}, u32[]{:S(2)}, u32[]{:S(2)}) collective-permute-start(f32[256,64]{0,1:T(8,128)S(1)} %select_add_fusion.1), channel_id=1, source_target_pairs={{0,8},{4,12},{8,0},{12,4},{16,24},{20,28},{24,16},{28,20},{32,40},... | collective-permute-start | bytes 196616 | tf_op jit(solution)/shard_map/ppermute | solution.py:17
  69.1 2.2 %collective-permute-done.13 = f32[256,64]{0,1:T(8,128)S(1)} collective-permute-done((f32[256,64]{0,1:T(8,128)S(1)}, f32[256,64]{0,1:T(8,128)S(1)}, u32[]{:S(2)}, u32[]{:S(2)}) %collective-permute-start.13) | collective-permute-done | bytes 65568 | tf_op jit(solution)/shard_map/ppermute | solution.py:17
  71.3 7.5 %collective-permute-start.14 = (f32[256,64]{0,1:T(8,128)S(1)}, f32[256,64]{0,1:T(8,128)S(1)}, u32[]{:S(2)}, u32[]{:S(2)}) collective-permute-start(f32[256,64]{0,1:T(8,128)S(1)} %add.139), channel_id=1, source_target_pairs={{0,16},{4,20},{8,24},{12,28},{16,0},{20,4},{24,8},{28,12},{32,48},... | collective-permute-start | bytes 196616 | tf_op jit(solution)/shard_map/ppermute | solution.py:17
  78.8 2.3 %collective-permute-done.14 = f32[256,64]{0,1:T(8,128)S(1)} collective-permute-done((f32[256,64]{0,1:T(8,128)S(1)}, f32[256,64]{0,1:T(8,128)S(1)}, u32[]{:S(2)}, u32[]{:S(2)}) %collective-permute-start.14) | collective-permute-done | bytes 65568 | tf_op jit(solution)/shard_map/ppermute | solution.py:17
  81.1 1.3 %collective-permute-start.15 = (f32[256,64]{0,1:T(8,128)S(1)}, f32[256,64]{0,1:T(8,128)S(1)}, u32[]{:S(2)}, u32[]{:S(2)}) collective-permute-start(f32[256,64]{0,1:T(8,128)S(1)} %add.140), channel_id=1, source_target_pairs={{0,32},{4,36},{8,40},{12,44},{16,48},{20,52},{24,56},{28,60},{32,0... | collective-permute-start | bytes 196616 | tf_op jit(solution)/shard_map/ppermute | solution.py:17
  82.5 4.5 %collective-permute-done.15 = f32[256,64]{0,1:T(8,128)S(1)} collective-permute-done((f32[256,64]{0,1:T(8,128)S(1)}, f32[256,64]{0,1:T(8,128)S(1)}, u32[]{:S(2)}, u32[]{:S(2)}) %collective-permute-start.15) | collective-permute-done | bytes 65568 | tf_op jit(solution)/shard_map/ppermute | solution.py:17
  87.0 1.7 %collective-permute-start.16 = (f32[256,64]{0,1:T(8,128)S(1)}, f32[256,64]{0,1:T(8,128)S(1)}, u32[]{:S(2)}, u32[]{:S(2)}) collective-permute-start(f32[256,64]{0,1:T(8,128)S(1)} %add.141), channel_id=1, source_target_pairs={{0,128},{4,132},{8,136},{12,140},{16,144},{20,148},{24,152},{28,15... | collective-permute-start | bytes 196616 | tf_op jit(solution)/shard_map/ppermute | solution.py:17
  88.7 1.0 %pad_maximum_fusion = bf16[512,1024]{1,0:T(8,128)(2,1)} fusion(bf16[256,1024]{1,0:T(8,128)(2,1)S(1)} %get-tuple-element.24, bf16[256,1024]{1,0:T(8,128)(2,1)S(1)} %get-tuple-element.22), kind=kLoop, calls=%fused_computation.42 | loop fusion | flops 2097152 | bytes 2097152 | tf_op jit(solution)/shard_map/concatenate | solution.py:237
  89.7 3.2 %collective-permute-done.16 = f32[256,64]{0,1:T(8,128)S(1)} collective-permute-done((f32[256,64]{0,1:T(8,128)S(1)}, f32[256,64]{0,1:T(8,128)S(1)}, u32[]{:S(2)}, u32[]{:S(2)}) %collective-permute-start.16) | collective-permute-done | bytes 65568 | tf_op jit(solution)/shard_map/ppermute | solution.py:17
  92.9 0.7 collective-permute-start.17
  93.6 3.7 %collective-permute-done.17 = f32[256,64]{0,1:T(8,128)S(1)} collective-permute-done((f32[256,64]{0,1:T(8,128)S(1)}, f32[256,64]{0,1:T(8,128)S(1)}, u32[]{:S(2)}, u32[]{:S(2)}) %collective-permute-start.17) | collective-permute-done | bytes 65568 | tf_op jit(solution)/shard_map/ppermute | solution.py:17
  97.3 0.4 collective-permute-start.18
  97.7 0.8 copy.36
  98.5 3.8 %collective-permute-done.18 = f32[512,64]{0,1:T(8,128)S(1)} collective-permute-done((f32[512,64]{0,1:T(8,128)S(1)}, f32[512,64]{0,1:T(8,128)S(1)}, u32[]{:S(2)}, u32[]{:S(2)}) %collective-permute-start.18) | collective-permute-done | bytes 131104 | tf_op jit(solution)/shard_map/ppermute | solution.py:17
  102.3 0.7 maximum_select_fusion
  (53 shorter events, 0.8 us)
Async XLA Ops:
  0.6 36.6 %copy-start = (f32[1024,64]{0,1:T(8,128)S(1)}, f32[1024,64]{0,1:T(8,128)}, u32[]{:S(2)}) copy-start(f32[1024,64]{0,1:T(8,128)} %param.16) | copy-start | bytes 786436
  0.6 6.8 %copy-start.1 = (bf16[8,64,1024]{2,1,0:T(8,128)(2,1)S(1)}, bf16[8,64,1024]{2,1,0:T(8,128)(2,1)}, u32[]{:S(2)}) copy-start(bf16[8,64,1024]{2,1,0:T(8,128)(2,1)} %param.11) | copy-start | bytes 3145732
  0.7 2.5 %copy-start.3 = (bf16[8,64,128]{2,1,0:T(8,128)(2,1)S(1)}, bf16[8,64,128]{2,1,0:T(8,128)(2,1)}, u32[]{:S(2)}) copy-start(bf16[8,64,128]{2,1,0:T(8,128)(2,1)} %param.12) | copy-start | bytes 393220
  0.7 3.1 %copy-start.7 = (bf16[8,64,128]{2,1,0:T(8,128)(2,1)S(1)}, bf16[8,64,128]{2,1,0:T(8,128)(2,1)}, u32[]{:S(2)}) copy-start(bf16[8,64,128]{2,1,0:T(8,128)(2,1)} %param.13) | copy-start | bytes 393220
  4.2 6.9 %collective-permute-start = (bf16[8,16,128]{2,0,1:T(8,128)(2,1)S(1)}, bf16[8,16,128]{2,0,1:T(8,128)(2,1)S(1)}, u32[]{:S(2)}, u32[]{:S(2)}) collective-permute-start(bf16[8,16,128]{2,0,1:T(8,128)(2,1)S(1)} %fusion.65), channel_id=1, source_target_pairs={{0,128},{4,132},{8,136},{12,140},{16,144},{20,148},{24,152},{28,15... | collective-permute-start | bytes 98312 | tf_op jit(solution)/shard_map/ppermute | solution.py:17
  9.7 1.2 %copy-start.2 = (bf16[8,64,1024]{2,1,0:T(8,128)(2,1)S(1)}, bf16[8,64,1024]{2,1,0:T(8,128)(2,1)}, u32[]{:S(2)}) copy-start(bf16[8,64,1024]{2,1,0:T(8,128)(2,1)} %param.10) | copy-start | bytes 3145732
  9.7 1.4 %copy-start.6 = (s32[8]{0:T(128)S(1)}, s32[8]{0:T(128)}, u32[]{:S(2)}) copy-start(s32[8]{0:T(128)} %param.17) | copy-start | bytes 100
  15.5 4.1 %collective-permute-start.1 = (bf16[256,1024]{1,0:T(8,128)(2,1)}, bf16[256,1024]{1,0:T(8,128)(2,1)}, u32[]{:S(2)}, u32[]{:S(2)}) collective-permute-start(bf16[256,1024]{1,0:T(8,128)(2,1)} %fusion.19), channel_id=1, source_target_pairs={{0,1},{1,0},{2,3},{3,2},{4,5},{5,4},{6,7},{7,6},{8,9},{9,8},{10,11... | collective-permute-start | bytes 1572872 | tf_op jit(solution)/shard_map/ppermute | solution.py:17
  16.2 3.2 %copy-start.5 = (s32[8,64]{1,0:T(8,128)S(1)}, s32[8,64]{1,0:T(8,128)}, u32[]{:S(2)}) copy-start(s32[8,64]{1,0:T(8,128)} %param.19) | copy-start | bytes 6148
  18.8 6.4 %collective-permute-start.4 = (bf16[256,1024]{1,0:T(8,128)(2,1)S(1)}, bf16[256,1024]{1,0:T(8,128)(2,1)}, u32[]{:S(2)}, u32[]{:S(2)}) collective-permute-start(bf16[256,1024]{1,0:T(8,128)(2,1)S(1)} %fusion.22), channel_id=1, source_target_pairs={{0,1},{1,0},{2,3},{3,2},{4,5},{5,4},{6,7},{7,6},{8,9},{9,8},{10,11... | collective-permute-start | bytes 1572872 | tf_op jit(solution)/shard_map/ppermute | solution.py:17
  22.0 14.9 %collective-permute-start.3 = (bf16[256,1024]{1,0:T(8,128)(2,1)S(1)}, bf16[256,1024]{1,0:T(8,128)(2,1)S(1)}, u32[]{:S(2)}, u32[]{:S(2)}) collective-permute-start(bf16[256,1024]{1,0:T(8,128)(2,1)S(1)} %add_convert_fusion.3), channel_id=1, source_target_pairs={{0,2},{1,3},{2,0},{3,1},{4,6},{5,7},{6,4},{7,5},{8,10},{9,11},{10,... | collective-permute-start | bytes 1572872 | tf_op jit(solution)/shard_map/ppermute | solution.py:17
  25.1 11.7 %collective-permute-start.2 = (bf16[256,1024]{1,0:T(8,128)(2,1)S(1)}, bf16[256,1024]{1,0:T(8,128)(2,1)S(1)}, u32[]{:S(2)}, u32[]{:S(2)}) collective-permute-start(bf16[256,1024]{1,0:T(8,128)(2,1)S(1)} %fusion.25), channel_id=1, source_target_pairs={{0,1},{1,0},{2,3},{3,2},{4,5},{5,4},{6,7},{7,6},{8,9},{9,8},{10,11... | collective-permute-start | bytes 1572872 | tf_op jit(solution)/shard_map/ppermute | solution.py:17
  29.9 8.1 %collective-permute-start.5 = (bf16[256,1024]{1,0:T(8,128)(2,1)S(1)}, bf16[256,1024]{1,0:T(8,128)(2,1)S(1)}, u32[]{:S(2)}, u32[]{:S(2)}) collective-permute-start(bf16[256,1024]{1,0:T(8,128)(2,1)S(1)} %fusion.28), channel_id=1, source_target_pairs={{0,1},{1,0},{2,3},{3,2},{4,5},{5,4},{6,7},{7,6},{8,9},{9,8},{10,11... | collective-permute-start | bytes 1572872 | tf_op jit(solution)/shard_map/ppermute | solution.py:17
  30.5 16.7 %collective-permute-start.6 = (bf16[256,1024]{1,0:T(8,128)(2,1)S(1)}, bf16[256,1024]{1,0:T(8,128)(2,1)S(1)}, u32[]{:S(2)}, u32[]{:S(2)}) collective-permute-start(bf16[256,1024]{1,0:T(8,128)(2,1)S(1)} %add_convert_fusion.1), channel_id=1, source_target_pairs={{0,2},{1,3},{2,0},{3,1},{4,6},{5,7},{6,4},{7,5},{8,10},{9,11},{10,... | collective-permute-start | bytes 1572872 | tf_op jit(solution)/shard_map/ppermute | solution.py:17
  36.4 0.9 copy-start.4
  38.0 10.4 %collective-permute-start.7 = (f32[256,65]{0,1:T(8,128)S(1)}, f32[256,65]{0,1:T(8,128)S(1)}, u32[]{:S(2)}, u32[]{:S(2)}) collective-permute-start(f32[256,65]{0,1:T(8,128)S(1)} %pad_maximum_fusion.2), channel_id=1, source_target_pairs={{0,1},{1,0},{2,3},{3,2},{4,5},{5,4},{6,7},{7,6},{8,9},{9,8},{10,11... | collective-permute-start | bytes 199688 | tf_op jit(solution)/shard_map/ppermute | solution.py:17
  48.3 1.4 %collective-permute-start.9 = (f32[256,65]{0,1:T(8,128)S(1)}, f32[256,65]{0,1:T(8,128)S(1)}, u32[]{:S(2)}, u32[]{:S(2)}) collective-permute-start(f32[256,65]{0,1:T(8,128)S(1)} %pad_maximum_fusion.3), channel_id=1, source_target_pairs={{0,1},{1,0},{2,3},{3,2},{4,5},{5,4},{6,7},{7,6},{8,9},{9,8},{10,11... | collective-permute-start | bytes 199688 | tf_op jit(solution)/shard_map/ppermute | solution.py:17
  48.4 5.2 %collective-permute-start.8 = (f32[256,65]{0,1:T(8,128)S(1)}, f32[256,65]{0,1:T(8,128)S(1)}, u32[]{:S(2)}, u32[]{:S(2)}) collective-permute-start(f32[256,65]{0,1:T(8,128)S(1)} %fusion.113), channel_id=1, source_target_pairs={{0,2},{1,3},{2,0},{3,1},{4,6},{5,7},{6,4},{7,5},{8,10},{9,11},{10,... | collective-permute-start | bytes 199688 | tf_op jit(solution)/shard_map/ppermute | solution.py:17
  49.6 5.1 %collective-permute-start.10 = (f32[256,65]{0,1:T(8,128)S(1)}, f32[256,65]{0,1:T(8,128)S(1)}, u32[]{:S(2)}, u32[]{:S(2)}) collective-permute-start(f32[256,65]{0,1:T(8,128)S(1)} %fusion.112), channel_id=1, source_target_pairs={{0,2},{1,3},{2,0},{3,1},{4,6},{5,7},{6,4},{7,5},{8,10},{9,11},{10,... | collective-permute-start | bytes 199688 | tf_op jit(solution)/shard_map/ppermute | solution.py:17
  56.0 5.3 %collective-permute-start.11 = (f32[512,64]{0,1:T(8,128)S(1)}, f32[512,64]{0,1:T(8,128)S(1)}, u32[]{:S(2)}, u32[]{:S(2)}) collective-permute-start(f32[512,64]{0,1:T(8,128)S(1)} %slice_select_fusion), channel_id=1, source_target_pairs={{0,4},{4,0},{8,12},{12,8},{16,20},{20,16},{24,28},{28,24},{32,36},... | collective-permute-start | bytes 393224 | tf_op jit(solution)/shard_map/ppermute | solution.py:17
  61.4 4.4 %collective-permute-start.12 = (f32[256,64]{0,1:T(8,128)S(1)}, f32[256,64]{0,1:T(8,128)S(1)}, u32[]{:S(2)}, u32[]{:S(2)}) collective-permute-start(f32[256,64]{0,1:T(8,128)S(1)} %slice_select_fusion.1), channel_id=1, source_target_pairs={{0,64},{4,68},{8,72},{12,76},{16,80},{20,84},{24,88},{28,92},{32,9... | collective-permute-start | bytes 196616 | tf_op jit(solution)/shard_map/ppermute | solution.py:17
  65.7 5.6 %collective-permute-start.13 = (f32[256,64]{0,1:T(8,128)S(1)}, f32[256,64]{0,1:T(8,128)S(1)}, u32[]{:S(2)}, u32[]{:S(2)}) collective-permute-start(f32[256,64]{0,1:T(8,128)S(1)} %select_add_fusion.1), channel_id=1, source_target_pairs={{0,8},{4,12},{8,0},{12,4},{16,24},{20,28},{24,16},{28,20},{32,40},... | collective-permute-start | bytes 196616 | tf_op jit(solution)/shard_map/ppermute | solution.py:17
  71.3 9.8 %collective-permute-start.14 = (f32[256,64]{0,1:T(8,128)S(1)}, f32[256,64]{0,1:T(8,128)S(1)}, u32[]{:S(2)}, u32[]{:S(2)}) collective-permute-start(f32[256,64]{0,1:T(8,128)S(1)} %add.139), channel_id=1, source_target_pairs={{0,16},{4,20},{8,24},{12,28},{16,0},{20,4},{24,8},{28,12},{32,48},... | collective-permute-start | bytes 196616 | tf_op jit(solution)/shard_map/ppermute | solution.py:17
  81.1 5.9 %collective-permute-start.15 = (f32[256,64]{0,1:T(8,128)S(1)}, f32[256,64]{0,1:T(8,128)S(1)}, u32[]{:S(2)}, u32[]{:S(2)}) collective-permute-start(f32[256,64]{0,1:T(8,128)S(1)} %add.140), channel_id=1, source_target_pairs={{0,32},{4,36},{8,40},{12,44},{16,48},{20,52},{24,56},{28,60},{32,0... | collective-permute-start | bytes 196616 | tf_op jit(solution)/shard_map/ppermute | solution.py:17
  87.0 5.9 %collective-permute-start.16 = (f32[256,64]{0,1:T(8,128)S(1)}, f32[256,64]{0,1:T(8,128)S(1)}, u32[]{:S(2)}, u32[]{:S(2)}) collective-permute-start(f32[256,64]{0,1:T(8,128)S(1)} %add.141), channel_id=1, source_target_pairs={{0,128},{4,132},{8,136},{12,140},{16,144},{20,148},{24,152},{28,15... | collective-permute-start | bytes 196616 | tf_op jit(solution)/shard_map/ppermute | solution.py:17
  92.9 4.4 %collective-permute-start.17 = (f32[256,64]{0,1:T(8,128)S(1)}, f32[256,64]{0,1:T(8,128)S(1)}, u32[]{:S(2)}, u32[]{:S(2)}) collective-permute-start(f32[256,64]{0,1:T(8,128)S(1)} %add.142), channel_id=1, source_target_pairs={{0,64},{4,68},{8,72},{12,76},{16,80},{20,84},{24,88},{28,92},{32,9... | collective-permute-start | bytes 196616 | tf_op jit(solution)/shard_map/ppermute | solution.py:17
  97.3 5.1 %collective-permute-start.18 = (f32[512,64]{0,1:T(8,128)S(1)}, f32[512,64]{0,1:T(8,128)S(1)}, u32[]{:S(2)}, u32[]{:S(2)}) collective-permute-start(f32[512,64]{0,1:T(8,128)S(1)} %maximum_select_fusion.1), channel_id=1, source_target_pairs={{0,4},{4,0},{8,12},{12,8},{16,20},{20,16},{24,28},{28,24},{32,36},... | collective-permute-start | bytes 393224 | tf_op jit(solution)/shard_map/ppermute | solution.py:17

commit v13 on v12

--- a/solution.py
+++ b/solution.py
@@ -79,7 +79,7 @@
 def dp_bits(count):
     low = [1 << k for k in range(count.bit_length() - 1)]
     if count == 64:
-        return [low[0], low[4]], [low[1], low[2], low[3], low[5]]
+        return [low[0], low[4]], [low[1], low[1] | low[2], low[3], low[5]]
     return [], low
 
 

time: 103 us -> 102 us (level)
  waiting for transfers between devices: 40.7 us -> 39 us
    ppermute x19, waiting for transfers between devices: 40.7 us -> 39 us  [exchanged(): return lax.ppermute(block, axis, [(i, i ^ bit) for i in range(count)])]
where the time goes in v13:
time: 102 us
  waiting for transfers between devices  39 us (38%)
  starting transfers between devices  26.3 us (26%)
  matrix products  26.2 us (26%)
  local copies, waits for them, and re-layouts  5.25 us (5%)
  other arithmetic  3.76 us (4%)
  between operations  1.08 us (1%)
    ppermute x19, waiting for transfers between devices, exchanged(): return lax.ppermute(block, axis, [(i, i ^ bit) for i in range(count)])  39 us
    ppermute x19, starting transfers between devices, exchanged(): return lax.ppermute(block, axis, [(i, i ^ bit) for i in range(count)])  26.3 us
    dot_general x8, matrix products, block(): return jnp.dot(heads, columns, preferred_element_type=jnp.float32)  19.4 us
  transfers between devices with their start and end apart: 19, of which 13 were waited for; matrix products, arithmetic and copies ran while one was open for 24% of the time, Pallas kernels for 0%

profile of v13, /device:TPU:24, one launch (start us, length us, event | category | flops | bytes accessed | tf_op | source)
XLA Modules:
  0.0 101.6 jit_solution(3634799946780960219)
XLA Ops:
  0.7 0.8 fusion.117
  1.6 1.5 %reshape.93 = bf16[8,512,128]{2,1,0:T(8,128)(2,1)S(1)} reshape(bf16[8,64,1024]{2,1,0:T(8,128)(2,1)} %param.11) | data formatting | bytes 2097152 | tf_op jit(solution)/shard_map/reshape | solution.py:118
  3.2 0.4 fusion.37
  3.6 0.2 fusion.121
  3.8 0.3 fusion.78
  4.2 3.1 %collective-permute-start = (bf16[8,16,128]{2,0,1:T(8,128)(2,1)S(1)}, bf16[8,16,128]{2,0,1:T(8,128)(2,1)S(1)}, u32[]{:S(2)}, u32[]{:S(2)}) collective-permute-start(bf16[8,16,128]{2,0,1:T(8,128)(2,1)S(1)} %fusion.65), channel_id=1, source_target_pairs={{0,128},{4,132},{8,136},{12,140},{16,144},{20,148},{24,152},{28,15... | collective-permute-start | bytes 98312 | tf_op jit(solution)/shard_map/ppermute | solution.py:17
  7.3 0.1 fusion.58
  7.4 1.1 %fusion.120 = (f32[8,8,64]{2,1,0:T(8,128)S(1)}, f32[8,1,8,64,64]{3,4,2,0,1:T(8,128)S(1)}) fusion(bf16[8,64,128]{2,1,0:T(8,128)(2,1)S(1)} %copy-done.3, pred[64,64]{0,1:T(8,128)(4,1)S(1)} %iota_compare_fusion.10, bf16[8,64,1024]{2,1,0:T(8,128)(2,1)S(1)} %copy-done.1), kind=kOutput, calls=%fused_computation.152 | convolution fusion | flops 67891200 | bytes 2248704 | tf_op jit(solution)/shard_map/pqkgd,pskd->pkgqs/dot_general | solution.py:95
  8.6 0.5 fusion.1
  9.1 0.6 fusion.18
  9.8 0.1 fusion.115
  9.9 1.1 %copy-done.2 = bf16[8,64,1024]{2,1,0:T(8,128)(2,1)S(1)} copy-done((bf16[8,64,1024]{2,1,0:T(8,128)(2,1)S(1)}, bf16[8,64,1024]{2,1,0:T(8,128)(2,1)}, u32[]{:S(2)}) %copy-start.2) | copy-done | bytes 1048600
  11.0 0.1 fusion.114
  11.1 0.2 convolution_convert_fusion.3
  11.3 0.8 fusion.31
  12.1 0.2 reshape.96
  12.4 3.1 %fusion.19 = bf16[256,1024]{1,0:T(8,128)(2,1)} fusion(bf16[256,1024]{1,0:T(8,128)(2,1)S(1)} %reshape.96, bf16[1024,4096]{1,0:T(8,128)(2,1)} %param.14, s32[]{:T(128)S(6)} %select_n.107), kind=kOutput, calls=%fused_computation.23 | convolution fusion | flops 537133056 | bytes 3145732 | tf_op jit(solution)/shard_map/dot_general | solution.py:53
  15.5 0.8 fusion.32
  16.3 0.2 reshape.97
  16.5 2.3 %fusion.22 = bf16[256,1024]{1,0:T(8,128)(2,1)S(1)} fusion(bf16[256,1024]{1,0:T(8,128)(2,1)S(1)} %reshape.97, bf16[1024,4096]{1,0:T(8,128)(2,1)} %param.14, s32[]{:T(128)S(6)} %select_n.107), kind=kOutput, calls=%fused_computation.24 | convolution fusion | flops 537133056 | bytes 3145732 | tf_op jit(solution)/shard_map/dot_general | solution.py:53
  18.8 0.6 collective-permute-start.4
  19.6 2.4 %add_convert_fusion.3 = bf16[256,1024]{1,0:T(8,128)(2,1)S(1)} fusion(bf16[256,1024]{1,0:T(8,128)(2,1)} %collective-permute-done.1, bf16[256,1024]{1,0:T(8,128)(2,1)S(1)} %reshape.96, bf16[1024,4096]{1,0:T(8,128)(2,1)} %param.14, s32[]{:T(128)S(6)} %select_n.106), kind=kOutput, calls=%fused_computation.54 | convolution fusion | flops 537657344 | bytes 3670020 | tf_op jit(solution)/shard_map/dot_general | solution.py:53
  22.0 0.8 collective-permute-start.3
  22.8 2.3 %fusion.25 = bf16[256,1024]{1,0:T(8,128)(2,1)S(1)} fusion(bf16[256,1024]{1,0:T(8,128)(2,1)S(1)} %reshape.96, bf16[1024,4096]{1,0:T(8,128)(2,1)} %param.14, s32[]{:T(128)S(6)} %select_n.109), kind=kOutput, calls=%fused_computation.25 | convolution fusion | flops 537133056 | bytes 3145732 | tf_op jit(solution)/shard_map/dot_general | solution.py:73
  25.1 0.1 collective-permute-start.2
  25.2 2.4 %add_convert_fusion.1 = bf16[256,1024]{1,0:T(8,128)(2,1)S(1)} fusion(bf16[256,1024]{1,0:T(8,128)(2,1)} %collective-permute-done.4, bf16[256,1024]{1,0:T(8,128)(2,1)S(1)} %reshape.97, bf16[1024,4096]{1,0:T(8,128)(2,1)} %param.14, s32[]{:T(128)S(6)} %select_n.106), kind=kOutput, calls=%fused_computation.52 | convolution fusion | flops 537657344 | bytes 3670020 | tf_op jit(solution)/shard_map/dot_general | solution.py:53
  27.6 2.3 %fusion.28 = bf16[256,1024]{1,0:T(8,128)(2,1)S(1)} fusion(bf16[256,1024]{1,0:T(8,128)(2,1)S(1)} %reshape.97, bf16[1024,4096]{1,0:T(8,128)(2,1)} %param.14, s32[]{:T(128)S(6)} %select_n.109), kind=kOutput, calls=%fused_computation.26 | convolution fusion | flops 537133056 | bytes 3145732 | tf_op jit(solution)/shard_map/dot_general | solution.py:73
  29.9 0.6 collective-permute-start.5
  30.5 1.3 %collective-permute-start.6 = (bf16[256,1024]{1,0:T(8,128)(2,1)S(1)}, bf16[256,1024]{1,0:T(8,128)(2,1)S(1)}, u32[]{:S(2)}, u32[]{:S(2)}) collective-permute-start(bf16[256,1024]{1,0:T(8,128)(2,1)S(1)} %add_convert_fusion.1), channel_id=1, source_target_pairs={{0,2},{1,3},{2,0},{3,1},{4,6},{5,7},{6,4},{7,5},{8,10},{9,11},{10,... | collective-permute-start | bytes 1572872 | tf_op jit(solution)/shard_map/ppermute | solution.py:17
  31.8 2.3 %fusion.8 = f32[256,1024]{1,0:T(8,128)S(1)} fusion(bf16[256,1024]{1,0:T(8,128)(2,1)S(1)} %reshape.96, bf16[1024,4096]{1,0:T(8,128)(2,1)} %param.14, s32[]{:T(128)S(6)} %select_n.108), kind=kOutput, calls=%fused_computation.11 | convolution fusion | flops 536870912 | bytes 3670020 | tf_op jit(solution)/shard_map/dot_general | solution.py:73
  34.1 2.3 %fusion.6 = f32[256,1024]{1,0:T(8,128)S(1)} fusion(bf16[256,1024]{1,0:T(8,128)(2,1)S(1)} %reshape.97, bf16[1024,4096]{1,0:T(8,128)(2,1)} %param.14, s32[]{:T(128)S(6)} %select_n.108), kind=kOutput, calls=%fused_computation.9 | convolution fusion | flops 536870912 | bytes 3670020 | tf_op jit(solution)/shard_map/dot_general | solution.py:73
  36.4 0.4 collective-permute-done.3
  36.9 0.4 multiply_reduce_fusion.1
  37.3 0.7 fusion.50
  38.0 0.1 collective-permute-start.7
  38.1 9.1 %collective-permute-done.6 = bf16[256,1024]{1,0:T(8,128)(2,1)S(1)} collective-permute-done((bf16[256,1024]{1,0:T(8,128)(2,1)S(1)}, bf16[256,1024]{1,0:T(8,128)(2,1)S(1)}, u32[]{:S(2)}, u32[]{:S(2)}) %collective-permute-start.6) | collective-permute-done | bytes 524320 | tf_op jit(solution)/shard_map/ppermute | solution.py:17
  47.2 0.4 multiply_reduce_fusion
  47.6 0.7 fusion.47
  48.4 0.8 collective-permute-start.8
  49.2 0.4 collective-permute-done.9
  49.6 1.0 collective-permute-start.10
  50.6 3.0 %collective-permute-done.8 = f32[256,65]{0,1:T(8,128)S(1)} collective-permute-done((f32[256,65]{0,1:T(8,128)S(1)}, f32[256,65]{0,1:T(8,128)S(1)}, u32[]{:S(2)}, u32[]{:S(2)}) %collective-permute-start.8) | collective-permute-done | bytes 66592 | tf_op jit(solution)/shard_map/ppermute | solution.py:17
  53.7 1.1 %collective-permute-done.10 = f32[256,65]{0,1:T(8,128)S(1)} collective-permute-done((f32[256,65]{0,1:T(8,128)S(1)}, f32[256,65]{0,1:T(8,128)S(1)}, u32[]{:S(2)}, u32[]{:S(2)}) %collective-permute-start.10) | collective-permute-done | bytes 66592 | tf_op jit(solution)/shard_map/ppermute | solution.py:17
  54.8 0.6 fusion.42
  55.4 0.6 fusion.33
  56.0 2.0 %collective-permute-start.11 = (f32[512,64]{0,1:T(8,128)S(1)}, f32[512,64]{0,1:T(8,128)S(1)}, u32[]{:S(2)}, u32[]{:S(2)}) collective-permute-start(f32[512,64]{0,1:T(8,128)S(1)} %slice_select_fusion), channel_id=1, source_target_pairs={{0,4},{4,0},{8,12},{12,8},{16,20},{20,16},{24,28},{28,24},{32,36},... | collective-permute-start | bytes 393224 | tf_op jit(solution)/shard_map/ppermute | solution.py:17
  58.0 3.3 %collective-permute-done.11 = f32[512,64]{0,1:T(8,128)S(1)} collective-permute-done((f32[512,64]{0,1:T(8,128)S(1)}, f32[512,64]{0,1:T(8,128)S(1)}, u32[]{:S(2)}, u32[]{:S(2)}) %collective-permute-start.11) | collective-permute-done | bytes 131104 | tf_op jit(solution)/shard_map/ppermute | solution.py:17
  61.4 0.7 collective-permute-start.12
  62.0 3.7 %collective-permute-done.12 = f32[256,64]{0,1:T(8,128)S(1)} collective-permute-done((f32[256,64]{0,1:T(8,128)S(1)}, f32[256,64]{0,1:T(8,128)S(1)}, u32[]{:S(2)}, u32[]{:S(2)}) %collective-permute-start.12) | collective-permute-done | bytes 65568 | tf_op jit(solution)/shard_map/ppermute | solution.py:17
  65.7 3.3 %collective-permute-start.13 = (f32[256,64]{0,1:T(8,128)S(1)}, f32[256,64]{0,1:T(8,128)S(1)}, u32[]{:S(2)}, u32[]{:S(2)}) collective-permute-start(f32[256,64]{0,1:T(8,128)S(1)} %select_add_fusion.1), channel_id=1, source_target_pairs={{0,8},{4,12},{8,0},{12,4},{16,24},{20,28},{24,16},{28,20},{32,40},... | collective-permute-start | bytes 196616 | tf_op jit(solution)/shard_map/ppermute | solution.py:17
  69.1 2.2 %collective-permute-done.13 = f32[256,64]{0,1:T(8,128)S(1)} collective-permute-done((f32[256,64]{0,1:T(8,128)S(1)}, f32[256,64]{0,1:T(8,128)S(1)}, u32[]{:S(2)}, u32[]{:S(2)}) %collective-permute-start.13) | collective-permute-done | bytes 65568 | tf_op jit(solution)/shard_map/ppermute | solution.py:17
  71.3 6.0 %collective-permute-start.14 = (f32[256,64]{0,1:T(8,128)S(1)}, f32[256,64]{0,1:T(8,128)S(1)}, u32[]{:S(2)}, u32[]{:S(2)}) collective-permute-start(f32[256,64]{0,1:T(8,128)S(1)} %add.139), channel_id=1, source_target_pairs={{0,24},{4,28},{8,16},{12,20},{16,8},{20,12},{24,0},{28,4},{32,56},... | collective-permute-start | bytes 196616 | tf_op jit(solution)/shard_map/ppermute | solution.py:17
  77.3 2.3 %collective-permute-done.14 = f32[256,64]{0,1:T(8,128)S(1)} collective-permute-done((f32[256,64]{0,1:T(8,128)S(1)}, f32[256,64]{0,1:T(8,128)S(1)}, u32[]{:S(2)}, u32[]{:S(2)}) %collective-permute-start.14) | collective-permute-done | bytes 65568 | tf_op jit(solution)/shard_map/ppermute | solution.py:17
  79.6 1.3 %collective-permute-start.15 = (f32[256,64]{0,1:T(8,128)S(1)}, f32[256,64]{0,1:T(8,128)S(1)}, u32[]{:S(2)}, u32[]{:S(2)}) collective-permute-start(f32[256,64]{0,1:T(8,128)S(1)} %add.140), channel_id=1, source_target_pairs={{0,32},{4,36},{8,40},{12,44},{16,48},{20,52},{24,56},{28,60},{32,0... | collective-permute-start | bytes 196616 | tf_op jit(solution)/shard_map/ppermute | solution.py:17
  80.9 4.5 %collective-permute-done.15 = f32[256,64]{0,1:T(8,128)S(1)} collective-permute-done((f32[256,64]{0,1:T(8,128)S(1)}, f32[256,64]{0,1:T(8,128)S(1)}, u32[]{:S(2)}, u32[]{:S(2)}) %collective-permute-start.15) | collective-permute-done | bytes 65568 | tf_op jit(solution)/shard_map/ppermute | solution.py:17
  85.5 1.7 %collective-permute-start.16 = (f32[256,64]{0,1:T(8,128)S(1)}, f32[256,64]{0,1:T(8,128)S(1)}, u32[]{:S(2)}, u32[]{:S(2)}) collective-permute-start(f32[256,64]{0,1:T(8,128)S(1)} %add.141), channel_id=1, source_target_pairs={{0,128},{4,132},{8,136},{12,140},{16,144},{20,148},{24,152},{28,15... | collective-permute-start | bytes 196616 | tf_op jit(solution)/shard_map/ppermute | solution.py:17
  87.2 1.0 %pad_maximum_fusion = bf16[512,1024]{1,0:T(8,128)(2,1)} fusion(bf16[256,1024]{1,0:T(8,128)(2,1)S(1)} %get-tuple-element.24, bf16[256,1024]{1,0:T(8,128)(2,1)S(1)} %get-tuple-element.22), kind=kLoop, calls=%fused_computation.42 | loop fusion | flops 2097152 | bytes 2097152 | tf_op jit(solution)/shard_map/concatenate | solution.py:237
  88.2 3.2 %collective-permute-done.16 = f32[256,64]{0,1:T(8,128)S(1)} collective-permute-done((f32[256,64]{0,1:T(8,128)S(1)}, f32[256,64]{0,1:T(8,128)S(1)}, u32[]{:S(2)}, u32[]{:S(2)}) %collective-permute-start.16) | collective-permute-done | bytes 65568 | tf_op jit(solution)/shard_map/ppermute | solution.py:17
  91.4 0.7 collective-permute-start.17
  92.0 3.7 %collective-permute-done.17 = f32[256,64]{0,1:T(8,128)S(1)} collective-permute-done((f32[256,64]{0,1:T(8,128)S(1)}, f32[256,64]{0,1:T(8,128)S(1)}, u32[]{:S(2)}, u32[]{:S(2)}) %collective-permute-start.17) | collective-permute-done | bytes 65568 | tf_op jit(solution)/shard_map/ppermute | solution.py:17
  95.7 2.2 %collective-permute-start.18 = (f32[512,64]{0,1:T(8,128)S(1)}, f32[512,64]{0,1:T(8,128)S(1)}, u32[]{:S(2)}, u32[]{:S(2)}) collective-permute-start(f32[512,64]{0,1:T(8,128)S(1)} %maximum_select_fusion.1), channel_id=1, source_target_pairs={{0,4},{4,0},{8,12},{12,8},{16,20},{20,16},{24,28},{28,24},{32,36},... | collective-permute-start | bytes 393224 | tf_op jit(solution)/shard_map/ppermute | solution.py:17
  97.9 0.8 copy.36
  98.8 2.1 %collective-permute-done.18 = f32[512,64]{0,1:T(8,128)S(1)} collective-permute-done((f32[512,64]{0,1:T(8,128)S(1)}, f32[512,64]{0,1:T(8,128)S(1)}, u32[]{:S(2)}, u32[]{:S(2)}) %collective-permute-start.18) | collective-permute-done | bytes 131104 | tf_op jit(solution)/shard_map/ppermute | solution.py:17
  100.9 0.7 maximum_select_fusion
  (53 shorter events, 0.8 us)
Async XLA Ops:
  0.6 36.6 %copy-start = (f32[1024,64]{0,1:T(8,128)S(1)}, f32[1024,64]{0,1:T(8,128)}, u32[]{:S(2)}) copy-start(f32[1024,64]{0,1:T(8,128)} %param.16) | copy-start | bytes 786436
  0.6 6.8 %copy-start.1 = (bf16[8,64,1024]{2,1,0:T(8,128)(2,1)S(1)}, bf16[8,64,1024]{2,1,0:T(8,128)(2,1)}, u32[]{:S(2)}) copy-start(bf16[8,64,1024]{2,1,0:T(8,128)(2,1)} %param.11) | copy-start | bytes 3145732
  0.7 2.5 %copy-start.3 = (bf16[8,64,128]{2,1,0:T(8,128)(2,1)S(1)}, bf16[8,64,128]{2,1,0:T(8,128)(2,1)}, u32[]{:S(2)}) copy-start(bf16[8,64,128]{2,1,0:T(8,128)(2,1)} %param.12) | copy-start | bytes 393220
  0.7 3.1 %copy-start.7 = (bf16[8,64,128]{2,1,0:T(8,128)(2,1)S(1)}, bf16[8,64,128]{2,1,0:T(8,128)(2,1)}, u32[]{:S(2)}) copy-start(bf16[8,64,128]{2,1,0:T(8,128)(2,1)} %param.13) | copy-start | bytes 393220
  4.2 6.9 %collective-permute-start = (bf16[8,16,128]{2,0,1:T(8,128)(2,1)S(1)}, bf16[8,16,128]{2,0,1:T(8,128)(2,1)S(1)}, u32[]{:S(2)}, u32[]{:S(2)}) collective-permute-start(bf16[8,16,128]{2,0,1:T(8,128)(2,1)S(1)} %fusion.65), channel_id=1, source_target_pairs={{0,128},{4,132},{8,136},{12,140},{16,144},{20,148},{24,152},{28,15... | collective-permute-start | bytes 98312 | tf_op jit(solution)/shard_map/ppermute | solution.py:17
  9.7 1.2 %copy-start.2 = (bf16[8,64,1024]{2,1,0:T(8,128)(2,1)S(1)}, bf16[8,64,1024]{2,1,0:T(8,128)(2,1)}, u32[]{:S(2)}) copy-start(bf16[8,64,1024]{2,1,0:T(8,128)(2,1)} %param.10) | copy-start | bytes 3145732
  9.7 1.4 %copy-start.6 = (s32[8]{0:T(128)S(1)}, s32[8]{0:T(128)}, u32[]{:S(2)}) copy-start(s32[8]{0:T(128)} %param.17) | copy-start | bytes 100
  15.5 4.1 %collective-permute-start.1 = (bf16[256,1024]{1,0:T(8,128)(2,1)}, bf16[256,1024]{1,0:T(8,128)(2,1)}, u32[]{:S(2)}, u32[]{:S(2)}) collective-permute-start(bf16[256,1024]{1,0:T(8,128)(2,1)} %fusion.19), channel_id=1, source_target_pairs={{0,1},{1,0},{2,3},{3,2},{4,5},{5,4},{6,7},{7,6},{8,9},{9,8},{10,11... | collective-permute-start | bytes 1572872 | tf_op jit(solution)/shard_map/ppermute | solution.py:17
  16.2 3.2 %copy-start.5 = (s32[8,64]{1,0:T(8,128)S(1)}, s32[8,64]{1,0:T(8,128)}, u32[]{:S(2)}) copy-start(s32[8,64]{1,0:T(8,128)} %param.19) | copy-start | bytes 6148
  18.8 6.4 %collective-permute-start.4 = (bf16[256,1024]{1,0:T(8,128)(2,1)S(1)}, bf16[256,1024]{1,0:T(8,128)(2,1)}, u32[]{:S(2)}, u32[]{:S(2)}) collective-permute-start(bf16[256,1024]{1,0:T(8,128)(2,1)S(1)} %fusion.22), channel_id=1, source_target_pairs={{0,1},{1,0},{2,3},{3,2},{4,5},{5,4},{6,7},{7,6},{8,9},{9,8},{10,11... | collective-permute-start | bytes 1572872 | tf_op jit(solution)/shard_map/ppermute | solution.py:17
  22.0 14.9 %collective-permute-start.3 = (bf16[256,1024]{1,0:T(8,128)(2,1)S(1)}, bf16[256,1024]{1,0:T(8,128)(2,1)S(1)}, u32[]{:S(2)}, u32[]{:S(2)}) collective-permute-start(bf16[256,1024]{1,0:T(8,128)(2,1)S(1)} %add_convert_fusion.3), channel_id=1, source_target_pairs={{0,2},{1,3},{2,0},{3,1},{4,6},{5,7},{6,4},{7,5},{8,10},{9,11},{10,... | collective-permute-start | bytes 1572872 | tf_op jit(solution)/shard_map/ppermute | solution.py:17
  25.1 11.7 %collective-permute-start.2 = (bf16[256,1024]{1,0:T(8,128)(2,1)S(1)}, bf16[256,1024]{1,0:T(8,128)(2,1)S(1)}, u32[]{:S(2)}, u32[]{:S(2)}) collective-permute-start(bf16[256,1024]{1,0:T(8,128)(2,1)S(1)} %fusion.25), channel_id=1, source_target_pairs={{0,1},{1,0},{2,3},{3,2},{4,5},{5,4},{6,7},{7,6},{8,9},{9,8},{10,11... | collective-permute-start | bytes 1572872 | tf_op jit(solution)/shard_map/ppermute | solution.py:17
  29.9 8.1 %collective-permute-start.5 = (bf16[256,1024]{1,0:T(8,128)(2,1)S(1)}, bf16[256,1024]{1,0:T(8,128)(2,1)S(1)}, u32[]{:S(2)}, u32[]{:S(2)}) collective-permute-start(bf16[256,1024]{1,0:T(8,128)(2,1)S(1)} %fusion.28), channel_id=1, source_target_pairs={{0,1},{1,0},{2,3},{3,2},{4,5},{5,4},{6,7},{7,6},{8,9},{9,8},{10,11... | collective-permute-start | bytes 1572872 | tf_op jit(solution)/shard_map/ppermute | solution.py:17
  30.5 16.7 %collective-permute-start.6 = (bf16[256,1024]{1,0:T(8,128)(2,1)S(1)}, bf16[256,1024]{1,0:T(8,128)(2,1)S(1)}, u32[]{:S(2)}, u32[]{:S(2)}) collective-permute-start(bf16[256,1024]{1,0:T(8,128)(2,1)S(1)} %add_convert_fusion.1), channel_id=1, source_target_pairs={{0,2},{1,3},{2,0},{3,1},{4,6},{5,7},{6,4},{7,5},{8,10},{9,11},{10,... | collective-permute-start | bytes 1572872 | tf_op jit(solution)/shard_map/ppermute | solution.py:17
  36.4 0.9 copy-start.4
  38.0 10.4 %collective-permute-start.7 = (f32[256,65]{0,1:T(8,128)S(1)}, f32[256,65]{0,1:T(8,128)S(1)}, u32[]{:S(2)}, u32[]{:S(2)}) collective-permute-start(f32[256,65]{0,1:T(8,128)S(1)} %pad_maximum_fusion.2), channel_id=1, source_target_pairs={{0,1},{1,0},{2,3},{3,2},{4,5},{5,4},{6,7},{7,6},{8,9},{9,8},{10,11... | collective-permute-start | bytes 199688 | tf_op jit(solution)/shard_map/ppermute | solution.py:17
  48.3 1.4 %collective-permute-start.9 = (f32[256,65]{0,1:T(8,128)S(1)}, f32[256,65]{0,1:T(8,128)S(1)}, u32[]{:S(2)}, u32[]{:S(2)}) collective-permute-start(f32[256,65]{0,1:T(8,128)S(1)} %pad_maximum_fusion.3), channel_id=1, source_target_pairs={{0,1},{1,0},{2,3},{3,2},{4,5},{5,4},{6,7},{7,6},{8,9},{9,8},{10,11... | collective-permute-start | bytes 199688 | tf_op jit(solution)/shard_map/ppermute | solution.py:17
  48.4 5.2 %collective-permute-start.8 = (f32[256,65]{0,1:T(8,128)S(1)}, f32[256,65]{0,1:T(8,128)S(1)}, u32[]{:S(2)}, u32[]{:S(2)}) collective-permute-start(f32[256,65]{0,1:T(8,128)S(1)} %fusion.113), channel_id=1, source_target_pairs={{0,2},{1,3},{2,0},{3,1},{4,6},{5,7},{6,4},{7,5},{8,10},{9,11},{10,... | collective-permute-start | bytes 199688 | tf_op jit(solution)/shard_map/ppermute | solution.py:17
  49.6 5.1 %collective-permute-start.10 = (f32[256,65]{0,1:T(8,128)S(1)}, f32[256,65]{0,1:T(8,128)S(1)}, u32[]{:S(2)}, u32[]{:S(2)}) collective-permute-start(f32[256,65]{0,1:T(8,128)S(1)} %fusion.112), channel_id=1, source_target_pairs={{0,2},{1,3},{2,0},{3,1},{4,6},{5,7},{6,4},{7,5},{8,10},{9,11},{10,... | collective-permute-start | bytes 199688 | tf_op jit(solution)/shard_map/ppermute | solution.py:17
  56.0 5.3 %collective-permute-start.11 = (f32[512,64]{0,1:T(8,128)S(1)}, f32[512,64]{0,1:T(8,128)S(1)}, u32[]{:S(2)}, u32[]{:S(2)}) collective-permute-start(f32[512,64]{0,1:T(8,128)S(1)} %slice_select_fusion), channel_id=1, source_target_pairs={{0,4},{4,0},{8,12},{12,8},{16,20},{20,16},{24,28},{28,24},{32,36},... | collective-permute-start | bytes 393224 | tf_op jit(solution)/shard_map/ppermute | solution.py:17
  61.4 4.4 %collective-permute-start.12 = (f32[256,64]{0,1:T(8,128)S(1)}, f32[256,64]{0,1:T(8,128)S(1)}, u32[]{:S(2)}, u32[]{:S(2)}) collective-permute-start(f32[256,64]{0,1:T(8,128)S(1)} %slice_select_fusion.1), channel_id=1, source_target_pairs={{0,64},{4,68},{8,72},{12,76},{16,80},{20,84},{24,88},{28,92},{32,9... | collective-permute-start | bytes 196616 | tf_op jit(solution)/shard_map/ppermute | solution.py:17
  65.7 5.6 %collective-permute-start.13 = (f32[256,64]{0,1:T(8,128)S(1)}, f32[256,64]{0,1:T(8,128)S(1)}, u32[]{:S(2)}, u32[]{:S(2)}) collective-permute-start(f32[256,64]{0,1:T(8,128)S(1)} %select_add_fusion.1), channel_id=1, source_target_pairs={{0,8},{4,12},{8,0},{12,4},{16,24},{20,28},{24,16},{28,20},{32,40},... | collective-permute-start | bytes 196616 | tf_op jit(solution)/shard_map/ppermute | solution.py:17
  71.3 8.3 %collective-permute-start.14 = (f32[256,64]{0,1:T(8,128)S(1)}, f32[256,64]{0,1:T(8,128)S(1)}, u32[]{:S(2)}, u32[]{:S(2)}) collective-permute-start(f32[256,64]{0,1:T(8,128)S(1)} %add.139), channel_id=1, source_target_pairs={{0,24},{4,28},{8,16},{12,20},{16,8},{20,12},{24,0},{28,4},{32,56},... | collective-permute-start | bytes 196616 | tf_op jit(solution)/shard_map/ppermute | solution.py:17
  79.6 5.9 %collective-permute-start.15 = (f32[256,64]{0,1:T(8,128)S(1)}, f32[256,64]{0,1:T(8,128)S(1)}, u32[]{:S(2)}, u32[]{:S(2)}) collective-permute-start(f32[256,64]{0,1:T(8,128)S(1)} %add.140), channel_id=1, source_target_pairs={{0,32},{4,36},{8,40},{12,44},{16,48},{20,52},{24,56},{28,60},{32,0... | collective-permute-start | bytes 196616 | tf_op jit(solution)/shard_map/ppermute | solution.py:17
  85.5 5.9 %collective-permute-start.16 = (f32[256,64]{0,1:T(8,128)S(1)}, f32[256,64]{0,1:T(8,128)S(1)}, u32[]{:S(2)}, u32[]{:S(2)}) collective-permute-start(f32[256,64]{0,1:T(8,128)S(1)} %add.141), channel_id=1, source_target_pairs={{0,128},{4,132},{8,136},{12,140},{16,144},{20,148},{24,152},{28,15... | collective-permute-start | bytes 196616 | tf_op jit(solution)/shard_map/ppermute | solution.py:17
  91.4 4.4 %collective-permute-start.17 = (f32[256,64]{0,1:T(8,128)S(1)}, f32[256,64]{0,1:T(8,128)S(1)}, u32[]{:S(2)}, u32[]{:S(2)}) collective-permute-start(f32[256,64]{0,1:T(8,128)S(1)} %add.142), channel_id=1, source_target_pairs={{0,64},{4,68},{8,72},{12,76},{16,80},{20,84},{24,88},{28,92},{32,9... | collective-permute-start | bytes 196616 | tf_op jit(solution)/shard_map/ppermute | solution.py:17
  95.7 5.1 %collective-permute-start.18 = (f32[512,64]{0,1:T(8,128)S(1)}, f32[512,64]{0,1:T(8,128)S(1)}, u32[]{:S(2)}, u32[]{:S(2)}) collective-permute-start(f32[512,64]{0,1:T(8,128)S(1)} %maximum_select_fusion.1), channel_id=1, source_target_pairs={{0,4},{4,0},{8,12},{12,8},{16,20},{20,16},{24,28},{28,24},{32,36},... | collective-permute-start | bytes 393224 | tf_op jit(solution)/shard_map/ppermute | solution.py:17

commit v14 on v13

--- a/solution.py
+++ b/solution.py
@@ -112,10 +112,19 @@
     local_kv = attn_keys.shape[2] // HDIM
     local_heads = queries.shape[2] // HDIM
     group_size = local_heads // local_kv
+    pos_pick = (
+        pos_ids[:, :, None] == jnp.arange(seq_length, dtype=pos_ids.dtype)[None, None, :]
+    ).astype(queries.dtype)
+    head_pick = (
+        head_ids[:, :, None] == jnp.arange(local_heads, dtype=head_ids.dtype)[None, None, :]
+    ).astype(queries.dtype)
+    query_lines = jnp.einsum(
+        "jks,jsf->jkf", pos_pick, queries, preferred_element_type=jnp.float32
+    ).astype(queries.dtype)
     query_rows = jnp.einsum(
-        "jkr,jrd->jkd",
-        pick_values,
-        queries.reshape(prompt_count, seq_length * local_heads, HDIM),
+        "jkh,jkhd->jkd",
+        head_pick,
+        query_lines.reshape(prompt_count, -1, local_heads, HDIM),
         preferred_element_type=jnp.float32,
     ).astype(queries.dtype)
     key_blocks = attn_keys.reshape(prompt_count, seq_length, local_kv, HDIM)

time: 102 us -> 107 us (1.049)
  waiting for transfers between devices: 39 us -> 42 us
  matrix products: 26.2 us -> 28.2 us
    ppermute x19, waiting for transfers between devices: 39 us -> 42 us  [exchanged(): return lax.ppermute(block, axis, [(i, i ^ bit) for i in range(count)])]
    reshape x1 -> x0, local copies, waits for them, and re-layouts: 1.52 us -> none  [attend_rows(): queries.reshape(prompt_count, seq_length * local_heads, HDIM)]
  transfers between devices with their start and end apart: 19 -> 19, of which waited for: 13 -> 13; matrix products, arithmetic and copies ran while one was open for 24% -> 26% of each run, Pallas kernels for 0% -> 0%
where the time goes in v14:
time: 107 us; the launch traced here: 106 us
  waiting for transfers between devices  42 us (39%)
  matrix products  28.2 us (26%)
  starting transfers between devices  26 us (24%)
  local copies, waits for them, and re-layouts  5.17 us (5%)
  other arithmetic  3.84 us (4%)
    ppermute x19, waiting for transfers between devices, exchanged(): return lax.ppermute(block, axis, [(i, i ^ bit) for i in range(count)])  42 us
    ppermute x19, starting transfers between devices, exchanged(): return lax.ppermute(block, axis, [(i, i ^ bit) for i in range(count)])  26 us
    dot_general x8, matrix products, block(): return jnp.dot(heads, columns, preferred_element_type=jnp.float32)  20.3 us
    dot_general x2, matrix products, per_device(): jnp.einsum('jkr,jkd->jrd', pick_values[prompts_here], incoming[prompts_he...  2.39 us
  transfers between devices with their start and end apart: 19, of which 13 were waited for; matrix products, arithmetic and copies ran while one was open for 26% of the time, Pallas kernels for 0%

profile of v14, /device:TPU:24, one launch (start us, length us, event | category | flops | bytes accessed | tf_op | source)
XLA Modules:
  0.0 106.3 jit_solution(7198108281274335472)
XLA Ops:
  0.7 0.8 fusion.122
  1.6 0.3 copy-done
  1.9 0.3 convolution_convert_fusion.3
  2.3 0.3 fusion.58
  2.6 0.2 fusion.37
  2.8 0.2 fusion.126
  3.0 0.3 fusion.80
  3.4 3.1 %collective-permute-start = (bf16[8,16,128]{2,0,1:T(8,128)(2,1)S(1)}, bf16[8,16,128]{2,0,1:T(8,128)(2,1)S(1)}, u32[]{:S(2)}, u32[]{:S(2)}) collective-permute-start(bf16[8,16,128]{2,0,1:T(8,128)(2,1)S(1)} %fusion.66), channel_id=1, source_target_pairs={{0,128},{4,132},{8,136},{12,140},{16,144},{20,148},{24,152},{28,15... | collective-permute-start | bytes 98312 | tf_op jit(solution)/shard_map/ppermute | solution.py:17
  6.5 1.1 %fusion.125 = (f32[8,8,64]{2,1,0:T(8,128)S(1)}, f32[8,1,8,64,64]{3,4,2,0,1:T(8,128)S(1)}) fusion(bf16[8,64,128]{2,1,0:T(8,128)(2,1)S(1)} %copy-done.3, pred[64,64]{0,1:T(8,128)(4,1)S(1)} %iota_compare_fusion.11, bf16[8,64,1024]{2,1,0:T(8,128)(2,1)S(1)} %copy-done), kind=kOutput, calls=%fused_computation.160 | convolution fusion | flops 67891200 | bytes 2248704 | tf_op jit(solution)/shard_map/pqkgd,pskd->pkgqs/dot_general | solution.py:95
  7.7 0.5 fusion.1
  8.2 0.6 fusion.18
  8.9 0.9 fusion.120
  9.7 0.1 fusion.60
  9.9 0.4 copy-done.1
  10.4 0.2 convolution_convert_fusion.4
  10.6 0.8 fusion.31
  11.4 0.2 reshape.96
  11.7 3.2 %fusion.19 = bf16[256,1024]{1,0:T(8,128)(2,1)} fusion(bf16[256,1024]{1,0:T(8,128)(2,1)S(1)} %reshape.96, bf16[1024,4096]{1,0:T(8,128)(2,1)} %param.14, s32[]{:T(128)S(6)} %select_n.108), kind=kOutput, calls=%fused_computation.23 | convolution fusion | flops 537133056 | bytes 3145732 | tf_op jit(solution)/shard_map/dot_general | solution.py:53
  14.8 1.6 %fusion.32 = bf16[4,512,128]{2,1,0:T(8,128)(2,1)} fusion(bf16[4,64,1,8,128]{4,1,3,0,2:T(8,128)(2,1)S(1)} %copy-done.4, pred[4,512]{1,0:T(4,128)(4,1)S(1)} %get-tuple-element.36, s32[8,16]{1,0:T(8,128)S(1)} %get-tuple-element.38, bf16[4,16,128]{2,0,1:T(4,128)(2,1)S(1)} %get-tuple-element.30), kind=kOutput, calls=%fused_computation.30 | convolution fusion | flops 8978432 | bytes 1067520 | tf_op jit(solution)/shard_map/jkr,jkd->jrd/dot_general | solution.py:195
  16.4 1.3 %reshape.97 = bf16[256,1024]{1,0:T(8,128)(2,1)S(1)} reshape(bf16[4,512,128]{2,1,0:T(8,128)(2,1)} %fusion.32) | data formatting | bytes 1048576 | tf_op jit(solution)/shard_map/reshape | solution.py:204
  17.7 3.1 %fusion.22 = bf16[256,1024]{1,0:T(8,128)(2,1)} fusion(bf16[256,1024]{1,0:T(8,128)(2,1)S(1)} %reshape.97, bf16[1024,4096]{1,0:T(8,128)(2,1)} %param.14, s32[]{:T(128)S(6)} %select_n.108), kind=kOutput, calls=%fused_computation.24 | convolution fusion | flops 537133056 | bytes 3145732 | tf_op jit(solution)/shard_map/dot_general | solution.py:53
  20.8 0.5 collective-permute-start.4
  21.5 2.4 %add_convert_fusion.3 = bf16[256,1024]{1,0:T(8,128)(2,1)S(1)} fusion(bf16[256,1024]{1,0:T(8,128)(2,1)} %collective-permute-done.1, bf16[256,1024]{1,0:T(8,128)(2,1)S(1)} %reshape.96, bf16[1024,4096]{1,0:T(8,128)(2,1)} %param.14, s32[]{:T(128)S(6)} %select_n.107), kind=kOutput, calls=%fused_computation.54 | convolution fusion | flops 537657344 | bytes 3670020 | tf_op jit(solution)/shard_map/dot_general | solution.py:53
  23.9 2.3 %fusion.25 = bf16[256,1024]{1,0:T(8,128)(2,1)S(1)} fusion(bf16[256,1024]{1,0:T(8,128)(2,1)S(1)} %reshape.96, bf16[1024,4096]{1,0:T(8,128)(2,1)} %param.14, s32[]{:T(128)S(6)} %select_n.110), kind=kOutput, calls=%fused_computation.25 | convolution fusion | flops 537133056 | bytes 3145732 | tf_op jit(solution)/shard_map/dot_general | solution.py:73
  26.2 0.1 collective-permute-start.2
  26.3 0.8 collective-permute-start.3
  27.2 2.4 %add_convert_fusion.1 = bf16[256,1024]{1,0:T(8,128)(2,1)S(1)} fusion(bf16[256,1024]{1,0:T(8,128)(2,1)} %collective-permute-done.4, bf16[256,1024]{1,0:T(8,128)(2,1)S(1)} %reshape.97, bf16[1024,4096]{1,0:T(8,128)(2,1)} %param.14, s32[]{:T(128)S(6)} %select_n.107), kind=kOutput, calls=%fused_computation.52 | convolution fusion | flops 537657344 | bytes 3670020 | tf_op jit(solution)/shard_map/dot_general | solution.py:53
  29.5 2.3 %fusion.28 = bf16[256,1024]{1,0:T(8,128)(2,1)S(1)} fusion(bf16[256,1024]{1,0:T(8,128)(2,1)S(1)} %reshape.97, bf16[1024,4096]{1,0:T(8,128)(2,1)} %param.14, s32[]{:T(128)S(6)} %select_n.110), kind=kOutput, calls=%fused_computation.26 | convolution fusion | flops 537133056 | bytes 3145732 | tf_op jit(solution)/shard_map/dot_general | solution.py:73
  31.9 0.2 collective-permute-start.5
  32.1 1.4 %collective-permute-start.6 = (bf16[256,1024]{1,0:T(8,128)(2,1)S(1)}, bf16[256,1024]{1,0:T(8,128)(2,1)S(1)}, u32[]{:S(2)}, u32[]{:S(2)}) collective-permute-start(bf16[256,1024]{1,0:T(8,128)(2,1)S(1)} %add_convert_fusion.1), channel_id=1, source_target_pairs={{0,2},{1,3},{2,0},{3,1},{4,6},{5,7},{6,4},{7,5},{8,10},{9,11},{10,... | collective-permute-start | bytes 1572872 | tf_op jit(solution)/shard_map/ppermute | solution.py:17
  33.5 2.3 %fusion.8 = f32[256,1024]{1,0:T(8,128)S(1)} fusion(bf16[256,1024]{1,0:T(8,128)(2,1)S(1)} %reshape.96, bf16[1024,4096]{1,0:T(8,128)(2,1)} %param.14, s32[]{:T(128)S(6)} %select_n.109), kind=kOutput, calls=%fused_computation.11 | convolution fusion | flops 536870912 | bytes 3670020 | tf_op jit(solution)/shard_map/dot_general | solution.py:73
  35.8 2.3 %fusion.6 = f32[256,1024]{1,0:T(8,128)S(1)} fusion(bf16[256,1024]{1,0:T(8,128)(2,1)S(1)} %reshape.97, bf16[1024,4096]{1,0:T(8,128)(2,1)} %param.14, s32[]{:T(128)S(6)} %select_n.109), kind=kOutput, calls=%fused_computation.9 | convolution fusion | flops 536870912 | bytes 3670020 | tf_op jit(solution)/shard_map/dot_general | solution.py:73
  38.1 3.1 %collective-permute-done.3 = bf16[256,1024]{1,0:T(8,128)(2,1)S(1)} collective-permute-done((bf16[256,1024]{1,0:T(8,128)(2,1)S(1)}, bf16[256,1024]{1,0:T(8,128)(2,1)S(1)}, u32[]{:S(2)}, u32[]{:S(2)}) %collective-permute-start.3) | collective-permute-done | bytes 524320 | tf_op jit(solution)/shard_map/ppermute | solution.py:17
  41.2 0.4 multiply_reduce_fusion.1
  41.6 0.7 fusion.50
  42.4 9.4 %collective-permute-done.6 = bf16[256,1024]{1,0:T(8,128)(2,1)S(1)} collective-permute-done((bf16[256,1024]{1,0:T(8,128)(2,1)S(1)}, bf16[256,1024]{1,0:T(8,128)(2,1)S(1)}, u32[]{:S(2)}, u32[]{:S(2)}) %collective-permute-start.6) | collective-permute-done | bytes 524320 | tf_op jit(solution)/shard_map/ppermute | solution.py:17
  51.9 0.4 multiply_reduce_fusion
  52.3 0.7 fusion.47
  53.1 0.8 collective-permute-start.8
  53.9 0.4 collective-permute-done.9
  54.3 1.0 collective-permute-start.10
  55.3 3.0 %collective-permute-done.8 = f32[256,65]{0,1:T(8,128)S(1)} collective-permute-done((f32[256,65]{0,1:T(8,128)S(1)}, f32[256,65]{0,1:T(8,128)S(1)}, u32[]{:S(2)}, u32[]{:S(2)}) %collective-permute-start.8) | collective-permute-done | bytes 66592 | tf_op jit(solution)/shard_map/ppermute | solution.py:17
  58.4 1.1 %collective-permute-done.10 = f32[256,65]{0,1:T(8,128)S(1)} collective-permute-done((f32[256,65]{0,1:T(8,128)S(1)}, f32[256,65]{0,1:T(8,128)S(1)}, u32[]{:S(2)}, u32[]{:S(2)}) %collective-permute-start.10) | collective-permute-done | bytes 66592 | tf_op jit(solution)/shard_map/ppermute | solution.py:17
  59.5 0.6 fusion.42
  60.1 0.6 fusion.33
  60.7 2.0 %collective-permute-start.11 = (f32[512,64]{0,1:T(8,128)S(1)}, f32[512,64]{0,1:T(8,128)S(1)}, u32[]{:S(2)}, u32[]{:S(2)}) collective-permute-start(f32[512,64]{0,1:T(8,128)S(1)} %slice_select_fusion), channel_id=1, source_target_pairs={{0,4},{4,0},{8,12},{12,8},{16,20},{20,16},{24,28},{28,24},{32,36},... | collective-permute-start | bytes 393224 | tf_op jit(solution)/shard_map/ppermute | solution.py:17
  62.7 3.3 %collective-permute-done.11 = f32[512,64]{0,1:T(8,128)S(1)} collective-permute-done((f32[512,64]{0,1:T(8,128)S(1)}, f32[512,64]{0,1:T(8,128)S(1)}, u32[]{:S(2)}, u32[]{:S(2)}) %collective-permute-start.11) | collective-permute-done | bytes 131104 | tf_op jit(solution)/shard_map/ppermute | solution.py:17
  66.1 0.7 collective-permute-start.12
  66.7 3.7 %collective-permute-done.12 = f32[256,64]{0,1:T(8,128)S(1)} collective-permute-done((f32[256,64]{0,1:T(8,128)S(1)}, f32[256,64]{0,1:T(8,128)S(1)}, u32[]{:S(2)}, u32[]{:S(2)}) %collective-permute-start.12) | collective-permute-done | bytes 65568 | tf_op jit(solution)/shard_map/ppermute | solution.py:17
  70.4 3.4 %collective-permute-start.13 = (f32[256,64]{0,1:T(8,128)S(1)}, f32[256,64]{0,1:T(8,128)S(1)}, u32[]{:S(2)}, u32[]{:S(2)}) collective-permute-start(f32[256,64]{0,1:T(8,128)S(1)} %select_add_fusion.1), channel_id=1, source_target_pairs={{0,8},{4,12},{8,0},{12,4},{16,24},{20,28},{24,16},{28,20},{32,40},... | collective-permute-start | bytes 196616 | tf_op jit(solution)/shard_map/ppermute | solution.py:17
  73.8 2.2 %collective-permute-done.13 = f32[256,64]{0,1:T(8,128)S(1)} collective-permute-done((f32[256,64]{0,1:T(8,128)S(1)}, f32[256,64]{0,1:T(8,128)S(1)}, u32[]{:S(2)}, u32[]{:S(2)}) %collective-permute-start.13) | collective-permute-done | bytes 65568 | tf_op jit(solution)/shard_map/ppermute | solution.py:17
  76.0 6.0 %collective-permute-start.14 = (f32[256,64]{0,1:T(8,128)S(1)}, f32[256,64]{0,1:T(8,128)S(1)}, u32[]{:S(2)}, u32[]{:S(2)}) collective-permute-start(f32[256,64]{0,1:T(8,128)S(1)} %add.140), channel_id=1, source_target_pairs={{0,24},{4,28},{8,16},{12,20},{16,8},{20,12},{24,0},{28,4},{32,56},... | collective-permute-start | bytes 196616 | tf_op jit(solution)/shard_map/ppermute | solution.py:17
  82.0 2.3 %collective-permute-done.14 = f32[256,64]{0,1:T(8,128)S(1)} collective-permute-done((f32[256,64]{0,1:T(8,128)S(1)}, f32[256,64]{0,1:T(8,128)S(1)}, u32[]{:S(2)}, u32[]{:S(2)}) %collective-permute-start.14) | collective-permute-done | bytes 65568 | tf_op jit(solution)/shard_map/ppermute | solution.py:17
  84.3 1.3 %collective-permute-start.15 = (f32[256,64]{0,1:T(8,128)S(1)}, f32[256,64]{0,1:T(8,128)S(1)}, u32[]{:S(2)}, u32[]{:S(2)}) collective-permute-start(f32[256,64]{0,1:T(8,128)S(1)} %add.141), channel_id=1, source_target_pairs={{0,32},{4,36},{8,40},{12,44},{16,48},{20,52},{24,56},{28,60},{32,0... | collective-permute-start | bytes 196616 | tf_op jit(solution)/shard_map/ppermute | solution.py:17
  85.6 4.5 %collective-permute-done.15 = f32[256,64]{0,1:T(8,128)S(1)} collective-permute-done((f32[256,64]{0,1:T(8,128)S(1)}, f32[256,64]{0,1:T(8,128)S(1)}, u32[]{:S(2)}, u32[]{:S(2)}) %collective-permute-start.15) | collective-permute-done | bytes 65568 | tf_op jit(solution)/shard_map/ppermute | solution.py:17
  90.2 1.6 %collective-permute-start.16 = (f32[256,64]{0,1:T(8,128)S(1)}, f32[256,64]{0,1:T(8,128)S(1)}, u32[]{:S(2)}, u32[]{:S(2)}) collective-permute-start(f32[256,64]{0,1:T(8,128)S(1)} %add.142), channel_id=1, source_target_pairs={{0,128},{4,132},{8,136},{12,140},{16,144},{20,148},{24,152},{28,15... | collective-permute-start | bytes 196616 | tf_op jit(solution)/shard_map/ppermute | solution.py:17
  91.8 1.0 pad_maximum_fusion
  92.9 3.2 %collective-permute-done.16 = f32[256,64]{0,1:T(8,128)S(1)} collective-permute-done((f32[256,64]{0,1:T(8,128)S(1)}, f32[256,64]{0,1:T(8,128)S(1)}, u32[]{:S(2)}, u32[]{:S(2)}) %collective-permute-start.16) | collective-permute-done | bytes 65568 | tf_op jit(solution)/shard_map/ppermute | solution.py:17
  96.1 0.7 collective-permute-start.17
  96.8 3.7 %collective-permute-done.17 = f32[256,64]{0,1:T(8,128)S(1)} collective-permute-done((f32[256,64]{0,1:T(8,128)S(1)}, f32[256,64]{0,1:T(8,128)S(1)}, u32[]{:S(2)}, u32[]{:S(2)}) %collective-permute-start.17) | collective-permute-done | bytes 65568 | tf_op jit(solution)/shard_map/ppermute | solution.py:17
  100.4 2.2 %collective-permute-start.18 = (f32[512,64]{0,1:T(8,128)S(1)}, f32[512,64]{0,1:T(8,128)S(1)}, u32[]{:S(2)}, u32[]{:S(2)}) collective-permute-start(f32[512,64]{0,1:T(8,128)S(1)} %maximum_select_fusion.1), channel_id=1, source_target_pairs={{0,4},{4,0},{8,12},{12,8},{16,20},{20,16},{24,28},{28,24},{32,36},... | collective-permute-start | bytes 393224 | tf_op jit(solution)/shard_map/ppermute | solution.py:17
  102.7 0.8 copy.38
  103.5 2.1 %collective-permute-done.18 = f32[512,64]{0,1:T(8,128)S(1)} collective-permute-done((f32[512,64]{0,1:T(8,128)S(1)}, f32[512,64]{0,1:T(8,128)S(1)}, u32[]{:S(2)}, u32[]{:S(2)}) %collective-permute-start.18) | collective-permute-done | bytes 131104 | tf_op jit(solution)/shard_map/ppermute | solution.py:17
  105.6 0.7 maximum_select_fusion
  (58 shorter events, 1.1 us)
Async XLA Ops:
  0.6 1.3 %copy-start = (bf16[8,64,1024]{2,1,0:T(8,128)(2,1)S(1)}, bf16[8,64,1024]{2,1,0:T(8,128)(2,1)}, u32[]{:S(2)}) copy-start(bf16[8,64,1024]{2,1,0:T(8,128)(2,1)} %param.11) | copy-start | bytes 3145732
  0.6 2.0 %copy-start.3 = (bf16[8,64,128]{2,1,0:T(8,128)(2,1)S(1)}, bf16[8,64,128]{2,1,0:T(8,128)(2,1)}, u32[]{:S(2)}) copy-start(bf16[8,64,128]{2,1,0:T(8,128)(2,1)} %param.12) | copy-start | bytes 393220
  0.7 2.4 %copy-start.8 = (bf16[8,64,128]{2,1,0:T(8,128)(2,1)S(1)}, bf16[8,64,128]{2,1,0:T(8,128)(2,1)}, u32[]{:S(2)}) copy-start(bf16[8,64,128]{2,1,0:T(8,128)(2,1)} %param.13) | copy-start | bytes 393220
  3.4 7.0 %collective-permute-start = (bf16[8,16,128]{2,0,1:T(8,128)(2,1)S(1)}, bf16[8,16,128]{2,0,1:T(8,128)(2,1)S(1)}, u32[]{:S(2)}, u32[]{:S(2)}) collective-permute-start(bf16[8,16,128]{2,0,1:T(8,128)(2,1)S(1)} %fusion.66), channel_id=1, source_target_pairs={{0,128},{4,132},{8,136},{12,140},{16,144},{20,148},{24,152},{28,15... | collective-permute-start | bytes 98312 | tf_op jit(solution)/shard_map/ppermute | solution.py:17
  8.8 1.4 %copy-start.1 = (bf16[8,64,1024]{2,1,0:T(8,128)(2,1)S(1)}, bf16[8,64,1024]{2,1,0:T(8,128)(2,1)}, u32[]{:S(2)}) copy-start(bf16[8,64,1024]{2,1,0:T(8,128)(2,1)} %param.10) | copy-start | bytes 3145732
  8.8 1.6 %copy-start.7 = (s32[8]{0:T(128)S(1)}, s32[8]{0:T(128)}, u32[]{:S(2)}) copy-start(s32[8]{0:T(128)} %param.17) | copy-start | bytes 100
  11.6 3.2 %copy-start.4 = (bf16[4,64,1,8,128]{4,1,3,0,2:T(8,128)(2,1)S(1)}, bf16[4,64,1,8,128]{4,1,3,0,2:T(8,128)(2,1)}, u32[]{:S(2)}) copy-start(bf16[4,64,1,8,128]{4,1,3,0,2:T(8,128)(2,1)} %get-tuple-element.28) | copy-start | bytes 1572868
  14.8 6.7 %collective-permute-start.1 = (bf16[256,1024]{1,0:T(8,128)(2,1)}, bf16[256,1024]{1,0:T(8,128)(2,1)}, u32[]{:S(2)}, u32[]{:S(2)}) collective-permute-start(bf16[256,1024]{1,0:T(8,128)(2,1)} %fusion.19), channel_id=1, source_target_pairs={{0,1},{1,0},{2,3},{3,2},{4,5},{5,4},{6,7},{7,6},{8,9},{9,8},{10,11... | collective-permute-start | bytes 1572872 | tf_op jit(solution)/shard_map/ppermute | solution.py:17
  16.4 4.9 %copy-start.6 = (s32[8,64]{1,0:T(8,128)S(1)}, s32[8,64]{1,0:T(8,128)}, u32[]{:S(2)}) copy-start(s32[8,64]{1,0:T(8,128)} %param.19) | copy-start | bytes 6148
  20.8 6.3 %collective-permute-start.4 = (bf16[256,1024]{1,0:T(8,128)(2,1)}, bf16[256,1024]{1,0:T(8,128)(2,1)}, u32[]{:S(2)}, u32[]{:S(2)}) collective-permute-start(bf16[256,1024]{1,0:T(8,128)(2,1)} %fusion.22), channel_id=1, source_target_pairs={{0,1},{1,0},{2,3},{3,2},{4,5},{5,4},{6,7},{7,6},{8,9},{9,8},{10,11... | collective-permute-start | bytes 1572872 | tf_op jit(solution)/shard_map/ppermute | solution.py:17
  26.2 15.0 %collective-permute-start.2 = (bf16[256,1024]{1,0:T(8,128)(2,1)S(1)}, bf16[256,1024]{1,0:T(8,128)(2,1)S(1)}, u32[]{:S(2)}, u32[]{:S(2)}) collective-permute-start(bf16[256,1024]{1,0:T(8,128)(2,1)S(1)} %fusion.25), channel_id=1, source_target_pairs={{0,1},{1,0},{2,3},{3,2},{4,5},{5,4},{6,7},{7,6},{8,9},{9,8},{10,11... | collective-permute-start | bytes 1572872 | tf_op jit(solution)/shard_map/ppermute | solution.py:17
  26.3 14.9 %collective-permute-start.3 = (bf16[256,1024]{1,0:T(8,128)(2,1)S(1)}, bf16[256,1024]{1,0:T(8,128)(2,1)S(1)}, u32[]{:S(2)}, u32[]{:S(2)}) collective-permute-start(bf16[256,1024]{1,0:T(8,128)(2,1)S(1)} %add_convert_fusion.3), channel_id=1, source_target_pairs={{0,2},{1,3},{2,0},{3,1},{4,6},{5,7},{6,4},{7,5},{8,10},{9,11},{10,... | collective-permute-start | bytes 1572872 | tf_op jit(solution)/shard_map/ppermute | solution.py:17
  31.9 10.6 %collective-permute-start.5 = (bf16[256,1024]{1,0:T(8,128)(2,1)S(1)}, bf16[256,1024]{1,0:T(8,128)(2,1)S(1)}, u32[]{:S(2)}, u32[]{:S(2)}) collective-permute-start(bf16[256,1024]{1,0:T(8,128)(2,1)S(1)} %fusion.28), channel_id=1, source_target_pairs={{0,1},{1,0},{2,3},{3,2},{4,5},{5,4},{6,7},{7,6},{8,9},{9,8},{10,11... | collective-permute-start | bytes 1572872 | tf_op jit(solution)/shard_map/ppermute | solution.py:17
  32.1 19.8 %collective-permute-start.6 = (bf16[256,1024]{1,0:T(8,128)(2,1)S(1)}, bf16[256,1024]{1,0:T(8,128)(2,1)S(1)}, u32[]{:S(2)}, u32[]{:S(2)}) collective-permute-start(bf16[256,1024]{1,0:T(8,128)(2,1)S(1)} %add_convert_fusion.1), channel_id=1, source_target_pairs={{0,2},{1,3},{2,0},{3,1},{4,6},{5,7},{6,4},{7,5},{8,10},{9,11},{10,... | collective-permute-start | bytes 1572872 | tf_op jit(solution)/shard_map/ppermute | solution.py:17
  38.1 3.5 %copy-start.2 = (f32[1024,64]{0,1:T(8,128)S(1)}, f32[1024,64]{0,1:T(8,128)}, u32[]{:S(2)}) copy-start(f32[1024,64]{0,1:T(8,128)} %param.16) | copy-start | bytes 786436
  38.1 3.5 %copy-start.5 = (f32[1024]{0:T(1024)S(1)}, f32[1024]{0:T(1024)}, u32[]{:S(2)}) copy-start(f32[1024]{0:T(1024)} %param.15) | copy-start | bytes 12292
  42.3 10.8 %collective-permute-start.7 = (f32[256,65]{0,1:T(8,128)S(1)}, f32[256,65]{0,1:T(8,128)S(1)}, u32[]{:S(2)}, u32[]{:S(2)}) collective-permute-start(f32[256,65]{0,1:T(8,128)S(1)} %pad_maximum_fusion.2), channel_id=1, source_target_pairs={{0,1},{1,0},{2,3},{3,2},{4,5},{5,4},{6,7},{7,6},{8,9},{9,8},{10,11... | collective-permute-start | bytes 199688 | tf_op jit(solution)/shard_map/ppermute | solution.py:17
  53.0 1.4 %collective-permute-start.9 = (f32[256,65]{0,1:T(8,128)S(1)}, f32[256,65]{0,1:T(8,128)S(1)}, u32[]{:S(2)}, u32[]{:S(2)}) collective-permute-start(f32[256,65]{0,1:T(8,128)S(1)} %pad_maximum_fusion.3), channel_id=1, source_target_pairs={{0,1},{1,0},{2,3},{3,2},{4,5},{5,4},{6,7},{7,6},{8,9},{9,8},{10,11... | collective-permute-start | bytes 199688 | tf_op jit(solution)/shard_map/ppermute | solution.py:17
  53.1 5.2 %collective-permute-start.8 = (f32[256,65]{0,1:T(8,128)S(1)}, f32[256,65]{0,1:T(8,128)S(1)}, u32[]{:S(2)}, u32[]{:S(2)}) collective-permute-start(f32[256,65]{0,1:T(8,128)S(1)} %fusion.118), channel_id=1, source_target_pairs={{0,2},{1,3},{2,0},{3,1},{4,6},{5,7},{6,4},{7,5},{8,10},{9,11},{10,... | collective-permute-start | bytes 199688 | tf_op jit(solution)/shard_map/ppermute | solution.py:17
  54.3 5.1 %collective-permute-start.10 = (f32[256,65]{0,1:T(8,128)S(1)}, f32[256,65]{0,1:T(8,128)S(1)}, u32[]{:S(2)}, u32[]{:S(2)}) collective-permute-start(f32[256,65]{0,1:T(8,128)S(1)} %fusion.117), channel_id=1, source_target_pairs={{0,2},{1,3},{2,0},{3,1},{4,6},{5,7},{6,4},{7,5},{8,10},{9,11},{10,... | collective-permute-start | bytes 199688 | tf_op jit(solution)/shard_map/ppermute | solution.py:17
  60.7 5.3 %collective-permute-start.11 = (f32[512,64]{0,1:T(8,128)S(1)}, f32[512,64]{0,1:T(8,128)S(1)}, u32[]{:S(2)}, u32[]{:S(2)}) collective-permute-start(f32[512,64]{0,1:T(8,128)S(1)} %slice_select_fusion), channel_id=1, source_target_pairs={{0,4},{4,0},{8,12},{12,8},{16,20},{20,16},{24,28},{28,24},{32,36},... | collective-permute-start | bytes 393224 | tf_op jit(solution)/shard_map/ppermute | solution.py:17
  66.1 4.4 %collective-permute-start.12 = (f32[256,64]{0,1:T(8,128)S(1)}, f32[256,64]{0,1:T(8,128)S(1)}, u32[]{:S(2)}, u32[]{:S(2)}) collective-permute-start(f32[256,64]{0,1:T(8,128)S(1)} %slice_select_fusion.1), channel_id=1, source_target_pairs={{0,64},{4,68},{8,72},{12,76},{16,80},{20,84},{24,88},{28,92},{32,9... | collective-permute-start | bytes 196616 | tf_op jit(solution)/shard_map/ppermute | solution.py:17
  70.4 5.6 %collective-permute-start.13 = (f32[256,64]{0,1:T(8,128)S(1)}, f32[256,64]{0,1:T(8,128)S(1)}, u32[]{:S(2)}, u32[]{:S(2)}) collective-permute-start(f32[256,64]{0,1:T(8,128)S(1)} %select_add_fusion.1), channel_id=1, source_target_pairs={{0,8},{4,12},{8,0},{12,4},{16,24},{20,28},{24,16},{28,20},{32,40},... | collective-permute-start | bytes 196616 | tf_op jit(solution)/shard_map/ppermute | solution.py:17
  76.0 8.3 %collective-permute-start.14 = (f32[256,64]{0,1:T(8,128)S(1)}, f32[256,64]{0,1:T(8,128)S(1)}, u32[]{:S(2)}, u32[]{:S(2)}) collective-permute-start(f32[256,64]{0,1:T(8,128)S(1)} %add.140), channel_id=1, source_target_pairs={{0,24},{4,28},{8,16},{12,20},{16,8},{20,12},{24,0},{28,4},{32,56},... | collective-permute-start | bytes 196616 | tf_op jit(solution)/shard_map/ppermute | solution.py:17
  84.3 5.9 %collective-permute-start.15 = (f32[256,64]{0,1:T(8,128)S(1)}, f32[256,64]{0,1:T(8,128)S(1)}, u32[]{:S(2)}, u32[]{:S(2)}) collective-permute-start(f32[256,64]{0,1:T(8,128)S(1)} %add.141), channel_id=1, source_target_pairs={{0,32},{4,36},{8,40},{12,44},{16,48},{20,52},{24,56},{28,60},{32,0... | collective-permute-start | bytes 196616 | tf_op jit(solution)/shard_map/ppermute | solution.py:17
  90.2 5.9 %collective-permute-start.16 = (f32[256,64]{0,1:T(8,128)S(1)}, f32[256,64]{0,1:T(8,128)S(1)}, u32[]{:S(2)}, u32[]{:S(2)}) collective-permute-start(f32[256,64]{0,1:T(8,128)S(1)} %add.142), channel_id=1, source_target_pairs={{0,128},{4,132},{8,136},{12,140},{16,144},{20,148},{24,152},{28,15... | collective-permute-start | bytes 196616 | tf_op jit(solution)/shard_map/ppermute | solution.py:17
  96.1 4.4 %collective-permute-start.17 = (f32[256,64]{0,1:T(8,128)S(1)}, f32[256,64]{0,1:T(8,128)S(1)}, u32[]{:S(2)}, u32[]{:S(2)}) collective-permute-start(f32[256,64]{0,1:T(8,128)S(1)} %add.143), channel_id=1, source_target_pairs={{0,64},{4,68},{8,72},{12,76},{16,80},{20,84},{24,88},{28,92},{32,9... | collective-permute-start | bytes 196616 | tf_op jit(solution)/shard_map/ppermute | solution.py:17
  100.4 5.1 %collective-permute-start.18 = (f32[512,64]{0,1:T(8,128)S(1)}, f32[512,64]{0,1:T(8,128)S(1)}, u32[]{:S(2)}, u32[]{:S(2)}) collective-permute-start(f32[512,64]{0,1:T(8,128)S(1)} %maximum_select_fusion.1), channel_id=1, source_target_pairs={{0,4},{4,0},{8,12},{12,8},{16,20},{20,16},{24,28},{28,24},{32,36},... | collective-permute-start | bytes 393224 | tf_op jit(solution)/shard_map/ppermute | solution.py:17

commit v15 on v13

--- a/solution.py
+++ b/solution.py
@@ -37,7 +37,7 @@
     block = butterfly_sum(block, axis, doubling_bits)
     for bit, upper in reversed(kept):
         other = exchanged(block, axis, bit)
-        block = jnp.where(upper, jnp.concatenate([other, block]), jnp.concatenate([block, other]))
+        block = jnp.concatenate([jnp.where(upper, other, block), jnp.where(upper, block, other)])
     return block
 
 

time: 102 us -> 102 us (level)
  no operation moved by 1% of the time
where the time goes in v15:
time: 102 us
  waiting for transfers between devices  39 us (38%)
  starting transfers between devices  26.3 us (26%)
  matrix products  26.2 us (26%)
  local copies, waits for them, and re-layouts  5.25 us (5%)
  other arithmetic  3.78 us (4%)
  between operations  1.09 us (1%)
    ppermute x19, waiting for transfers between devices, exchanged(): return lax.ppermute(block, axis, [(i, i ^ bit) for i in range(count)])  39 us
    ppermute x19, starting transfers between devices, exchanged(): return lax.ppermute(block, axis, [(i, i ^ bit) for i in range(count)])  26.3 us
    dot_general x8, matrix products, block(): return jnp.dot(heads, columns, preferred_element_type=jnp.float32)  19.4 us
  transfers between devices with their start and end apart: 19, of which 13 were waited for; matrix products, arithmetic and copies ran while one was open for 24% of the time, Pallas kernels for 0%

profile of v15, /device:TPU:24, one launch (start us, length us, event | category | flops | bytes accessed | tf_op | source)
XLA Modules:
  0.0 101.6 jit_solution(5409181497967604087)
XLA Ops:
  0.7 0.8 fusion.117
  1.6 1.5 %reshape.93 = bf16[8,512,128]{2,1,0:T(8,128)(2,1)S(1)} reshape(bf16[8,64,1024]{2,1,0:T(8,128)(2,1)} %param.11) | data formatting | bytes 2097152 | tf_op jit(solution)/shard_map/reshape | solution.py:118
  3.2 0.4 fusion.37
  3.6 0.2 fusion.121
  3.8 0.3 fusion.78
  4.2 3.1 %collective-permute-start = (bf16[8,16,128]{2,0,1:T(8,128)(2,1)S(1)}, bf16[8,16,128]{2,0,1:T(8,128)(2,1)S(1)}, u32[]{:S(2)}, u32[]{:S(2)}) collective-permute-start(bf16[8,16,128]{2,0,1:T(8,128)(2,1)S(1)} %fusion.65), channel_id=1, source_target_pairs={{0,128},{4,132},{8,136},{12,140},{16,144},{20,148},{24,152},{28,15... | collective-permute-start | bytes 98312 | tf_op jit(solution)/shard_map/ppermute | solution.py:17
  7.3 0.1 fusion.58
  7.4 1.1 %fusion.120 = (f32[8,8,64]{2,1,0:T(8,128)S(1)}, f32[8,1,8,64,64]{3,4,2,0,1:T(8,128)S(1)}) fusion(bf16[8,64,128]{2,1,0:T(8,128)(2,1)S(1)} %copy-done.3, pred[64,64]{0,1:T(8,128)(4,1)S(1)} %iota_compare_fusion.10, bf16[8,64,1024]{2,1,0:T(8,128)(2,1)S(1)} %copy-done.1), kind=kOutput, calls=%fused_computation.156 | convolution fusion | flops 67891200 | bytes 2248704 | tf_op jit(solution)/shard_map/pqkgd,pskd->pkgqs/dot_general | solution.py:95
  8.6 0.5 fusion.1
  9.1 0.6 fusion.18
  9.8 0.1 fusion.115
  9.9 1.1 %copy-done.2 = bf16[8,64,1024]{2,1,0:T(8,128)(2,1)S(1)} copy-done((bf16[8,64,1024]{2,1,0:T(8,128)(2,1)S(1)}, bf16[8,64,1024]{2,1,0:T(8,128)(2,1)}, u32[]{:S(2)}) %copy-start.2) | copy-done | bytes 1048600
  11.0 0.1 fusion.114
  11.1 0.2 convolution_convert_fusion.3
  11.3 0.8 fusion.31
  12.1 0.2 reshape.96
  12.4 3.1 %fusion.19 = bf16[256,1024]{1,0:T(8,128)(2,1)} fusion(bf16[256,1024]{1,0:T(8,128)(2,1)S(1)} %reshape.96, bf16[1024,4096]{1,0:T(8,128)(2,1)} %param.14, s32[]{:T(128)S(6)} %select_n.109), kind=kOutput, calls=%fused_computation.23 | convolution fusion | flops 537133056 | bytes 3145732 | tf_op jit(solution)/shard_map/dot_general | solution.py:53
  15.5 0.8 fusion.32
  16.3 0.2 reshape.97
  16.5 2.3 %fusion.22 = bf16[256,1024]{1,0:T(8,128)(2,1)S(1)} fusion(bf16[256,1024]{1,0:T(8,128)(2,1)S(1)} %reshape.97, bf16[1024,4096]{1,0:T(8,128)(2,1)} %param.14, s32[]{:T(128)S(6)} %select_n.109), kind=kOutput, calls=%fused_computation.24 | convolution fusion | flops 537133056 | bytes 3145732 | tf_op jit(solution)/shard_map/dot_general | solution.py:53
  18.8 0.6 collective-permute-start.4
  19.6 2.4 %add_convert_fusion.3 = bf16[256,1024]{1,0:T(8,128)(2,1)S(1)} fusion(bf16[256,1024]{1,0:T(8,128)(2,1)} %collective-permute-done.1, bf16[256,1024]{1,0:T(8,128)(2,1)S(1)} %reshape.96, bf16[1024,4096]{1,0:T(8,128)(2,1)} %param.14, s32[]{:T(128)S(6)} %select_n.108), kind=kOutput, calls=%fused_computation.54 | convolution fusion | flops 537657344 | bytes 3670020 | tf_op jit(solution)/shard_map/dot_general | solution.py:53
  22.0 0.8 collective-permute-start.3
  22.8 2.3 %fusion.25 = bf16[256,1024]{1,0:T(8,128)(2,1)S(1)} fusion(bf16[256,1024]{1,0:T(8,128)(2,1)S(1)} %reshape.96, bf16[1024,4096]{1,0:T(8,128)(2,1)} %param.14, s32[]{:T(128)S(6)} %select_n.111), kind=kOutput, calls=%fused_computation.25 | convolution fusion | flops 537133056 | bytes 3145732 | tf_op jit(solution)/shard_map/dot_general | solution.py:73
  25.1 0.1 collective-permute-start.2
  25.2 2.4 %add_convert_fusion.1 = bf16[256,1024]{1,0:T(8,128)(2,1)S(1)} fusion(bf16[256,1024]{1,0:T(8,128)(2,1)} %collective-permute-done.4, bf16[256,1024]{1,0:T(8,128)(2,1)S(1)} %reshape.97, bf16[1024,4096]{1,0:T(8,128)(2,1)} %param.14, s32[]{:T(128)S(6)} %select_n.108), kind=kOutput, calls=%fused_computation.52 | convolution fusion | flops 537657344 | bytes 3670020 | tf_op jit(solution)/shard_map/dot_general | solution.py:53
  27.6 2.3 %fusion.28 = bf16[256,1024]{1,0:T(8,128)(2,1)S(1)} fusion(bf16[256,1024]{1,0:T(8,128)(2,1)S(1)} %reshape.97, bf16[1024,4096]{1,0:T(8,128)(2,1)} %param.14, s32[]{:T(128)S(6)} %select_n.111), kind=kOutput, calls=%fused_computation.26 | convolution fusion | flops 537133056 | bytes 3145732 | tf_op jit(solution)/shard_map/dot_general | solution.py:73
  29.9 0.6 collective-permute-start.5
  30.5 1.3 %collective-permute-start.6 = (bf16[256,1024]{1,0:T(8,128)(2,1)S(1)}, bf16[256,1024]{1,0:T(8,128)(2,1)S(1)}, u32[]{:S(2)}, u32[]{:S(2)}) collective-permute-start(bf16[256,1024]{1,0:T(8,128)(2,1)S(1)} %add_convert_fusion.1), channel_id=1, source_target_pairs={{0,2},{1,3},{2,0},{3,1},{4,6},{5,7},{6,4},{7,5},{8,10},{9,11},{10,... | collective-permute-start | bytes 1572872 | tf_op jit(solution)/shard_map/ppermute | solution.py:17
  31.8 2.3 %fusion.8 = f32[256,1024]{1,0:T(8,128)S(1)} fusion(bf16[256,1024]{1,0:T(8,128)(2,1)S(1)} %reshape.96, bf16[1024,4096]{1,0:T(8,128)(2,1)} %param.14, s32[]{:T(128)S(6)} %select_n.110), kind=kOutput, calls=%fused_computation.11 | convolution fusion | flops 536870912 | bytes 3670020 | tf_op jit(solution)/shard_map/dot_general | solution.py:73
  34.1 2.3 %fusion.6 = f32[256,1024]{1,0:T(8,128)S(1)} fusion(bf16[256,1024]{1,0:T(8,128)(2,1)S(1)} %reshape.97, bf16[1024,4096]{1,0:T(8,128)(2,1)} %param.14, s32[]{:T(128)S(6)} %select_n.110), kind=kOutput, calls=%fused_computation.9 | convolution fusion | flops 536870912 | bytes 3670020 | tf_op jit(solution)/shard_map/dot_general | solution.py:73
  36.4 0.4 collective-permute-done.3
  36.9 0.4 multiply_reduce_fusion.1
  37.3 0.7 fusion.50
  38.0 0.1 collective-permute-start.7
  38.1 9.1 %collective-permute-done.6 = bf16[256,1024]{1,0:T(8,128)(2,1)S(1)} collective-permute-done((bf16[256,1024]{1,0:T(8,128)(2,1)S(1)}, bf16[256,1024]{1,0:T(8,128)(2,1)S(1)}, u32[]{:S(2)}, u32[]{:S(2)}) %collective-permute-start.6) | collective-permute-done | bytes 524320 | tf_op jit(solution)/shard_map/ppermute | solution.py:17
  47.2 0.4 multiply_reduce_fusion
  47.6 0.7 fusion.47
  48.4 0.8 collective-permute-start.8
  49.2 0.4 collective-permute-done.9
  49.6 1.0 collective-permute-start.10
  50.6 3.0 %collective-permute-done.8 = f32[256,65]{0,1:T(8,128)S(1)} collective-permute-done((f32[256,65]{0,1:T(8,128)S(1)}, f32[256,65]{0,1:T(8,128)S(1)}, u32[]{:S(2)}, u32[]{:S(2)}) %collective-permute-start.8) | collective-permute-done | bytes 66592 | tf_op jit(solution)/shard_map/ppermute | solution.py:17
  53.7 1.1 %collective-permute-done.10 = f32[256,65]{0,1:T(8,128)S(1)} collective-permute-done((f32[256,65]{0,1:T(8,128)S(1)}, f32[256,65]{0,1:T(8,128)S(1)}, u32[]{:S(2)}, u32[]{:S(2)}) %collective-permute-start.10) | collective-permute-done | bytes 66592 | tf_op jit(solution)/shard_map/ppermute | solution.py:17
  54.8 0.6 fusion.42
  55.4 0.6 fusion.33
  56.0 2.0 %collective-permute-start.11 = (f32[512,64]{0,1:T(8,128)S(1)}, f32[512,64]{0,1:T(8,128)S(1)}, u32[]{:S(2)}, u32[]{:S(2)}) collective-permute-start(f32[512,64]{0,1:T(8,128)S(1)} %slice_select_fusion), channel_id=1, source_target_pairs={{0,4},{4,0},{8,12},{12,8},{16,20},{20,16},{24,28},{28,24},{32,36},... | collective-permute-start | bytes 393224 | tf_op jit(solution)/shard_map/ppermute | solution.py:17
  58.0 3.3 %collective-permute-done.11 = f32[512,64]{0,1:T(8,128)S(1)} collective-permute-done((f32[512,64]{0,1:T(8,128)S(1)}, f32[512,64]{0,1:T(8,128)S(1)}, u32[]{:S(2)}, u32[]{:S(2)}) %collective-permute-start.11) | collective-permute-done | bytes 131104 | tf_op jit(solution)/shard_map/ppermute | solution.py:17
  61.4 0.7 collective-permute-start.12
  62.0 3.7 %collective-permute-done.12 = f32[256,64]{0,1:T(8,128)S(1)} collective-permute-done((f32[256,64]{0,1:T(8,128)S(1)}, f32[256,64]{0,1:T(8,128)S(1)}, u32[]{:S(2)}, u32[]{:S(2)}) %collective-permute-start.12) | collective-permute-done | bytes 65568 | tf_op jit(solution)/shard_map/ppermute | solution.py:17
  65.7 3.3 %collective-permute-start.13 = (f32[256,64]{0,1:T(8,128)S(1)}, f32[256,64]{0,1:T(8,128)S(1)}, u32[]{:S(2)}, u32[]{:S(2)}) collective-permute-start(f32[256,64]{0,1:T(8,128)S(1)} %select_add_fusion.1), channel_id=1, source_target_pairs={{0,8},{4,12},{8,0},{12,4},{16,24},{20,28},{24,16},{28,20},{32,40},... | collective-permute-start | bytes 196616 | tf_op jit(solution)/shard_map/ppermute | solution.py:17
  69.1 2.2 %collective-permute-done.13 = f32[256,64]{0,1:T(8,128)S(1)} collective-permute-done((f32[256,64]{0,1:T(8,128)S(1)}, f32[256,64]{0,1:T(8,128)S(1)}, u32[]{:S(2)}, u32[]{:S(2)}) %collective-permute-start.13) | collective-permute-done | bytes 65568 | tf_op jit(solution)/shard_map/ppermute | solution.py:17
  71.3 6.0 %collective-permute-start.14 = (f32[256,64]{0,1:T(8,128)S(1)}, f32[256,64]{0,1:T(8,128)S(1)}, u32[]{:S(2)}, u32[]{:S(2)}) collective-permute-start(f32[256,64]{0,1:T(8,128)S(1)} %add.139), channel_id=1, source_target_pairs={{0,24},{4,28},{8,16},{12,20},{16,8},{20,12},{24,0},{28,4},{32,56},... | collective-permute-start | bytes 196616 | tf_op jit(solution)/shard_map/ppermute | solution.py:17
  77.3 2.3 %collective-permute-done.14 = f32[256,64]{0,1:T(8,128)S(1)} collective-permute-done((f32[256,64]{0,1:T(8,128)S(1)}, f32[256,64]{0,1:T(8,128)S(1)}, u32[]{:S(2)}, u32[]{:S(2)}) %collective-permute-start.14) | collective-permute-done | bytes 65568 | tf_op jit(solution)/shard_map/ppermute | solution.py:17
  79.6 1.3 %collective-permute-start.15 = (f32[256,64]{0,1:T(8,128)S(1)}, f32[256,64]{0,1:T(8,128)S(1)}, u32[]{:S(2)}, u32[]{:S(2)}) collective-permute-start(f32[256,64]{0,1:T(8,128)S(1)} %add.140), channel_id=1, source_target_pairs={{0,32},{4,36},{8,40},{12,44},{16,48},{20,52},{24,56},{28,60},{32,0... | collective-permute-start | bytes 196616 | tf_op jit(solution)/shard_map/ppermute | solution.py:17
  80.9 4.5 %collective-permute-done.15 = f32[256,64]{0,1:T(8,128)S(1)} collective-permute-done((f32[256,64]{0,1:T(8,128)S(1)}, f32[256,64]{0,1:T(8,128)S(1)}, u32[]{:S(2)}, u32[]{:S(2)}) %collective-permute-start.15) | collective-permute-done | bytes 65568 | tf_op jit(solution)/shard_map/ppermute | solution.py:17
  85.5 1.7 %collective-permute-start.16 = (f32[256,64]{0,1:T(8,128)S(1)}, f32[256,64]{0,1:T(8,128)S(1)}, u32[]{:S(2)}, u32[]{:S(2)}) collective-permute-start(f32[256,64]{0,1:T(8,128)S(1)} %add.141), channel_id=1, source_target_pairs={{0,128},{4,132},{8,136},{12,140},{16,144},{20,148},{24,152},{28,15... | collective-permute-start | bytes 196616 | tf_op jit(solution)/shard_map/ppermute | solution.py:17
  87.2 1.0 %pad_maximum_fusion = bf16[512,1024]{1,0:T(8,128)(2,1)} fusion(bf16[256,1024]{1,0:T(8,128)(2,1)S(1)} %get-tuple-element.24, bf16[256,1024]{1,0:T(8,128)(2,1)S(1)} %get-tuple-element.22), kind=kLoop, calls=%fused_computation.42 | loop fusion | flops 2097152 | bytes 2097152 | tf_op jit(solution)/shard_map/concatenate | solution.py:237
  88.2 3.2 %collective-permute-done.16 = f32[256,64]{0,1:T(8,128)S(1)} collective-permute-done((f32[256,64]{0,1:T(8,128)S(1)}, f32[256,64]{0,1:T(8,128)S(1)}, u32[]{:S(2)}, u32[]{:S(2)}) %collective-permute-start.16) | collective-permute-done | bytes 65568 | tf_op jit(solution)/shard_map/ppermute | solution.py:17
  91.4 0.7 collective-permute-start.17
  92.0 3.7 %collective-permute-done.17 = f32[256,64]{0,1:T(8,128)S(1)} collective-permute-done((f32[256,64]{0,1:T(8,128)S(1)}, f32[256,64]{0,1:T(8,128)S(1)}, u32[]{:S(2)}, u32[]{:S(2)}) %collective-permute-start.17) | collective-permute-done | bytes 65568 | tf_op jit(solution)/shard_map/ppermute | solution.py:17
  95.8 2.2 %collective-permute-start.18 = (f32[512,64]{0,1:T(8,128)S(1)}, f32[512,64]{0,1:T(8,128)S(1)}, u32[]{:S(2)}, u32[]{:S(2)}) collective-permute-start(f32[512,64]{0,1:T(8,128)S(1)} %pad_maximum_fusion.3), channel_id=1, source_target_pairs={{0,4},{4,0},{8,12},{12,8},{16,20},{20,16},{24,28},{28,24},{32,36},... | collective-permute-start | bytes 393224 | tf_op jit(solution)/shard_map/ppermute | solution.py:17
  98.0 0.8 copy.36
  98.8 2.1 %collective-permute-done.18 = f32[512,64]{0,1:T(8,128)S(1)} collective-permute-done((f32[512,64]{0,1:T(8,128)S(1)}, f32[512,64]{0,1:T(8,128)S(1)}, u32[]{:S(2)}, u32[]{:S(2)}) %collective-permute-start.18) | collective-permute-done | bytes 131104 | tf_op jit(solution)/shard_map/ppermute | solution.py:17
  100.9 0.7 pad_maximum_fusion.1
  (55 shorter events, 0.8 us)
Async XLA Ops:
  0.6 36.6 %copy-start = (f32[1024,64]{0,1:T(8,128)S(1)}, f32[1024,64]{0,1:T(8,128)}, u32[]{:S(2)}) copy-start(f32[1024,64]{0,1:T(8,128)} %param.16) | copy-start | bytes 786436
  0.6 6.8 %copy-start.1 = (bf16[8,64,1024]{2,1,0:T(8,128)(2,1)S(1)}, bf16[8,64,1024]{2,1,0:T(8,128)(2,1)}, u32[]{:S(2)}) copy-start(bf16[8,64,1024]{2,1,0:T(8,128)(2,1)} %param.11) | copy-start | bytes 3145732
  0.7 2.5 %copy-start.3 = (bf16[8,64,128]{2,1,0:T(8,128)(2,1)S(1)}, bf16[8,64,128]{2,1,0:T(8,128)(2,1)}, u32[]{:S(2)}) copy-start(bf16[8,64,128]{2,1,0:T(8,128)(2,1)} %param.12) | copy-start | bytes 393220
  0.7 3.1 %copy-start.7 = (bf16[8,64,128]{2,1,0:T(8,128)(2,1)S(1)}, bf16[8,64,128]{2,1,0:T(8,128)(2,1)}, u32[]{:S(2)}) copy-start(bf16[8,64,128]{2,1,0:T(8,128)(2,1)} %param.13) | copy-start | bytes 393220
  4.2 6.9 %collective-permute-start = (bf16[8,16,128]{2,0,1:T(8,128)(2,1)S(1)}, bf16[8,16,128]{2,0,1:T(8,128)(2,1)S(1)}, u32[]{:S(2)}, u32[]{:S(2)}) collective-permute-start(bf16[8,16,128]{2,0,1:T(8,128)(2,1)S(1)} %fusion.65), channel_id=1, source_target_pairs={{0,128},{4,132},{8,136},{12,140},{16,144},{20,148},{24,152},{28,15... | collective-permute-start | bytes 98312 | tf_op jit(solution)/shard_map/ppermute | solution.py:17
  9.7 1.2 %copy-start.2 = (bf16[8,64,1024]{2,1,0:T(8,128)(2,1)S(1)}, bf16[8,64,1024]{2,1,0:T(8,128)(2,1)}, u32[]{:S(2)}) copy-start(bf16[8,64,1024]{2,1,0:T(8,128)(2,1)} %param.10) | copy-start | bytes 3145732
  9.7 1.4 %copy-start.6 = (s32[8]{0:T(128)S(1)}, s32[8]{0:T(128)}, u32[]{:S(2)}) copy-start(s32[8]{0:T(128)} %param.17) | copy-start | bytes 100
  15.5 4.1 %collective-permute-start.1 = (bf16[256,1024]{1,0:T(8,128)(2,1)}, bf16[256,1024]{1,0:T(8,128)(2,1)}, u32[]{:S(2)}, u32[]{:S(2)}) collective-permute-start(bf16[256,1024]{1,0:T(8,128)(2,1)} %fusion.19), channel_id=1, source_target_pairs={{0,1},{1,0},{2,3},{3,2},{4,5},{5,4},{6,7},{7,6},{8,9},{9,8},{10,11... | collective-permute-start | bytes 1572872 | tf_op jit(solution)/shard_map/ppermute | solution.py:17
  16.2 3.2 %copy-start.5 = (s32[8,64]{1,0:T(8,128)S(1)}, s32[8,64]{1,0:T(8,128)}, u32[]{:S(2)}) copy-start(s32[8,64]{1,0:T(8,128)} %param.19) | copy-start | bytes 6148
  18.8 6.4 %collective-permute-start.4 = (bf16[256,1024]{1,0:T(8,128)(2,1)S(1)}, bf16[256,1024]{1,0:T(8,128)(2,1)}, u32[]{:S(2)}, u32[]{:S(2)}) collective-permute-start(bf16[256,1024]{1,0:T(8,128)(2,1)S(1)} %fusion.22), channel_id=1, source_target_pairs={{0,1},{1,0},{2,3},{3,2},{4,5},{5,4},{6,7},{7,6},{8,9},{9,8},{10,11... | collective-permute-start | bytes 1572872 | tf_op jit(solution)/shard_map/ppermute | solution.py:17
  22.0 14.9 %collective-permute-start.3 = (bf16[256,1024]{1,0:T(8,128)(2,1)S(1)}, bf16[256,1024]{1,0:T(8,128)(2,1)S(1)}, u32[]{:S(2)}, u32[]{:S(2)}) collective-permute-start(bf16[256,1024]{1,0:T(8,128)(2,1)S(1)} %add_convert_fusion.3), channel_id=1, source_target_pairs={{0,2},{1,3},{2,0},{3,1},{4,6},{5,7},{6,4},{7,5},{8,10},{9,11},{10,... | collective-permute-start | bytes 1572872 | tf_op jit(solution)/shard_map/ppermute | solution.py:17
  25.1 11.7 %collective-permute-start.2 = (bf16[256,1024]{1,0:T(8,128)(2,1)S(1)}, bf16[256,1024]{1,0:T(8,128)(2,1)S(1)}, u32[]{:S(2)}, u32[]{:S(2)}) collective-permute-start(bf16[256,1024]{1,0:T(8,128)(2,1)S(1)} %fusion.25), channel_id=1, source_target_pairs={{0,1},{1,0},{2,3},{3,2},{4,5},{5,4},{6,7},{7,6},{8,9},{9,8},{10,11... | collective-permute-start | bytes 1572872 | tf_op jit(solution)/shard_map/ppermute | solution.py:17
  29.9 8.1 %collective-permute-start.5 = (bf16[256,1024]{1,0:T(8,128)(2,1)S(1)}, bf16[256,1024]{1,0:T(8,128)(2,1)S(1)}, u32[]{:S(2)}, u32[]{:S(2)}) collective-permute-start(bf16[256,1024]{1,0:T(8,128)(2,1)S(1)} %fusion.28), channel_id=1, source_target_pairs={{0,1},{1,0},{2,3},{3,2},{4,5},{5,4},{6,7},{7,6},{8,9},{9,8},{10,11... | collective-permute-start | bytes 1572872 | tf_op jit(solution)/shard_map/ppermute | solution.py:17
  30.5 16.7 %collective-permute-start.6 = (bf16[256,1024]{1,0:T(8,128)(2,1)S(1)}, bf16[256,1024]{1,0:T(8,128)(2,1)S(1)}, u32[]{:S(2)}, u32[]{:S(2)}) collective-permute-start(bf16[256,1024]{1,0:T(8,128)(2,1)S(1)} %add_convert_fusion.1), channel_id=1, source_target_pairs={{0,2},{1,3},{2,0},{3,1},{4,6},{5,7},{6,4},{7,5},{8,10},{9,11},{10,... | collective-permute-start | bytes 1572872 | tf_op jit(solution)/shard_map/ppermute | solution.py:17
  36.4 0.9 copy-start.4
  38.0 10.4 %collective-permute-start.7 = (f32[256,65]{0,1:T(8,128)S(1)}, f32[256,65]{0,1:T(8,128)S(1)}, u32[]{:S(2)}, u32[]{:S(2)}) collective-permute-start(f32[256,65]{0,1:T(8,128)S(1)} %pad_maximum_fusion.4), channel_id=1, source_target_pairs={{0,1},{1,0},{2,3},{3,2},{4,5},{5,4},{6,7},{7,6},{8,9},{9,8},{10,11... | collective-permute-start | bytes 199688 | tf_op jit(solution)/shard_map/ppermute | solution.py:17
  48.3 1.4 %collective-permute-start.9 = (f32[256,65]{0,1:T(8,128)S(1)}, f32[256,65]{0,1:T(8,128)S(1)}, u32[]{:S(2)}, u32[]{:S(2)}) collective-permute-start(f32[256,65]{0,1:T(8,128)S(1)} %pad_maximum_fusion.5), channel_id=1, source_target_pairs={{0,1},{1,0},{2,3},{3,2},{4,5},{5,4},{6,7},{7,6},{8,9},{9,8},{10,11... | collective-permute-start | bytes 199688 | tf_op jit(solution)/shard_map/ppermute | solution.py:17
  48.4 5.2 %collective-permute-start.8 = (f32[256,65]{0,1:T(8,128)S(1)}, f32[256,65]{0,1:T(8,128)S(1)}, u32[]{:S(2)}, u32[]{:S(2)}) collective-permute-start(f32[256,65]{0,1:T(8,128)S(1)} %fusion.113), channel_id=1, source_target_pairs={{0,2},{1,3},{2,0},{3,1},{4,6},{5,7},{6,4},{7,5},{8,10},{9,11},{10,... | collective-permute-start | bytes 199688 | tf_op jit(solution)/shard_map/ppermute | solution.py:17
  49.6 5.1 %collective-permute-start.10 = (f32[256,65]{0,1:T(8,128)S(1)}, f32[256,65]{0,1:T(8,128)S(1)}, u32[]{:S(2)}, u32[]{:S(2)}) collective-permute-start(f32[256,65]{0,1:T(8,128)S(1)} %fusion.112), channel_id=1, source_target_pairs={{0,2},{1,3},{2,0},{3,1},{4,6},{5,7},{6,4},{7,5},{8,10},{9,11},{10,... | collective-permute-start | bytes 199688 | tf_op jit(solution)/shard_map/ppermute | solution.py:17
  56.0 5.3 %collective-permute-start.11 = (f32[512,64]{0,1:T(8,128)S(1)}, f32[512,64]{0,1:T(8,128)S(1)}, u32[]{:S(2)}, u32[]{:S(2)}) collective-permute-start(f32[512,64]{0,1:T(8,128)S(1)} %slice_select_fusion), channel_id=1, source_target_pairs={{0,4},{4,0},{8,12},{12,8},{16,20},{20,16},{24,28},{28,24},{32,36},... | collective-permute-start | bytes 393224 | tf_op jit(solution)/shard_map/ppermute | solution.py:17
  61.4 4.4 %collective-permute-start.12 = (f32[256,64]{0,1:T(8,128)S(1)}, f32[256,64]{0,1:T(8,128)S(1)}, u32[]{:S(2)}, u32[]{:S(2)}) collective-permute-start(f32[256,64]{0,1:T(8,128)S(1)} %slice_select_fusion.1), channel_id=1, source_target_pairs={{0,64},{4,68},{8,72},{12,76},{16,80},{20,84},{24,88},{28,92},{32,9... | collective-permute-start | bytes 196616 | tf_op jit(solution)/shard_map/ppermute | solution.py:17
  65.7 5.6 %collective-permute-start.13 = (f32[256,64]{0,1:T(8,128)S(1)}, f32[256,64]{0,1:T(8,128)S(1)}, u32[]{:S(2)}, u32[]{:S(2)}) collective-permute-start(f32[256,64]{0,1:T(8,128)S(1)} %select_add_fusion.1), channel_id=1, source_target_pairs={{0,8},{4,12},{8,0},{12,4},{16,24},{20,28},{24,16},{28,20},{32,40},... | collective-permute-start | bytes 196616 | tf_op jit(solution)/shard_map/ppermute | solution.py:17
  71.3 8.3 %collective-permute-start.14 = (f32[256,64]{0,1:T(8,128)S(1)}, f32[256,64]{0,1:T(8,128)S(1)}, u32[]{:S(2)}, u32[]{:S(2)}) collective-permute-start(f32[256,64]{0,1:T(8,128)S(1)} %add.139), channel_id=1, source_target_pairs={{0,24},{4,28},{8,16},{12,20},{16,8},{20,12},{24,0},{28,4},{32,56},... | collective-permute-start | bytes 196616 | tf_op jit(solution)/shard_map/ppermute | solution.py:17
  79.6 5.9 %collective-permute-start.15 = (f32[256,64]{0,1:T(8,128)S(1)}, f32[256,64]{0,1:T(8,128)S(1)}, u32[]{:S(2)}, u32[]{:S(2)}) collective-permute-start(f32[256,64]{0,1:T(8,128)S(1)} %add.140), channel_id=1, source_target_pairs={{0,32},{4,36},{8,40},{12,44},{16,48},{20,52},{24,56},{28,60},{32,0... | collective-permute-start | bytes 196616 | tf_op jit(solution)/shard_map/ppermute | solution.py:17
  85.5 5.9 %collective-permute-start.16 = (f32[256,64]{0,1:T(8,128)S(1)}, f32[256,64]{0,1:T(8,128)S(1)}, u32[]{:S(2)}, u32[]{:S(2)}) collective-permute-start(f32[256,64]{0,1:T(8,128)S(1)} %add.141), channel_id=1, source_target_pairs={{0,128},{4,132},{8,136},{12,140},{16,144},{20,148},{24,152},{28,15... | collective-permute-start | bytes 196616 | tf_op jit(solution)/shard_map/ppermute | solution.py:17
  91.4 4.4 %collective-permute-start.17 = (f32[256,64]{0,1:T(8,128)S(1)}, f32[256,64]{0,1:T(8,128)S(1)}, u32[]{:S(2)}, u32[]{:S(2)}) collective-permute-start(f32[256,64]{0,1:T(8,128)S(1)} %add.142), channel_id=1, source_target_pairs={{0,64},{4,68},{8,72},{12,76},{16,80},{20,84},{24,88},{28,92},{32,9... | collective-permute-start | bytes 196616 | tf_op jit(solution)/shard_map/ppermute | solution.py:17
  95.8 5.1 %collective-permute-start.18 = (f32[512,64]{0,1:T(8,128)S(1)}, f32[512,64]{0,1:T(8,128)S(1)}, u32[]{:S(2)}, u32[]{:S(2)}) collective-permute-start(f32[512,64]{0,1:T(8,128)S(1)} %pad_maximum_fusion.3), channel_id=1, source_target_pairs={{0,4},{4,0},{8,12},{12,8},{16,20},{20,16},{24,28},{28,24},{32,36},... | collective-permute-start | bytes 393224 | tf_op jit(solution)/shard_map/ppermute | solution.py:17
